TPU v7x, 32 devices: a whole 2x2x4 slice. The times are simulated.
32 devices in a mesh: dp: 8 (over y, x, core), tensor: 4 (over z).
Axes of the slice: x: 2, y: 2, z: 4, core: 2. Of those that a mesh axis runs over, the one named last changes fastest.
Arguments:
- tokens: bfloat16 [16384, 2048], P(('dp', 'tensor')), may hold values from -6 to 6
- doc_start: int32 [16384], P('dp'), may hold values from 0 to 1, as said below
- piece_ids: int32 [16384], P('dp'), may hold values from 0 to 64, as said below
- attn_gain: float32 [2048], P('dp'), may hold values from 0.5 to 1.5
- w_query: float32 [2048, 2048], P('dp', 'tensor'), may hold values from -0.125 to 0.125
- key_projection: float32 [2048, 1024], P('dp', 'tensor'), may hold values from -0.125 to 0.125
- value_projection: float32 [2048, 1024], P('dp', 'tensor'), may hold values from -0.125 to 0.125
- query_gain: float32 [128], P('dp'), may hold values from 0.5 to 1.5
- key_gain: float32 [128], P('dp'), may hold values from 0.5 to 1.5
- w_out: float32 [2048, 2048], P('tensor', 'dp'), may hold values from -1 to 1
- mlp_gain: float32 [2048], P('dp'), may hold values from 0.5 to 1.5
- w_gate: float32 [2048, 6144], P('dp', 'tensor'), may hold values from -0.125 to 0.125
- w_up: float32 [2048, 6144], P('dp', 'tensor'), may hold values from -0.125 to 0.125
- w_down: float32 [6144, 2048], P('tensor', 'dp'), may hold values from -0.078125 to 0.078125
- out_grad: bfloat16 [16384, 2048], P(('dp', 'tensor')), may hold values from -6 to 6
Outputs:
- layer_out: bfloat16 [16384, 2048], P(('dp', 'tensor'))
- grad_tokens: float32 [16384, 2048], P(('dp', 'tensor'))
- grad_attn_gain: float32 [2048], P('dp')
- grad_query: float32 [2048, 2048], P('dp', 'tensor')
- grad_key: float32 [2048, 1024], P('dp', 'tensor')
- grad_value: float32 [2048, 1024], P('dp', 'tensor')
- grad_query_gain: float32 [128], P('dp')
- grad_key_gain: float32 [128], P('dp')
- grad_out: float32 [2048, 2048], P('tensor', 'dp')
- grad_mlp_gain: float32 [2048], P('dp')
- grad_gate: float32 [2048, 6144], P('dp', 'tensor')
- grad_up: float32 [2048, 6144], P('dp', 'tensor')
- grad_down: float32 [6144, 2048], P('tensor', 'dp')
Inputs may be any that keep to these rules, and one draw needn't show every extreme that they name: `doc_start`: 1 exactly at the first token of each document; documents start only at multiples of 256 within a sequence of 2048, and every sequence's first token starts one. `piece_ids`: an image piece is an aligned block of 256 tokens with one positive number that no other block carries; the last block of the array is an image piece.
All inputs are finite; a program needn't handle non-finite values.
Results may differ from a plain program's by a relative error of at most 0.024.
Values may be sent and summed in bfloat16 or wider, within the bound.
No kernel may reach another device: no remote copies, remote signals or barrier semaphores. Data moves between devices by JAX's collectives and lax.ppermute only.
A program may use at most 256 MiB of HBM per device.

v0:
```python
import jax
import jax.numpy as jnp
from jax import lax
from jax.sharding import PartitionSpec as P

HEAD_SIZE = 128
SEQUENCE_TOKENS = 2048
QB = 512


EPSILON = 1e-06
ROPE_BASE = 1000000.0
MASKED = -1e30
CONTRACT_ROWS = (((0,), (0,)), ((), ()))
CONTRACT_COLS = (((1,), (1,)), ((), ()))


def rms_scale(row_data, gain_vec):
    inverse = lax.rsqrt(jnp.mean(row_data * row_data, axis=-1, keepdims=True) + EPSILON)
    return row_data * inverse * gain_vec


def rope_tables(length, head_width):
    half_width = head_width // 2
    frequency = jnp.power(
        ROPE_BASE, -jnp.arange(half_width, dtype=jnp.float32) * (2.0 / head_width)
    )
    angles = jnp.arange(length, dtype=jnp.float32)[:, None] * frequency[None, :]
    return (jnp.cos(angles), jnp.sin(angles))


def head_norm_rotary(raw_heads, gain_vec, cosine_lookup, sine_lookup):
    normalized_input = rms_scale(raw_heads, gain_vec)
    half_width = raw_heads.shape[-1] // 2
    first_half = normalized_input[..., :half_width]
    second = normalized_input[..., half_width:]
    cos_part = cosine_lookup[:, None, :]
    sin_part = sine_lookup[:, None, :]
    return jnp.concatenate(
        [first_half * cos_part - second * sin_part, second * cos_part + first_half * sin_part],
        axis=-1,
    )


def block_mask(doc_start, piece_ids, row_start, row_count):
    doc_ids = jnp.cumsum(doc_start)
    key_pos = jnp.arange(doc_ids.shape[0], dtype=jnp.int32)
    query_pos = row_start + jnp.arange(row_count, dtype=jnp.int32)
    query_doc = lax.dynamic_slice_in_dim(doc_ids, row_start, row_count)
    query_piece = lax.dynamic_slice_in_dim(piece_ids, row_start, row_count)
    causal = (key_pos[None, :] <= query_pos[:, None]) & (query_doc[:, None] == doc_ids[None, :])
    inside = (query_piece[:, None] == piece_ids[None, :]) & (query_piece[:, None] > 0)
    return causal | inside


def attend_sequence(query_tensor, key_rows, value_tensor, seq_starts, seq_pieces):
    length = key_rows.shape[0]
    scale = query_tensor.shape[-1] ** (-0.5)

    def one_block(row_start):
        q_rows = lax.dynamic_slice_in_dim(query_tensor, row_start, QB, 0)
        allowed = block_mask(seq_starts, seq_pieces, row_start, QB)
        scores = (
            jnp.einsum("qkgd,skd->kgqs", q_rows, key_rows, preferred_element_type=jnp.float32)
            * scale
        )
        scores = jnp.where(allowed[None, None], scores, MASKED)
        row_max = jnp.max(scores, axis=-1, keepdims=True)
        exponent = jnp.exp(scores - row_max)
        row_total = jnp.sum(exponent, axis=-1, keepdims=True)
        attn_probs = (exponent / row_total).astype(jnp.bfloat16)
        block_out = jnp.einsum(
            "kgqs,skd->qkgd", attn_probs, value_tensor, preferred_element_type=jnp.float32
        )
        return (block_out, (row_max + jnp.log(row_total))[..., 0])

    block_starts = jnp.arange(length // QB, dtype=jnp.int32) * QB
    outs_f, log_totals = lax.map(one_block, block_starts)
    return (outs_f.reshape(length, -1), log_totals)


def attend_back(
    query_tensor, key_rows, value_tensor, grad_rows, log_totals, seq_starts, seq_pieces
):
    length = key_rows.shape[0]
    scale = query_tensor.shape[-1] ** (-0.5)

    def one_block(carried, inputs):
        row_start, block_lse = inputs
        q_rows = lax.dynamic_slice_in_dim(query_tensor, row_start, QB, 0)
        g_rows = lax.dynamic_slice_in_dim(grad_rows, row_start, QB, 0)
        allowed = block_mask(seq_starts, seq_pieces, row_start, QB)
        scores = (
            jnp.einsum("qkgd,skd->kgqs", q_rows, key_rows, preferred_element_type=jnp.float32)
            * scale
        )
        attn_probs = jnp.where(allowed[None, None], jnp.exp(scores - block_lse[..., None]), 0.0)
        d_probs = jnp.einsum(
            "qkgd,skd->kgqs", g_rows, value_tensor, preferred_element_type=jnp.float32
        )
        d_scores = attn_probs * (d_probs - jnp.sum(attn_probs * d_probs, axis=-1, keepdims=True))
        d_scores_b = d_scores.astype(jnp.bfloat16)
        d_query = (
            jnp.einsum("kgqs,skd->qkgd", d_scores_b, key_rows, preferred_element_type=jnp.float32)
            * scale
        )
        d_key = (
            carried[0]
            + jnp.einsum("kgqs,qkgd->skd", d_scores_b, q_rows, preferred_element_type=jnp.float32)
            * scale
        )
        d_value = carried[1] + jnp.einsum(
            "kgqs,qkgd->skd",
            attn_probs.astype(jnp.bfloat16),
            g_rows,
            preferred_element_type=jnp.float32,
        )
        return ((d_key, d_value), d_query)

    block_starts = jnp.arange(length // QB, dtype=jnp.int32) * QB
    zero_kv = jnp.zeros(key_rows.shape, jnp.float32)
    (d_key, d_value), d_query = lax.scan(one_block, (zero_kv, zero_kv), (block_starts, log_totals))
    return (d_query.reshape(query_tensor.shape), d_key, d_value)


def on_device(
    tokens,
    doc_start,
    piece_ids,
    attn_gain,
    w_query,
    key_projection,
    value_projection,
    query_gain,
    key_gain,
    w_out,
    mlp_gain,
    w_gate,
    w_up,
    w_down,
    out_grad,
):
    bf16 = jnp.bfloat16
    f32 = jnp.float32
    tok_rows = tokens.astype(f32)
    total_rows = doc_start.shape[0]
    seq_count = total_rows // SEQUENCE_TOKENS
    cosine_lookup, sine_lookup = rope_tables(SEQUENCE_TOKENS, HEAD_SIZE)
    seq_starts = doc_start.reshape(seq_count, SEQUENCE_TOKENS)
    seq_pieces = piece_ids.reshape(seq_count, SEQUENCE_TOKENS)
    wq_b, wk_b, wv_b, wo_b, ga_b, gq_b, gk_b = (
        lax.all_gather(w_query.astype(bf16), "dp", axis=0, tiled=True),
        lax.all_gather(key_projection.astype(bf16), "dp", axis=0, tiled=True),
        lax.all_gather(value_projection.astype(bf16), "dp", axis=0, tiled=True),
        lax.all_gather(w_out.astype(bf16), "dp", axis=1, tiled=True),
        lax.all_gather(attn_gain.astype(bf16), "dp", axis=0, tiled=True),
        lax.all_gather(query_gain.astype(bf16), "dp", axis=0, tiled=True),
        lax.all_gather(key_gain.astype(bf16), "dp", axis=0, tiled=True),
    )
    w_qkv = jnp.concatenate([wq_b, wk_b, wv_b], axis=1)
    q_width = wq_b.shape[1]
    kv_width = wk_b.shape[1]
    heads_local = q_width // HEAD_SIZE
    kv_local = kv_width // HEAD_SIZE
    heads_per_group = heads_local // kv_local
    attn_g = ga_b.astype(f32)
    query_norm_gain = gq_b.astype(f32)
    gain_k = gk_b.astype(f32)
    normalized_input = rms_scale(tok_rows, attn_g).astype(bf16)
    gathered = lax.all_gather(normalized_input, "tensor", axis=0, tiled=True)
    projected = jnp.dot(gathered, w_qkv, preferred_element_type=f32)
    query_unrotated = projected[:, :q_width].reshape(
        seq_count, SEQUENCE_TOKENS, heads_local, HEAD_SIZE
    )
    key_unrotated = projected[:, q_width : q_width + kv_width].reshape(
        seq_count, SEQUENCE_TOKENS, kv_local, HEAD_SIZE
    )
    v_b = (
        projected[:, q_width + kv_width :]
        .astype(bf16)
        .reshape(seq_count, SEQUENCE_TOKENS, kv_local, HEAD_SIZE)
    )

    def rope_query(raw_heads, gain_vec):
        return head_norm_rotary(raw_heads, gain_vec, cosine_lookup, sine_lookup)

    q_b = rope_query(query_unrotated, query_norm_gain).astype(bf16)
    k_b = rope_query(key_unrotated, gain_k).astype(bf16)
    q_grouped = q_b.reshape(seq_count, SEQUENCE_TOKENS, kv_local, heads_per_group, HEAD_SIZE)

    def forward_seq(inputs):
        return attend_sequence(inputs[0], inputs[1], inputs[2], inputs[3], inputs[4])

    attn_f, log_totals = lax.map(forward_seq, (q_grouped, k_b, v_b, seq_starts, seq_pieces))
    attended = attn_f.reshape(total_rows, q_width).astype(bf16)
    wg_b, wu_b, wd_b, gm_b = (
        lax.all_gather(w_gate.astype(bf16), "dp", axis=0, tiled=True),
        lax.all_gather(w_up.astype(bf16), "dp", axis=0, tiled=True),
        lax.all_gather(w_down.astype(bf16), "dp", axis=1, tiled=True),
        lax.all_gather(mlp_gain.astype(bf16), "dp", axis=0, tiled=True),
    )
    w_gu = jnp.concatenate([wg_b, wu_b], axis=1)
    hidden_width = wg_b.shape[1]
    mlp_g = gm_b.astype(f32)
    residual = tok_rows + lax.psum_scatter(
        jnp.dot(attended, wo_b, preferred_element_type=f32).astype(jnp.bfloat16),
        "tensor",
        scatter_dimension=0,
        tiled=True,
    ).astype(jnp.float32)
    normed_two = rms_scale(residual, mlp_g).astype(bf16)
    gathered_two = lax.all_gather(normed_two, "tensor", axis=0, tiled=True)
    gate_up = jnp.dot(gathered_two, w_gu, preferred_element_type=f32)
    gate_pre = gate_up[:, :hidden_width]
    up_pre = gate_up[:, hidden_width:]
    hidden_b = (jax.nn.silu(gate_pre) * up_pre).astype(bf16)
    layer_out = (
        residual
        + lax.psum_scatter(
            jnp.dot(hidden_b, wd_b, preferred_element_type=f32).astype(jnp.bfloat16),
            "tensor",
            scatter_dimension=0,
            tiled=True,
        ).astype(jnp.float32)
    ).astype(bf16)
    wg_c, wu_c, wd_back = (
        lax.all_gather(w_gate.astype(bf16), "dp", axis=0, tiled=True),
        lax.all_gather(w_up.astype(bf16), "dp", axis=0, tiled=True),
        lax.all_gather(w_down.astype(bf16), "dp", axis=1, tiled=True),
    )
    w_gu_back = jnp.concatenate([wg_c, wu_c], axis=1)
    grad_whole = lax.all_gather(out_grad, "tensor", axis=0, tiled=True)
    grad_down = lax.dot_general(hidden_b, grad_whole, CONTRACT_ROWS, preferred_element_type=f32)
    d_hidden = lax.dot_general(grad_whole, wd_back, CONTRACT_COLS, preferred_element_type=f32)

    def swiglu(gate_in, up_in):
        return jax.nn.silu(gate_in) * up_in

    swiglu_value, swiglu_back = jax.vjp(swiglu, gate_pre, up_pre)
    d_gate, d_up = swiglu_back(d_hidden)
    d_gate_up = jnp.concatenate([d_gate, d_up], axis=1).astype(bf16)
    grad_gate_up = lax.dot_general(
        gathered_two, d_gate_up, CONTRACT_ROWS, preferred_element_type=f32
    )
    rows_b = d_gate_up
    d_normed_two = lax.psum_scatter(
        lax.dot_general(rows_b, w_gu_back, CONTRACT_COLS, preferred_element_type=f32).astype(
            jnp.bfloat16
        ),
        "tensor",
        scatter_dimension=0,
        tiled=True,
    ).astype(jnp.float32)
    norm_value, norm_two_back = jax.vjp(rms_scale, residual, mlp_g)
    d_resid_norm, d_mlp_gain = norm_two_back(d_normed_two)
    d_residual = out_grad.astype(f32) + d_resid_norm
    wq_c, wk_c, wv_c, wo_back = (
        lax.all_gather(w_query.astype(bf16), "dp", axis=0, tiled=True),
        lax.all_gather(key_projection.astype(bf16), "dp", axis=0, tiled=True),
        lax.all_gather(value_projection.astype(bf16), "dp", axis=0, tiled=True),
        lax.all_gather(w_out.astype(bf16), "dp", axis=1, tiled=True),
    )
    w_qkv_back = jnp.concatenate([wq_c, wk_c, wv_c], axis=1)
    attn_grad_whole = lax.all_gather(d_residual.astype(bf16), "tensor", axis=0, tiled=True)
    grad_out = lax.dot_general(attended, attn_grad_whole, CONTRACT_ROWS, preferred_element_type=f32)
    d_attended = lax.dot_general(
        attn_grad_whole, wo_back, CONTRACT_COLS, preferred_element_type=f32
    ).astype(bf16)
    d_grouped = d_attended.reshape(seq_count, SEQUENCE_TOKENS, kv_local, heads_per_group, HEAD_SIZE)

    def back_seq(inputs):
        return attend_back(
            inputs[0], inputs[1], inputs[2], inputs[3], inputs[4], inputs[5], inputs[6]
        )

    d_query, d_key, d_value = lax.map(
        back_seq, (q_grouped, k_b, v_b, d_grouped, log_totals, seq_starts, seq_pieces)
    )
    query_value, query_back = jax.vjp(rope_query, query_unrotated, query_norm_gain)
    d_q_raw, d_query_gain = query_back(d_query.reshape(query_unrotated.shape))
    key_value, key_back = jax.vjp(rope_query, key_unrotated, gain_k)
    d_k_raw, d_key_gain = key_back(d_key)
    d_qkv = jnp.concatenate(
        [
            d_q_raw.reshape(total_rows, q_width),
            d_k_raw.reshape(total_rows, kv_width),
            d_value.reshape(total_rows, kv_width),
        ],
        axis=1,
    ).astype(bf16)
    grad_qkv = lax.dot_general(gathered, d_qkv, CONTRACT_ROWS, preferred_element_type=f32)
    rows_b = d_qkv
    d_normed = lax.psum_scatter(
        lax.dot_general(rows_b, w_qkv_back, CONTRACT_COLS, preferred_element_type=f32).astype(
            jnp.bfloat16
        ),
        "tensor",
        scatter_dimension=0,
        tiled=True,
    ).astype(jnp.float32)
    norm_one, norm_back = jax.vjp(rms_scale, tok_rows, attn_g)
    d_x_norm, d_attn_gain = norm_back(d_normed)
    grad_tokens = d_residual + d_x_norm
    owned = (
        lax.psum_scatter(
            grad_qkv[:, :q_width].astype(jnp.bfloat16), "dp", scatter_dimension=0, tiled=True
        ).astype(jnp.float32),
        lax.psum_scatter(
            grad_qkv[:, q_width : q_width + kv_width].astype(jnp.bfloat16),
            "dp",
            scatter_dimension=0,
            tiled=True,
        ).astype(jnp.float32),
        lax.psum_scatter(
            grad_qkv[:, q_width + kv_width :].astype(jnp.bfloat16),
            "dp",
            scatter_dimension=0,
            tiled=True,
        ).astype(jnp.float32),
        lax.psum_scatter(
            grad_out.astype(jnp.bfloat16), "dp", scatter_dimension=1, tiled=True
        ).astype(jnp.float32),
        lax.psum_scatter(
            grad_gate_up[:, :hidden_width].astype(jnp.bfloat16),
            "dp",
            scatter_dimension=0,
            tiled=True,
        ).astype(jnp.float32),
        lax.psum_scatter(
            grad_gate_up[:, hidden_width:].astype(jnp.bfloat16),
            "dp",
            scatter_dimension=0,
            tiled=True,
        ).astype(jnp.float32),
        lax.psum_scatter(
            grad_down.astype(jnp.bfloat16), "dp", scatter_dimension=1, tiled=True
        ).astype(jnp.float32),
        lax.psum_scatter(
            d_attn_gain.astype(jnp.bfloat16), "dp", scatter_dimension=0, tiled=True
        ).astype(jnp.float32),
        lax.psum_scatter(
            d_query_gain.astype(jnp.bfloat16), "dp", scatter_dimension=0, tiled=True
        ).astype(jnp.float32),
        lax.psum_scatter(
            d_key_gain.astype(jnp.bfloat16), "dp", scatter_dimension=0, tiled=True
        ).astype(jnp.float32),
        lax.psum_scatter(
            d_mlp_gain.astype(jnp.bfloat16), "dp", scatter_dimension=0, tiled=True
        ).astype(jnp.float32),
    )
    gains_sum = lax.psum((owned[7], owned[8], owned[9], owned[10]), "tensor")
    return (
        layer_out,
        grad_tokens,
        gains_sum[0],
        owned[0],
        owned[1],
        owned[2],
        gains_sum[1],
        gains_sum[2],
        owned[3],
        gains_sum[3],
        owned[4],
        owned[5],
        owned[6],
    )


def solution(mesh):
    return jax.shard_map(
        on_device,
        mesh=mesh,
        in_specs=(
            P(("dp", "tensor"), None),
            P("dp"),
            P("dp"),
            P("dp"),
            P("dp", "tensor"),
            P("dp", "tensor"),
            P("dp", "tensor"),
            P("dp"),
            P("dp"),
            P("tensor", "dp"),
            P("dp"),
            P("dp", "tensor"),
            P("dp", "tensor"),
            P("tensor", "dp"),
            P(("dp", "tensor"), None),
        ),
        out_specs=(
            P(("dp", "tensor"), None),
            P(("dp", "tensor"), None),
            P("dp"),
            P("dp", "tensor"),
            P("dp", "tensor"),
            P("dp", "tensor"),
            P("dp"),
            P("dp"),
            P("tensor", "dp"),
            P("dp"),
            P("dp", "tensor"),
            P("dp", "tensor"),
            P("tensor", "dp"),
        ),
        check_vma=False,
    )
```

profile of v0, /device:TPU:0, one launch (start us, length us, event | category | flops | bytes accessed | tf_op | source)
XLA Modules:
  0.0 2135.5 jit_solution(13192153790921202493)
XLA Ops:
  31.7 13.8 all-reduce.12
  53.7 13.4 all-gather.18.cloned.1.call-done
  69.3 23.6 %all-gather.20.cloned.1.call-done = bf16[2048,256]{1,0:T(8,128)(2,1)} async-done(((bf16[256,256]{1,0:T(8,128)(2,1)}), bf16[2048,256]{1,0:T(8,128)(2,1)}) %all-gather.20.cloned.1.call-update) | async-done | bytes 1048592 | tf_op jit(solution)/shard_map/all_gather | solution.py:154
  95.2 148.8 %all-gather.14.cloned.1.call-done = bf16[2048,2048]{1,0:T(8,128)(2,1)} async-done(((bf16[512,2048]{1,0:T(8,128)(2,1)}), bf16[2048,2048]{1,0:T(8,128)(2,1)}) %all-gather.14.cloned.1.call-update) | async-done | bytes 8388624 | tf_op jit(solution)/shard_map/all_gather | solution.py:170
  244.0 13.1 fusion.87
  289.3 86.2 %while.51 = (s32[]{:T(128)}, bf16[4,512,2,2,128]{4,1,3,2,0:T(8,128)(2,1)}, f32[4,2,2,512]{3,2,1,0:T(2,128)}, s32[4]{0:T(128)S(1)}, s32[17,1]{0,1:T(1,128)S(1)}, ...) while((s32[]{:T(128)}, ...), condition=%wide.region_8.9_spmd, body=%wide.region_5.0_spmd.sunk | while | flops 2204107776 | bytes 58313080 | solution.py:78
  409.9 128.8 %reduce-scatter.12.cloned.1.call-done = bf16[512,2048]{1,0:T(8,128)(2,1)} async-done(((bf16[2048,2048]{1,0:T(8,128)(2,1)}), bf16[512,2048]{1,0:T(8,128)(2,1)}) %reduce-scatter.12.cloned.1.call-update) | async-done | bytes 2097168 | tf_op jit(solution)/shard_map/reduce_scatter | solution.py:205
  548.0 38.5 %all-gather.26.cloned.1.call-done = bf16[2048,1536]{1,0:T(8,128)(2,1)} async-done(((bf16[256,1536]{1,0:T(8,128)(2,1)}), bf16[2048,1536]{1,0:T(8,128)(2,1)}) %all-gather.26.cloned.1.call-update) | async-done | bytes 6291472 | tf_op jit(solution)/shard_map/all_gather | solution.py:197
  592.4 41.5 %all-gather.28.cloned.1.call-done = bf16[2048,1536]{1,0:T(8,128)(2,1)} async-done(((bf16[256,1536]{1,0:T(8,128)(2,1)}), bf16[2048,1536]{1,0:T(8,128)(2,1)}) %all-gather.28.cloned.1.call-update) | async-done | bytes 6291472 | tf_op jit(solution)/shard_map/all_gather | solution.py:198
  639.8 145.9 %all-gather.24.cloned.1.call-done = bf16[2048,2048]{1,0:T(8,128)(2,1)} async-done(((bf16[512,2048]{1,0:T(8,128)(2,1)}), bf16[2048,2048]{1,0:T(8,128)(2,1)}) %all-gather.24.cloned.1.call-update) | async-done | bytes 8388624 | tf_op jit(solution)/shard_map/all_gather | solution.py:212
  785.6 34.1 %fusion.88 = f32[2048,3072]{1,0:T(8,128)} fusion(bf16[2048,2048]{1,0:T(8,128)(2,1)} %all-gather.24.cloned.1.call-done, bf16[2048,3072]{1,0:T(8,128)(2,1)} %constant_dynamic-update-slice_fusion.3), kind=kOutput, calls=%fused_computation.175 | convolution fusion | flops 25769803776 | bytes 46137344 | tf_op jit(solution)/shard_map/dot_general | solution.py:213
  832.2 151.2 %all-gather.32.cloned.1.call-done = bf16[2048,2048]{1,0:T(8,128)(2,1)} async-done(((bf16[512,2048]{1,0:T(8,128)(2,1)}), bf16[2048,2048]{1,0:T(8,128)(2,1)}) %all-gather.32.cloned.1.call-update) | async-done | bytes 8388624 | tf_op jit(solution)/shard_map/all_gather | solution.py:232
  983.4 30.2 %fusion.53 = (bf16[2048,1536]{1,0:T(8,128)(2,1)}, bf16[2048,1536]{1,0:T(8,128)(2,1)}, bf16[2048,1536]{1,0:T(8,128)(2,1)}) fusion(f32[2048,3072]{1,0:T(8,128)} %fusion.88, bf16[2048,2048]{1,0:T(8,128)(2,1)} %all-gather.32.cloned.1.call-done, bf16[1536,2048]{1,0:T(8,128)(2,1)} %all-gather.30.cloned.1.call-done), kind=kOutput, calls=%fused_computation.70 | convolution fusion | flops 12935233536 | bytes 58720256 | tf_op jit(solution)/shard_map/dot_general | solution.py:234
  1013.6 33.7 %fusion.56 = bf16[2048,2048]{1,0:T(8,128)(2,1)} fusion(bf16[2048,3072]{1,0:T(8,128)(2,1)} %constant_dynamic-update-slice_fusion.3, bf16[2048,1536]{1,0:T(8,128)(2,1)} %get-tuple-element.538, bf16[2048,1536]{1,0:T(8,128)(2,1)} %get-tuple-element.537), kind=kOutput, calls=%fused_computation.87 | convolution fusion | flops 25799163904 | bytes 33554432 | tf_op jit(solution)/shard_map/dot_general | solution.py:247
  1047.6 142.7 %reduce-scatter.16.cloned.1.call-done = bf16[512,2048]{1,0:T(8,128)(2,1)} async-done(((bf16[2048,2048]{1,0:T(8,128)(2,1)}), bf16[512,2048]{1,0:T(8,128)(2,1)}) %reduce-scatter.16.cloned.1.call-update) | async-done | bytes 2097168 | tf_op jit(solution)/shard_map/reduce_scatter | solution.py:246
  1199.4 32.0 %convolution_convert_fusion = bf16[2048,3072]{1,0:T(8,128)(2,1)S(1)} fusion(bf16[2048,2048]{1,0:T(8,128)(2,1)} %all-gather.24.cloned.1.call-done, bf16[2048,1536]{1,0:T(8,128)(2,1)} %get-tuple-element.538, bf16[2048,1536]{1,0:T(8,128)(2,1)} %get-tuple-element.537), kind=kOutput, calls=%fused_computation.76 | convolution fusion | flops 25801261056 | bytes 33554432 | tf_op jit(solution)/shard_map/dot_general | solution.py:242
  1237.3 19.2 convolution_convert_fusion.4
  1256.6 93.2 %all-gather.34.cloned.1.call-done = bf16[2048,2048]{1,0:T(8,128)(2,1)} async-done(((bf16[512,2048]{1,0:T(8,128)(2,1)}), bf16[2048,2048]{1,0:T(8,128)(2,1)}) %all-gather.34.cloned.1.call-update) | async-done | bytes 8388624 | tf_op jit(solution)/shard_map/all_gather | solution.py:264
  1359.7 265.6 %while.52 = (s32[]{:T(128)}, f32[2048,2,128]{0,2,1:T(8,128)S(1)}, f32[2048,2,128]{0,2,1:T(8,128)}, f32[4,512,2,2,128]{4,1,0,3,2:T(8,128)}, s32[4]{0:T(128)S(1)},...) while((s32[]{:T(128)}, f32[2048,2,128]{0,2,1:T(8,128)S(1)}, ...), condition=%wide.region_16.17_spmd.clone, body=%wide.region_14.16_spmd.clone.sunk | while | flops 5440799744 | bytes 186755056 | solution.py:122
  1376.3 13.4 fusion.144
  1442.2 13.4 fusion.144
  1455.7 12.8 fusion.145
  1509.7 13.5 fusion.144
  1575.6 13.4 fusion.144
  1677.3 13.7 convolution_convert_fusion.1
  1691.0 19.3 convolution_convert_fusion.2
  1720.8 15.6 reduce-scatter.24.cloned.1.call-done
  1738.1 42.8 %reduce-scatter.26.cloned.1.call-done = bf16[512,256]{1,0:T(8,128)(2,1)} async-done(((bf16[512,2048]{1,0:T(8,128)(2,1)}), bf16[512,256]{1,0:T(8,128)(2,1)}) %reduce-scatter.26.cloned.1.call-update) | async-done | bytes 262160 | tf_op jit(solution)/shard_map/reduce_scatter | solution.py:320
  1782.7 43.1 %reduce-scatter.20.cloned.1.call-done = bf16[256,512]{1,0:T(8,128)(2,1)} async-done(((bf16[2048,512]{1,0:T(8,128)(2,1)}), bf16[256,512]{1,0:T(8,128)(2,1)}) %reduce-scatter.20.cloned.1.call-update) | async-done | bytes 262160 | tf_op jit(solution)/shard_map/reduce_scatter | solution.py:305
  1827.6 145.2 %reduce-scatter.18.cloned.1.call-done = bf16[512,2048]{1,0:T(8,128)(2,1)} async-done(((bf16[2048,2048]{1,0:T(8,128)(2,1)}), bf16[512,2048]{1,0:T(8,128)(2,1)}) %reduce-scatter.18.cloned.1.call-update) | async-done | bytes 2097168 | tf_op jit(solution)/shard_map/reduce_scatter | solution.py:293
  1976.1 14.1 all-reduce.11
  2003.3 117.3 %reduce-scatter.14.cloned.1.call-done = bf16[512,2048]{1,0:T(8,128)(2,1)} async-done(((bf16[2048,2048]{1,0:T(8,128)(2,1)}), bf16[512,2048]{1,0:T(8,128)(2,1)}) %reduce-scatter.14.cloned.1.call-update) | async-done | bytes 2097168 | tf_op jit(solution)/shard_map/reduce_scatter | solution.py:219
  (416 shorter events, 520.1 us)
Async XLA Ops:
  7.2 43.4 %all-gather.16.cloned.1.call-start = ((), (), s32[]{:S(2)}) async-start(), calls=%async_computation.12 | async-start | bytes 2359296 | tf_op jit(solution)/shard_map/all_gather | solution.py:152
  9.2 57.9 %all-gather.18.cloned.1.call-start = ((), (), s32[]{:S(2)}) async-start(), calls=%async_computation.13 | async-start | bytes 1179648 | tf_op jit(solution)/shard_map/all_gather | solution.py:153
  10.9 82.0 %all-gather.20.cloned.1.call-start = ((), (), s32[]{:S(2)}) async-start(), calls=%async_computation.14 | async-start | bytes 1179648 | tf_op jit(solution)/shard_map/all_gather | solution.py:154
  12.6 231.4 %all-gather.14.cloned.1.call-start = ((), (), s32[]{:S(2)}) async-start(), calls=%async_computation.11 | async-start | bytes 10485760 | tf_op jit(solution)/shard_map/all_gather | solution.py:170
  28.9 356.8 %all-gather.22.cloned.1.call-start = ((), (), s32[]{:S(2)}) async-start(), calls=%async_computation.15 | async-start | bytes 2359296 | tf_op jit(solution)/shard_map/all_gather | solution.py:155
  29.8 508.9 %reduce-scatter.12.cloned.1.call-start = ((), (), s32[]{:S(2)}) async-start(), calls=%async_computation.16 | async-start | bytes 10485760 | tf_op jit(solution)/shard_map/reduce_scatter | solution.py:205
  49.7 232.6 %copy-start.21 = (f32[2048,64]{0,1:T(8,128)}, f32[2048,64]{0,1:T(8,128)S(1)}, u32[]{:S(2)}) copy-start(f32[2048,64]{0,1:T(8,128)S(1)} %copy.83) | copy-start | bytes 1572868
  50.1 232.3 %copy-start.23 = (f32[2048,64]{0,1:T(8,128)}, f32[2048,64]{0,1:T(8,128)S(1)}, u32[]{:S(2)}) copy-start(f32[2048,64]{0,1:T(8,128)S(1)} %copy.84) | copy-start | bytes 1572868
  395.8 190.8 %all-gather.26.cloned.1.call-start = ((), (), s32[]{:S(2)}) async-start(), calls=%async_computation.18 | async-start | bytes 7077888 | tf_op jit(solution)/shard_map/all_gather | solution.py:197
  398.4 235.5 %all-gather.28.cloned.1.call-start = ((), (), s32[]{:S(2)}) async-start(), calls=%async_computation.19 | async-start | bytes 7077888 | tf_op jit(solution)/shard_map/all_gather | solution.py:198
  400.8 384.8 %all-gather.24.cloned.1.call-start = ((), (), s32[]{:S(2)}) async-start(), calls=%async_computation.17 | async-start | bytes 10485760 | tf_op jit(solution)/shard_map/all_gather | solution.py:212
  544.7 287.4 %all-gather.30.cloned.1.call-start = ((), (), s32[]{:S(2)}) async-start(), calls=%async_computation.20 | async-start | bytes 7077888 | tf_op jit(solution)/shard_map/all_gather | solution.py:199
  547.2 436.1 %all-gather.32.cloned.1.call-start = ((), (), s32[]{:S(2)}) async-start(), calls=%async_computation.22 | async-start | bytes 10485760 | tf_op jit(solution)/shard_map/all_gather | solution.py:232
  548.0 642.3 %reduce-scatter.16.cloned.1.call-start = ((), (), s32[]{:S(2)}) async-start(), calls=%async_computation.23 | async-start | bytes 10485760 | tf_op jit(solution)/shard_map/reduce_scatter | solution.py:246
  1047.3 302.4 %all-gather.34.cloned.1.call-start = ((), (), s32[]{:S(2)}) async-start(), calls=%async_computation.24 | async-start | bytes 10485760 | tf_op jit(solution)/shard_map/all_gather | solution.py:264
  1199.4 512.3 %reduce-scatter.28.cloned.1.call-start = ((), (), s32[]{:S(2)}) async-start(), calls=%async_computation.30 | async-start | bytes 7077888 | tf_op jit(solution)/shard_map/reduce_scatter | solution.py:323
  1236.6 477.7 %reduce-scatter.30.cloned.1.call-start = ((), (), s32[]{:S(2)}) async-start(), calls=%async_computation.31 | async-start | bytes 7077888 | tf_op jit(solution)/shard_map/reduce_scatter | solution.py:329
  1237.2 479.6 %reduce-scatter.32.cloned.1.call-start = ((), (), s32[]{:S(2)}) async-start(), calls=%async_computation.32 | async-start | bytes 7077888 | tf_op jit(solution)/shard_map/reduce_scatter | solution.py:335
  1256.5 462.7 %reduce-scatter.22.cloned.1.call-start = ((), (), s32[]{:S(2)}) async-start(), calls=%async_computation.27 | async-start | bytes 1179648 | tf_op jit(solution)/shard_map/reduce_scatter | solution.py:308
  1663.9 72.6 %reduce-scatter.24.cloned.1.call-start = ((), (), s32[]{:S(2)}) async-start(), calls=%async_computation.28 | async-start | bytes 1179648 | tf_op jit(solution)/shard_map/reduce_scatter | solution.py:314
  1664.4 116.5 %reduce-scatter.26.cloned.1.call-start = ((), (), s32[]{:S(2)}) async-start(), calls=%async_computation.29 | async-start | bytes 2359296 | tf_op jit(solution)/shard_map/reduce_scatter | solution.py:320
  1673.9 151.9 %reduce-scatter.20.cloned.1.call-start = ((), (), s32[]{:S(2)}) async-start(), calls=%async_computation.26 | async-start | bytes 2359296 | tf_op jit(solution)/shard_map/reduce_scatter | solution.py:305
  1677.2 295.6 %reduce-scatter.18.cloned.1.call-start = ((), (), s32[]{:S(2)}) async-start(), calls=%async_computation.25 | async-start | bytes 10485760 | tf_op jit(solution)/shard_map/reduce_scatter | solution.py:293
  1691.0 429.6 %reduce-scatter.14.cloned.1.call-start = ((), (), s32[]{:S(2)}) async-start(), calls=%async_computation.21 | async-start | bytes 10485760 | tf_op jit(solution)/shard_map/reduce_scatter | solution.py:219
  1711.6 261.2 %copy-start.4 = (bf16[512,2048]{1,0:T(8,128)(2,1)S(1)}, bf16[512,2048]{1,0:T(8,128)(2,1)}, u32[]{:S(2)}) copy-start(bf16[512,2048]{1,0:T(8,128)(2,1)} %param.19) | copy-start | bytes 6291460
  1711.7 261.2 %copy-start.50 = (f32[8,1,256]{2,1,0:T(1,128)S(1)}, f32[8,1,256]{2,1,0:T(1,128)}, u32[]{:S(2)}) copy-start(f32[8,1,256]{2,1,0:T(1,128)} %copy-done.49) | copy-start | bytes 24580
  1711.7 261.1 %copy-start.55 = (f32[512]{0:T(512)S(1)}, f32[512]{0:T(512)}, u32[]{:S(2)}) copy-start(f32[512]{0:T(512)} %copy-done.54) | copy-start | bytes 6148
  1716.8 259.4 %copy-start.62 = (bf16[2048]{0:T(1024)(128)(2,1)S(1)}, bf16[2048]{0:T(1024)(128)(2,1)}, u32[]{:S(2)}) copy-start(bf16[2048]{0:T(1024)(128)(2,1)} %get-tuple-element.467) | copy-start | bytes 12292
  1716.8 286.5 %copy-start.57 = (f32[512]{0:T(512)S(1)}, f32[512]{0:T(512)}, u32[]{:S(2)}) copy-start(f32[512]{0:T(512)} %copy-done.56) | copy-start | bytes 6148
  1716.8 403.8 %copy-start.46 = (f32[8,1,256]{2,1,0:T(1,128)S(1)}, f32[8,1,256]{2,1,0:T(1,128)}, u32[]{:S(2)}) copy-start(f32[8,1,256]{2,1,0:T(1,128)} %copy-done.44) | copy-start | bytes 24580
  1716.8 403.8 %copy-start.53 = (f32[512]{0:T(512)S(1)}, f32[512]{0:T(512)}, u32[]{:S(2)}) copy-start(f32[512]{0:T(512)} %copy-done.51) | copy-start | bytes 6148
  1716.8 403.8 %copy-start.61 = (f32[512]{0:T(512)S(1)}, f32[512]{0:T(512)}, u32[]{:S(2)}) copy-start(f32[512]{0:T(512)} %copy-done.60) | copy-start | bytes 6148
  (75 other events, 2545.1 us)
Sparse Core Ops, SparseCore 0:
  10.5 30.5 all-gather.15
  43.5 23.4 all-gather.17
  69.5 23.3 all-gather.19
  94.3 149.5 all-gather.13
  246.3 26.2 all-gather.21
  395.9 142.7 reduce-scatter.11
  540.5 45.9 all-gather.25
  588.4 45.3 all-gather.27
  636.0 149.5 all-gather.23
  787.4 44.7 all-gather.29
  833.7 149.5 all-gather.31
  1047.4 142.7 reduce-scatter.15
  1199.5 150.2 all-gather.33
  1353.0 59.9 reduce-scatter.27
  1416.2 61.7 reduce-scatter.29
  1481.2 61.5 reduce-scatter.31
  1664.0 33.4 reduce-scatter.21
  1700.5 35.9 reduce-scatter.23
  1739.8 41.1 reduce-scatter.25
  1784.6 41.1 reduce-scatter.19
  1828.2 144.6 reduce-scatter.17
  1975.2 145.3 reduce-scatter.13
where the time goes:
time: 2140 us
  waiting for transfers between devices  1310 us (61%)
  matrix products  458 us (21%)
  other arithmetic  184 us (9%)
  local copies, waits for them, and re-layouts  91.7 us (4%)
  blocking collectives  60.1 us (3%)
    all_gather x1, waiting for transfers between devices, on_device(): grad_whole = lax.all_gather(out_grad, 'tensor', axis=0, tiled=True)  151 us
    all_gather x1, waiting for transfers between devices, on_device(): gathered = lax.all_gather(normalized_input, 'tensor', axis=0, tiled=True)  149 us
    all_gather x1, waiting for transfers between devices, on_device(): gathered_two = lax.all_gather(normed_two, 'tensor', axis=0, tiled=True)  146 us
    reduce_scatter x1, waiting for transfers between devices, on_device(): lax.psum_scatter(lax.dot_general(rows_b, w_qkv_back, CONTRACT_COLS, prefe...  145 us
    reduce_scatter x1, waiting for transfers between devices, on_device(): lax.psum_scatter(lax.dot_general(rows_b, w_gu_back, CONTRACT_COLS, prefer...  143 us
    reduce_scatter x1, waiting for transfers between devices, on_device(): lax.psum_scatter(jnp.dot(attended, wo_b, preferred_element_type=f32).asty...  129 us
    reduce_scatter x1, waiting for transfers between devices, on_device(): lax.psum_scatter(jnp.dot(hidden_b, wd_b, preferred_element_type=f32).asty...  117 us
    all_gather x1, waiting for transfers between devices, on_device(): lax.all_gather(d_residual.astype(bf16), 'tensor', axis=0, tiled=True)  93.2 us
  transfers between devices with their start and end apart: 22, of which 16 were waited for; matrix products, arithmetic and copies ran while one was open for 29% of the time, Pallas kernels for 0%

commit v1 on v0

--- a/solution.py
+++ b/solution.py
@@ -1,3 +1,5 @@
+import functools
+
 import jax
 import jax.numpy as jnp
 from jax import lax
@@ -13,6 +15,53 @@
 MASKED = -1e30
 CONTRACT_ROWS = (((0,), (0,)), ((), ()))
 CONTRACT_COLS = (((1,), (1,)), ((), ()))
+
+
+def tensor_gather(rows, n):
+    if n == 1:
+        return rows
+    j = lax.axis_index("tensor")
+    count = rows.shape[0]
+    up = rows
+    down = rows
+    ups = {}
+    downs = {}
+    for s in range(1, n):
+        up = lax.ppermute(up, "tensor", [(i, i + 1) for i in range(s - 1, n - 1)])
+        down = lax.ppermute(down, "tensor", [(i, i - 1) for i in range(1, n - s + 1)])
+        ups[s] = up
+        downs[s] = down
+    rel = [rows]
+    for m in range(1, n):
+        rel.append(jnp.where(j + m <= n - 1, downs[m], ups[n - m]))
+    rel = jnp.concatenate(rel, axis=0)
+    twice = jnp.concatenate([rel, rel], axis=0)
+    start = ((n - j) % n) * count
+    return lax.dynamic_slice_in_dim(twice, start, n * count, 0)
+
+
+def tensor_scatter(partial, n):
+    if n == 1:
+        return partial.astype(jnp.float32)
+    j = lax.axis_index("tensor")
+    count = partial.shape[0] // n
+
+    def block(t):
+        return lax.dynamic_slice_in_dim(partial, t * count, count, 0).astype(jnp.float32)
+
+    up = None
+    down = None
+    for s in range(1, n):
+        acc_up = block(jnp.minimum(j + n - s, n - 1))
+        acc_down = block(jnp.maximum(j - n + s, 0))
+        if up is not None:
+            acc_up = acc_up + up.astype(jnp.float32)
+            acc_down = acc_down + down.astype(jnp.float32)
+        up = lax.ppermute(acc_up.astype(jnp.bfloat16), "tensor", [(i, i + 1) for i in range(0, s)])
+        down = lax.ppermute(
+            acc_down.astype(jnp.bfloat16), "tensor", [(i, i - 1) for i in range(n - s, n)]
+        )
+    return block(j) + up.astype(jnp.float32) + down.astype(jnp.float32)
 
 
 def rms_scale(row_data, gain_vec):
@@ -139,6 +188,7 @@
     w_up,
     w_down,
     out_grad,
+    tensor_n=1,
 ):
     bf16 = jnp.bfloat16
     f32 = jnp.float32
@@ -167,7 +217,7 @@
     query_norm_gain = gq_b.astype(f32)
     gain_k = gk_b.astype(f32)
     normalized_input = rms_scale(tok_rows, attn_g).astype(bf16)
-    gathered = lax.all_gather(normalized_input, "tensor", axis=0, tiled=True)
+    gathered = tensor_gather(normalized_input, tensor_n)
     projected = jnp.dot(gathered, w_qkv, preferred_element_type=f32)
     query_unrotated = projected[:, :q_width].reshape(
         seq_count, SEQUENCE_TOKENS, heads_local, HEAD_SIZE
@@ -202,26 +252,16 @@
     w_gu = jnp.concatenate([wg_b, wu_b], axis=1)
     hidden_width = wg_b.shape[1]
     mlp_g = gm_b.astype(f32)
-    residual = tok_rows + lax.psum_scatter(
-        jnp.dot(attended, wo_b, preferred_element_type=f32).astype(jnp.bfloat16),
-        "tensor",
-        scatter_dimension=0,
-        tiled=True,
-    ).astype(jnp.float32)
+    residual = tok_rows + tensor_scatter(jnp.dot(attended, wo_b, preferred_element_type=f32), tensor_n)
     normed_two = rms_scale(residual, mlp_g).astype(bf16)
-    gathered_two = lax.all_gather(normed_two, "tensor", axis=0, tiled=True)
+    gathered_two = tensor_gather(normed_two, tensor_n)
     gate_up = jnp.dot(gathered_two, w_gu, preferred_element_type=f32)
     gate_pre = gate_up[:, :hidden_width]
     up_pre = gate_up[:, hidden_width:]
     hidden_b = (jax.nn.silu(gate_pre) * up_pre).astype(bf16)
     layer_out = (
         residual
-        + lax.psum_scatter(
-            jnp.dot(hidden_b, wd_b, preferred_element_type=f32).astype(jnp.bfloat16),
-            "tensor",
-            scatter_dimension=0,
-            tiled=True,
-        ).astype(jnp.float32)
+        + tensor_scatter(jnp.dot(hidden_b, wd_b, preferred_element_type=f32), tensor_n)
     ).astype(bf16)
     wg_c, wu_c, wd_back = (
         lax.all_gather(w_gate.astype(bf16), "dp", axis=0, tiled=True),
@@ -229,7 +269,7 @@
         lax.all_gather(w_down.astype(bf16), "dp", axis=1, tiled=True),
     )
     w_gu_back = jnp.concatenate([wg_c, wu_c], axis=1)
-    grad_whole = lax.all_gather(out_grad, "tensor", axis=0, tiled=True)
+    grad_whole = tensor_gather(out_grad, tensor_n)
     grad_down = lax.dot_general(hidden_b, grad_whole, CONTRACT_ROWS, preferred_element_type=f32)
     d_hidden = lax.dot_general(grad_whole, wd_back, CONTRACT_COLS, preferred_element_type=f32)
 
@@ -243,14 +283,7 @@
         gathered_two, d_gate_up, CONTRACT_ROWS, preferred_element_type=f32
     )
     rows_b = d_gate_up
-    d_normed_two = lax.psum_scatter(
-        lax.dot_general(rows_b, w_gu_back, CONTRACT_COLS, preferred_element_type=f32).astype(
-            jnp.bfloat16
-        ),
-        "tensor",
-        scatter_dimension=0,
-        tiled=True,
-    ).astype(jnp.float32)
+    d_normed_two = tensor_scatter(lax.dot_general(rows_b, w_gu_back, CONTRACT_COLS, preferred_element_type=f32), tensor_n)
     norm_value, norm_two_back = jax.vjp(rms_scale, residual, mlp_g)
     d_resid_norm, d_mlp_gain = norm_two_back(d_normed_two)
     d_residual = out_grad.astype(f32) + d_resid_norm
@@ -261,7 +294,7 @@
         lax.all_gather(w_out.astype(bf16), "dp", axis=1, tiled=True),
     )
     w_qkv_back = jnp.concatenate([wq_c, wk_c, wv_c], axis=1)
-    attn_grad_whole = lax.all_gather(d_residual.astype(bf16), "tensor", axis=0, tiled=True)
+    attn_grad_whole = tensor_gather(d_residual.astype(bf16), tensor_n)
     grad_out = lax.dot_general(attended, attn_grad_whole, CONTRACT_ROWS, preferred_element_type=f32)
     d_attended = lax.dot_general(
         attn_grad_whole, wo_back, CONTRACT_COLS, preferred_element_type=f32
@@ -290,14 +323,7 @@
     ).astype(bf16)
     grad_qkv = lax.dot_general(gathered, d_qkv, CONTRACT_ROWS, preferred_element_type=f32)
     rows_b = d_qkv
-    d_normed = lax.psum_scatter(
-        lax.dot_general(rows_b, w_qkv_back, CONTRACT_COLS, preferred_element_type=f32).astype(
-            jnp.bfloat16
-        ),
-        "tensor",
-        scatter_dimension=0,
-        tiled=True,
-    ).astype(jnp.float32)
+    d_normed = tensor_scatter(lax.dot_general(rows_b, w_qkv_back, CONTRACT_COLS, preferred_element_type=f32), tensor_n)
     norm_one, norm_back = jax.vjp(rms_scale, tok_rows, attn_g)
     d_x_norm, d_attn_gain = norm_back(d_normed)
     grad_tokens = d_residual + d_x_norm
@@ -368,7 +394,7 @@
 
 def solution(mesh):
     return jax.shard_map(
-        on_device,
+        functools.partial(on_device, tensor_n=mesh.shape["tensor"]),
         mesh=mesh,
         in_specs=(
             P(("dp", "tensor"), None),

time: 2140 us -> 2010 us (0.939)
  waiting for transfers between devices: 1310 us -> 797 us
  other arithmetic: 184 us -> 345 us
  starting transfers between devices: 1.08 us -> 133 us
  blocking collectives: 60.1 us -> 111 us
  local copies, waits for them, and re-layouts: 91.7 us -> 128 us
    ppermute x0 -> x48, waiting for transfers between devices: none -> 790 us  [the longest x12 302 us: tensor_scatter(): lax.ppermute(acc_up.astype(jnp.bfloat16), 'tensor', [(i, i + 1) for i in...]
    all_gather x4 -> x0, waiting for transfers between devices: 539 us -> none  [the longest x1 151 us: on_device(): grad_whole = lax.all_gather(out_grad, 'tensor', axis=0, tiled=True)]
    reduce_scatter x4 -> x0, waiting for transfers between devices: 534 us -> none  [the longest x1 145 us: on_device(): lax.psum_scatter(lax.dot_general(rows_b, w_qkv_back, CONTRACT_COLS, prefe...]
    ppermute x0 -> x48, starting transfers between devices: none -> 132 us  [the longest x12 59.4 us: tensor_scatter(): lax.ppermute(acc_up.astype(jnp.bfloat16), 'tensor', [(i, i + 1) for i in...]
    unnamed x2 -> x25, other arithmetic: 0.01 us -> 79.9 us
    convert_element_type x3 -> x12, other arithmetic: 7.94 us -> 62.2 us  [the longest x8 45.5 us: tensor_scatter(): acc_up.astype(jnp.bfloat16)]
    psum x1, blocking collectives: 12.8 us -> 59.9 us  [on_device(): gains_sum = lax.psum((owned[7], owned[8], owned[9], owned[10]), 'tensor')]
    reduce_scatter x1, waiting for transfers between devices: 42.8 us -> 0.01 us  [on_device(): lax.psum_scatter(grad_out.astype(jnp.bfloat16), 'dp', scatter_dimension=1...]
  transfers between devices with their start and end apart: 22 -> 62, of which waited for: 16 -> 29; matrix products, arithmetic and copies ran while one was open for 29% -> 40% of each run, Pallas kernels for 0% -> 0%
where the time goes in v1:
time: 2010 us; the launch traced here: 2000 us
  waiting for transfers between devices  797 us (40%)
  matrix products  449 us (22%)
  other arithmetic  345 us (17%)
  starting transfers between devices  133 us (7%)
  local copies, waits for them, and re-layouts  128 us (6%)
  blocking collectives  111 us (6%)
    ppermute x12, waiting for transfers between devices, tensor_scatter(): lax.ppermute(acc_up.astype(jnp.bfloat16), 'tensor', [(i, i + 1) for i in...  302 us
    ppermute x12, waiting for transfers between devices, tensor_gather(): lax.ppermute(down, 'tensor', [(i, i - 1) for i in range(1, n - s + 1)])  251 us
    ppermute x12, waiting for transfers between devices, tensor_gather(): up = lax.ppermute(up, 'tensor', [(i, i + 1) for i in range(s - 1, n - 1)])  143 us
    ppermute x12, waiting for transfers between devices, tensor_scatter(): lax.ppermute(acc_down.astype(jnp.bfloat16), 'tensor', [(i, i - 1) for i i...  93.3 us
    unnamed x25, other arithmetic  79.9 us
    psum x1, blocking collectives, on_device(): gains_sum = lax.psum((owned[7], owned[8], owned[9], owned[10]), 'tensor')  59.9 us
    ppermute x12, starting transfers between devices, tensor_scatter(): lax.ppermute(acc_up.astype(jnp.bfloat16), 'tensor', [(i, i + 1) for i in...  59.4 us
    dot_general x8, matrix products, one_block(): jnp.einsum('qkgd,skd->kgqs', q_rows, key_rows, preferred_element_type=jnp...  57.3 us
  transfers between devices with their start and end apart: 62, of which 29 were waited for; matrix products, arithmetic and copies ran while one was open for 40% of the time, Pallas kernels for 0%

profile of v1, /device:TPU:0, one launch (start us, length us, event | category | flops | bytes accessed | tf_op | source)
XLA Modules:
  0.0 1997.0 jit_solution(12816764206857950400)
XLA Ops:
  43.3 35.6 %collective-permute-done.1 = bf16[512,2048]{1,0:T(8,128)(2,1)} collective-permute-done((bf16[512,2048]{1,0:T(8,128)(2,1)}, bf16[512,2048]{1,0:T(8,128)(2,1)}, u32[]{:S(2)}, u32[]{:S(2)}) %collective-permute-start.1) | collective-permute-done | bytes 2097184 | tf_op jit(solution)/shard_map/ppermute | solution.py:30
  86.9 36.3 %collective-permute-done.25 = bf16[512,2048]{1,0:T(8,128)(2,1)} collective-permute-done((bf16[512,2048]{1,0:T(8,128)(2,1)}, bf16[512,2048]{1,0:T(8,128)(2,1)}, u32[]{:S(2)}, u32[]{:S(2)}) %collective-permute-start.25) | collective-permute-done | bytes 2097184 | tf_op jit(solution)/shard_map/ppermute | solution.py:30
  160.1 15.4 collective-permute-done.4
  185.2 35.2 %collective-permute-done.28 = bf16[512,2048]{1,0:T(8,128)(2,1)} collective-permute-done((bf16[512,2048]{1,0:T(8,128)(2,1)}, bf16[512,2048]{1,0:T(8,128)(2,1)}, u32[]{:S(2)}, u32[]{:S(2)}) %collective-permute-start.28) | collective-permute-done | bytes 2097184 | tf_op jit(solution)/shard_map/ppermute | solution.py:31
  229.5 35.8 %collective-permute-done.5 = bf16[512,2048]{1,0:T(8,128)(2,1)} collective-permute-done((bf16[512,2048]{1,0:T(8,128)(2,1)}, bf16[512,2048]{1,0:T(8,128)(2,1)}, u32[]{:S(2)}, u32[]{:S(2)}) %collective-permute-start.5) | collective-permute-done | bytes 2097184 | tf_op jit(solution)/shard_map/ppermute | solution.py:31
  280.0 29.2 %collective-permute-done.29 = bf16[512,2048]{1,0:T(8,128)(2,1)S(1)} collective-permute-done((bf16[512,2048]{1,0:T(8,128)(2,1)}, bf16[512,2048]{1,0:T(8,128)(2,1)S(1)}, u32[]{:S(2)}, u32[]{:S(2)}) %collective-permute-start.29) | collective-permute-done | bytes 2097184 | tf_op jit(solution)/shard_map/ppermute | solution.py:31
  374.2 86.6 %while.51 = (s32[]{:T(128)}, bf16[4,512,2,2,128]{4,1,3,2,0:T(8,128)(2,1)}, f32[4,2,2,512]{3,2,1,0:T(2,128)}, s32[4]{0:T(128)S(1)}, s32[17,1]{0,1:T(1,128)S(1)}, ...) while((s32[]{:T(128)}, ...), condition=%wide.region_8.9_spmd, body=%wide.region_5.8_spmd.sunk | while | flops 2204107776 | bytes 58313080 | solution.py:127
  492.1 41.1 %collective-permute-done.6 = bf16[512,2048]{1,0:T(8,128)(2,1)} collective-permute-done((bf16[512,2048]{1,0:T(8,128)(2,1)}, bf16[512,2048]{1,0:T(8,128)(2,1)}, u32[]{:S(2)}, u32[]{:S(2)}) %collective-permute-start.6) | collective-permute-done | bytes 2097184 | tf_op jit(solution)/shard_map/ppermute | solution.py:60
  544.9 41.3 %collective-permute-done.7 = bf16[512,2048]{1,0:T(8,128)(2,1)} collective-permute-done((bf16[512,2048]{1,0:T(8,128)(2,1)}, bf16[512,2048]{1,0:T(8,128)(2,1)}, u32[]{:S(2)}, u32[]{:S(2)}) %collective-permute-start.7) | collective-permute-done | bytes 2097184 | tf_op jit(solution)/shard_map/ppermute | solution.py:60
  616.9 26.5 %collective-permute-done.8 = bf16[512,2048]{1,0:T(8,128)(2,1)} collective-permute-done((bf16[512,2048]{1,0:T(8,128)(2,1)}, bf16[512,2048]{1,0:T(8,128)(2,1)}, u32[]{:S(2)}, u32[]{:S(2)}) %collective-permute-start.8) | collective-permute-done | bytes 2097184 | tf_op jit(solution)/shard_map/ppermute | solution.py:60
  643.4 50.6 %collective-permute-done.11 = bf16[512,2048]{1,0:T(8,128)(2,1)} collective-permute-done((bf16[512,2048]{1,0:T(8,128)(2,1)}, bf16[512,2048]{1,0:T(8,128)(2,1)}, u32[]{:S(2)}, u32[]{:S(2)}) %collective-permute-start.11) | collective-permute-done | bytes 2097184 | tf_op jit(solution)/shard_map/ppermute | solution.py:61
  707.8 38.3 %collective-permute-done.13 = bf16[512,2048]{1,0:T(8,128)(2,1)} collective-permute-done((bf16[512,2048]{1,0:T(8,128)(2,1)S(1)}, bf16[512,2048]{1,0:T(8,128)(2,1)}, u32[]{:S(2)}, u32[]{:S(2)}) %collective-permute-start.13) | collective-permute-done | bytes 2097184 | tf_op jit(solution)/shard_map/ppermute | solution.py:30
  762.5 34.0 %collective-permute-done.16 = bf16[512,2048]{1,0:T(8,128)(2,1)} collective-permute-done((bf16[512,2048]{1,0:T(8,128)(2,1)}, bf16[512,2048]{1,0:T(8,128)(2,1)}, u32[]{:S(2)}, u32[]{:S(2)}) %collective-permute-start.16) | collective-permute-done | bytes 2097184 | tf_op jit(solution)/shard_map/ppermute | solution.py:31
  817.7 25.9 %collective-permute-done.17 = bf16[512,2048]{1,0:T(8,128)(2,1)S(1)} collective-permute-done((bf16[512,2048]{1,0:T(8,128)(2,1)}, bf16[512,2048]{1,0:T(8,128)(2,1)S(1)}, u32[]{:S(2)}, u32[]{:S(2)}) %collective-permute-start.17) | collective-permute-done | bytes 2097184 | tf_op jit(solution)/shard_map/ppermute | solution.py:31
  857.7 31.8 %fusion.64 = f32[2048,3072]{1,0:T(8,128)} fusion(bf16[2048,3072]{1,0:T(8,128)(2,1)S(1)} %bitcast.216, bf16[4096,2048]{1,0:T(8,128)(2,1)} %fusion.111, s32[]{:T(128)S(6)} %select_n.153), kind=kOutput, calls=%fused_computation.92 | convolution fusion | flops 25769803776 | bytes 46137348 | tf_op jit(solution)/shard_map/dot_general | solution.py:258
  889.5 30.0 %fusion.53 = (bf16[2048,1536]{1,0:T(8,128)(2,1)}, bf16[2048,1536]{1,0:T(8,128)(2,1)}, bf16[2048,1536]{1,0:T(8,128)(2,1)}) fusion(f32[2048,3072]{1,0:T(8,128)} %fusion.64, bf16[1536,2048]{1,0:T(8,128)(2,1)} %all-gather.22.cloned.1.call-done, bf16[4096,2048]{1,0:T(8,128)(2,1)} %fusion.113, s32[]{:T(128)S(6)} %select_n.153), kind=kOutput, calls=%fused_computation.70 | convolution fusion | flops 12935233536 | bytes 58720260 | tf_op jit(solution)/shard_map/dot_general | solution.py:274
  919.5 34.5 %convolution_convert_fusion = bf16[2048,3072]{1,0:T(8,128)(2,1)} fusion(bf16[2048,1536]{1,0:T(8,128)(2,1)} %get-tuple-element.548, bf16[2048,1536]{1,0:T(8,128)(2,1)} %get-tuple-element.547, bf16[4096,2048]{1,0:T(8,128)(2,1)} %fusion.111, s32[]{:T(128)S(6)} %select_n.153), kind=kOutput, calls=%fused_computation.76 | convolution fusion | flops 25801261056 | bytes 33554436 | tf_op jit(solution)/shard_map/dot_general | solution.py:282
  964.3 34.5 %fusion.55 = f32[2048,2048]{1,0:T(8,128)} fusion(bf16[2048,3072]{1,0:T(8,128)(2,1)} %constant_dynamic-update-slice_fusion.7, bf16[2048,1536]{1,0:T(8,128)(2,1)} %get-tuple-element.548, bf16[2048,1536]{1,0:T(8,128)(2,1)} %get-tuple-element.547), kind=kOutput, calls=%fused_computation.82 | convolution fusion | flops 25794969600 | bytes 41943040 | tf_op jit(solution)/shard_map/dot_general | solution.py:286
  1009.3 37.9 %collective-permute-done.30 = bf16[512,2048]{1,0:T(8,128)(2,1)S(1)} collective-permute-done((bf16[512,2048]{1,0:T(8,128)(2,1)S(1)}, bf16[512,2048]{1,0:T(8,128)(2,1)S(1)}, u32[]{:S(2)}, u32[]{:S(2)}) %collective-permute-start.30) | collective-permute-done | bytes 2097184 | tf_op jit(solution)/shard_map/ppermute | solution.py:60
  1055.8 36.7 %collective-permute-done.31 = bf16[512,2048]{1,0:T(8,128)(2,1)} collective-permute-done((bf16[512,2048]{1,0:T(8,128)(2,1)S(1)}, bf16[512,2048]{1,0:T(8,128)(2,1)}, u32[]{:S(2)}, u32[]{:S(2)}) %collective-permute-start.31) | collective-permute-done | bytes 2097184 | tf_op jit(solution)/shard_map/ppermute | solution.py:60
  1108.6 32.5 %collective-permute-done.32 = bf16[512,2048]{1,0:T(8,128)(2,1)} collective-permute-done((bf16[512,2048]{1,0:T(8,128)(2,1)}, bf16[512,2048]{1,0:T(8,128)(2,1)}, u32[]{:S(2)}, u32[]{:S(2)}) %collective-permute-start.32) | collective-permute-done | bytes 2097184 | tf_op jit(solution)/shard_map/ppermute | solution.py:60
  1141.1 42.7 %collective-permute-done.35 = bf16[512,2048]{1,0:T(8,128)(2,1)} collective-permute-done((bf16[512,2048]{1,0:T(8,128)(2,1)}, bf16[512,2048]{1,0:T(8,128)(2,1)}, u32[]{:S(2)}, u32[]{:S(2)}) %collective-permute-start.35) | collective-permute-done | bytes 2097184 | tf_op jit(solution)/shard_map/ppermute | solution.py:61
  1201.7 32.9 %collective-permute-done.37 = bf16[512,2048]{1,0:T(8,128)(2,1)} collective-permute-done((bf16[512,2048]{1,0:T(8,128)(2,1)S(1)}, bf16[512,2048]{1,0:T(8,128)(2,1)}, u32[]{:S(2)}, u32[]{:S(2)}) %collective-permute-start.37) | collective-permute-done | bytes 2097184 | tf_op jit(solution)/shard_map/ppermute | solution.py:30
  1249.3 42.5 %collective-permute-done.40 = bf16[512,2048]{1,0:T(8,128)(2,1)} collective-permute-done((bf16[512,2048]{1,0:T(8,128)(2,1)}, bf16[512,2048]{1,0:T(8,128)(2,1)}, u32[]{:S(2)}, u32[]{:S(2)}) %collective-permute-start.40) | collective-permute-done | bytes 2097184 | tf_op jit(solution)/shard_map/ppermute | solution.py:31
  1293.1 19.1 convolution_convert_fusion.1
  1356.4 261.0 %while.52 = (s32[]{:T(128)}, f32[2048,2,128]{0,2,1:T(8,128)S(1)}, f32[2048,2,128]{0,2,1:T(8,128)}, f32[4,512,2,2,128]{4,1,0,3,2:T(8,128)}, s32[4]{0:T(128)S(1)},...) while((s32[]{:T(128)}, f32[2048,2,128]{0,2,1:T(8,128)S(1)}, ...), condition=%wide.region_13.14_spmd.clone, body=%wide.region_11.13_spmd.clone.sunk | while | flops 5440799744 | bytes 186755056 | solution.py:171
  1678.6 17.2 fusion.141
  1728.5 23.8 %collective-permute-done.18 = bf16[512,2048]{1,0:T(8,128)(2,1)} collective-permute-done((bf16[512,2048]{1,0:T(8,128)(2,1)}, bf16[512,2048]{1,0:T(8,128)(2,1)}, u32[]{:S(2)}, u32[]{:S(2)}) %collective-permute-start.18) | collective-permute-done | bytes 2097184 | tf_op jit(solution)/shard_map/ppermute | solution.py:60
  1760.4 36.9 %collective-permute-done.43 = bf16[512,2048]{1,0:T(8,128)(2,1)} collective-permute-done((bf16[512,2048]{1,0:T(8,128)(2,1)}, bf16[512,2048]{1,0:T(8,128)(2,1)}, u32[]{:S(2)}, u32[]{:S(2)}) %collective-permute-start.43) | collective-permute-done | bytes 2097184 | tf_op jit(solution)/shard_map/ppermute | solution.py:60
  1807.1 22.4 %collective-permute-done.19 = bf16[512,2048]{1,0:T(8,128)(2,1)S(1)} collective-permute-done((bf16[512,2048]{1,0:T(8,128)(2,1)S(1)}, bf16[512,2048]{1,0:T(8,128)(2,1)S(1)}, u32[]{:S(2)}, u32[]{:S(2)}) %collective-permute-start.19) | collective-permute-done | bytes 2097184 | tf_op jit(solution)/shard_map/ppermute | solution.py:60
  1897.7 20.3 %all-reduce.11 = (bf16[2048]{0:T(1024)(128)(2,1)S(1)}, bf16[128]{0:T(256)(128)(2,1)S(1)}, bf16[128]{0:T(256)(128)(2,1)S(1)}, bf16[2048]{0:T(1024)(128)(2,1)S(1)}) all-reduce(bf16[2048]{0:T(1024)(128)(2,1)S(1)} %get-tuple-element.469, bf16[128]{0:T(256)(128)(2,1)S(1)} %get-tuple-element.465, ...), channel_id=2, replica_groups=mesh['dp'=8,'tensor'=4] {'dp'}, use_global_device_ids=true, to_apply=%region_18.19.clone | all-reduce | flops 4352 | bytes 17408
  1918.3 59.9 %all-reduce.10 = (f32[256]{0:T(256)}, f32[16]{0:T(128)}, f32[16]{0:T(128)}, f32[256]{0:T(256)}) all-reduce(f32[256]{0:T(256)S(1)} %dynamic-slice_convert_fusion.11, f32[16]{0:T(128)S(1)} %dynamic-slice_convert_fusion.10, f32[16]{0:T(128)S(1)} %dynamic-slice_convert_fusion.9, ...), channel_id=1, replica_groups=mesh['dp'=8,'tensor'=4] {'tensor'}, use_global_device_ids=true, to_apply=%region_19.20 | all-reduce | flops 544 | bytes 4352 | tf_op jit(solution)/shard_map/psum | solution.py:377
  (557 shorter events, 961.8 us)
Async XLA Ops:
  7.2 169.6 %all-gather.10.cloned.1.call-start = ((), (), s32[]{:S(2)}) async-start(), calls=%async_computation.7 | async-start | bytes 2359296 | tf_op jit(solution)/shard_map/all_gather | solution.py:202
  9.2 170.7 %all-gather.12.cloned.1.call-start = ((), (), s32[]{:S(2)}) async-start(), calls=%async_computation.8 | async-start | bytes 1179648 | tf_op jit(solution)/shard_map/all_gather | solution.py:203
  10.9 171.2 %all-gather.14.cloned.1.call-start = ((), (), s32[]{:S(2)}) async-start(), calls=%async_computation.9 | async-start | bytes 1179648 | tf_op jit(solution)/shard_map/all_gather | solution.py:204
  12.6 458.4 %all-gather.16.cloned.1.call-start = ((), (), s32[]{:S(2)}) async-start(), calls=%async_computation.10 | async-start | bytes 2359296 | tf_op jit(solution)/shard_map/all_gather | solution.py:205
  34.7 763.2 %all-gather.18.cloned.1.call-start = ((), (), s32[]{:S(2)}) async-start(), calls=%async_computation.11 | async-start | bytes 7077888 | tf_op jit(solution)/shard_map/all_gather | solution.py:247
  36.2 87.0 %collective-permute-start.25 = (bf16[512,2048]{1,0:T(8,128)(2,1)}, bf16[512,2048]{1,0:T(8,128)(2,1)}, u32[]{:S(2)}, u32[]{:S(2)}) collective-permute-start(bf16[512,2048]{1,0:T(8,128)(2,1)} %param.33), channel_id=1, source_target_pairs={{0,1},{1,2},{2,3},{4,5},{5,6},{6,7},{8,9},{9,10},{10,11},{12,13},{... | collective-permute-start | bytes 6291464 | tf_op jit(solution)/shard_map/ppermute | solution.py:30
  42.0 88.5 %collective-permute-start.24 = (bf16[512,2048]{1,0:T(8,128)(2,1)}, bf16[512,2048]{1,0:T(8,128)(2,1)}, u32[]{:S(2)}, u32[]{:S(2)}) collective-permute-start(bf16[512,2048]{1,0:T(8,128)(2,1)} %param.33), channel_id=1, source_target_pairs={{1,0},{2,1},{3,2},{5,4},{6,5},{7,6},{9,8},{10,9},{11,10},{13,12},{... | collective-permute-start | bytes 6291464 | tf_op jit(solution)/shard_map/ppermute | solution.py:31
  85.6 89.9 %collective-permute-start.4 = (bf16[512,2048]{1,0:T(8,128)(2,1)}, bf16[512,2048]{1,0:T(8,128)(2,1)}, u32[]{:S(2)}, u32[]{:S(2)}) collective-permute-start(bf16[512,2048]{1,0:T(8,128)(2,1)} %collective-permute-done), channel_id=1, source_target_pairs={{1,0},{2,1},{5,4},{6,5},{9,8},{10,9},{13,12},{14,13},{17,16},{18,1... | collective-permute-start | bytes 6291464 | tf_op jit(solution)/shard_map/ppermute | solution.py:31
  123.2 61.3 %collective-permute-start.26 = (bf16[512,2048]{1,0:T(8,128)(2,1)}, bf16[512,2048]{1,0:T(8,128)(2,1)}, u32[]{:S(2)}, u32[]{:S(2)}) collective-permute-start(bf16[512,2048]{1,0:T(8,128)(2,1)} %collective-permute-done.25), channel_id=1, source_target_pairs={{1,2},{2,3},{5,6},{6,7},{9,10},{10,11},{13,14},{14,15},{17,18},{18... | collective-permute-start | bytes 6291464 | tf_op jit(solution)/shard_map/ppermute | solution.py:30
  130.5 89.9 %collective-permute-start.28 = (bf16[512,2048]{1,0:T(8,128)(2,1)}, bf16[512,2048]{1,0:T(8,128)(2,1)}, u32[]{:S(2)}, u32[]{:S(2)}) collective-permute-start(bf16[512,2048]{1,0:T(8,128)(2,1)} %collective-permute-done.24), channel_id=1, source_target_pairs={{1,0},{2,1},{5,4},{6,5},{9,8},{10,9},{13,12},{14,13},{17,16},{18,1... | collective-permute-start | bytes 6291464 | tf_op jit(solution)/shard_map/ppermute | solution.py:31
  131.8 90.0 %collective-permute-start.3 = (bf16[512,2048]{1,0:T(8,128)(2,1)}, bf16[512,2048]{1,0:T(8,128)(2,1)}, u32[]{:S(2)}, u32[]{:S(2)}) collective-permute-start(bf16[512,2048]{1,0:T(8,128)(2,1)} %collective-permute-done.2), channel_id=1, source_target_pairs={{2,3},{6,7},{10,11},{14,15},{18,19},{22,23},{26,27},{30,31}} | collective-permute-start | bytes 6291464 | tf_op jit(solution)/shard_map/ppermute | solution.py:30
  136.3 667.9 %all-gather.20.cloned.1.call-start = ((), (), s32[]{:S(2)}) async-start(), calls=%async_computation.12 | async-start | bytes 7077888 | tf_op jit(solution)/shard_map/all_gather | solution.py:248
  175.5 89.9 %collective-permute-start.5 = (bf16[512,2048]{1,0:T(8,128)(2,1)}, bf16[512,2048]{1,0:T(8,128)(2,1)}, u32[]{:S(2)}, u32[]{:S(2)}) collective-permute-start(bf16[512,2048]{1,0:T(8,128)(2,1)} %collective-permute-done.4), channel_id=1, source_target_pairs={{1,0},{5,4},{9,8},{13,12},{17,16},{21,20},{25,24},{29,28}} | collective-permute-start | bytes 6291464 | tf_op jit(solution)/shard_map/ppermute | solution.py:31
  184.5 87.9 %collective-permute-start.27 = (bf16[512,2048]{1,0:T(8,128)(2,1)}, bf16[512,2048]{1,0:T(8,128)(2,1)S(1)}, u32[]{:S(2)}, u32[]{:S(2)}) collective-permute-start(bf16[512,2048]{1,0:T(8,128)(2,1)} %collective-permute-done.26), channel_id=1, source_target_pairs={{2,3},{6,7},{10,11},{14,15},{18,19},{22,23},{26,27},{30,31}} | collective-permute-start | bytes 6291464 | tf_op jit(solution)/shard_map/ppermute | solution.py:30
  220.4 88.9 %collective-permute-start.29 = (bf16[512,2048]{1,0:T(8,128)(2,1)}, bf16[512,2048]{1,0:T(8,128)(2,1)S(1)}, u32[]{:S(2)}, u32[]{:S(2)}) collective-permute-start(bf16[512,2048]{1,0:T(8,128)(2,1)} %collective-permute-done.28), channel_id=1, source_target_pairs={{1,0},{5,4},{9,8},{13,12},{17,16},{21,20},{25,24},{29,28}} | collective-permute-start | bytes 6291464 | tf_op jit(solution)/shard_map/ppermute | solution.py:31
  544.8 344.7 %all-gather.22.cloned.1.call-start = ((), (), s32[]{:S(2)}) async-start(), calls=%async_computation.13 | async-start | bytes 7077888 | tf_op jit(solution)/shard_map/all_gather | solution.py:249
  606.6 87.4 %collective-permute-start.11 = (bf16[512,2048]{1,0:T(8,128)(2,1)}, bf16[512,2048]{1,0:T(8,128)(2,1)}, u32[]{:S(2)}, u32[]{:S(2)}) collective-permute-start(bf16[512,2048]{1,0:T(8,128)(2,1)} %add_convert_fusion.13), channel_id=1, source_target_pairs={{1,0},{2,1},{3,2},{5,4},{6,5},{7,6},{9,8},{10,9},{11,10},{13,12},{... | collective-permute-start | bytes 6291464 | tf_op jit(solution)/shard_map/ppermute | solution.py:61
  754.4 1112.5 %reduce-scatter.16.cloned.1.call-start = ((), (), s32[]{:S(2)}) async-start(), calls=%async_computation.18 | async-start | bytes 7077888 | tf_op jit(solution)/shard_map/reduce_scatter | solution.py:349
  754.4 55.7 %collective-permute-start.15 = (bf16[512,2048]{1,0:T(8,128)(2,1)}, bf16[512,2048]{1,0:T(8,128)(2,1)}, u32[]{:S(2)}, u32[]{:S(2)}) collective-permute-start(bf16[512,2048]{1,0:T(8,128)(2,1)} %collective-permute-done.14), channel_id=1, source_target_pairs={{2,3},{6,7},{10,11},{14,15},{18,19},{22,23},{26,27},{30,31}} | collective-permute-start | bytes 6291464 | tf_op jit(solution)/shard_map/ppermute | solution.py:30
  964.3 905.2 %reduce-scatter.18.cloned.1.call-start = ((), (), s32[]{:S(2)}) async-start(), calls=%async_computation.19 | async-start | bytes 7077888 | tf_op jit(solution)/shard_map/reduce_scatter | solution.py:355
  1107.1 76.7 %collective-permute-start.35 = (bf16[512,2048]{1,0:T(8,128)(2,1)}, bf16[512,2048]{1,0:T(8,128)(2,1)}, u32[]{:S(2)}, u32[]{:S(2)}) collective-permute-start(bf16[512,2048]{1,0:T(8,128)(2,1)} %add_convert_fusion.4), channel_id=1, source_target_pairs={{1,0},{2,1},{3,2},{5,4},{6,5},{7,6},{9,8},{10,9},{11,10},{13,12},{... | collective-permute-start | bytes 6291464 | tf_op jit(solution)/shard_map/ppermute | solution.py:61
  1108.5 763.4 %reduce-scatter.20.cloned.1.call-start = ((), (), s32[]{:S(2)}) async-start(), calls=%async_computation.20 | async-start | bytes 7077888 | tf_op jit(solution)/shard_map/reduce_scatter | solution.py:361
  1247.3 65.0 %collective-permute-start.39 = (bf16[512,2048]{1,0:T(8,128)(2,1)}, bf16[512,2048]{1,0:T(8,128)(2,1)}, u32[]{:S(2)}, u32[]{:S(2)}) collective-permute-start(bf16[512,2048]{1,0:T(8,128)(2,1)} %collective-permute-done.38), channel_id=1, source_target_pairs={{2,3},{6,7},{10,11},{14,15},{18,19},{22,23},{26,27},{30,31}} | collective-permute-start | bytes 6291464 | tf_op jit(solution)/shard_map/ppermute | solution.py:30
  1312.2 562.1 %reduce-scatter.10.cloned.1.call-start = ((), (), s32[]{:S(2)}) async-start(), calls=%async_computation.15 | async-start | bytes 1179648 | tf_op jit(solution)/shard_map/reduce_scatter | solution.py:334
  1678.5 197.4 %reduce-scatter.12.cloned.1.call-start = ((), (), s32[]{:S(2)}) async-start(), calls=%async_computation.16 | async-start | bytes 1179648 | tf_op jit(solution)/shard_map/reduce_scatter | solution.py:340
  1707.4 170.2 %reduce-scatter.14.cloned.1.call-start = ((), (), s32[]{:S(2)}) async-start(), calls=%async_computation.17 | async-start | bytes 2359296 | tf_op jit(solution)/shard_map/reduce_scatter | solution.py:346
  1707.4 99.7 %collective-permute-start.21 = (bf16[512,2048]{1,0:T(8,128)(2,1)}, bf16[512,2048]{1,0:T(8,128)(2,1)}, u32[]{:S(2)}, u32[]{:S(2)}) collective-permute-start(bf16[512,2048]{1,0:T(8,128)(2,1)} %get-tuple-element.561), channel_id=1, source_target_pairs={{3,2},{7,6},{11,10},{15,14},{19,18},{23,22},{27,26},{31,30}} | collective-permute-start | bytes 6291464 | tf_op jit(solution)/shard_map/ppermute | solution.py:61
  1716.7 80.6 %collective-permute-start.43 = (bf16[512,2048]{1,0:T(8,128)(2,1)}, bf16[512,2048]{1,0:T(8,128)(2,1)}, u32[]{:S(2)}, u32[]{:S(2)}) collective-permute-start(bf16[512,2048]{1,0:T(8,128)(2,1)} %add_convert_fusion.3), channel_id=1, source_target_pairs={{0,1},{1,2},{4,5},{5,6},{8,9},{9,10},{12,13},{13,14},{16,17},{17,1... | collective-permute-start | bytes 6291464 | tf_op jit(solution)/shard_map/ppermute | solution.py:60
  1728.5 158.0 %reduce-scatter.8.cloned.1.call-start = ((), (), s32[]{:S(2)}) async-start(), calls=%async_computation.14 | async-start | bytes 2359296 | tf_op jit(solution)/shard_map/reduce_scatter | solution.py:331
  1755.9 73.6 %collective-permute-start.19 = (bf16[512,2048]{1,0:T(8,128)(2,1)S(1)}, bf16[512,2048]{1,0:T(8,128)(2,1)S(1)}, u32[]{:S(2)}, u32[]{:S(2)}) collective-permute-start(bf16[512,2048]{1,0:T(8,128)(2,1)S(1)} %add_convert_fusion.12), channel_id=1, source_target_pairs={{0,1},{1,2},{4,5},{5,6},{8,9},{9,10},{12,13},{13,14},{16,17},{17,1... | collective-permute-start | bytes 6291464 | tf_op jit(solution)/shard_map/ppermute | solution.py:60
  1852.0 126.2 %collective-permute-start.20 = (bf16[512,2048]{1,0:T(8,128)(2,1)}, bf16[512,2048]{1,0:T(8,128)(2,1)}, u32[]{:S(2)}, u32[]{:S(2)}) collective-permute-start(bf16[512,2048]{1,0:T(8,128)(2,1)} %get-tuple-element.558), channel_id=1, source_target_pairs={{0,1},{1,2},{2,3},{4,5},{5,6},{6,7},{8,9},{9,10},{10,11},{12,13},{... | collective-permute-start | bytes 6291464 | tf_op jit(solution)/shard_map/ppermute | solution.py:60
  1864.2 114.0 %collective-permute-start.23 = (bf16[512,2048]{1,0:T(8,128)(2,1)}, bf16[512,2048]{1,0:T(8,128)(2,1)}, u32[]{:S(2)}, u32[]{:S(2)}) collective-permute-start(bf16[512,2048]{1,0:T(8,128)(2,1)} %add_convert_fusion.9), channel_id=1, source_target_pairs={{1,0},{2,1},{3,2},{5,4},{6,5},{7,6},{9,8},{10,9},{11,10},{13,12},{... | collective-permute-start | bytes 6291464 | tf_op jit(solution)/shard_map/ppermute | solution.py:61
  (126 other events, 4244.4 us)
Sparse Core Ops, SparseCore 0:
  10.5 30.4 all-gather.9
  43.5 23.3 all-gather.11
  69.3 23.3 all-gather.13
  95.0 28.0 all-gather.15
  136.4 85.3 all-gather.17
  545.0 42.6 all-gather.19
  754.5 47.5 all-gather.21
  964.4 65.1 reduce-scatter.15
  1108.6 101.3 reduce-scatter.17
  1312.3 63.4 reduce-scatter.19
  1678.7 40.1 reduce-scatter.9
  1721.9 35.9 reduce-scatter.11
  1761.1 41.0 reduce-scatter.13
  1840.8 45.5 reduce-scatter.7

commit v2 on v1

--- a/solution.py
+++ b/solution.py
@@ -1,9 +1,11 @@
 import functools
+
 
 import jax
 import jax.numpy as jnp
 from jax import lax
 from jax.sharding import PartitionSpec as P
+
 
 HEAD_SIZE = 128
 SEQUENCE_TOKENS = 2048
@@ -64,6 +66,50 @@
     return block(j) + up.astype(jnp.float32) + down.astype(jnp.float32)
 
 
+def tensor_gather_direct(rows, n):
+    if n == 1:
+        return rows
+    j = lax.axis_index("tensor")
+    count = rows.shape[0]
+    ups = {}
+    downs = {}
+    for d in range(1, n):
+        ups[d] = lax.ppermute(rows, "tensor", [(i, i + d) for i in range(n - d)])
+        downs[d] = lax.ppermute(rows, "tensor", [(i, i - d) for i in range(d, n)])
+    rel = [rows]
+    for m in range(1, n):
+        rel.append(jnp.where(j + m <= n - 1, downs[m], ups[n - m]))
+    rel = jnp.concatenate(rel, axis=0)
+    twice = jnp.concatenate([rel, rel], axis=0)
+    start = ((n - j) % n) * count
+    return lax.dynamic_slice_in_dim(twice, start, n * count, 0)
+
+
+def tensor_scatter_direct(partial, n):
+    if n == 1:
+        return partial.astype(jnp.float32)
+    j = lax.axis_index("tensor")
+    count = partial.shape[0] // n
+
+    def block(t):
+        return lax.dynamic_slice_in_dim(partial, t * count, count, 0).astype(jnp.float32)
+
+    total = block(j)
+    for d in range(1, n):
+        up = lax.ppermute(
+            block(jnp.minimum(j + d, n - 1)).astype(jnp.bfloat16),
+            "tensor",
+            [(i, i + d) for i in range(n - d)],
+        )
+        down = lax.ppermute(
+            block(jnp.maximum(j - d, 0)).astype(jnp.bfloat16),
+            "tensor",
+            [(i, i - d) for i in range(d, n)],
+        )
+        total = total + up.astype(jnp.float32) + down.astype(jnp.float32)
+    return total
+
+
 def rms_scale(row_data, gain_vec):
     inverse = lax.rsqrt(jnp.mean(row_data * row_data, axis=-1, keepdims=True) + EPSILON)
     return row_data * inverse * gain_vec
@@ -172,7 +218,7 @@
     return (d_query.reshape(query_tensor.shape), d_key, d_value)
 
 
-def on_device(
+def on_device_body(
     tokens,
     doc_start,
     piece_ids,
@@ -237,11 +283,14 @@
     q_b = rope_query(query_unrotated, query_norm_gain).astype(bf16)
     k_b = rope_query(key_unrotated, gain_k).astype(bf16)
     q_grouped = q_b.reshape(seq_count, SEQUENCE_TOKENS, kv_local, heads_per_group, HEAD_SIZE)
+    out_grad_late, q_grouped, k_b = lax.optimization_barrier((out_grad, q_grouped, k_b))
 
     def forward_seq(inputs):
         return attend_sequence(inputs[0], inputs[1], inputs[2], inputs[3], inputs[4])
 
-    attn_f, log_totals = lax.map(forward_seq, (q_grouped, k_b, v_b, seq_starts, seq_pieces))
+    attn_f, log_totals = lax.map(
+        forward_seq, (q_grouped, k_b, v_b, seq_starts, seq_pieces)
+    )
     attended = attn_f.reshape(total_rows, q_width).astype(bf16)
     wg_b, wu_b, wd_b, gm_b = (
         lax.all_gather(w_gate.astype(bf16), "dp", axis=0, tiled=True),
@@ -259,24 +308,22 @@
     gate_pre = gate_up[:, :hidden_width]
     up_pre = gate_up[:, hidden_width:]
     hidden_b = (jax.nn.silu(gate_pre) * up_pre).astype(bf16)
-    layer_out = (
-        residual
-        + tensor_scatter(jnp.dot(hidden_b, wd_b, preferred_element_type=f32), tensor_n)
-    ).astype(bf16)
+    mlp_sum = tensor_scatter_direct(jnp.dot(hidden_b, wd_b, preferred_element_type=f32), tensor_n)
+    layer_out = (residual + mlp_sum).astype(bf16)
     wg_c, wu_c, wd_back = (
         lax.all_gather(w_gate.astype(bf16), "dp", axis=0, tiled=True),
         lax.all_gather(w_up.astype(bf16), "dp", axis=0, tiled=True),
         lax.all_gather(w_down.astype(bf16), "dp", axis=1, tiled=True),
     )
     w_gu_back = jnp.concatenate([wg_c, wu_c], axis=1)
-    grad_whole = tensor_gather(out_grad, tensor_n)
+    grad_whole = tensor_gather_direct(out_grad_late, tensor_n)
     grad_down = lax.dot_general(hidden_b, grad_whole, CONTRACT_ROWS, preferred_element_type=f32)
     d_hidden = lax.dot_general(grad_whole, wd_back, CONTRACT_COLS, preferred_element_type=f32)
 
     def swiglu(gate_in, up_in):
         return jax.nn.silu(gate_in) * up_in
 
-    swiglu_value, swiglu_back = jax.vjp(swiglu, gate_pre, up_pre)
+    _, swiglu_back = jax.vjp(swiglu, gate_pre, up_pre)
     d_gate, d_up = swiglu_back(d_hidden)
     d_gate_up = jnp.concatenate([d_gate, d_up], axis=1).astype(bf16)
     grad_gate_up = lax.dot_general(
@@ -284,7 +331,7 @@
     )
     rows_b = d_gate_up
     d_normed_two = tensor_scatter(lax.dot_general(rows_b, w_gu_back, CONTRACT_COLS, preferred_element_type=f32), tensor_n)
-    norm_value, norm_two_back = jax.vjp(rms_scale, residual, mlp_g)
+    _, norm_two_back = jax.vjp(rms_scale, residual, mlp_g)
     d_resid_norm, d_mlp_gain = norm_two_back(d_normed_two)
     d_residual = out_grad.astype(f32) + d_resid_norm
     wq_c, wk_c, wv_c, wo_back = (
@@ -300,18 +347,41 @@
         attn_grad_whole, wo_back, CONTRACT_COLS, preferred_element_type=f32
     ).astype(bf16)
     d_grouped = d_attended.reshape(seq_count, SEQUENCE_TOKENS, kv_local, heads_per_group, HEAD_SIZE)
+    grad_gate_up, grad_down, grad_out, d_grouped = lax.optimization_barrier(
+        (grad_gate_up, grad_down, grad_out, d_grouped)
+    )
 
     def back_seq(inputs):
         return attend_back(
             inputs[0], inputs[1], inputs[2], inputs[3], inputs[4], inputs[5], inputs[6]
         )
 
+    mlp_owned = (
+        lax.psum_scatter(
+            grad_out.astype(jnp.bfloat16), "dp", scatter_dimension=1, tiled=True
+        ).astype(jnp.float32),
+        lax.psum_scatter(
+            grad_gate_up[:, :hidden_width].astype(jnp.bfloat16),
+            "dp",
+            scatter_dimension=0,
+            tiled=True,
+        ).astype(jnp.float32),
+        lax.psum_scatter(
+            grad_gate_up[:, hidden_width:].astype(jnp.bfloat16),
+            "dp",
+            scatter_dimension=0,
+            tiled=True,
+        ).astype(jnp.float32),
+        lax.psum_scatter(
+            grad_down.astype(jnp.bfloat16), "dp", scatter_dimension=1, tiled=True
+        ).astype(jnp.float32),
+    )
     d_query, d_key, d_value = lax.map(
         back_seq, (q_grouped, k_b, v_b, d_grouped, log_totals, seq_starts, seq_pieces)
     )
-    query_value, query_back = jax.vjp(rope_query, query_unrotated, query_norm_gain)
+    _, query_back = jax.vjp(rope_query, query_unrotated, query_norm_gain)
     d_q_raw, d_query_gain = query_back(d_query.reshape(query_unrotated.shape))
-    key_value, key_back = jax.vjp(rope_query, key_unrotated, gain_k)
+    _, key_back = jax.vjp(rope_query, key_unrotated, gain_k)
     d_k_raw, d_key_gain = key_back(d_key)
     d_qkv = jnp.concatenate(
         [
@@ -324,10 +394,10 @@
     grad_qkv = lax.dot_general(gathered, d_qkv, CONTRACT_ROWS, preferred_element_type=f32)
     rows_b = d_qkv
     d_normed = tensor_scatter(lax.dot_general(rows_b, w_qkv_back, CONTRACT_COLS, preferred_element_type=f32), tensor_n)
-    norm_one, norm_back = jax.vjp(rms_scale, tok_rows, attn_g)
+    _, norm_back = jax.vjp(rms_scale, tok_rows, attn_g)
     d_x_norm, d_attn_gain = norm_back(d_normed)
     grad_tokens = d_residual + d_x_norm
-    owned = (
+    attn_owned = (
         lax.psum_scatter(
             grad_qkv[:, :q_width].astype(jnp.bfloat16), "dp", scatter_dimension=0, tiled=True
         ).astype(jnp.float32),
@@ -343,24 +413,15 @@
             scatter_dimension=0,
             tiled=True,
         ).astype(jnp.float32),
-        lax.psum_scatter(
-            grad_out.astype(jnp.bfloat16), "dp", scatter_dimension=1, tiled=True
-        ).astype(jnp.float32),
-        lax.psum_scatter(
-            grad_gate_up[:, :hidden_width].astype(jnp.bfloat16),
-            "dp",
-            scatter_dimension=0,
-            tiled=True,
-        ).astype(jnp.float32),
-        lax.psum_scatter(
-            grad_gate_up[:, hidden_width:].astype(jnp.bfloat16),
-            "dp",
-            scatter_dimension=0,
-            tiled=True,
-        ).astype(jnp.float32),
-        lax.psum_scatter(
-            grad_down.astype(jnp.bfloat16), "dp", scatter_dimension=1, tiled=True
-        ).astype(jnp.float32),
+    )
+    owned = (
+        attn_owned[0],
+        attn_owned[1],
+        attn_owned[2],
+        mlp_owned[0],
+        mlp_owned[1],
+        mlp_owned[2],
+        mlp_owned[3],
         lax.psum_scatter(
             d_attn_gain.astype(jnp.bfloat16), "dp", scatter_dimension=0, tiled=True
         ).astype(jnp.float32),
@@ -392,6 +453,10 @@
     )
 
 
+def on_device(*args, tensor_n=1):
+    return on_device_body(*args, tensor_n=tensor_n)
+
+
 def solution(mesh):
     return jax.shard_map(
         functools.partial(on_device, tensor_n=mesh.shape["tensor"]),

time: 2010 us -> 2100 us (1.045)
  starting transfers between devices: 133 us -> 175 us
  waiting for transfers between devices: 797 us -> 838 us
  blocking collectives: 111 us -> 146 us
  other arithmetic: 345 us -> 312 us
    ppermute x0 -> x12, waiting for transfers between devices: none -> 155 us  [the longest x3 105 us: tensor_gather_direct(): downs[d] = lax.ppermute(rows, 'tensor', [(i, i - d) for i in range(d, n)])]
    ppermute x0 -> x12, starting transfers between devices: none -> 75.3 us  [the longest x3 50.6 us: tensor_gather_direct(): ups[d] = lax.ppermute(rows, 'tensor', [(i, i + d) for i in range(n - d)])]
    ppermute x12 -> x9, waiting for transfers between devices: 143 us -> 74.2 us  [tensor_gather(): up = lax.ppermute(up, 'tensor', [(i, i + 1) for i in range(s - 1, n - 1)])]
    ppermute x12 -> x9, waiting for transfers between devices: 251 us -> 192 us  [tensor_gather(): lax.ppermute(down, 'tensor', [(i, i - 1) for i in range(1, n - s + 1)])]
    psum x1, blocking collectives: 59.9 us -> 101 us  [on_device_body(): gains_sum = lax.psum((owned[7], owned[8], owned[9], owned[10]), 'tensor')]
    ppermute x12 -> x9, waiting for transfers between devices: 302 us -> 322 us  [tensor_scatter(): lax.ppermute(acc_up.astype(jnp.bfloat16), 'tensor', [(i, i + 1) for i in...]
    ppermute x12 -> x9, starting transfers between devices: 59.4 us -> 40.4 us  [tensor_scatter(): lax.ppermute(acc_up.astype(jnp.bfloat16), 'tensor', [(i, i + 1) for i in...]
    convert_element_type x8 -> x6, other arithmetic: 45.5 us -> 30 us  [tensor_scatter(): acc_up.astype(jnp.bfloat16)]
  transfers between devices with their start and end apart: 62 -> 62, of which waited for: 29 -> 26; matrix products, arithmetic and copies ran while one was open for 40% -> 22% of each run, Pallas kernels for 0% -> 0%
where the time goes in v2:
time: 2100 us; the launch traced here: 2090 us
  waiting for transfers between devices  838 us (40%)
  matrix products  446 us (21%)
  other arithmetic  312 us (15%)
  starting transfers between devices  175 us (8%)
  blocking collectives  146 us (7%)
  local copies, waits for them, and re-layouts  141 us (7%)
    ppermute x9, waiting for transfers between devices, tensor_scatter(): lax.ppermute(acc_up.astype(jnp.bfloat16), 'tensor', [(i, i + 1) for i in...  322 us
    ppermute x9, waiting for transfers between devices, tensor_gather(): lax.ppermute(down, 'tensor', [(i, i - 1) for i in range(1, n - s + 1)])  192 us
    ppermute x3, waiting for transfers between devices, tensor_gather_direct(): downs[d] = lax.ppermute(rows, 'tensor', [(i, i - d) for i in range(d, n)])  105 us
    psum x1, blocking collectives, on_device_body(): gains_sum = lax.psum((owned[7], owned[8], owned[9], owned[10]), 'tensor')  101 us
    ppermute x9, waiting for transfers between devices, tensor_scatter(): lax.ppermute(acc_down.astype(jnp.bfloat16), 'tensor', [(i, i - 1) for i i...  92.7 us
    unnamed x25, other arithmetic  76 us
    ppermute x9, waiting for transfers between devices, tensor_gather(): up = lax.ppermute(up, 'tensor', [(i, i + 1) for i in range(s - 1, n - 1)])  74.2 us
    dot_general x8, matrix products, one_block(): jnp.einsum('qkgd,skd->kgqs', q_rows, key_rows, preferred_element_type=jnp...  57.3 us
  transfers between devices with their start and end apart: 62, of which 26 were waited for; matrix products, arithmetic and copies ran while one was open for 22% of the time, Pallas kernels for 0%

profile of v2, /device:TPU:0, one launch (start us, length us, event | category | flops | bytes accessed | tf_op | source)
XLA Modules:
  0.0 2091.1 jit_solution(7332784427770260844)
XLA Ops:
  33.7 43.4 %collective-permute-done.1 = bf16[512,2048]{1,0:T(8,128)(2,1)S(1)} collective-permute-done((bf16[512,2048]{1,0:T(8,128)(2,1)}, bf16[512,2048]{1,0:T(8,128)(2,1)S(1)}, u32[]{:S(2)}, u32[]{:S(2)}) %collective-permute-start.1) | collective-permute-done | bytes 2097184 | tf_op jit(solution)/shard_map/ppermute | solution.py:32
  108.7 22.9 %collective-permute-done.4 = bf16[512,2048]{1,0:T(8,128)(2,1)} collective-permute-done((bf16[512,2048]{1,0:T(8,128)(2,1)}, bf16[512,2048]{1,0:T(8,128)(2,1)}, u32[]{:S(2)}, u32[]{:S(2)}) %collective-permute-start.4) | collective-permute-done | bytes 2097184 | tf_op jit(solution)/shard_map/ppermute | solution.py:33
  149.0 50.9 %collective-permute-done.5 = bf16[512,2048]{1,0:T(8,128)(2,1)} collective-permute-done((bf16[512,2048]{1,0:T(8,128)(2,1)}, bf16[512,2048]{1,0:T(8,128)(2,1)}, u32[]{:S(2)}, u32[]{:S(2)}) %collective-permute-start.5) | collective-permute-done | bytes 2097184 | tf_op jit(solution)/shard_map/ppermute | solution.py:33
  256.5 86.4 %while.51 = (s32[]{:T(128)}, bf16[4,512,2,2,128]{4,1,3,2,0:T(8,128)(2,1)}, f32[4,2,2,512]{3,2,1,0:T(2,128)}, s32[4]{0:T(128)S(1)}, s32[17,1]{0,1:T(1,128)S(1)}, ...) while((s32[]{:T(128)}, ...), condition=%wide.region_8.9_spmd, body=%wide.region_5.8_spmd.sunk | while | flops 2204107776 | bytes 58313080 | solution.py:173
  372.5 41.5 %collective-permute-done.6 = bf16[512,2048]{1,0:T(8,128)(2,1)} collective-permute-done((bf16[512,2048]{1,0:T(8,128)(2,1)}, bf16[512,2048]{1,0:T(8,128)(2,1)}, u32[]{:S(2)}, u32[]{:S(2)}) %collective-permute-start.6) | collective-permute-done | bytes 2097184 | tf_op jit(solution)/shard_map/ppermute | solution.py:62
  425.7 41.6 %collective-permute-done.7 = bf16[512,2048]{1,0:T(8,128)(2,1)} collective-permute-done((bf16[512,2048]{1,0:T(8,128)(2,1)}, bf16[512,2048]{1,0:T(8,128)(2,1)}, u32[]{:S(2)}, u32[]{:S(2)}) %collective-permute-start.7) | collective-permute-done | bytes 2097184 | tf_op jit(solution)/shard_map/ppermute | solution.py:62
  499.1 25.7 %collective-permute-done.8 = bf16[512,2048]{1,0:T(8,128)(2,1)} collective-permute-done((bf16[512,2048]{1,0:T(8,128)(2,1)}, bf16[512,2048]{1,0:T(8,128)(2,1)}, u32[]{:S(2)}, u32[]{:S(2)}) %collective-permute-start.8) | collective-permute-done | bytes 2097184 | tf_op jit(solution)/shard_map/ppermute | solution.py:62
  524.8 54.5 %collective-permute-done.11 = bf16[512,2048]{1,0:T(8,128)(2,1)} collective-permute-done((bf16[512,2048]{1,0:T(8,128)(2,1)}, bf16[512,2048]{1,0:T(8,128)(2,1)}, u32[]{:S(2)}, u32[]{:S(2)}) %collective-permute-start.11) | collective-permute-done | bytes 2097184 | tf_op jit(solution)/shard_map/ppermute | solution.py:63
  597.3 29.0 %collective-permute-done.24 = bf16[512,2048]{1,0:T(8,128)(2,1)S(1)} collective-permute-done((bf16[512,2048]{1,0:T(8,128)(2,1)}, bf16[512,2048]{1,0:T(8,128)(2,1)S(1)}, u32[]{:S(2)}, u32[]{:S(2)}) %collective-permute-start.24) | collective-permute-done | bytes 2097184 | tf_op jit(solution)/shard_map/ppermute | solution.py:78
  626.3 46.6 %collective-permute-start.27 = (bf16[512,2048]{1,0:T(8,128)(2,1)S(1)}, bf16[512,2048]{1,0:T(8,128)(2,1)}, u32[]{:S(2)}, u32[]{:S(2)}) collective-permute-start(bf16[512,2048]{1,0:T(8,128)(2,1)S(1)} %copy-done.15), channel_id=1, source_target_pairs={{0,2},{1,3},{4,6},{5,7},{8,10},{9,11},{12,14},{13,15},{16,18},{17,... | collective-permute-start | bytes 6291464 | tf_op jit(solution)/shard_map/ppermute | solution.py:77
  684.4 76.1 %collective-permute-done.26 = bf16[512,2048]{1,0:T(8,128)(2,1)S(1)} collective-permute-done((bf16[512,2048]{1,0:T(8,128)(2,1)S(1)}, bf16[512,2048]{1,0:T(8,128)(2,1)S(1)}, u32[]{:S(2)}, u32[]{:S(2)}) %collective-permute-start.26) | collective-permute-done | bytes 2097184 | tf_op jit(solution)/shard_map/ppermute | solution.py:78
  770.1 15.2 collective-permute-done.29
  794.2 52.2 %collective-permute-done.16 = bf16[512,2048]{1,0:T(8,128)(2,1)} collective-permute-done((bf16[512,2048]{1,0:T(8,128)(2,1)}, bf16[512,2048]{1,0:T(8,128)(2,1)}, u32[]{:S(2)}, u32[]{:S(2)}) %collective-permute-start.16) | collective-permute-done | bytes 2097184 | tf_op jit(solution)/shard_map/ppermute | solution.py:33
  867.3 35.8 %collective-permute-done.17 = bf16[512,2048]{1,0:T(8,128)(2,1)S(1)} collective-permute-done((bf16[512,2048]{1,0:T(8,128)(2,1)}, bf16[512,2048]{1,0:T(8,128)(2,1)S(1)}, u32[]{:S(2)}, u32[]{:S(2)}) %collective-permute-start.17) | collective-permute-done | bytes 2097184 | tf_op jit(solution)/shard_map/ppermute | solution.py:33
  926.9 31.6 %fusion.66 = f32[2048,3072]{1,0:T(8,128)} fusion(bf16[2048,3072]{1,0:T(8,128)(2,1)S(1)} %bitcast.217, bf16[4096,2048]{1,0:T(8,128)(2,1)} %fusion.110, s32[]{:T(128)S(6)} %select_n.153), kind=kOutput, calls=%fused_computation.92 | convolution fusion | flops 25769803776 | bytes 46137348 | tf_op jit(solution)/shard_map/dot_general | solution.py:307
  958.6 29.9 %fusion.53 = (bf16[2048,1536]{1,0:T(8,128)(2,1)}, bf16[2048,1536]{1,0:T(8,128)(2,1)}, bf16[2048,1536]{1,0:T(8,128)(2,1)}) fusion(f32[2048,3072]{1,0:T(8,128)} %fusion.66, bf16[1536,2048]{1,0:T(8,128)(2,1)} %all-gather.22.cloned.1.call-done, bf16[4096,2048]{1,0:T(8,128)(2,1)} %fusion.112, s32[]{:T(128)S(6)} %select_n.153), kind=kOutput, calls=%fused_computation.70 | convolution fusion | flops 12935233536 | bytes 58720260 | tf_op jit(solution)/shard_map/dot_general | solution.py:321
  988.5 34.7 %fusion.56 = f32[2048,2048]{1,0:T(8,128)} fusion(bf16[2048,3072]{1,0:T(8,128)(2,1)} %constant_dynamic-update-slice_fusion.7, bf16[2048,1536]{1,0:T(8,128)(2,1)} %get-tuple-element.562, bf16[2048,1536]{1,0:T(8,128)(2,1)} %get-tuple-element.561), kind=kOutput, calls=%fused_computation.82 | convolution fusion | flops 25794969600 | bytes 41943040 | tf_op jit(solution)/shard_map/dot_general | solution.py:333
  1034.6 36.4 %collective-permute-done.30 = bf16[512,2048]{1,0:T(8,128)(2,1)S(1)} collective-permute-done((bf16[512,2048]{1,0:T(8,128)(2,1)S(1)}, bf16[512,2048]{1,0:T(8,128)(2,1)S(1)}, u32[]{:S(2)}, u32[]{:S(2)}) %collective-permute-start.30) | collective-permute-done | bytes 2097184 | tf_op jit(solution)/shard_map/ppermute | solution.py:62
  1079.6 34.3 %collective-permute-done.31 = bf16[512,2048]{1,0:T(8,128)(2,1)} collective-permute-done((bf16[512,2048]{1,0:T(8,128)(2,1)S(1)}, bf16[512,2048]{1,0:T(8,128)(2,1)}, u32[]{:S(2)}, u32[]{:S(2)}) %collective-permute-start.31) | collective-permute-done | bytes 2097184 | tf_op jit(solution)/shard_map/ppermute | solution.py:62
  1128.2 32.9 %collective-permute-done.32 = bf16[512,2048]{1,0:T(8,128)(2,1)S(1)} collective-permute-done((bf16[512,2048]{1,0:T(8,128)(2,1)}, bf16[512,2048]{1,0:T(8,128)(2,1)S(1)}, u32[]{:S(2)}, u32[]{:S(2)}) %collective-permute-start.32) | collective-permute-done | bytes 2097184 | tf_op jit(solution)/shard_map/ppermute | solution.py:62
  1161.1 38.1 %collective-permute-done.35 = bf16[512,2048]{1,0:T(8,128)(2,1)S(1)} collective-permute-done((bf16[512,2048]{1,0:T(8,128)(2,1)S(1)}, bf16[512,2048]{1,0:T(8,128)(2,1)S(1)}, u32[]{:S(2)}, u32[]{:S(2)}) %collective-permute-start.35) | collective-permute-done | bytes 2097184 | tf_op jit(solution)/shard_map/ppermute | solution.py:63
  1221.7 30.7 %collective-permute-done.37 = bf16[512,2048]{1,0:T(8,128)(2,1)} collective-permute-done((bf16[512,2048]{1,0:T(8,128)(2,1)}, bf16[512,2048]{1,0:T(8,128)(2,1)}, u32[]{:S(2)}, u32[]{:S(2)}) %collective-permute-start.37) | collective-permute-done | bytes 2097184 | tf_op jit(solution)/shard_map/ppermute | solution.py:32
  1267.5 34.5 %fusion.55 = bf16[2048,3072]{1,0:T(8,128)(2,1)} fusion(bf16[2048,1536]{1,0:T(8,128)(2,1)} %get-tuple-element.562, bf16[2048,1536]{1,0:T(8,128)(2,1)} %get-tuple-element.561, bf16[4096,2048]{1,0:T(8,128)(2,1)} %fusion.110, s32[]{:T(128)S(6)} %select_n.153), kind=kOutput, calls=%fused_computation.81 | convolution fusion | flops 25794969600 | bytes 33554436 | tf_op jit(solution)/shard_map/dot_general | solution.py:329
  1313.3 19.6 fusion.61
  1389.5 256.9 %while.52 = (s32[]{:T(128)}, f32[2048,2,128]{0,2,1:T(8,128)S(1)}, f32[2048,2,128]{0,2,1:T(8,128)}, f32[4,512,2,2,128]{4,1,0,3,2:T(8,128)}, s32[4]{0:T(128)S(1)},...) while((s32[]{:T(128)}, f32[2048,2,128]{0,2,1:T(8,128)S(1)}, ...), condition=%wide.region_13.14_spmd.clone, body=%wide.region_11.13_spmd.clone.sunk | while | flops 5440799744 | bytes 186755056 | solution.py:217
  1720.8 36.2 %collective-permute-done.42 = bf16[512,2048]{1,0:T(8,128)(2,1)S(1)} collective-permute-done((bf16[512,2048]{1,0:T(8,128)(2,1)S(1)}, bf16[512,2048]{1,0:T(8,128)(2,1)S(1)}, u32[]{:S(2)}, u32[]{:S(2)}) %collective-permute-start.42) | collective-permute-done | bytes 2097184 | tf_op jit(solution)/shard_map/ppermute | solution.py:62
  1763.7 29.5 %collective-permute-done.43 = bf16[512,2048]{1,0:T(8,128)(2,1)S(1)} collective-permute-done((bf16[512,2048]{1,0:T(8,128)(2,1)}, bf16[512,2048]{1,0:T(8,128)(2,1)S(1)}, u32[]{:S(2)}, u32[]{:S(2)}) %collective-permute-start.43) | collective-permute-done | bytes 2097184 | tf_op jit(solution)/shard_map/ppermute | solution.py:62
  1799.7 19.6 fusion.138
  1856.2 26.4 %collective-permute-done.18 = bf16[512,2048]{1,0:T(8,128)(2,1)} collective-permute-done((bf16[512,2048]{1,0:T(8,128)(2,1)S(1)}, bf16[512,2048]{1,0:T(8,128)(2,1)}, u32[]{:S(2)}, u32[]{:S(2)}) %collective-permute-start.18) | collective-permute-done | bytes 2097184 | tf_op jit(solution)/shard_map/ppermute | solution.py:99
  1883.9 43.7 %collective-permute-done.44 = bf16[512,2048]{1,0:T(8,128)(2,1)} collective-permute-done((bf16[512,2048]{1,0:T(8,128)(2,1)S(1)}, bf16[512,2048]{1,0:T(8,128)(2,1)}, u32[]{:S(2)}, u32[]{:S(2)}) %collective-permute-start.44) | collective-permute-done | bytes 2097184 | tf_op jit(solution)/shard_map/ppermute | solution.py:62
  1960.9 100.5 %all-reduce.10 = (f32[256]{0:T(256)}, f32[16]{0:T(128)}, f32[16]{0:T(128)}, f32[256]{0:T(256)}) all-reduce(f32[256]{0:T(256)S(1)} %dynamic-slice_convert_fusion.15, f32[16]{0:T(128)S(1)} %dynamic-slice_convert_fusion.14, f32[16]{0:T(128)S(1)} %dynamic-slice_convert_fusion.13, ...), channel_id=1, replica_groups=mesh['dp'=8,'tensor'=4] {'tensor'}, use_global_device_ids=true, to_apply=%region_19.20 | all-reduce | flops 544 | bytes 4352 | tf_op jit(solution)/shard_map/psum | solution.py:438
  2061.5 15.6 fusion.78
  (567 shorter events, 926.9 us)
Async XLA Ops:
  7.2 126.2 %all-gather.10.cloned.1.call-start = ((), (), s32[]{:S(2)}) async-start(), calls=%async_computation.7 | async-start | bytes 2359296 | tf_op jit(solution)/shard_map/all_gather | solution.py:248
  9.2 127.3 %all-gather.12.cloned.1.call-start = ((), (), s32[]{:S(2)}) async-start(), calls=%async_computation.8 | async-start | bytes 1179648 | tf_op jit(solution)/shard_map/all_gather | solution.py:249
  10.9 127.9 %all-gather.14.cloned.1.call-start = ((), (), s32[]{:S(2)}) async-start(), calls=%async_computation.9 | async-start | bytes 1179648 | tf_op jit(solution)/shard_map/all_gather | solution.py:250
  12.6 340.7 %all-gather.16.cloned.1.call-start = ((), (), s32[]{:S(2)}) async-start(), calls=%async_computation.10 | async-start | bytes 2359296 | tf_op jit(solution)/shard_map/all_gather | solution.py:251
  32.3 815.4 %all-gather.18.cloned.1.call-start = ((), (), s32[]{:S(2)}) async-start(), calls=%async_computation.11 | async-start | bytes 7077888 | tf_op jit(solution)/shard_map/all_gather | solution.py:296
  88.0 765.6 %all-gather.20.cloned.1.call-start = ((), (), s32[]{:S(2)}) async-start(), calls=%async_computation.12 | async-start | bytes 7077888 | tf_op jit(solution)/shard_map/all_gather | solution.py:297
  425.6 533.0 %all-gather.22.cloned.1.call-start = ((), (), s32[]{:S(2)}) async-start(), calls=%async_computation.13 | async-start | bytes 7077888 | tf_op jit(solution)/shard_map/all_gather | solution.py:298
  487.7 91.7 %collective-permute-start.11 = (bf16[512,2048]{1,0:T(8,128)(2,1)}, bf16[512,2048]{1,0:T(8,128)(2,1)}, u32[]{:S(2)}, u32[]{:S(2)}) collective-permute-start(bf16[512,2048]{1,0:T(8,128)(2,1)} %add_convert_fusion.9), channel_id=1, source_target_pairs={{1,0},{2,1},{3,2},{5,4},{6,5},{7,6},{9,8},{10,9},{11,10},{13,12},{... | collective-permute-start | bytes 6291464 | tf_op jit(solution)/shard_map/ppermute | solution.py:63
  497.8 128.5 %collective-permute-start.24 = (bf16[512,2048]{1,0:T(8,128)(2,1)}, bf16[512,2048]{1,0:T(8,128)(2,1)S(1)}, u32[]{:S(2)}, u32[]{:S(2)}) collective-permute-start(bf16[512,2048]{1,0:T(8,128)(2,1)} %param.33), channel_id=1, source_target_pairs={{1,0},{2,1},{3,2},{5,4},{6,5},{7,6},{9,8},{10,9},{11,10},{13,12},{... | collective-permute-start | bytes 6291464 | tf_op jit(solution)/shard_map/ppermute | solution.py:78
  588.0 84.9 %collective-permute-start.13 = (bf16[512,2048]{1,0:T(8,128)(2,1)}, bf16[512,2048]{1,0:T(8,128)(2,1)}, u32[]{:S(2)}, u32[]{:S(2)}) collective-permute-start(bf16[512,2048]{1,0:T(8,128)(2,1)} %get-tuple-element.552), channel_id=1, source_target_pairs={{0,1},{1,2},{2,3},{4,5},{5,6},{6,7},{8,9},{9,10},{10,11},{12,13},{... | collective-permute-start | bytes 6291464 | tf_op jit(solution)/shard_map/ppermute | solution.py:32
  593.3 89.8 %collective-permute-start.25 = (bf16[512,2048]{1,0:T(8,128)(2,1)S(1)}, bf16[512,2048]{1,0:T(8,128)(2,1)S(1)}, u32[]{:S(2)}, u32[]{:S(2)}) collective-permute-start(bf16[512,2048]{1,0:T(8,128)(2,1)S(1)} %copy-done.15), channel_id=1, source_target_pairs={{0,3},{4,7},{8,11},{12,15},{16,19},{20,23},{24,27},{28,31}} | collective-permute-start | bytes 6291464 | tf_op jit(solution)/shard_map/ppermute | solution.py:77
  594.7 165.8 %collective-permute-start.26 = (bf16[512,2048]{1,0:T(8,128)(2,1)S(1)}, bf16[512,2048]{1,0:T(8,128)(2,1)S(1)}, u32[]{:S(2)}, u32[]{:S(2)}) collective-permute-start(bf16[512,2048]{1,0:T(8,128)(2,1)S(1)} %copy-done.15), channel_id=1, source_target_pairs={{2,0},{3,1},{6,4},{7,5},{10,8},{11,9},{14,12},{15,13},{18,16},{19,... | collective-permute-start | bytes 6291464 | tf_op jit(solution)/shard_map/ppermute | solution.py:78
  596.0 168.4 %collective-permute-start.12 = (bf16[512,2048]{1,0:T(8,128)(2,1)}, bf16[512,2048]{1,0:T(8,128)(2,1)}, u32[]{:S(2)}, u32[]{:S(2)}) collective-permute-start(bf16[512,2048]{1,0:T(8,128)(2,1)} %get-tuple-element.552), channel_id=1, source_target_pairs={{1,0},{2,1},{3,2},{5,4},{6,5},{7,6},{9,8},{10,9},{11,10},{13,12},{... | collective-permute-start | bytes 6291464 | tf_op jit(solution)/shard_map/ppermute | solution.py:33
  626.3 140.9 %collective-permute-start.27 = (bf16[512,2048]{1,0:T(8,128)(2,1)S(1)}, bf16[512,2048]{1,0:T(8,128)(2,1)}, u32[]{:S(2)}, u32[]{:S(2)}) collective-permute-start(bf16[512,2048]{1,0:T(8,128)(2,1)S(1)} %copy-done.15), channel_id=1, source_target_pairs={{0,2},{1,3},{4,6},{5,7},{8,10},{9,11},{12,14},{13,15},{16,18},{17,... | collective-permute-start | bytes 6291464 | tf_op jit(solution)/shard_map/ppermute | solution.py:77
  672.9 95.2 %collective-permute-start.14 = (bf16[512,2048]{1,0:T(8,128)(2,1)}, bf16[512,2048]{1,0:T(8,128)(2,1)}, u32[]{:S(2)}, u32[]{:S(2)}) collective-permute-start(bf16[512,2048]{1,0:T(8,128)(2,1)} %collective-permute-done.13), channel_id=1, source_target_pairs={{1,2},{2,3},{5,6},{6,7},{9,10},{10,11},{13,14},{14,15},{17,18},{18... | collective-permute-start | bytes 6291464 | tf_op jit(solution)/shard_map/ppermute | solution.py:32
  683.1 87.0 %collective-permute-start.28 = (bf16[512,2048]{1,0:T(8,128)(2,1)S(1)}, bf16[512,2048]{1,0:T(8,128)(2,1)}, u32[]{:S(2)}, u32[]{:S(2)}) collective-permute-start(bf16[512,2048]{1,0:T(8,128)(2,1)S(1)} %copy-done.15), channel_id=1, source_target_pairs={{3,0},{7,4},{11,8},{15,12},{19,16},{23,20},{27,24},{31,28}} | collective-permute-start | bytes 6291464 | tf_op jit(solution)/shard_map/ppermute | solution.py:78
  764.1 1168.7 %reduce-scatter.10.cloned.1.call-start = ((), (), s32[]{:S(2)}) async-start(), calls=%async_computation.15 | async-start | bytes 1179648 | tf_op jit(solution)/shard_map/reduce_scatter | solution.py:404
  764.4 82.0 %collective-permute-start.16 = (bf16[512,2048]{1,0:T(8,128)(2,1)}, bf16[512,2048]{1,0:T(8,128)(2,1)}, u32[]{:S(2)}, u32[]{:S(2)}) collective-permute-start(bf16[512,2048]{1,0:T(8,128)(2,1)} %collective-permute-done.12), channel_id=1, source_target_pairs={{1,0},{2,1},{5,4},{6,5},{9,8},{10,9},{13,12},{14,13},{17,16},{18,1... | collective-permute-start | bytes 6291464 | tf_op jit(solution)/shard_map/ppermute | solution.py:33
  768.1 91.6 %collective-permute-start.15 = (bf16[512,2048]{1,0:T(8,128)(2,1)}, bf16[512,2048]{1,0:T(8,128)(2,1)}, u32[]{:S(2)}, u32[]{:S(2)}) collective-permute-start(bf16[512,2048]{1,0:T(8,128)(2,1)} %collective-permute-done.14), channel_id=1, source_target_pairs={{2,3},{6,7},{10,11},{14,15},{18,19},{22,23},{26,27},{30,31}} | collective-permute-start | bytes 6291464 | tf_op jit(solution)/shard_map/ppermute | solution.py:32
  1686.1 248.3 %reduce-scatter.12.cloned.1.call-start = ((), (), s32[]{:S(2)}) async-start(), calls=%async_computation.16 | async-start | bytes 1179648 | tf_op jit(solution)/shard_map/reduce_scatter | solution.py:410
  1686.9 249.2 %reduce-scatter.8.cloned.1.call-start = ((), (), s32[]{:S(2)}) async-start(), calls=%async_computation.14 | async-start | bytes 2359296 | tf_op jit(solution)/shard_map/reduce_scatter | solution.py:401
  1690.0 247.9 %reduce-scatter.14.cloned.1.call-start = ((), (), s32[]{:S(2)}) async-start(), calls=%async_computation.17 | async-start | bytes 2359296 | tf_op jit(solution)/shard_map/reduce_scatter | solution.py:360
  1690.8 386.3 %reduce-scatter.16.cloned.1.call-start = ((), (), s32[]{:S(2)}) async-start(), calls=%async_computation.18 | async-start | bytes 7077888 | tf_op jit(solution)/shard_map/reduce_scatter | solution.py:363
  1701.3 378.2 %reduce-scatter.18.cloned.1.call-start = ((), (), s32[]{:S(2)}) async-start(), calls=%async_computation.19 | async-start | bytes 7077888 | tf_op jit(solution)/shard_map/reduce_scatter | solution.py:369
  1702.1 379.9 %reduce-scatter.20.cloned.1.call-start = ((), (), s32[]{:S(2)}) async-start(), calls=%async_computation.20 | async-start | bytes 7077888 | tf_op jit(solution)/shard_map/reduce_scatter | solution.py:375
  1838.0 89.6 %collective-permute-start.44 = (bf16[512,2048]{1,0:T(8,128)(2,1)S(1)}, bf16[512,2048]{1,0:T(8,128)(2,1)}, u32[]{:S(2)}, u32[]{:S(2)}) collective-permute-start(bf16[512,2048]{1,0:T(8,128)(2,1)S(1)} %get-tuple-element.564), channel_id=1, source_target_pairs={{0,1},{1,2},{2,3},{4,5},{5,6},{6,7},{8,9},{9,10},{10,11},{12,13},{... | collective-permute-start | bytes 6291464 | tf_op jit(solution)/shard_map/ppermute | solution.py:62
  1845.7 84.5 %collective-permute-start.47 = (bf16[512,2048]{1,0:T(8,128)(2,1)S(1)}, bf16[512,2048]{1,0:T(8,128)(2,1)}, u32[]{:S(2)}, u32[]{:S(2)}) collective-permute-start(bf16[512,2048]{1,0:T(8,128)(2,1)S(1)} %add_convert_fusion), channel_id=1, source_target_pairs={{1,0},{2,1},{3,2},{5,4},{6,5},{7,6},{9,8},{10,9},{11,10},{13,12},{... | collective-permute-start | bytes 6291464 | tf_op jit(solution)/shard_map/ppermute | solution.py:63
  1847.0 214.4 %collective-permute-start.19 = (bf16[512,2048]{1,0:T(8,128)(2,1)}, bf16[512,2048]{1,0:T(8,128)(2,1)}, u32[]{:S(2)}, u32[]{:S(2)}) collective-permute-start(bf16[512,2048]{1,0:T(8,128)(2,1)} %get-tuple-element.577), channel_id=1, source_target_pairs={{1,0},{2,1},{3,2},{5,4},{6,5},{7,6},{9,8},{10,9},{11,10},{13,12},{... | collective-permute-start | bytes 6291464 | tf_op jit(solution)/shard_map/ppermute | solution.py:104
  1848.3 213.1 %collective-permute-start.20 = (bf16[512,2048]{1,0:T(8,128)(2,1)}, bf16[512,2048]{1,0:T(8,128)(2,1)}, u32[]{:S(2)}, u32[]{:S(2)}) collective-permute-start(bf16[512,2048]{1,0:T(8,128)(2,1)} %get-tuple-element.576), channel_id=1, source_target_pairs={{0,2},{1,3},{4,6},{5,7},{8,10},{9,11},{12,14},{13,15},{16,18},{17,... | collective-permute-start | bytes 6291464 | tf_op jit(solution)/shard_map/ppermute | solution.py:99
  1882.6 178.8 %collective-permute-start.21 = (bf16[512,2048]{1,0:T(8,128)(2,1)}, bf16[512,2048]{1,0:T(8,128)(2,1)}, u32[]{:S(2)}, u32[]{:S(2)}) collective-permute-start(bf16[512,2048]{1,0:T(8,128)(2,1)} %get-tuple-element.575), channel_id=1, source_target_pairs={{2,0},{3,1},{6,4},{7,5},{10,8},{11,9},{14,12},{15,13},{18,16},{19,... | collective-permute-start | bytes 6291464 | tf_op jit(solution)/shard_map/ppermute | solution.py:104
  1927.6 133.8 %collective-permute-start.22 = (bf16[512,2048]{1,0:T(8,128)(2,1)}, bf16[512,2048]{1,0:T(8,128)(2,1)}, u32[]{:S(2)}, u32[]{:S(2)}) collective-permute-start(bf16[512,2048]{1,0:T(8,128)(2,1)} %get-tuple-element.574), channel_id=1, source_target_pairs={{0,3},{4,7},{8,11},{12,15},{16,19},{20,23},{24,27},{28,31}} | collective-permute-start | bytes 6291464 | tf_op jit(solution)/shard_map/ppermute | solution.py:99
  1930.2 131.2 %collective-permute-start.23 = (bf16[512,2048]{1,0:T(8,128)(2,1)}, bf16[512,2048]{1,0:T(8,128)(2,1)}, u32[]{:S(2)}, u32[]{:S(2)}) collective-permute-start(bf16[512,2048]{1,0:T(8,128)(2,1)} %get-tuple-element.573), channel_id=1, source_target_pairs={{3,0},{7,4},{11,8},{15,12},{19,16},{23,20},{27,24},{31,28}} | collective-permute-start | bytes 6291464 | tf_op jit(solution)/shard_map/ppermute | solution.py:104
  (132 other events, 4507.2 us)
Sparse Core Ops, SparseCore 0:
  10.5 30.4 all-gather.9
  43.5 23.3 all-gather.11
  69.3 23.3 all-gather.13
  95.0 28.0 all-gather.15
  124.9 54.1 all-gather.17
  425.7 42.5 all-gather.19
  764.2 43.5 all-gather.21
  1686.2 37.0 reduce-scatter.9
  1727.1 35.9 reduce-scatter.11
  1766.2 41.1 reduce-scatter.7
  1810.7 41.0 reduce-scatter.13
  1855.0 61.7 reduce-scatter.15
  1920.2 62.6 reduce-scatter.17
  1986.1 61.6 reduce-scatter.19

commit v3 on v2

--- a/solution.py
+++ b/solution.py
@@ -151,12 +151,16 @@
 def attend_sequence(query_tensor, key_rows, value_tensor, seq_starts, seq_pieces):
     length = key_rows.shape[0]
     scale = query_tensor.shape[-1] ** (-0.5)
-
-    def one_block(row_start):
-        q_rows = lax.dynamic_slice_in_dim(query_tensor, row_start, QB, 0)
-        allowed = block_mask(seq_starts, seq_pieces, row_start, QB)
+    outs = []
+    totals = []
+    for row_start in range(0, length, QB):
+        key_end = row_start + QB
+        q_rows = query_tensor[row_start:key_end]
+        allowed = block_mask(seq_starts, seq_pieces, row_start, QB)[:, :key_end]
         scores = (
-            jnp.einsum("qkgd,skd->kgqs", q_rows, key_rows, preferred_element_type=jnp.float32)
+            jnp.einsum(
+                "qkgd,skd->kgqs", q_rows, key_rows[:key_end], preferred_element_type=jnp.float32
+            )
             * scale
         )
         scores = jnp.where(allowed[None, None], scores, MASKED)
@@ -165,13 +169,15 @@
         row_total = jnp.sum(exponent, axis=-1, keepdims=True)
         attn_probs = (exponent / row_total).astype(jnp.bfloat16)
         block_out = jnp.einsum(
-            "kgqs,skd->qkgd", attn_probs, value_tensor, preferred_element_type=jnp.float32
-        )
-        return (block_out, (row_max + jnp.log(row_total))[..., 0])
-
-    block_starts = jnp.arange(length // QB, dtype=jnp.int32) * QB
-    outs_f, log_totals = lax.map(one_block, block_starts)
-    return (outs_f.reshape(length, -1), log_totals)
+            "kgqs,skd->qkgd",
+            attn_probs,
+            value_tensor[:key_end],
+            preferred_element_type=jnp.float32,
+        )
+        outs.append(block_out)
+        totals.append((row_max + jnp.log(row_total))[..., 0])
+    outs_f = jnp.concatenate(outs, axis=0)
+    return (outs_f.reshape(length, -1), jnp.stack(totals))
 
 
 def attend_back(
@@ -179,42 +185,48 @@
 ):
     length = key_rows.shape[0]
     scale = query_tensor.shape[-1] ** (-0.5)
-
-    def one_block(carried, inputs):
-        row_start, block_lse = inputs
-        q_rows = lax.dynamic_slice_in_dim(query_tensor, row_start, QB, 0)
-        g_rows = lax.dynamic_slice_in_dim(grad_rows, row_start, QB, 0)
-        allowed = block_mask(seq_starts, seq_pieces, row_start, QB)
+    d_key = jnp.zeros(key_rows.shape, jnp.float32)
+    d_value = jnp.zeros(key_rows.shape, jnp.float32)
+    d_queries = []
+    for index, row_start in enumerate(range(0, length, QB)):
+        key_end = row_start + QB
+        block_lse = log_totals[index]
+        q_rows = query_tensor[row_start:key_end]
+        g_rows = grad_rows[row_start:key_end]
+        if index > 0:
+            q_rows, g_rows, block_lse, d_key, d_value = lax.optimization_barrier(
+                (q_rows, g_rows, block_lse, d_key, d_value)
+            )
+        keys = key_rows[:key_end]
+        values = value_tensor[:key_end]
+        allowed = block_mask(seq_starts, seq_pieces, row_start, QB)[:, :key_end]
         scores = (
-            jnp.einsum("qkgd,skd->kgqs", q_rows, key_rows, preferred_element_type=jnp.float32)
+            jnp.einsum("qkgd,skd->kgqs", q_rows, keys, preferred_element_type=jnp.float32)
             * scale
         )
         attn_probs = jnp.where(allowed[None, None], jnp.exp(scores - block_lse[..., None]), 0.0)
         d_probs = jnp.einsum(
-            "qkgd,skd->kgqs", g_rows, value_tensor, preferred_element_type=jnp.float32
+            "qkgd,skd->kgqs", g_rows, values, preferred_element_type=jnp.float32
         )
         d_scores = attn_probs * (d_probs - jnp.sum(attn_probs * d_probs, axis=-1, keepdims=True))
         d_scores_b = d_scores.astype(jnp.bfloat16)
-        d_query = (
-            jnp.einsum("kgqs,skd->qkgd", d_scores_b, key_rows, preferred_element_type=jnp.float32)
+        d_queries.append(
+            jnp.einsum("kgqs,skd->qkgd", d_scores_b, keys, preferred_element_type=jnp.float32)
             * scale
         )
-        d_key = (
-            carried[0]
-            + jnp.einsum("kgqs,qkgd->skd", d_scores_b, q_rows, preferred_element_type=jnp.float32)
+        d_key = d_key.at[:key_end].add(
+            jnp.einsum("kgqs,qkgd->skd", d_scores_b, q_rows, preferred_element_type=jnp.float32)
             * scale
         )
-        d_value = carried[1] + jnp.einsum(
-            "kgqs,qkgd->skd",
-            attn_probs.astype(jnp.bfloat16),
-            g_rows,
-            preferred_element_type=jnp.float32,
-        )
-        return ((d_key, d_value), d_query)
-
-    block_starts = jnp.arange(length // QB, dtype=jnp.int32) * QB
-    zero_kv = jnp.zeros(key_rows.shape, jnp.float32)
-    (d_key, d_value), d_query = lax.scan(one_block, (zero_kv, zero_kv), (block_starts, log_totals))
+        d_value = d_value.at[:key_end].add(
+            jnp.einsum(
+                "kgqs,qkgd->skd",
+                attn_probs.astype(jnp.bfloat16),
+                g_rows,
+                preferred_element_type=jnp.float32,
+            )
+        )
+    d_query = jnp.concatenate(d_queries, axis=0)
     return (d_query.reshape(query_tensor.shape), d_key, d_value)
 
 
@@ -264,6 +276,8 @@
     gain_k = gk_b.astype(f32)
     normalized_input = rms_scale(tok_rows, attn_g).astype(bf16)
     gathered = tensor_gather(normalized_input, tensor_n)
+    half_width = out_grad.shape[1] // 2
+    grad_half_a = tensor_gather_direct(out_grad[:, :half_width], tensor_n)
     projected = jnp.dot(gathered, w_qkv, preferred_element_type=f32)
     query_unrotated = projected[:, :q_width].reshape(
         seq_count, SEQUENCE_TOKENS, heads_local, HEAD_SIZE
@@ -283,14 +297,16 @@
     q_b = rope_query(query_unrotated, query_norm_gain).astype(bf16)
     k_b = rope_query(key_unrotated, gain_k).astype(bf16)
     q_grouped = q_b.reshape(seq_count, SEQUENCE_TOKENS, kv_local, heads_per_group, HEAD_SIZE)
-    out_grad_late, q_grouped, k_b = lax.optimization_barrier((out_grad, q_grouped, k_b))
 
     def forward_seq(inputs):
         return attend_sequence(inputs[0], inputs[1], inputs[2], inputs[3], inputs[4])
 
-    attn_f, log_totals = lax.map(
-        forward_seq, (q_grouped, k_b, v_b, seq_starts, seq_pieces)
-    )
+    fwd_results = [
+        forward_seq((q_grouped[i], k_b[i], v_b[i], seq_starts[i], seq_pieces[i]))
+        for i in range(seq_count)
+    ]
+    attn_f = jnp.stack([r[0] for r in fwd_results])
+    log_totals = jnp.stack([r[1] for r in fwd_results])
     attended = attn_f.reshape(total_rows, q_width).astype(bf16)
     wg_b, wu_b, wd_b, gm_b = (
         lax.all_gather(w_gate.astype(bf16), "dp", axis=0, tiled=True),
@@ -301,14 +317,17 @@
     w_gu = jnp.concatenate([wg_b, wu_b], axis=1)
     hidden_width = wg_b.shape[1]
     mlp_g = gm_b.astype(f32)
-    residual = tok_rows + tensor_scatter(jnp.dot(attended, wo_b, preferred_element_type=f32), tensor_n)
+    attn_partial = jnp.dot(attended, wo_b, preferred_element_type=f32)
+    residual = tok_rows + tensor_scatter(attn_partial, tensor_n)
     normed_two = rms_scale(residual, mlp_g).astype(bf16)
     gathered_two = tensor_gather(normed_two, tensor_n)
+    grad_half_b = tensor_gather_direct(out_grad[:, half_width:], tensor_n)
     gate_up = jnp.dot(gathered_two, w_gu, preferred_element_type=f32)
     gate_pre = gate_up[:, :hidden_width]
     up_pre = gate_up[:, hidden_width:]
     hidden_b = (jax.nn.silu(gate_pre) * up_pre).astype(bf16)
-    mlp_sum = tensor_scatter_direct(jnp.dot(hidden_b, wd_b, preferred_element_type=f32), tensor_n)
+    down_partial = jnp.dot(hidden_b, wd_b, preferred_element_type=f32)
+    mlp_sum = tensor_scatter_direct(down_partial, tensor_n)
     layer_out = (residual + mlp_sum).astype(bf16)
     wg_c, wu_c, wd_back = (
         lax.all_gather(w_gate.astype(bf16), "dp", axis=0, tiled=True),
@@ -316,8 +335,7 @@
         lax.all_gather(w_down.astype(bf16), "dp", axis=1, tiled=True),
     )
     w_gu_back = jnp.concatenate([wg_c, wu_c], axis=1)
-    grad_whole = tensor_gather_direct(out_grad_late, tensor_n)
-    grad_down = lax.dot_general(hidden_b, grad_whole, CONTRACT_ROWS, preferred_element_type=f32)
+    grad_whole = jnp.concatenate([grad_half_a, grad_half_b], axis=1)
     d_hidden = lax.dot_general(grad_whole, wd_back, CONTRACT_COLS, preferred_element_type=f32)
 
     def swiglu(gate_in, up_in):
@@ -326,11 +344,16 @@
     _, swiglu_back = jax.vjp(swiglu, gate_pre, up_pre)
     d_gate, d_up = swiglu_back(d_hidden)
     d_gate_up = jnp.concatenate([d_gate, d_up], axis=1).astype(bf16)
+    rows_b = d_gate_up
+    dxn2_partial = lax.dot_general(rows_b, w_gu_back, CONTRACT_COLS, preferred_element_type=f32)
+    dxn2_partial, gathered_two, d_gate_up_w, grad_whole_w = lax.optimization_barrier(
+        (dxn2_partial, gathered_two, d_gate_up, grad_whole)
+    )
+    grad_down = lax.dot_general(hidden_b, grad_whole_w, CONTRACT_ROWS, preferred_element_type=bf16)
     grad_gate_up = lax.dot_general(
-        gathered_two, d_gate_up, CONTRACT_ROWS, preferred_element_type=f32
-    )
-    rows_b = d_gate_up
-    d_normed_two = tensor_scatter(lax.dot_general(rows_b, w_gu_back, CONTRACT_COLS, preferred_element_type=f32), tensor_n)
+        gathered_two, d_gate_up_w, CONTRACT_ROWS, preferred_element_type=bf16
+    )
+    d_normed_two = tensor_scatter(dxn2_partial, tensor_n)
     _, norm_two_back = jax.vjp(rms_scale, residual, mlp_g)
     d_resid_norm, d_mlp_gain = norm_two_back(d_normed_two)
     d_residual = out_grad.astype(f32) + d_resid_norm
@@ -342,9 +365,9 @@
     )
     w_qkv_back = jnp.concatenate([wq_c, wk_c, wv_c], axis=1)
     attn_grad_whole = tensor_gather(d_residual.astype(bf16), tensor_n)
-    grad_out = lax.dot_general(attended, attn_grad_whole, CONTRACT_ROWS, preferred_element_type=f32)
+    grad_out = lax.dot_general(attended, attn_grad_whole, CONTRACT_ROWS, preferred_element_type=bf16)
     d_attended = lax.dot_general(
-        attn_grad_whole, wo_back, CONTRACT_COLS, preferred_element_type=f32
+        attn_grad_whole, wo_back, CONTRACT_COLS, preferred_element_type=bf16
     ).astype(bf16)
     d_grouped = d_attended.reshape(seq_count, SEQUENCE_TOKENS, kv_local, heads_per_group, HEAD_SIZE)
     grad_gate_up, grad_down, grad_out, d_grouped = lax.optimization_barrier(
@@ -376,9 +399,21 @@
             grad_down.astype(jnp.bfloat16), "dp", scatter_dimension=1, tiled=True
         ).astype(jnp.float32),
     )
-    d_query, d_key, d_value = lax.map(
-        back_seq, (q_grouped, k_b, v_b, d_grouped, log_totals, seq_starts, seq_pieces)
-    )
+    bwd_results = [
+        back_seq(
+            (
+                q_grouped[i],
+                k_b[i],
+                v_b[i],
+                d_grouped[i],
+                log_totals[i],
+                seq_starts[i],
+                seq_pieces[i],
+            )
+        )
+        for i in range(seq_count)
+    ]
+    d_query, d_key, d_value = (jnp.stack([r[t] for r in bwd_results]) for t in range(3))
     _, query_back = jax.vjp(rope_query, query_unrotated, query_norm_gain)
     d_q_raw, d_query_gain = query_back(d_query.reshape(query_unrotated.shape))
     _, key_back = jax.vjp(rope_query, key_unrotated, gain_k)
@@ -391,7 +426,7 @@
         ],
         axis=1,
     ).astype(bf16)
-    grad_qkv = lax.dot_general(gathered, d_qkv, CONTRACT_ROWS, preferred_element_type=f32)
+    grad_qkv = lax.dot_general(gathered, d_qkv, CONTRACT_ROWS, preferred_element_type=bf16)
     rows_b = d_qkv
     d_normed = tensor_scatter(lax.dot_general(rows_b, w_qkv_back, CONTRACT_COLS, preferred_element_type=f32), tensor_n)
     _, norm_back = jax.vjp(rms_scale, tok_rows, attn_g)

time: 2100 us -> 1830 us (0.87)
  waiting for transfers between devices: 838 us -> 692 us
  matrix products: 446 us -> 324 us
  starting transfers between devices: 175 us -> 274 us
  blocking collectives: 146 us -> 93.4 us
  other arithmetic: 312 us -> 291 us
    dot_general x33 -> x32, matrix products: 307 us -> 186 us  [the longest x1 33 us: on_device_body(): lax.dot_general(gathered_two, d_gate_up_w, CONTRACT_ROWS, preferred_eleme...]
    ppermute x3 -> x6, starting transfers between devices: 50.6 us -> 122 us  [tensor_gather_direct(): ups[d] = lax.ppermute(rows, 'tensor', [(i, i + d) for i in range(n - d)])]
    psum x1, blocking collectives: 101 us -> 48.4 us  [on_device_body(): gains_sum = lax.psum((owned[7], owned[8], owned[9], owned[10]), 'tensor')]
    ppermute x9, waiting for transfers between devices: 322 us -> 277 us  [tensor_scatter(): lax.ppermute(acc_up.astype(jnp.bfloat16), 'tensor', [(i, i + 1) for i in...]
    ppermute x9, waiting for transfers between devices: 192 us -> 147 us  [tensor_gather(): lax.ppermute(down, 'tensor', [(i, i - 1) for i in range(1, n - s + 1)])]
    ppermute x3, starting transfers between devices: 17 us -> 53.9 us  [tensor_scatter_direct(): lax.ppermute(block(jnp.minimum(j + d, n - 1)).astype(jnp.bfloat16), 'tens...]
    convert_element_type x4, other arithmetic: 48.6 us -> 19.9 us  [attend_back(): d_scores_b = d_scores.astype(jnp.bfloat16)]
    concatenate x0 -> x4, other arithmetic: none -> 21.5 us  [the longest x1 10.6 us: on_device_body(): d_gate_up = jnp.concatenate([d_gate, d_up], axis=1).astype(bf16)]
  transfers between devices with their start and end apart: 62 -> 68, of which waited for: 26 -> 28; matrix products, arithmetic and copies ran while one was open for 22% -> 25% of each run, Pallas kernels for 0% -> 0%
where the time goes in v3:
time: 1830 us; the launch traced here: 1820 us
  waiting for transfers between devices  692 us (38%)
  matrix products  324 us (18%)
  other arithmetic  291 us (16%)
  starting transfers between devices  274 us (15%)
  local copies, waits for them, and re-layouts  128 us (7%)
  blocking collectives  93.4 us (5%)
  between operations  18.8 us (1%)
    ppermute x9, waiting for transfers between devices, tensor_scatter(): lax.ppermute(acc_up.astype(jnp.bfloat16), 'tensor', [(i, i + 1) for i in...  277 us
    ppermute x9, waiting for transfers between devices, tensor_gather(): lax.ppermute(down, 'tensor', [(i, i - 1) for i in range(1, n - s + 1)])  147 us
    ppermute x6, starting transfers between devices, tensor_gather_direct(): ups[d] = lax.ppermute(rows, 'tensor', [(i, i + d) for i in range(n - d)])  122 us
    unnamed x32, other arithmetic  89.6 us
    ppermute x6, waiting for transfers between devices, tensor_gather_direct(): downs[d] = lax.ppermute(rows, 'tensor', [(i, i - d) for i in range(d, n)])  89.4 us
    ppermute x9, waiting for transfers between devices, tensor_scatter(): lax.ppermute(acc_down.astype(jnp.bfloat16), 'tensor', [(i, i - 1) for i i...  72.1 us
    ppermute x9, waiting for transfers between devices, tensor_gather(): up = lax.ppermute(up, 'tensor', [(i, i + 1) for i in range(s - 1, n - 1)])  58.5 us
    ppermute x3, starting transfers between devices, tensor_scatter_direct(): lax.ppermute(block(jnp.minimum(j + d, n - 1)).astype(jnp.bfloat16), 'tens...  53.9 us
  transfers between devices with their start and end apart: 68, of which 28 were waited for; matrix products, arithmetic and copies ran while one was open for 25% of the time, Pallas kernels for 0%

profile of v3, /device:TPU:0, one launch (start us, length us, event | category | flops | bytes accessed | tf_op | source)
XLA Modules:
  0.0 1821.2 jit_solution(14212482956496711198)
XLA Ops:
  37.2 41.5 %collective-permute-done.1 = bf16[512,2048]{1,0:T(8,128)(2,1)} collective-permute-done((bf16[512,2048]{1,0:T(8,128)(2,1)}, bf16[512,2048]{1,0:T(8,128)(2,1)}, u32[]{:S(2)}, u32[]{:S(2)}) %collective-permute-start.1) | collective-permute-done | bytes 2097184 | tf_op jit(solution)/shard_map/ppermute | solution.py:32
  97.0 36.4 %collective-permute-done.4 = bf16[512,2048]{1,0:T(8,128)(2,1)} collective-permute-done((bf16[512,2048]{1,0:T(8,128)(2,1)}, bf16[512,2048]{1,0:T(8,128)(2,1)}, u32[]{:S(2)}, u32[]{:S(2)}) %collective-permute-start.4) | collective-permute-done | bytes 2097184 | tf_op jit(solution)/shard_map/ppermute | solution.py:33
  166.6 15.2 collective-permute-done.5
  308.9 38.8 %collective-permute-done.6 = bf16[512,2048]{1,0:T(8,128)(2,1)} collective-permute-done((bf16[512,2048]{1,0:T(8,128)(2,1)}, bf16[512,2048]{1,0:T(8,128)(2,1)}, u32[]{:S(2)}, u32[]{:S(2)}) %collective-permute-start.6) | collective-permute-done | bytes 2097184 | tf_op jit(solution)/shard_map/ppermute | solution.py:62
  358.4 41.0 %collective-permute-done.7 = bf16[512,2048]{1,0:T(8,128)(2,1)} collective-permute-done((bf16[512,2048]{1,0:T(8,128)(2,1)}, bf16[512,2048]{1,0:T(8,128)(2,1)}, u32[]{:S(2)}, u32[]{:S(2)}) %collective-permute-start.7) | collective-permute-done | bytes 2097184 | tf_op jit(solution)/shard_map/ppermute | solution.py:62
  424.0 48.1 %collective-permute-start.25 = (bf16[512,1024]{1,0:T(8,128)(2,1)}, bf16[512,1024]{1,0:T(8,128)(2,1)}, u32[]{:S(2)}, u32[]{:S(2)}) collective-permute-start(bf16[512,1024]{1,0:T(8,128)(2,1)} %get-tuple-element.239), channel_id=1, source_target_pairs={{0,3},{4,7},{8,11},{12,15},{16,19},{20,23},{24,27},{28,31}} | collective-permute-start | bytes 3145736 | tf_op jit(solution)/shard_map/ppermute | solution.py:77
  489.9 18.9 %collective-permute-done.11 = bf16[512,2048]{1,0:T(8,128)(2,1)} collective-permute-done((bf16[512,2048]{1,0:T(8,128)(2,1)}, bf16[512,2048]{1,0:T(8,128)(2,1)}, u32[]{:S(2)}, u32[]{:S(2)}) %collective-permute-start.11) | collective-permute-done | bytes 2097184 | tf_op jit(solution)/shard_map/ppermute | solution.py:63
  527.4 53.5 %collective-permute-start.29 = (bf16[512,1024]{1,0:T(8,128)(2,1)}, bf16[512,1024]{1,0:T(8,128)(2,1)}, u32[]{:S(2)}, u32[]{:S(2)}) collective-permute-start(bf16[512,1024]{1,0:T(8,128)(2,1)} %get-tuple-element.239), channel_id=1, source_target_pairs={{0,1},{1,2},{2,3},{4,5},{5,6},{6,7},{8,9},{9,10},{10,11},{12,13},{... | collective-permute-start | bytes 3145736 | tf_op jit(solution)/shard_map/ppermute | solution.py:77
  582.2 51.6 %collective-permute-done.26 = bf16[512,1024]{1,0:T(8,128)(2,1)} collective-permute-done((bf16[512,1024]{1,0:T(8,128)(2,1)}, bf16[512,1024]{1,0:T(8,128)(2,1)}, u32[]{:S(2)}, u32[]{:S(2)}) %collective-permute-start.26) | collective-permute-done | bytes 1048608 | tf_op jit(solution)/shard_map/ppermute | solution.py:78
  662.2 25.1 %collective-permute-done.32 = bf16[512,1024]{1,0:T(8,128)(2,1)} collective-permute-done((bf16[512,1024]{1,0:T(8,128)(2,1)}, bf16[512,1024]{1,0:T(8,128)(2,1)}, u32[]{:S(2)}, u32[]{:S(2)}) %collective-permute-start.32) | collective-permute-done | bytes 1048608 | tf_op jit(solution)/shard_map/ppermute | solution.py:78
  757.2 52.6 %collective-permute-done.16 = bf16[512,2048]{1,0:T(8,128)(2,1)} collective-permute-done((bf16[512,2048]{1,0:T(8,128)(2,1)}, bf16[512,2048]{1,0:T(8,128)(2,1)}, u32[]{:S(2)}, u32[]{:S(2)}) %collective-permute-start.16) | collective-permute-done | bytes 2097184 | tf_op jit(solution)/shard_map/ppermute | solution.py:33
  864.8 34.1 %fusion.215 = f32[2048,3072]{1,0:T(8,128)} fusion(bf16[2048,2048]{1,0:T(8,128)(2,1)} %constant_dynamic-slice_fusion.2, bf16[2048,3072]{1,0:T(8,128)(2,1)} %constant_dynamic-update-slice_fusion.7), kind=kOutput, calls=%fused_computation.370 | convolution fusion | flops 25769803776 | bytes 46137344 | tf_op jit(solution)/shard_map/dot_general | solution.py:325
  898.9 26.2 %fusion.9 = (bf16[2048,1536]{1,0:T(8,128)(2,1)}, bf16[2048,1536]{1,0:T(8,128)(2,1)}, bf16[2048,1536]{1,0:T(8,128)(2,1)}) fusion(f32[2048,3072]{1,0:T(8,128)} %fusion.215, bf16[1536,2048]{1,0:T(8,128)(2,1)} %all-gather.22.cloned.1.call-done, bf16[2048,1024]{1,0:T(8,128)(2,1)} %constant_dynamic-slice_fusion, bf16[2048,1024]{1,0:T(8,128)(2,1)} %constant_dynamic-slice_fusion.1), kind=kOutput, calls=%fused_computation.16 | convolution fusion | flops 12952010752 | bytes 58720256 | tf_op jit(solution)/shard_map/dot_general | solution.py:339
  935.7 34.5 %fusion.205 = f32[2048,2048]{1,0:T(8,128)} fusion(bf16[2048,3072]{1,0:T(8,128)(2,1)} %constant_dynamic-update-slice_fusion.7, bf16[2048,1536]{1,0:T(8,128)(2,1)} %get-tuple-element.200, bf16[2048,1536]{1,0:T(8,128)(2,1)} %get-tuple-element.199), kind=kOutput, calls=%fused_computation.362 | convolution fusion | flops 25794969600 | bytes 41943040 | tf_op jit(solution)/shard_map/dot_general | solution.py:348
  978.3 40.5 %collective-permute-done.36 = bf16[512,2048]{1,0:T(8,128)(2,1)S(1)} collective-permute-done((bf16[512,2048]{1,0:T(8,128)(2,1)S(1)}, bf16[512,2048]{1,0:T(8,128)(2,1)S(1)}, u32[]{:S(2)}, u32[]{:S(2)}) %collective-permute-start.36) | collective-permute-done | bytes 2097184 | tf_op jit(solution)/shard_map/ppermute | solution.py:62
  1027.4 37.5 %collective-permute-done.37 = bf16[512,2048]{1,0:T(8,128)(2,1)} collective-permute-done((bf16[512,2048]{1,0:T(8,128)(2,1)S(1)}, bf16[512,2048]{1,0:T(8,128)(2,1)}, u32[]{:S(2)}, u32[]{:S(2)}) %collective-permute-start.37) | collective-permute-done | bytes 2097184 | tf_op jit(solution)/shard_map/ppermute | solution.py:62
  1079.3 21.6 %collective-permute-done.38 = bf16[512,2048]{1,0:T(8,128)(2,1)S(1)} collective-permute-done((bf16[512,2048]{1,0:T(8,128)(2,1)}, bf16[512,2048]{1,0:T(8,128)(2,1)S(1)}, u32[]{:S(2)}, u32[]{:S(2)}) %collective-permute-start.38) | collective-permute-done | bytes 2097184 | tf_op jit(solution)/shard_map/ppermute | solution.py:62
  1101.0 53.2 %collective-permute-done.41 = bf16[512,2048]{1,0:T(8,128)(2,1)S(1)} collective-permute-done((bf16[512,2048]{1,0:T(8,128)(2,1)S(1)}, bf16[512,2048]{1,0:T(8,128)(2,1)S(1)}, u32[]{:S(2)}, u32[]{:S(2)}) %collective-permute-start.41) | collective-permute-done | bytes 2097184 | tf_op jit(solution)/shard_map/ppermute | solution.py:63
  1174.9 17.0 collective-permute-done.43
  1193.9 15.7 collective-permute-done.42
  1210.9 33.0 %fusion.217 = bf16[2048,3072]{1,0:T(8,128)(2,1)} fusion(bf16[2048,2048]{1,0:T(8,128)(2,1)} %constant_dynamic-slice_fusion.2, bf16[2048,3072]{1,0:T(8,128)(2,1)} %pad_maximum_fusion), kind=kOutput, calls=%fused_computation.372 | convolution fusion | flops 25769803776 | bytes 33554432 | tf_op jit(solution)/shard_map/dot_general | solution.py:353
  1247.3 15.8 fusion.218
  1474.1 28.8 %collective-permute-done.48 = bf16[512,2048]{1,0:T(8,128)(2,1)S(1)} collective-permute-done((bf16[512,2048]{1,0:T(8,128)(2,1)S(1)}, bf16[512,2048]{1,0:T(8,128)(2,1)S(1)}, u32[]{:S(2)}, u32[]{:S(2)}) %collective-permute-start.48) | collective-permute-done | bytes 2097184 | tf_op jit(solution)/shard_map/ppermute | solution.py:62
  1509.6 24.9 %collective-permute-done.49 = bf16[512,2048]{1,0:T(8,128)(2,1)S(1)} collective-permute-done((bf16[512,2048]{1,0:T(8,128)(2,1)}, bf16[512,2048]{1,0:T(8,128)(2,1)S(1)}, u32[]{:S(2)}, u32[]{:S(2)}) %collective-permute-start.49) | collective-permute-done | bytes 2097184 | tf_op jit(solution)/shard_map/ppermute | solution.py:62
  1540.9 19.4 %fusion.216 = f32[2048,2048]{1,0:T(8,128)} fusion(bf16[2048,1536]{1,0:T(8,128)(2,1)} %get-tuple-element.201, bf16[1536,2048]{1,0:T(8,128)(2,1)} %all-gather.22.cloned.1.call-done), kind=kOutput, calls=%fused_computation.371 | convolution fusion | flops 12884901888 | bytes 29360128 | tf_op jit(solution)/shard_map/dot_general | solution.py:329
  1589.7 14.7 collective-permute-start.20
  1604.4 19.0 %collective-permute-done.18 = bf16[512,2048]{1,0:T(8,128)(2,1)} collective-permute-done((bf16[512,2048]{1,0:T(8,128)(2,1)S(1)}, bf16[512,2048]{1,0:T(8,128)(2,1)}, u32[]{:S(2)}, u32[]{:S(2)}) %collective-permute-start.18) | collective-permute-done | bytes 2097184 | tf_op jit(solution)/shard_map/ppermute | solution.py:99
  1624.7 43.3 %collective-permute-done.50 = bf16[512,2048]{1,0:T(8,128)(2,1)} collective-permute-done((bf16[512,2048]{1,0:T(8,128)(2,1)S(1)}, bf16[512,2048]{1,0:T(8,128)(2,1)}, u32[]{:S(2)}, u32[]{:S(2)}) %collective-permute-start.50) | collective-permute-done | bytes 2097184 | tf_op jit(solution)/shard_map/ppermute | solution.py:62
  1668.0 33.0 %collective-permute-start.22 = (bf16[512,2048]{1,0:T(8,128)(2,1)}, bf16[512,2048]{1,0:T(8,128)(2,1)}, u32[]{:S(2)}, u32[]{:S(2)}) collective-permute-start(bf16[512,2048]{1,0:T(8,128)(2,1)} %get-tuple-element.212), channel_id=1, source_target_pairs={{0,3},{4,7},{8,11},{12,15},{16,19},{20,23},{24,27},{28,31}} | collective-permute-start | bytes 6291464 | tf_op jit(solution)/shard_map/ppermute | solution.py:99
  1717.5 13.5 all-reduce.13
  1731.3 48.4 %all-reduce.12 = (f32[256]{0:T(256)}, f32[16]{0:T(128)}, f32[16]{0:T(128)}, f32[256]{0:T(256)}) all-reduce(f32[256]{0:T(256)S(1)} %dynamic-slice_convert_fusion.15, f32[16]{0:T(128)S(1)} %dynamic-slice_convert_fusion.14, f32[16]{0:T(128)S(1)} %dynamic-slice_convert_fusion.13, ...), channel_id=1, replica_groups=mesh['dp'=8,'tensor'=4] {'tensor'}, use_global_device_ids=true, to_apply=%region_24.25 | all-reduce | flops 544 | bytes 4352 | tf_op jit(solution)/shard_map/psum | solution.py:473
  1791.3 15.8 fusion.48
  (657 shorter events, 789.7 us)
Async XLA Ops:
  7.2 144.2 %all-gather.10.cloned.1.call-start = ((), (), s32[]{:S(2)}) async-start(), calls=%async_computation.7 | async-start | bytes 2359296 | tf_op jit(solution)/shard_map/all_gather | solution.py:260
  9.2 145.2 %all-gather.12.cloned.1.call-start = ((), (), s32[]{:S(2)}) async-start(), calls=%async_computation.8 | async-start | bytes 1179648 | tf_op jit(solution)/shard_map/all_gather | solution.py:261
  10.9 145.8 %all-gather.14.cloned.1.call-start = ((), (), s32[]{:S(2)}) async-start(), calls=%async_computation.9 | async-start | bytes 1179648 | tf_op jit(solution)/shard_map/all_gather | solution.py:262
  12.6 275.1 %all-gather.16.cloned.1.call-start = ((), (), s32[]{:S(2)}) async-start(), calls=%async_computation.10 | async-start | bytes 2359296 | tf_op jit(solution)/shard_map/all_gather | solution.py:263
  14.4 797.2 %all-gather.18.cloned.1.call-start = ((), (), s32[]{:S(2)}) async-start(), calls=%async_computation.11 | async-start | bytes 7077888 | tf_op jit(solution)/shard_map/all_gather | solution.py:312
  36.6 780.9 %all-gather.20.cloned.1.call-start = ((), (), s32[]{:S(2)}) async-start(), calls=%async_computation.12 | async-start | bytes 7077888 | tf_op jit(solution)/shard_map/all_gather | solution.py:313
  306.8 592.1 %all-gather.22.cloned.1.call-start = ((), (), s32[]{:S(2)}) async-start(), calls=%async_computation.13 | async-start | bytes 7077888 | tf_op jit(solution)/shard_map/all_gather | solution.py:314
  419.0 89.8 %collective-permute-start.11 = (bf16[512,2048]{1,0:T(8,128)(2,1)}, bf16[512,2048]{1,0:T(8,128)(2,1)}, u32[]{:S(2)}, u32[]{:S(2)}) collective-permute-start(bf16[512,2048]{1,0:T(8,128)(2,1)} %add_convert_fusion.9), channel_id=1, source_target_pairs={{1,0},{2,1},{3,2},{5,4},{6,5},{7,6},{9,8},{10,9},{11,10},{13,12},{... | collective-permute-start | bytes 6291464 | tf_op jit(solution)/shard_map/ppermute | solution.py:63
  422.7 104.7 %collective-permute-start.24 = (bf16[512,1024]{1,0:T(8,128)(2,1)}, bf16[512,1024]{1,0:T(8,128)(2,1)S(1)}, u32[]{:S(2)}, u32[]{:S(2)}) collective-permute-start(bf16[512,1024]{1,0:T(8,128)(2,1)} %get-tuple-element.239), channel_id=1, source_target_pairs={{1,0},{2,1},{3,2},{5,4},{6,5},{7,6},{9,8},{10,9},{11,10},{13,12},{... | collective-permute-start | bytes 3145736 | tf_op jit(solution)/shard_map/ppermute | solution.py:78
  424.0 156.9 %collective-permute-start.25 = (bf16[512,1024]{1,0:T(8,128)(2,1)}, bf16[512,1024]{1,0:T(8,128)(2,1)}, u32[]{:S(2)}, u32[]{:S(2)}) collective-permute-start(bf16[512,1024]{1,0:T(8,128)(2,1)} %get-tuple-element.239), channel_id=1, source_target_pairs={{0,3},{4,7},{8,11},{12,15},{16,19},{20,23},{24,27},{28,31}} | collective-permute-start | bytes 3145736 | tf_op jit(solution)/shard_map/ppermute | solution.py:77
  472.2 161.6 %collective-permute-start.26 = (bf16[512,1024]{1,0:T(8,128)(2,1)}, bf16[512,1024]{1,0:T(8,128)(2,1)}, u32[]{:S(2)}, u32[]{:S(2)}) collective-permute-start(bf16[512,1024]{1,0:T(8,128)(2,1)} %get-tuple-element.239), channel_id=1, source_target_pairs={{2,0},{3,1},{6,4},{7,5},{10,8},{11,9},{14,12},{15,13},{18,16},{19,... | collective-permute-start | bytes 3145736 | tf_op jit(solution)/shard_map/ppermute | solution.py:78
  473.5 162.6 %collective-permute-start.27 = (bf16[512,1024]{1,0:T(8,128)(2,1)}, bf16[512,1024]{1,0:T(8,128)(2,1)}, u32[]{:S(2)}, u32[]{:S(2)}) collective-permute-start(bf16[512,1024]{1,0:T(8,128)(2,1)} %get-tuple-element.239), channel_id=1, source_target_pairs={{0,2},{1,3},{4,6},{5,7},{8,10},{9,11},{12,14},{13,15},{16,18},{17,... | collective-permute-start | bytes 3145736 | tf_op jit(solution)/shard_map/ppermute | solution.py:77
  508.8 131.1 %collective-permute-start.28 = (bf16[512,1024]{1,0:T(8,128)(2,1)}, bf16[512,1024]{1,0:T(8,128)(2,1)S(1)}, u32[]{:S(2)}, u32[]{:S(2)}) collective-permute-start(bf16[512,1024]{1,0:T(8,128)(2,1)} %get-tuple-element.239), channel_id=1, source_target_pairs={{3,0},{7,4},{11,8},{15,12},{19,16},{23,20},{27,24},{31,28}} | collective-permute-start | bytes 3145736 | tf_op jit(solution)/shard_map/ppermute | solution.py:78
  527.4 116.2 %collective-permute-start.29 = (bf16[512,1024]{1,0:T(8,128)(2,1)}, bf16[512,1024]{1,0:T(8,128)(2,1)}, u32[]{:S(2)}, u32[]{:S(2)}) collective-permute-start(bf16[512,1024]{1,0:T(8,128)(2,1)} %get-tuple-element.239), channel_id=1, source_target_pairs={{0,1},{1,2},{2,3},{4,5},{5,6},{6,7},{8,9},{9,10},{10,11},{12,13},{... | collective-permute-start | bytes 3145736 | tf_op jit(solution)/shard_map/ppermute | solution.py:77
  580.9 71.2 %collective-permute-start.30 = (bf16[512,1024]{1,0:T(8,128)(2,1)}, bf16[512,1024]{1,0:T(8,128)(2,1)}, u32[]{:S(2)}, u32[]{:S(2)}) collective-permute-start(bf16[512,1024]{1,0:T(8,128)(2,1)} %get-tuple-element.242), channel_id=1, source_target_pairs={{1,0},{2,1},{3,2},{5,4},{6,5},{7,6},{9,8},{10,9},{11,10},{13,12},{... | collective-permute-start | bytes 3145736 | tf_op jit(solution)/shard_map/ppermute | solution.py:78
  643.6 1060.0 %reduce-scatter.10.cloned.1.call-start = ((), (), s32[]{:S(2)}) async-start(), calls=%async_computation.15 | async-start | bytes 1179648 | tf_op jit(solution)/shard_map/reduce_scatter | solution.py:439
  732.9 77.0 %collective-permute-start.16 = (bf16[512,2048]{1,0:T(8,128)(2,1)}, bf16[512,2048]{1,0:T(8,128)(2,1)}, u32[]{:S(2)}, u32[]{:S(2)}) collective-permute-start(bf16[512,2048]{1,0:T(8,128)(2,1)} %collective-permute-done.12), channel_id=1, source_target_pairs={{1,0},{2,1},{5,4},{6,5},{9,8},{10,9},{13,12},{14,13},{17,16},{18,1... | collective-permute-start | bytes 6291464 | tf_op jit(solution)/shard_map/ppermute | solution.py:33
  744.5 78.9 %collective-permute-start.15 = (bf16[512,2048]{1,0:T(8,128)(2,1)}, bf16[512,2048]{1,0:T(8,128)(2,1)}, u32[]{:S(2)}, u32[]{:S(2)}) collective-permute-start(bf16[512,2048]{1,0:T(8,128)(2,1)} %collective-permute-done.14), channel_id=1, source_target_pairs={{2,3},{6,7},{10,11},{14,15},{18,19},{22,23},{26,27},{30,31}} | collective-permute-start | bytes 6291464 | tf_op jit(solution)/shard_map/ppermute | solution.py:32
  1078.0 76.2 %collective-permute-start.41 = (bf16[512,2048]{1,0:T(8,128)(2,1)S(1)}, bf16[512,2048]{1,0:T(8,128)(2,1)S(1)}, u32[]{:S(2)}, u32[]{:S(2)}) collective-permute-start(bf16[512,2048]{1,0:T(8,128)(2,1)S(1)} %add_convert_fusion.4), channel_id=1, source_target_pairs={{1,0},{2,1},{3,2},{5,4},{6,5},{7,6},{9,8},{10,9},{11,10},{13,12},{... | collective-permute-start | bytes 6291464 | tf_op jit(solution)/shard_map/ppermute | solution.py:63
  1439.1 266.1 %reduce-scatter.12.cloned.1.call-start = ((), (), s32[]{:S(2)}) async-start(), calls=%async_computation.16 | async-start | bytes 1179648 | tf_op jit(solution)/shard_map/reduce_scatter | solution.py:445
  1439.8 267.0 %reduce-scatter.8.cloned.1.call-start = ((), (), s32[]{:S(2)}) async-start(), calls=%async_computation.14 | async-start | bytes 2359296 | tf_op jit(solution)/shard_map/reduce_scatter | solution.py:436
  1442.9 265.7 %reduce-scatter.14.cloned.1.call-start = ((), (), s32[]{:S(2)}) async-start(), calls=%async_computation.17 | async-start | bytes 2359296 | tf_op jit(solution)/shard_map/reduce_scatter | solution.py:383
  1443.7 363.5 %reduce-scatter.16.cloned.1.call-start = ((), (), s32[]{:S(2)}) async-start(), calls=%async_computation.18 | async-start | bytes 7077888 | tf_op jit(solution)/shard_map/reduce_scatter | solution.py:386
  1454.4 355.2 %reduce-scatter.18.cloned.1.call-start = ((), (), s32[]{:S(2)}) async-start(), calls=%async_computation.19 | async-start | bytes 7077888 | tf_op jit(solution)/shard_map/reduce_scatter | solution.py:392
  1455.1 356.9 %reduce-scatter.20.cloned.1.call-start = ((), (), s32[]{:S(2)}) async-start(), calls=%async_computation.20 | async-start | bytes 7077888 | tf_op jit(solution)/shard_map/reduce_scatter | solution.py:398
  1578.7 89.3 %collective-permute-start.50 = (bf16[512,2048]{1,0:T(8,128)(2,1)S(1)}, bf16[512,2048]{1,0:T(8,128)(2,1)}, u32[]{:S(2)}, u32[]{:S(2)}) collective-permute-start(bf16[512,2048]{1,0:T(8,128)(2,1)S(1)} %get-tuple-element.202), channel_id=1, source_target_pairs={{0,1},{1,2},{2,3},{4,5},{5,6},{6,7},{8,9},{9,10},{10,11},{12,13},{... | collective-permute-start | bytes 6291464 | tf_op jit(solution)/shard_map/ppermute | solution.py:62
  1587.1 113.9 %collective-permute-start.53 = (bf16[512,2048]{1,0:T(8,128)(2,1)S(1)}, bf16[512,2048]{1,0:T(8,128)(2,1)}, u32[]{:S(2)}, u32[]{:S(2)}) collective-permute-start(bf16[512,2048]{1,0:T(8,128)(2,1)S(1)} %add_convert_fusion), channel_id=1, source_target_pairs={{1,0},{2,1},{3,2},{5,4},{6,5},{7,6},{9,8},{10,9},{11,10},{13,12},{... | collective-permute-start | bytes 6291464 | tf_op jit(solution)/shard_map/ppermute | solution.py:63
  1588.4 191.3 %collective-permute-start.19 = (bf16[512,2048]{1,0:T(8,128)(2,1)}, bf16[512,2048]{1,0:T(8,128)(2,1)}, u32[]{:S(2)}, u32[]{:S(2)}) collective-permute-start(bf16[512,2048]{1,0:T(8,128)(2,1)} %get-tuple-element.215), channel_id=1, source_target_pairs={{1,0},{2,1},{3,2},{5,4},{6,5},{7,6},{9,8},{10,9},{11,10},{13,12},{... | collective-permute-start | bytes 6291464 | tf_op jit(solution)/shard_map/ppermute | solution.py:104
  1589.7 190.0 %collective-permute-start.20 = (bf16[512,2048]{1,0:T(8,128)(2,1)}, bf16[512,2048]{1,0:T(8,128)(2,1)}, u32[]{:S(2)}, u32[]{:S(2)}) collective-permute-start(bf16[512,2048]{1,0:T(8,128)(2,1)} %get-tuple-element.214), channel_id=1, source_target_pairs={{0,2},{1,3},{4,6},{5,7},{8,10},{9,11},{12,14},{13,15},{16,18},{17,... | collective-permute-start | bytes 6291464 | tf_op jit(solution)/shard_map/ppermute | solution.py:99
  1623.4 167.8 %collective-permute-start.21 = (bf16[512,2048]{1,0:T(8,128)(2,1)}, bf16[512,2048]{1,0:T(8,128)(2,1)}, u32[]{:S(2)}, u32[]{:S(2)}) collective-permute-start(bf16[512,2048]{1,0:T(8,128)(2,1)} %get-tuple-element.213), channel_id=1, source_target_pairs={{2,0},{3,1},{6,4},{7,5},{10,8},{11,9},{14,12},{15,13},{18,16},{19,... | collective-permute-start | bytes 6291464 | tf_op jit(solution)/shard_map/ppermute | solution.py:104
  1668.0 123.3 %collective-permute-start.22 = (bf16[512,2048]{1,0:T(8,128)(2,1)}, bf16[512,2048]{1,0:T(8,128)(2,1)}, u32[]{:S(2)}, u32[]{:S(2)}) collective-permute-start(bf16[512,2048]{1,0:T(8,128)(2,1)} %get-tuple-element.212), channel_id=1, source_target_pairs={{0,3},{4,7},{8,11},{12,15},{16,19},{20,23},{24,27},{28,31}} | collective-permute-start | bytes 6291464 | tf_op jit(solution)/shard_map/ppermute | solution.py:99
  1701.0 90.3 %collective-permute-start.23 = (bf16[512,2048]{1,0:T(8,128)(2,1)}, bf16[512,2048]{1,0:T(8,128)(2,1)}, u32[]{:S(2)}, u32[]{:S(2)}) collective-permute-start(bf16[512,2048]{1,0:T(8,128)(2,1)} %get-tuple-element.211), channel_id=1, source_target_pairs={{3,0},{7,4},{11,8},{15,12},{19,16},{23,20},{27,24},{31,28}} | collective-permute-start | bytes 6291464 | tf_op jit(solution)/shard_map/ppermute | solution.py:104
  (194 other events, 5443.3 us)
Sparse Core Ops, SparseCore 0:
  10.5 30.4 all-gather.9
  43.5 23.3 all-gather.11
  68.8 23.3 all-gather.13
  93.9 28.0 all-gather.15
  123.8 45.3 all-gather.17
  306.9 47.9 all-gather.19
  643.7 48.8 all-gather.21
  1439.2 36.6 reduce-scatter.9
  1479.7 35.9 reduce-scatter.11
  1518.8 41.1 reduce-scatter.7
  1563.2 41.1 reduce-scatter.13
  1607.6 61.7 reduce-scatter.15
  1672.8 62.2 reduce-scatter.17
  1738.3 61.7 reduce-scatter.19

commit v4 on v3

--- a/solution.py
+++ b/solution.py
@@ -19,7 +19,7 @@
 CONTRACT_COLS = (((1,), (1,)), ((), ()))
 
 
-def tensor_gather(rows, n):
+def tensor_gather(rows, n, rotated=False):
     if n == 1:
         return rows
     j = lax.axis_index("tensor")
@@ -37,18 +37,22 @@
     for m in range(1, n):
         rel.append(jnp.where(j + m <= n - 1, downs[m], ups[n - m]))
     rel = jnp.concatenate(rel, axis=0)
+    if rotated:
+        return rel
     twice = jnp.concatenate([rel, rel], axis=0)
     start = ((n - j) % n) * count
     return lax.dynamic_slice_in_dim(twice, start, n * count, 0)
 
 
-def tensor_scatter(partial, n):
+def tensor_scatter(partial, n, rotated=False):
     if n == 1:
         return partial.astype(jnp.float32)
     j = lax.axis_index("tensor")
     count = partial.shape[0] // n
 
     def block(t):
+        if rotated:
+            t = (t - j) % n
         return lax.dynamic_slice_in_dim(partial, t * count, count, 0).astype(jnp.float32)
 
     up = None
@@ -66,7 +70,7 @@
     return block(j) + up.astype(jnp.float32) + down.astype(jnp.float32)
 
 
-def tensor_gather_direct(rows, n):
+def tensor_gather_direct(rows, n, rotated=False):
     if n == 1:
         return rows
     j = lax.axis_index("tensor")
@@ -80,18 +84,22 @@
     for m in range(1, n):
         rel.append(jnp.where(j + m <= n - 1, downs[m], ups[n - m]))
     rel = jnp.concatenate(rel, axis=0)
+    if rotated:
+        return rel
     twice = jnp.concatenate([rel, rel], axis=0)
     start = ((n - j) % n) * count
     return lax.dynamic_slice_in_dim(twice, start, n * count, 0)
 
 
-def tensor_scatter_direct(partial, n):
+def tensor_scatter_direct(partial, n, rotated=False):
     if n == 1:
         return partial.astype(jnp.float32)
     j = lax.axis_index("tensor")
     count = partial.shape[0] // n
 
     def block(t):
+        if rotated:
+            t = (t - j) % n
         return lax.dynamic_slice_in_dim(partial, t * count, count, 0).astype(jnp.float32)
 
     total = block(j)
@@ -277,7 +285,9 @@
     normalized_input = rms_scale(tok_rows, attn_g).astype(bf16)
     gathered = tensor_gather(normalized_input, tensor_n)
     half_width = out_grad.shape[1] // 2
-    grad_half_a = tensor_gather_direct(out_grad[:, :half_width], tensor_n)
+    grad_half_a = tensor_gather_direct(
+        out_grad[:, :half_width], tensor_n, rotated=True
+    )
     projected = jnp.dot(gathered, w_qkv, preferred_element_type=f32)
     query_unrotated = projected[:, :q_width].reshape(
         seq_count, SEQUENCE_TOKENS, heads_local, HEAD_SIZE
@@ -320,14 +330,16 @@
     attn_partial = jnp.dot(attended, wo_b, preferred_element_type=f32)
     residual = tok_rows + tensor_scatter(attn_partial, tensor_n)
     normed_two = rms_scale(residual, mlp_g).astype(bf16)
-    gathered_two = tensor_gather(normed_two, tensor_n)
-    grad_half_b = tensor_gather_direct(out_grad[:, half_width:], tensor_n)
+    gathered_two = tensor_gather(normed_two, tensor_n, rotated=True)
+    grad_half_b = tensor_gather_direct(
+        out_grad[:, half_width:], tensor_n, rotated=True
+    )
     gate_up = jnp.dot(gathered_two, w_gu, preferred_element_type=f32)
     gate_pre = gate_up[:, :hidden_width]
     up_pre = gate_up[:, hidden_width:]
     hidden_b = (jax.nn.silu(gate_pre) * up_pre).astype(bf16)
     down_partial = jnp.dot(hidden_b, wd_b, preferred_element_type=f32)
-    mlp_sum = tensor_scatter_direct(down_partial, tensor_n)
+    mlp_sum = tensor_scatter_direct(down_partial, tensor_n, rotated=True)
     layer_out = (residual + mlp_sum).astype(bf16)
     wg_c, wu_c, wd_back = (
         lax.all_gather(w_gate.astype(bf16), "dp", axis=0, tiled=True),
@@ -353,7 +365,7 @@
     grad_gate_up = lax.dot_general(
         gathered_two, d_gate_up_w, CONTRACT_ROWS, preferred_element_type=bf16
     )
-    d_normed_two = tensor_scatter(dxn2_partial, tensor_n)
+    d_normed_two = tensor_scatter(dxn2_partial, tensor_n, rotated=True)
     _, norm_two_back = jax.vjp(rms_scale, residual, mlp_g)
     d_resid_norm, d_mlp_gain = norm_two_back(d_normed_two)
     d_residual = out_grad.astype(f32) + d_resid_norm
@@ -379,22 +391,15 @@
             inputs[0], inputs[1], inputs[2], inputs[3], inputs[4], inputs[5], inputs[6]
         )
 
+    gate_up_owned = lax.psum_scatter(
+        grad_gate_up.astype(jnp.bfloat16), "dp", scatter_dimension=0, tiled=True
+    ).astype(jnp.float32)
     mlp_owned = (
         lax.psum_scatter(
             grad_out.astype(jnp.bfloat16), "dp", scatter_dimension=1, tiled=True
         ).astype(jnp.float32),
-        lax.psum_scatter(
-            grad_gate_up[:, :hidden_width].astype(jnp.bfloat16),
-            "dp",
-            scatter_dimension=0,
-            tiled=True,
-        ).astype(jnp.float32),
-        lax.psum_scatter(
-            grad_gate_up[:, hidden_width:].astype(jnp.bfloat16),
-            "dp",
-            scatter_dimension=0,
-            tiled=True,
-        ).astype(jnp.float32),
+        gate_up_owned[:, :hidden_width],
+        gate_up_owned[:, hidden_width:],
         lax.psum_scatter(
             grad_down.astype(jnp.bfloat16), "dp", scatter_dimension=1, tiled=True
         ).astype(jnp.float32),

time: 1830 us -> 1960 us (1.071)
  starting transfers between devices: 274 us -> 380 us
  waiting for transfers between devices: 692 us -> 773 us
  blocking collectives: 93.4 us -> 56.1 us
  local copies, waits for them, and re-layouts: 128 us -> 108 us
    reduce_scatter x2 -> x1, waiting for transfers between devices: 0.02 us -> 93.4 us  [on_device_body(): lax.psum_scatter(grad_gate_up.astype(jnp.bfloat16), 'dp', scatter_dimensi...]
    ppermute x9, waiting for transfers between devices: 277 us -> 213 us  [tensor_scatter(): lax.ppermute(acc_up.astype(jnp.bfloat16), 'tensor', [(i, i + 1) for i in...]
    ppermute x3, starting transfers between devices: 53.9 us -> 101 us  [tensor_scatter_direct(): lax.ppermute(block(jnp.minimum(j + d, n - 1)).astype(jnp.bfloat16), 'tens...]
    unnamed x32 -> x15, other arithmetic: 89.6 us -> 47.6 us
    ppermute x9, starting transfers between devices: 22.1 us -> 61.2 us  [tensor_gather(): up = lax.ppermute(up, 'tensor', [(i, i + 1) for i in range(s - 1, n - 1)])]
    psum x1, blocking collectives: 48.4 us -> 10.6 us  [on_device_body(): gains_sum = lax.psum((owned[7], owned[8], owned[9], owned[10]), 'tensor')]
    reduce_scatter x1, waiting for transfers between devices: 0.01 us -> 37.5 us  [on_device_body(): lax.psum_scatter(grad_qkv[:, :q_width].astype(jnp.bfloat16), 'dp', scatte...]
    ppermute x6, waiting for transfers between devices: 16.3 us -> 53.3 us  [tensor_gather_direct(): ups[d] = lax.ppermute(rows, 'tensor', [(i, i + d) for i in range(n - d)])]
  transfers between devices with their start and end apart: 68 -> 67, of which waited for: 28 -> 29; matrix products, arithmetic and copies ran while one was open for 25% -> 21% of each run, Pallas kernels for 0% -> 0%
where the time goes in v4:
time: 1960 us; the launch traced here: 1950 us
  waiting for transfers between devices  773 us (39%)
  starting transfers between devices  380 us (19%)
  matrix products  339 us (17%)
  other arithmetic  272 us (14%)
  local copies, waits for them, and re-layouts  108 us (6%)
  blocking collectives  56.1 us (3%)
    ppermute x9, waiting for transfers between devices, tensor_scatter(): lax.ppermute(acc_up.astype(jnp.bfloat16), 'tensor', [(i, i + 1) for i in...  213 us
    ppermute x6, starting transfers between devices, tensor_gather_direct(): ups[d] = lax.ppermute(rows, 'tensor', [(i, i + d) for i in range(n - d)])  117 us
    ppermute x9, waiting for transfers between devices, tensor_gather(): lax.ppermute(down, 'tensor', [(i, i - 1) for i in range(1, n - s + 1)])  113 us
    ppermute x3, starting transfers between devices, tensor_scatter_direct(): lax.ppermute(block(jnp.minimum(j + d, n - 1)).astype(jnp.bfloat16), 'tens...  101 us
    reduce_scatter x1, waiting for transfers between devices, on_device_body(): lax.psum_scatter(grad_gate_up.astype(jnp.bfloat16), 'dp', scatter_dimensi...  93.4 us
    ppermute x6, waiting for transfers between devices, tensor_gather_direct(): downs[d] = lax.ppermute(rows, 'tensor', [(i, i - d) for i in range(d, n)])  91.1 us
    ppermute x9, waiting for transfers between devices, tensor_scatter(): lax.ppermute(acc_down.astype(jnp.bfloat16), 'tensor', [(i, i - 1) for i i...  76.5 us
    ppermute x9, waiting for transfers between devices, tensor_gather(): up = lax.ppermute(up, 'tensor', [(i, i + 1) for i in range(s - 1, n - 1)])  62.9 us
  transfers between devices with their start and end apart: 67, of which 29 were waited for; matrix products, arithmetic and copies ran while one was open for 21% of the time, Pallas kernels for 0%

profile of v4, /device:TPU:0, one launch (start us, length us, event | category | flops | bytes accessed | tf_op | source)
XLA Modules:
  0.0 1946.4 jit_solution(18186910992446920861)
XLA Ops:
  37.1 41.5 %collective-permute-done.1 = bf16[512,2048]{1,0:T(8,128)(2,1)} collective-permute-done((bf16[512,2048]{1,0:T(8,128)(2,1)}, bf16[512,2048]{1,0:T(8,128)(2,1)}, u32[]{:S(2)}, u32[]{:S(2)}) %collective-permute-start.1) | collective-permute-done | bytes 2097184 | tf_op jit(solution)/shard_map/ppermute | solution.py:32
  97.1 36.3 %collective-permute-done.4 = bf16[512,2048]{1,0:T(8,128)(2,1)} collective-permute-done((bf16[512,2048]{1,0:T(8,128)(2,1)}, bf16[512,2048]{1,0:T(8,128)(2,1)}, u32[]{:S(2)}, u32[]{:S(2)}) %collective-permute-start.4) | collective-permute-done | bytes 2097184 | tf_op jit(solution)/shard_map/ppermute | solution.py:33
  166.8 15.0 collective-permute-done.5
  304.1 39.8 %collective-permute-done.6 = bf16[512,2048]{1,0:T(8,128)(2,1)} collective-permute-done((bf16[512,2048]{1,0:T(8,128)(2,1)}, bf16[512,2048]{1,0:T(8,128)(2,1)}, u32[]{:S(2)}, u32[]{:S(2)}) %collective-permute-start.6) | collective-permute-done | bytes 2097184 | tf_op jit(solution)/shard_map/ppermute | solution.py:66
  355.4 40.1 %collective-permute-done.7 = bf16[512,2048]{1,0:T(8,128)(2,1)} collective-permute-done((bf16[512,2048]{1,0:T(8,128)(2,1)}, bf16[512,2048]{1,0:T(8,128)(2,1)}, u32[]{:S(2)}, u32[]{:S(2)}) %collective-permute-start.7) | collective-permute-done | bytes 2097184 | tf_op jit(solution)/shard_map/ppermute | solution.py:66
  417.8 44.6 %collective-permute-start.29 = (bf16[512,1024]{1,0:T(8,128)(2,1)S(1)}, bf16[512,1024]{1,0:T(8,128)(2,1)}, u32[]{:S(2)}, u32[]{:S(2)}) collective-permute-start(bf16[512,1024]{1,0:T(8,128)(2,1)S(1)} %get-tuple-element.232), channel_id=1, source_target_pairs={{0,1},{1,2},{2,3},{4,5},{5,6},{6,7},{8,9},{9,10},{10,11},{12,13},{... | collective-permute-start | bytes 3145736 | tf_op jit(solution)/shard_map/ppermute | solution.py:81
  472.7 30.8 %collective-permute-done.11 = bf16[512,2048]{1,0:T(8,128)(2,1)} collective-permute-done((bf16[512,2048]{1,0:T(8,128)(2,1)}, bf16[512,2048]{1,0:T(8,128)(2,1)}, u32[]{:S(2)}, u32[]{:S(2)}) %collective-permute-start.11) | collective-permute-done | bytes 2097184 | tf_op jit(solution)/shard_map/ppermute | solution.py:67
  530.4 53.2 %collective-permute-done.27 = bf16[512,1024]{1,0:T(8,128)(2,1)S(1)} collective-permute-done((bf16[512,1024]{1,0:T(8,128)(2,1)S(1)}, bf16[512,1024]{1,0:T(8,128)(2,1)S(1)}, u32[]{:S(2)}, u32[]{:S(2)}) %collective-permute-start.27) | collective-permute-done | bytes 1048608 | tf_op jit(solution)/shard_map/ppermute | solution.py:81
  583.6 58.0 %collective-permute-start.35 = (bf16[512,1024]{1,0:T(8,128)(2,1)}, bf16[512,1024]{1,0:T(8,128)(2,1)}, u32[]{:S(2)}, u32[]{:S(2)}) collective-permute-start(bf16[512,1024]{1,0:T(8,128)(2,1)} %get-tuple-element.233), channel_id=1, source_target_pairs={{0,1},{1,2},{2,3},{4,5},{5,6},{6,7},{8,9},{9,10},{10,11},{12,13},{... | collective-permute-start | bytes 3145736 | tf_op jit(solution)/shard_map/ppermute | solution.py:81
  656.7 42.3 %collective-permute-done.34 = bf16[512,1024]{1,0:T(8,128)(2,1)} collective-permute-done((bf16[512,1024]{1,0:T(8,128)(2,1)}, bf16[512,1024]{1,0:T(8,128)(2,1)}, u32[]{:S(2)}, u32[]{:S(2)}) %collective-permute-start.34) | collective-permute-done | bytes 1048608 | tf_op jit(solution)/shard_map/ppermute | solution.py:82
  706.7 43.9 %collective-permute-done.32 = bf16[512,1024]{1,0:T(8,128)(2,1)S(1)} collective-permute-done((bf16[512,1024]{1,0:T(8,128)(2,1)}, bf16[512,1024]{1,0:T(8,128)(2,1)S(1)}, u32[]{:S(2)}, u32[]{:S(2)}) %collective-permute-start.32) | collective-permute-done | bytes 1048608 | tf_op jit(solution)/shard_map/ppermute | solution.py:82
  752.9 30.3 %maximum_maximum_fusion = bf16[2048,2048]{1,0:T(8,128)(2,1)} fusion(bf16[512,1024]{1,0:T(8,128)(2,1)S(1)} %broadcast_select_fusion.9, bf16[512,1024]{1,0:T(8,128)(2,1)S(1)} %broadcast_select_fusion.11, bf16[512,1024]{1,0:T(8,128)(2,1)S(1)} %broadcast_select_fusion.13, bf16[512,1024]{1,0:T(8,128)(2,1)} %get-tuple-element.233, ...), kind=kLoop, calls=%fused_computation.37 | loop fusion | flops 67108864 | bytes 16777216 | tf_op jit(solution)/shard_map/concatenate | solution.py:350
  800.4 31.3 %collective-permute-done.17 = bf16[512,2048]{1,0:T(8,128)(2,1)} collective-permute-done((bf16[512,2048]{1,0:T(8,128)(2,1)}, bf16[512,2048]{1,0:T(8,128)(2,1)}, u32[]{:S(2)}, u32[]{:S(2)}) %collective-permute-start.17) | collective-permute-done | bytes 2097184 | tf_op jit(solution)/shard_map/ppermute | solution.py:33
  837.4 33.0 %fusion.193 = f32[2048,3072]{1,0:T(8,128)} fusion(bf16[2048,3072]{1,0:T(8,128)(2,1)} %constant_dynamic-update-slice_fusion.5, bf16[512,2048]{1,0:T(8,128)(2,1)S(1)} %broadcast_select_fusion.1, bf16[512,2048]{1,0:T(8,128)(2,1)S(1)} %broadcast_select_fusion.4, bf16[512,2048]{1,0:T(8,128)(2,1)S(1)} %broadcast_select_fusion.7, ...), kind=kOutput, calls=%fused_computation.342 | convolution fusion | flops 25803358208 | bytes 46137344 | tf_op jit(solution)/shard_map/dot_general | solution.py:337
  870.4 37.8 %fusion.9 = (bf16[2048,1536]{1,0:T(8,128)(2,1)}, bf16[2048,1536]{1,0:T(8,128)(2,1)}, bf16[2048,1536]{1,0:T(8,128)(2,1)}) fusion(f32[2048,3072]{1,0:T(8,128)} %fusion.193, bf16[1536,2048]{1,0:T(8,128)(2,1)} %all-gather.22.cloned.1.call-done, bf16[512,1024]{1,0:T(8,128)(2,1)} %copy-done.59, bf16[512,1024]{1,0:T(8,128)(2,1)} %copy-done.60, ...), kind=kOutput, calls=%fused_computation.16 | convolution fusion | flops 13002342400 | bytes 58720256 | tf_op jit(solution)/shard_map/dot_general | solution.py:351
  908.3 34.4 %fusion.192 = f32[2048,2048]{1,0:T(8,128)} fusion(bf16[2048,3072]{1,0:T(8,128)(2,1)} %constant_dynamic-update-slice_fusion.5, bf16[2048,1536]{1,0:T(8,128)(2,1)} %get-tuple-element.198, bf16[2048,1536]{1,0:T(8,128)(2,1)} %get-tuple-element.197), kind=kOutput, calls=%fused_computation.341 | convolution fusion | flops 25794969600 | bytes 41943040 | tf_op jit(solution)/shard_map/dot_general | solution.py:360
  963.7 41.3 %collective-permute-done.36 = bf16[512,2048]{1,0:T(8,128)(2,1)} collective-permute-done((bf16[512,2048]{1,0:T(8,128)(2,1)}, bf16[512,2048]{1,0:T(8,128)(2,1)}, u32[]{:S(2)}, u32[]{:S(2)}) %collective-permute-start.36) | collective-permute-done | bytes 2097184 | tf_op jit(solution)/shard_map/ppermute | solution.py:66
  1015.6 22.5 %collective-permute-done.37 = bf16[512,2048]{1,0:T(8,128)(2,1)} collective-permute-done((bf16[512,2048]{1,0:T(8,128)(2,1)}, bf16[512,2048]{1,0:T(8,128)(2,1)}, u32[]{:S(2)}, u32[]{:S(2)}) %collective-permute-start.37) | collective-permute-done | bytes 2097184 | tf_op jit(solution)/shard_map/ppermute | solution.py:66
  1047.6 19.4 fusion.203
  1092.4 90.1 %collective-permute-start.20 = (bf16[512,2048]{1,0:T(8,128)(2,1)}, bf16[512,2048]{1,0:T(8,128)(2,1)S(1)}, u32[]{:S(2)}, u32[]{:S(2)}) collective-permute-start(bf16[512,2048]{1,0:T(8,128)(2,1)} %get-tuple-element.212), channel_id=1, source_target_pairs={{0,2},{1,3},{4,6},{5,7},{8,10},{9,11},{12,14},{13,15},{16,18},{17,... | collective-permute-start | bytes 6291464 | tf_op jit(solution)/shard_map/ppermute | solution.py:107
  1187.4 24.8 %collective-permute-start.38 = (bf16[512,2048]{1,0:T(8,128)(2,1)S(1)}, bf16[512,2048]{1,0:T(8,128)(2,1)S(1)}, u32[]{:S(2)}, u32[]{:S(2)}) collective-permute-start(bf16[512,2048]{1,0:T(8,128)(2,1)S(1)} %get-tuple-element.204), channel_id=1, source_target_pairs={{0,1},{1,2},{2,3},{4,5},{5,6},{6,7},{8,9},{9,10},{10,11},{12,13},{... | collective-permute-start | bytes 6291464 | tf_op jit(solution)/shard_map/ppermute | solution.py:66
  1243.8 21.1 %collective-permute-done.41 = bf16[512,2048]{1,0:T(8,128)(2,1)S(1)} collective-permute-done((bf16[512,2048]{1,0:T(8,128)(2,1)S(1)}, bf16[512,2048]{1,0:T(8,128)(2,1)S(1)}, u32[]{:S(2)}, u32[]{:S(2)}) %collective-permute-start.41) | collective-permute-done | bytes 2097184 | tf_op jit(solution)/shard_map/ppermute | solution.py:67
  1282.0 38.1 %collective-permute-start.43 = (bf16[512,2048]{1,0:T(8,128)(2,1)}, bf16[512,2048]{1,0:T(8,128)(2,1)S(1)}, u32[]{:S(2)}, u32[]{:S(2)}) collective-permute-start(bf16[512,2048]{1,0:T(8,128)(2,1)} %get-tuple-element.191), channel_id=1, source_target_pairs={{0,1},{1,2},{2,3},{4,5},{5,6},{6,7},{8,9},{9,10},{10,11},{12,13},{... | collective-permute-start | bytes 6291464 | tf_op jit(solution)/shard_map/ppermute | solution.py:32
  1326.3 21.4 %collective-permute-done.43 = bf16[512,2048]{1,0:T(8,128)(2,1)S(1)} collective-permute-done((bf16[512,2048]{1,0:T(8,128)(2,1)}, bf16[512,2048]{1,0:T(8,128)(2,1)S(1)}, u32[]{:S(2)}, u32[]{:S(2)}) %collective-permute-start.43) | collective-permute-done | bytes 2097184 | tf_op jit(solution)/shard_map/ppermute | solution.py:32
  1349.6 16.0 collective-permute-done.42
  1366.9 33.0 %fusion.204 = bf16[2048,3072]{1,0:T(8,128)(2,1)} fusion(bf16[2048,2048]{1,0:T(8,128)(2,1)} %pad_maximum_fusion.1, bf16[2048,3072]{1,0:T(8,128)(2,1)} %pad_maximum_fusion), kind=kOutput, calls=%fused_computation.351 | convolution fusion | flops 25769803776 | bytes 33554432 | tf_op jit(solution)/shard_map/dot_general | solution.py:365
  1412.7 19.2 fusion.205
  1635.4 37.8 %collective-permute-done.48 = bf16[512,2048]{1,0:T(8,128)(2,1)S(1)} collective-permute-done((bf16[512,2048]{1,0:T(8,128)(2,1)S(1)}, bf16[512,2048]{1,0:T(8,128)(2,1)S(1)}, u32[]{:S(2)}, u32[]{:S(2)}) %collective-permute-start.48) | collective-permute-done | bytes 2097184 | tf_op jit(solution)/shard_map/ppermute | solution.py:66
  1679.8 32.0 %collective-permute-done.49 = bf16[512,2048]{1,0:T(8,128)(2,1)} collective-permute-done((bf16[512,2048]{1,0:T(8,128)(2,1)S(1)}, bf16[512,2048]{1,0:T(8,128)(2,1)}, u32[]{:S(2)}, u32[]{:S(2)}) %collective-permute-start.49) | collective-permute-done | bytes 2097184 | tf_op jit(solution)/shard_map/ppermute | solution.py:66
  1737.1 37.5 %reduce-scatter.7.cloned.1.call-done = bf16[256,512]{1,0:T(8,128)(2,1)} async-done(((bf16[2048,512]{1,0:T(8,128)(2,1)}), bf16[256,512]{1,0:T(8,128)(2,1)}) %reduce-scatter.7.cloned.1.call-update) | async-done | bytes 262160 | tf_op jit(solution)/shard_map/reduce_scatter | solution.py:441
  1776.4 24.5 %collective-permute-done.53 = bf16[512,2048]{1,0:T(8,128)(2,1)} collective-permute-done((bf16[512,2048]{1,0:T(8,128)(2,1)}, bf16[512,2048]{1,0:T(8,128)(2,1)}, u32[]{:S(2)}, u32[]{:S(2)}) %collective-permute-start.53) | collective-permute-done | bytes 2097184 | tf_op jit(solution)/shard_map/ppermute | solution.py:67
  1842.8 93.4 %reduce-scatter.15.cloned.1.call-done = bf16[256,3072]{1,0:T(8,128)(2,1)} async-done(((bf16[2048,3072]{1,0:T(8,128)(2,1)}), bf16[256,3072]{1,0:T(8,128)(2,1)}) %reduce-scatter.15.cloned.1.call-update) | async-done | bytes 1572880 | tf_op jit(solution)/shard_map/reduce_scatter | solution.py:394
  (636 shorter events, 743.2 us)
Async XLA Ops:
  7.2 144.2 %all-gather.10.cloned.1.call-start = ((), (), s32[]{:S(2)}) async-start(), calls=%async_computation.6 | async-start | bytes 2359296 | tf_op jit(solution)/shard_map/all_gather | solution.py:268
  9.2 145.3 %all-gather.12.cloned.1.call-start = ((), (), s32[]{:S(2)}) async-start(), calls=%async_computation.7 | async-start | bytes 1179648 | tf_op jit(solution)/shard_map/all_gather | solution.py:269
  10.9 145.9 %all-gather.14.cloned.1.call-start = ((), (), s32[]{:S(2)}) async-start(), calls=%async_computation.8 | async-start | bytes 1179648 | tf_op jit(solution)/shard_map/all_gather | solution.py:270
  12.6 271.4 %all-gather.16.cloned.1.call-start = ((), (), s32[]{:S(2)}) async-start(), calls=%async_computation.9 | async-start | bytes 2359296 | tf_op jit(solution)/shard_map/all_gather | solution.py:271
  14.4 770.6 %all-gather.18.cloned.1.call-start = ((), (), s32[]{:S(2)}) async-start(), calls=%async_computation.10 | async-start | bytes 7077888 | tf_op jit(solution)/shard_map/all_gather | solution.py:322
  36.5 754.4 %all-gather.20.cloned.1.call-start = ((), (), s32[]{:S(2)}) async-start(), calls=%async_computation.11 | async-start | bytes 7077888 | tf_op jit(solution)/shard_map/all_gather | solution.py:323
  90.9 68.1 %collective-permute-start.3 = (bf16[512,2048]{1,0:T(8,128)(2,1)}, bf16[512,2048]{1,0:T(8,128)(2,1)}, u32[]{:S(2)}, u32[]{:S(2)}) collective-permute-start(bf16[512,2048]{1,0:T(8,128)(2,1)} %collective-permute-done.2), channel_id=1, source_target_pairs={{2,3},{6,7},{10,11},{14,15},{18,19},{22,23},{26,27},{30,31}} | collective-permute-start | bytes 6291464 | tf_op jit(solution)/shard_map/ppermute | solution.py:32
  355.4 515.1 %all-gather.22.cloned.1.call-start = ((), (), s32[]{:S(2)}) async-start(), calls=%async_computation.12 | async-start | bytes 7077888 | tf_op jit(solution)/shard_map/all_gather | solution.py:324
  405.1 67.5 %collective-permute-start.8 = (bf16[512,2048]{1,0:T(8,128)(2,1)}, bf16[512,2048]{1,0:T(8,128)(2,1)}, u32[]{:S(2)}, u32[]{:S(2)}) collective-permute-start(bf16[512,2048]{1,0:T(8,128)(2,1)} %get-tuple-element.214), channel_id=1, source_target_pairs={{0,1},{1,2},{2,3},{4,5},{5,6},{6,7},{8,9},{9,10},{10,11},{12,13},{... | collective-permute-start | bytes 6291464 | tf_op jit(solution)/shard_map/ppermute | solution.py:66
  415.2 88.3 %collective-permute-start.11 = (bf16[512,2048]{1,0:T(8,128)(2,1)}, bf16[512,2048]{1,0:T(8,128)(2,1)}, u32[]{:S(2)}, u32[]{:S(2)}) collective-permute-start(bf16[512,2048]{1,0:T(8,128)(2,1)} %add_convert_fusion.8), channel_id=1, source_target_pairs={{1,0},{2,1},{3,2},{5,4},{6,5},{7,6},{9,8},{10,9},{11,10},{13,12},{... | collective-permute-start | bytes 6291464 | tf_op jit(solution)/shard_map/ppermute | solution.py:67
  417.8 101.6 %collective-permute-start.29 = (bf16[512,1024]{1,0:T(8,128)(2,1)S(1)}, bf16[512,1024]{1,0:T(8,128)(2,1)}, u32[]{:S(2)}, u32[]{:S(2)}) collective-permute-start(bf16[512,1024]{1,0:T(8,128)(2,1)S(1)} %get-tuple-element.232), channel_id=1, source_target_pairs={{0,1},{1,2},{2,3},{4,5},{5,6},{6,7},{8,9},{9,10},{10,11},{12,13},{... | collective-permute-start | bytes 3145736 | tf_op jit(solution)/shard_map/ppermute | solution.py:81
  510.5 140.2 %collective-permute-start.13 = (bf16[512,2048]{1,0:T(8,128)(2,1)S(1)}, bf16[512,2048]{1,0:T(8,128)(2,1)}, u32[]{:S(2)}, u32[]{:S(2)}) collective-permute-start(bf16[512,2048]{1,0:T(8,128)(2,1)S(1)} %multiply_convert_fusion.2), channel_id=1, source_target_pairs={{0,1},{1,2},{2,3},{4,5},{5,6},{6,7},{8,9},{9,10},{10,11},{12,13},{... | collective-permute-start | bytes 6291464 | tf_op jit(solution)/shard_map/ppermute | solution.py:32
  516.6 67.0 %collective-permute-start.27 = (bf16[512,1024]{1,0:T(8,128)(2,1)S(1)}, bf16[512,1024]{1,0:T(8,128)(2,1)S(1)}, u32[]{:S(2)}, u32[]{:S(2)}) collective-permute-start(bf16[512,1024]{1,0:T(8,128)(2,1)S(1)} %get-tuple-element.232), channel_id=1, source_target_pairs={{0,2},{1,3},{4,6},{5,7},{8,10},{9,11},{12,14},{13,15},{16,18},{17,... | collective-permute-start | bytes 3145736 | tf_op jit(solution)/shard_map/ppermute | solution.py:81
  518.0 123.6 %collective-permute-start.26 = (bf16[512,1024]{1,0:T(8,128)(2,1)S(1)}, bf16[512,1024]{1,0:T(8,128)(2,1)S(1)}, u32[]{:S(2)}, u32[]{:S(2)}) collective-permute-start(bf16[512,1024]{1,0:T(8,128)(2,1)S(1)} %get-tuple-element.232), channel_id=1, source_target_pairs={{2,0},{3,1},{6,4},{7,5},{10,8},{11,9},{14,12},{15,13},{18,16},{19,... | collective-permute-start | bytes 3145736 | tf_op jit(solution)/shard_map/ppermute | solution.py:82
  519.4 123.6 %collective-permute-start.25 = (bf16[512,1024]{1,0:T(8,128)(2,1)S(1)}, bf16[512,1024]{1,0:T(8,128)(2,1)S(1)}, u32[]{:S(2)}, u32[]{:S(2)}) collective-permute-start(bf16[512,1024]{1,0:T(8,128)(2,1)S(1)} %get-tuple-element.232), channel_id=1, source_target_pairs={{0,3},{4,7},{8,11},{12,15},{16,19},{20,23},{24,27},{28,31}} | collective-permute-start | bytes 3145736 | tf_op jit(solution)/shard_map/ppermute | solution.py:81
  529.1 115.3 %collective-permute-start.24 = (bf16[512,1024]{1,0:T(8,128)(2,1)S(1)}, bf16[512,1024]{1,0:T(8,128)(2,1)S(1)}, u32[]{:S(2)}, u32[]{:S(2)}) collective-permute-start(bf16[512,1024]{1,0:T(8,128)(2,1)S(1)} %get-tuple-element.232), channel_id=1, source_target_pairs={{1,0},{2,1},{3,2},{5,4},{6,5},{7,6},{9,8},{10,9},{11,10},{13,12},{... | collective-permute-start | bytes 3145736 | tf_op jit(solution)/shard_map/ppermute | solution.py:82
  583.6 70.3 %collective-permute-start.35 = (bf16[512,1024]{1,0:T(8,128)(2,1)}, bf16[512,1024]{1,0:T(8,128)(2,1)}, u32[]{:S(2)}, u32[]{:S(2)}) collective-permute-start(bf16[512,1024]{1,0:T(8,128)(2,1)} %get-tuple-element.233), channel_id=1, source_target_pairs={{0,1},{1,2},{2,3},{4,5},{5,6},{6,7},{8,9},{9,10},{10,11},{12,13},{... | collective-permute-start | bytes 3145736 | tf_op jit(solution)/shard_map/ppermute | solution.py:81
  650.7 100.2 %collective-permute-start.14 = (bf16[512,2048]{1,0:T(8,128)(2,1)}, bf16[512,2048]{1,0:T(8,128)(2,1)}, u32[]{:S(2)}, u32[]{:S(2)}) collective-permute-start(bf16[512,2048]{1,0:T(8,128)(2,1)} %collective-permute-done.13), channel_id=1, source_target_pairs={{1,2},{2,3},{5,6},{6,7},{9,10},{10,11},{13,14},{14,15},{17,18},{18... | collective-permute-start | bytes 6291464 | tf_op jit(solution)/shard_map/ppermute | solution.py:32
  653.8 1078.3 %reduce-scatter.9.cloned.1.call-start = ((), (), s32[]{:S(2)}) async-start(), calls=%async_computation.14 | async-start | bytes 1179648 | tf_op jit(solution)/shard_map/reduce_scatter | solution.py:444
  654.0 96.6 %collective-permute-start.32 = (bf16[512,1024]{1,0:T(8,128)(2,1)}, bf16[512,1024]{1,0:T(8,128)(2,1)S(1)}, u32[]{:S(2)}, u32[]{:S(2)}) collective-permute-start(bf16[512,1024]{1,0:T(8,128)(2,1)} %get-tuple-element.233), channel_id=1, source_target_pairs={{2,0},{3,1},{6,4},{7,5},{10,8},{11,9},{14,12},{15,13},{18,16},{19,... | collective-permute-start | bytes 3145736 | tf_op jit(solution)/shard_map/ppermute | solution.py:82
  705.4 77.9 %collective-permute-start.16 = (bf16[512,2048]{1,0:T(8,128)(2,1)}, bf16[512,2048]{1,0:T(8,128)(2,1)}, u32[]{:S(2)}, u32[]{:S(2)}) collective-permute-start(bf16[512,2048]{1,0:T(8,128)(2,1)} %collective-permute-done.12), channel_id=1, source_target_pairs={{1,0},{2,1},{5,4},{6,5},{9,8},{10,9},{13,12},{14,13},{17,16},{18,1... | collective-permute-start | bytes 6291464 | tf_op jit(solution)/shard_map/ppermute | solution.py:33
  1079.0 107.0 %collective-permute-start.18 = (bf16[512,2048]{1,0:T(8,128)(2,1)}, bf16[512,2048]{1,0:T(8,128)(2,1)S(1)}, u32[]{:S(2)}, u32[]{:S(2)}) collective-permute-start(bf16[512,2048]{1,0:T(8,128)(2,1)} %get-tuple-element.208), channel_id=1, source_target_pairs={{0,1},{1,2},{2,3},{4,5},{5,6},{6,7},{8,9},{9,10},{10,11},{12,13},{... | collective-permute-start | bytes 6291464 | tf_op jit(solution)/shard_map/ppermute | solution.py:107
  1083.1 104.2 %collective-permute-start.23 = (bf16[512,2048]{1,0:T(8,128)(2,1)S(1)}, bf16[512,2048]{1,0:T(8,128)(2,1)S(1)}, u32[]{:S(2)}, u32[]{:S(2)}) collective-permute-start(bf16[512,2048]{1,0:T(8,128)(2,1)S(1)} %get-tuple-element.209), channel_id=1, source_target_pairs={{3,0},{7,4},{11,8},{15,12},{19,16},{23,20},{27,24},{31,28}} | collective-permute-start | bytes 6291464 | tf_op jit(solution)/shard_map/ppermute | solution.py:112
  1084.4 127.8 %collective-permute-start.22 = (bf16[512,2048]{1,0:T(8,128)(2,1)}, bf16[512,2048]{1,0:T(8,128)(2,1)S(1)}, u32[]{:S(2)}, u32[]{:S(2)}) collective-permute-start(bf16[512,2048]{1,0:T(8,128)(2,1)} %get-tuple-element.210), channel_id=1, source_target_pairs={{0,3},{4,7},{8,11},{12,15},{16,19},{20,23},{24,27},{28,31}} | collective-permute-start | bytes 6291464 | tf_op jit(solution)/shard_map/ppermute | solution.py:107
  1091.1 137.2 %collective-permute-start.21 = (bf16[512,2048]{1,0:T(8,128)(2,1)}, bf16[512,2048]{1,0:T(8,128)(2,1)S(1)}, u32[]{:S(2)}, u32[]{:S(2)}) collective-permute-start(bf16[512,2048]{1,0:T(8,128)(2,1)} %get-tuple-element.211), channel_id=1, source_target_pairs={{2,0},{3,1},{6,4},{7,5},{10,8},{11,9},{14,12},{15,13},{18,16},{19,... | collective-permute-start | bytes 6291464 | tf_op jit(solution)/shard_map/ppermute | solution.py:112
  1092.4 135.9 %collective-permute-start.20 = (bf16[512,2048]{1,0:T(8,128)(2,1)}, bf16[512,2048]{1,0:T(8,128)(2,1)S(1)}, u32[]{:S(2)}, u32[]{:S(2)}) collective-permute-start(bf16[512,2048]{1,0:T(8,128)(2,1)} %get-tuple-element.212), channel_id=1, source_target_pairs={{0,2},{1,3},{4,6},{5,7},{8,10},{9,11},{12,14},{13,15},{16,18},{17,... | collective-permute-start | bytes 6291464 | tf_op jit(solution)/shard_map/ppermute | solution.py:107
  1612.2 121.5 %reduce-scatter.11.cloned.1.call-start = ((), (), s32[]{:S(2)}) async-start(), calls=%async_computation.15 | async-start | bytes 1179648 | tf_op jit(solution)/shard_map/reduce_scatter | solution.py:450
  1613.0 122.4 %reduce-scatter.13.cloned.1.call-start = ((), (), s32[]{:S(2)}) async-start(), calls=%async_computation.16 | async-start | bytes 2359296 | tf_op jit(solution)/shard_map/reduce_scatter | solution.py:398
  1613.6 161.1 %reduce-scatter.7.cloned.1.call-start = ((), (), s32[]{:S(2)}) async-start(), calls=%async_computation.13 | async-start | bytes 2359296 | tf_op jit(solution)/shard_map/reduce_scatter | solution.py:441
  1616.7 223.7 %reduce-scatter.17.cloned.1.call-start = ((), (), s32[]{:S(2)}) async-start(), calls=%async_computation.18 | async-start | bytes 7077888 | tf_op jit(solution)/shard_map/reduce_scatter | solution.py:403
  1617.3 318.9 %reduce-scatter.15.cloned.1.call-start = ((), (), s32[]{:S(2)}) async-start(), calls=%async_computation.17 | async-start | bytes 14155776 | tf_op jit(solution)/shard_map/reduce_scatter | solution.py:394
  1729.5 71.4 %collective-permute-start.53 = (bf16[512,2048]{1,0:T(8,128)(2,1)}, bf16[512,2048]{1,0:T(8,128)(2,1)}, u32[]{:S(2)}, u32[]{:S(2)}) collective-permute-start(bf16[512,2048]{1,0:T(8,128)(2,1)} %add_convert_fusion), channel_id=1, source_target_pairs={{1,0},{2,1},{3,2},{5,4},{6,5},{7,6},{9,8},{10,9},{11,10},{13,12},{... | collective-permute-start | bytes 6291464 | tf_op jit(solution)/shard_map/ppermute | solution.py:67
  (192 other events, 6054.9 us)
Sparse Core Ops, SparseCore 0:
  10.5 30.4 all-gather.9
  43.5 23.3 all-gather.11
  68.8 23.3 all-gather.13
  94.5 28.0 all-gather.15
  124.3 45.4 all-gather.17
  355.5 42.6 all-gather.19
  653.9 47.7 all-gather.21
  1612.3 33.8 reduce-scatter.8
  1650.0 35.9 reduce-scatter.10
  1689.1 41.0 reduce-scatter.12
  1733.5 41.0 reduce-scatter.6
  1777.9 62.5 reduce-scatter.16
  1843.9 92.2 reduce-scatter.14

commit v5 on v3

--- a/solution.py
+++ b/solution.py
@@ -276,7 +276,7 @@
     gain_k = gk_b.astype(f32)
     normalized_input = rms_scale(tok_rows, attn_g).astype(bf16)
     gathered = tensor_gather(normalized_input, tensor_n)
-    half_width = out_grad.shape[1] // 2
+    half_width = (out_grad.shape[1] * 11 // 16) // 128 * 128
     grad_half_a = tensor_gather_direct(out_grad[:, :half_width], tensor_n)
     projected = jnp.dot(gathered, w_qkv, preferred_element_type=f32)
     query_unrotated = projected[:, :q_width].reshape(
@@ -379,22 +379,15 @@
             inputs[0], inputs[1], inputs[2], inputs[3], inputs[4], inputs[5], inputs[6]
         )
 
+    gate_up_owned = lax.psum_scatter(
+        grad_gate_up.astype(jnp.bfloat16), "dp", scatter_dimension=0, tiled=True
+    ).astype(jnp.float32)
     mlp_owned = (
         lax.psum_scatter(
             grad_out.astype(jnp.bfloat16), "dp", scatter_dimension=1, tiled=True
         ).astype(jnp.float32),
-        lax.psum_scatter(
-            grad_gate_up[:, :hidden_width].astype(jnp.bfloat16),
-            "dp",
-            scatter_dimension=0,
-            tiled=True,
-        ).astype(jnp.float32),
-        lax.psum_scatter(
-            grad_gate_up[:, hidden_width:].astype(jnp.bfloat16),
-            "dp",
-            scatter_dimension=0,
-            tiled=True,
-        ).astype(jnp.float32),
+        gate_up_owned[:, :hidden_width],
+        gate_up_owned[:, hidden_width:],
         lax.psum_scatter(
             grad_down.astype(jnp.bfloat16), "dp", scatter_dimension=1, tiled=True
         ).astype(jnp.float32),

time: 1830 us -> 1810 us (0.989); the launches traced: 1820 us -> 1770 us
  starting transfers between devices: 274 us -> 383 us
  waiting for transfers between devices: 692 us -> 604 us
  blocking collectives: 93.4 us -> 55.3 us
  other arithmetic: 291 us -> 270 us
    ppermute x3, starting transfers between devices: 53.9 us -> 117 us  [tensor_scatter_direct(): lax.ppermute(block(jnp.minimum(j + d, n - 1)).astype(jnp.bfloat16), 'tens...]
    ppermute x6, waiting for transfers between devices: 89.4 us -> 42 us  [tensor_gather_direct(): downs[d] = lax.ppermute(rows, 'tensor', [(i, i - d) for i in range(d, n)])]
    ppermute x6, starting transfers between devices: 122 us -> 163 us  [tensor_gather_direct(): ups[d] = lax.ppermute(rows, 'tensor', [(i, i + d) for i in range(n - d)])]
    psum x1, blocking collectives: 48.4 us -> 9.11 us  [on_device_body(): gains_sum = lax.psum((owned[7], owned[8], owned[9], owned[10]), 'tensor')]
    ppermute x9, waiting for transfers between devices: 277 us -> 240 us  [tensor_scatter(): lax.ppermute(acc_up.astype(jnp.bfloat16), 'tensor', [(i, i + 1) for i in...]
    ppermute x9, waiting for transfers between devices: 147 us -> 167 us  [tensor_gather(): lax.ppermute(down, 'tensor', [(i, i - 1) for i in range(1, n - s + 1)])]
    ppermute x3, waiting for transfers between devices: 19 us -> 0.01 us  [tensor_scatter_direct(): lax.ppermute(block(jnp.minimum(j + d, n - 1)).astype(jnp.bfloat16), 'tens...]
    unnamed x328 -> x323, local copies, waits for them, and re-layouts: 46.7 us -> 52.6 us
  transfers between devices with their start and end apart: 68 -> 67, of which waited for: 28 -> 25; matrix products, arithmetic and copies ran while one was open for 25% -> 24% of each run, Pallas kernels for 0% -> 0%
where the time goes in v5:
time: 1810 us; the launch traced here: 1770 us
  waiting for transfers between devices  604 us (33%)
  starting transfers between devices  383 us (21%)
  matrix products  314 us (17%)
  other arithmetic  270 us (15%)
  local copies, waits for them, and re-layouts  127 us (7%)
  blocking collectives  55.3 us (3%)
  between operations  18.8 us (1%)
    ppermute x9, waiting for transfers between devices, tensor_scatter(): lax.ppermute(acc_up.astype(jnp.bfloat16), 'tensor', [(i, i + 1) for i in...  240 us
    ppermute x9, waiting for transfers between devices, tensor_gather(): lax.ppermute(down, 'tensor', [(i, i - 1) for i in range(1, n - s + 1)])  167 us
    ppermute x6, starting transfers between devices, tensor_gather_direct(): ups[d] = lax.ppermute(rows, 'tensor', [(i, i + d) for i in range(n - d)])  163 us
    ppermute x3, starting transfers between devices, tensor_scatter_direct(): lax.ppermute(block(jnp.minimum(j + d, n - 1)).astype(jnp.bfloat16), 'tens...  117 us
    unnamed x31, other arithmetic  83.9 us
    ppermute x9, waiting for transfers between devices, tensor_scatter(): lax.ppermute(acc_down.astype(jnp.bfloat16), 'tensor', [(i, i - 1) for i i...  81.8 us
    ppermute x9, waiting for transfers between devices, tensor_gather(): up = lax.ppermute(up, 'tensor', [(i, i + 1) for i in range(s - 1, n - 1)])  67.3 us
    unnamed x323, local copies, waits for them, and re-layouts  52.6 us
  transfers between devices with their start and end apart: 67, of which 25 were waited for; matrix products, arithmetic and copies ran while one was open for 24% of the time, Pallas kernels for 0%

profile of v5, /device:TPU:0, one launch (start us, length us, event | category | flops | bytes accessed | tf_op | source)
XLA Modules:
  0.0 1772.0 jit_solution(12412687725016097692)
XLA Ops:
  39.0 41.5 %collective-permute-done.1 = bf16[512,2048]{1,0:T(8,128)(2,1)} collective-permute-done((bf16[512,2048]{1,0:T(8,128)(2,1)}, bf16[512,2048]{1,0:T(8,128)(2,1)}, u32[]{:S(2)}, u32[]{:S(2)}) %collective-permute-start.1) | collective-permute-done | bytes 2097184 | tf_op jit(solution)/shard_map/ppermute | solution.py:32
  98.8 36.4 %collective-permute-done.4 = bf16[512,2048]{1,0:T(8,128)(2,1)} collective-permute-done((bf16[512,2048]{1,0:T(8,128)(2,1)}, bf16[512,2048]{1,0:T(8,128)(2,1)}, u32[]{:S(2)}, u32[]{:S(2)}) %collective-permute-start.4) | collective-permute-done | bytes 2097184 | tf_op jit(solution)/shard_map/ppermute | solution.py:33
  168.3 15.3 collective-permute-done.5
  292.1 39.7 %collective-permute-done.6 = bf16[512,2048]{1,0:T(8,128)(2,1)} collective-permute-done((bf16[512,2048]{1,0:T(8,128)(2,1)S(1)}, bf16[512,2048]{1,0:T(8,128)(2,1)}, u32[]{:S(2)}, u32[]{:S(2)}) %collective-permute-start.6) | collective-permute-done | bytes 2097184 | tf_op jit(solution)/shard_map/ppermute | solution.py:62
  342.5 41.0 %collective-permute-done.7 = bf16[512,2048]{1,0:T(8,128)(2,1)} collective-permute-done((bf16[512,2048]{1,0:T(8,128)(2,1)}, bf16[512,2048]{1,0:T(8,128)(2,1)}, u32[]{:S(2)}, u32[]{:S(2)}) %collective-permute-start.7) | collective-permute-done | bytes 2097184 | tf_op jit(solution)/shard_map/ppermute | solution.py:62
  420.0 69.8 %collective-permute-start.35 = (bf16[512,640]{1,0:T(8,128)(2,1)}, bf16[512,640]{1,0:T(8,128)(2,1)}, u32[]{:S(2)}, u32[]{:S(2)}) collective-permute-start(bf16[512,640]{1,0:T(8,128)(2,1)} %get-tuple-element.237), channel_id=1, source_target_pairs={{0,1},{1,2},{2,3},{4,5},{5,6},{6,7},{8,9},{9,10},{10,11},{12,13},{... | collective-permute-start | bytes 1966088 | tf_op jit(solution)/shard_map/ppermute | solution.py:77
  534.9 13.7 collective-permute-done.11
  557.9 15.9 collective-permute-done.24
  573.8 67.5 %collective-permute-start.29 = (bf16[512,1408]{1,0:T(8,128)(2,1)S(1)}, bf16[512,1408]{1,0:T(8,128)(2,1)S(1)}, u32[]{:S(2)}, u32[]{:S(2)}) collective-permute-start(bf16[512,1408]{1,0:T(8,128)(2,1)S(1)} %copy-done.86), channel_id=1, source_target_pairs={{0,1},{1,2},{2,3},{4,5},{5,6},{6,7},{8,9},{9,10},{10,11},{12,13},{... | collective-permute-start | bytes 4325384 | tf_op jit(solution)/shard_map/ppermute | solution.py:77
  646.5 20.7 %collective-permute-done.26 = bf16[512,1408]{1,0:T(8,128)(2,1)S(1)} collective-permute-done((bf16[512,1408]{1,0:T(8,128)(2,1)}, bf16[512,1408]{1,0:T(8,128)(2,1)S(1)}, u32[]{:S(2)}, u32[]{:S(2)}) %collective-permute-start.26) | collective-permute-done | bytes 1441824 | tf_op jit(solution)/shard_map/ppermute | solution.py:78
  684.9 27.9 %collective-permute-done.12 = bf16[512,2048]{1,0:T(8,128)(2,1)} collective-permute-done((bf16[512,2048]{1,0:T(8,128)(2,1)S(1)}, bf16[512,2048]{1,0:T(8,128)(2,1)}, u32[]{:S(2)}, u32[]{:S(2)}) %collective-permute-start.12) | collective-permute-done | bytes 2097184 | tf_op jit(solution)/shard_map/ppermute | solution.py:33
  731.7 33.3 %collective-permute-done.16 = bf16[512,2048]{1,0:T(8,128)(2,1)} collective-permute-done((bf16[512,2048]{1,0:T(8,128)(2,1)}, bf16[512,2048]{1,0:T(8,128)(2,1)}, u32[]{:S(2)}, u32[]{:S(2)}) %collective-permute-start.16) | collective-permute-done | bytes 2097184 | tf_op jit(solution)/shard_map/ppermute | solution.py:33
  825.4 34.5 %fusion.216 = f32[2048,3072]{1,0:T(8,128)} fusion(bf16[2048,2048]{1,0:T(8,128)(2,1)} %constant_dynamic-slice_fusion.2, bf16[2048,3072]{1,0:T(8,128)(2,1)} %constant_dynamic-update-slice_fusion.7), kind=kOutput, calls=%fused_computation.371 | convolution fusion | flops 25769803776 | bytes 46137344 | tf_op jit(solution)/shard_map/dot_general | solution.py:325
  859.9 26.8 %fusion.9 = (bf16[2048,1536]{1,0:T(8,128)(2,1)}, bf16[2048,1536]{1,0:T(8,128)(2,1)}, bf16[2048,1536]{1,0:T(8,128)(2,1)}) fusion(f32[2048,3072]{1,0:T(8,128)} %fusion.216, bf16[1536,2048]{1,0:T(8,128)(2,1)} %all-gather.22.cloned.1.call-done, bf16[2048,640]{1,0:T(8,128)(2,1)S(1)} %copy-done.39, bf16[2048,1408]{1,0:T(8,128)(2,1)} %constant_dynamic-slice_fusion.1), kind=kOutput, calls=%fused_computation.16 | convolution fusion | flops 12952010752 | bytes 58720256 | tf_op jit(solution)/shard_map/dot_general | solution.py:339
  886.7 34.5 %fusion.205 = f32[2048,2048]{1,0:T(8,128)} fusion(bf16[2048,3072]{1,0:T(8,128)(2,1)} %constant_dynamic-update-slice_fusion.7, bf16[2048,1536]{1,0:T(8,128)(2,1)} %get-tuple-element.200, bf16[2048,1536]{1,0:T(8,128)(2,1)} %get-tuple-element.199), kind=kOutput, calls=%fused_computation.362 | convolution fusion | flops 25794969600 | bytes 41943040 | tf_op jit(solution)/shard_map/dot_general | solution.py:348
  939.4 38.5 %collective-permute-done.36 = bf16[512,2048]{1,0:T(8,128)(2,1)S(1)} collective-permute-done((bf16[512,2048]{1,0:T(8,128)(2,1)S(1)}, bf16[512,2048]{1,0:T(8,128)(2,1)S(1)}, u32[]{:S(2)}, u32[]{:S(2)}) %collective-permute-start.36) | collective-permute-done | bytes 2097184 | tf_op jit(solution)/shard_map/ppermute | solution.py:62
  984.4 32.1 %collective-permute-done.37 = bf16[512,2048]{1,0:T(8,128)(2,1)} collective-permute-done((bf16[512,2048]{1,0:T(8,128)(2,1)S(1)}, bf16[512,2048]{1,0:T(8,128)(2,1)}, u32[]{:S(2)}, u32[]{:S(2)}) %collective-permute-start.37) | collective-permute-done | bytes 2097184 | tf_op jit(solution)/shard_map/ppermute | solution.py:62
  1030.9 26.4 %collective-permute-done.38 = bf16[512,2048]{1,0:T(8,128)(2,1)S(1)} collective-permute-done((bf16[512,2048]{1,0:T(8,128)(2,1)}, bf16[512,2048]{1,0:T(8,128)(2,1)S(1)}, u32[]{:S(2)}, u32[]{:S(2)}) %collective-permute-start.38) | collective-permute-done | bytes 2097184 | tf_op jit(solution)/shard_map/ppermute | solution.py:62
  1057.2 43.6 %collective-permute-done.41 = bf16[512,2048]{1,0:T(8,128)(2,1)S(1)} collective-permute-done((bf16[512,2048]{1,0:T(8,128)(2,1)S(1)}, bf16[512,2048]{1,0:T(8,128)(2,1)S(1)}, u32[]{:S(2)}, u32[]{:S(2)}) %collective-permute-start.41) | collective-permute-done | bytes 2097184 | tf_op jit(solution)/shard_map/ppermute | solution.py:63
  1124.3 17.0 collective-permute-done.43
  1143.3 23.6 %collective-permute-done.42 = bf16[512,2048]{1,0:T(8,128)(2,1)} collective-permute-done((bf16[512,2048]{1,0:T(8,128)(2,1)}, bf16[512,2048]{1,0:T(8,128)(2,1)}, u32[]{:S(2)}, u32[]{:S(2)}) %collective-permute-start.42) | collective-permute-done | bytes 2097184 | tf_op jit(solution)/shard_map/ppermute | solution.py:33
  1168.2 33.0 %fusion.218 = bf16[2048,3072]{1,0:T(8,128)(2,1)} fusion(bf16[2048,2048]{1,0:T(8,128)(2,1)} %constant_dynamic-slice_fusion.2, bf16[2048,3072]{1,0:T(8,128)(2,1)} %pad_maximum_fusion), kind=kOutput, calls=%fused_computation.373 | convolution fusion | flops 25769803776 | bytes 33554432 | tf_op jit(solution)/shard_map/dot_general | solution.py:353
  1203.2 14.2 collective-permute-done.46
  1218.6 19.4 %fusion.219 = bf16[1536,2048]{1,0:T(8,128)(2,1)} fusion(bf16[2048,1536]{1,0:T(8,128)(2,1)} %get-tuple-element.201, bf16[2048,2048]{1,0:T(8,128)(2,1)} %pad_maximum_fusion.1), kind=kOutput, calls=%fused_computation.374 | convolution fusion | flops 12884901888 | bytes 20971520 | tf_op jit(solution)/shard_map/dot_general | solution.py:352
  1436.8 40.5 %collective-permute-done.48 = bf16[512,2048]{1,0:T(8,128)(2,1)S(1)} collective-permute-done((bf16[512,2048]{1,0:T(8,128)(2,1)S(1)}, bf16[512,2048]{1,0:T(8,128)(2,1)S(1)}, u32[]{:S(2)}, u32[]{:S(2)}) %collective-permute-start.48) | collective-permute-done | bytes 2097184 | tf_op jit(solution)/shard_map/ppermute | solution.py:62
  1483.8 22.2 %collective-permute-done.49 = bf16[512,2048]{1,0:T(8,128)(2,1)} collective-permute-done((bf16[512,2048]{1,0:T(8,128)(2,1)S(1)}, bf16[512,2048]{1,0:T(8,128)(2,1)}, u32[]{:S(2)}, u32[]{:S(2)}) %collective-permute-start.49) | collective-permute-done | bytes 2097184 | tf_op jit(solution)/shard_map/ppermute | solution.py:62
  1512.8 19.5 %fusion.217 = f32[2048,2048]{1,0:T(8,128)} fusion(bf16[2048,1536]{1,0:T(8,128)(2,1)} %get-tuple-element.201, bf16[1536,2048]{1,0:T(8,128)(2,1)} %all-gather.22.cloned.1.call-done), kind=kOutput, calls=%fused_computation.372 | convolution fusion | flops 12884901888 | bytes 29360128 | tf_op jit(solution)/shard_map/dot_general | solution.py:329
  1558.0 52.3 %collective-permute-start.22 = (bf16[512,2048]{1,0:T(8,128)(2,1)}, bf16[512,2048]{1,0:T(8,128)(2,1)}, u32[]{:S(2)}, u32[]{:S(2)}) collective-permute-start(bf16[512,2048]{1,0:T(8,128)(2,1)} %get-tuple-element.212), channel_id=1, source_target_pairs={{0,3},{4,7},{8,11},{12,15},{16,19},{20,23},{24,27},{28,31}} | collective-permute-start | bytes 6291464 | tf_op jit(solution)/shard_map/ppermute | solution.py:99
  1621.0 24.4 %collective-permute-done.53 = bf16[512,2048]{1,0:T(8,128)(2,1)} collective-permute-done((bf16[512,2048]{1,0:T(8,128)(2,1)S(1)}, bf16[512,2048]{1,0:T(8,128)(2,1)}, u32[]{:S(2)}, u32[]{:S(2)}) %collective-permute-start.53) | collective-permute-done | bytes 2097184 | tf_op jit(solution)/shard_map/ppermute | solution.py:63
  1645.3 57.1 %collective-permute-start.18 = (bf16[512,2048]{1,0:T(8,128)(2,1)}, bf16[512,2048]{1,0:T(8,128)(2,1)}, u32[]{:S(2)}, u32[]{:S(2)}) collective-permute-start(bf16[512,2048]{1,0:T(8,128)(2,1)} %get-tuple-element.210), channel_id=1, source_target_pairs={{0,1},{1,2},{2,3},{4,5},{5,6},{6,7},{8,9},{9,10},{10,11},{12,13},{... | collective-permute-start | bytes 6291464 | tf_op jit(solution)/shard_map/ppermute | solution.py:99
  1717.5 14.6 all-reduce.13
  1743.8 15.6 fusion.48
  (647 shorter events, 740.8 us)
Async XLA Ops:
  7.2 145.9 %all-gather.10.cloned.1.call-start = ((), (), s32[]{:S(2)}) async-start(), calls=%async_computation.6 | async-start | bytes 2359296 | tf_op jit(solution)/shard_map/all_gather | solution.py:260
  9.2 147.0 %all-gather.12.cloned.1.call-start = ((), (), s32[]{:S(2)}) async-start(), calls=%async_computation.7 | async-start | bytes 1179648 | tf_op jit(solution)/shard_map/all_gather | solution.py:261
  10.9 147.6 %all-gather.14.cloned.1.call-start = ((), (), s32[]{:S(2)}) async-start(), calls=%async_computation.8 | async-start | bytes 1179648 | tf_op jit(solution)/shard_map/all_gather | solution.py:262
  12.6 259.5 %all-gather.16.cloned.1.call-start = ((), (), s32[]{:S(2)}) async-start(), calls=%async_computation.9 | async-start | bytes 2359296 | tf_op jit(solution)/shard_map/all_gather | solution.py:263
  14.4 752.3 %all-gather.18.cloned.1.call-start = ((), (), s32[]{:S(2)}) async-start(), calls=%async_computation.10 | async-start | bytes 7077888 | tf_op jit(solution)/shard_map/all_gather | solution.py:312
  16.9 755.9 %all-gather.20.cloned.1.call-start = ((), (), s32[]{:S(2)}) async-start(), calls=%async_computation.11 | async-start | bytes 7077888 | tf_op jit(solution)/shard_map/all_gather | solution.py:313
  38.4 821.5 %all-gather.22.cloned.1.call-start = ((), (), s32[]{:S(2)}) async-start(), calls=%async_computation.12 | async-start | bytes 7077888 | tf_op jit(solution)/shard_map/all_gather | solution.py:314
  92.8 67.9 %collective-permute-start.3 = (bf16[512,2048]{1,0:T(8,128)(2,1)}, bf16[512,2048]{1,0:T(8,128)(2,1)}, u32[]{:S(2)}, u32[]{:S(2)}) collective-permute-start(bf16[512,2048]{1,0:T(8,128)(2,1)} %collective-permute-done.2), channel_id=1, source_target_pairs={{2,3},{6,7},{10,11},{14,15},{18,19},{22,23},{26,27},{30,31}} | collective-permute-start | bytes 6291464 | tf_op jit(solution)/shard_map/ppermute | solution.py:32
  396.5 93.4 %collective-permute-start.31 = (bf16[512,640]{1,0:T(8,128)(2,1)}, bf16[512,640]{1,0:T(8,128)(2,1)S(1)}, u32[]{:S(2)}, u32[]{:S(2)}) collective-permute-start(bf16[512,640]{1,0:T(8,128)(2,1)} %get-tuple-element.237), channel_id=1, source_target_pairs={{0,3},{4,7},{8,11},{12,15},{16,19},{20,23},{24,27},{28,31}} | collective-permute-start | bytes 1966088 | tf_op jit(solution)/shard_map/ppermute | solution.py:77
  404.3 93.7 %collective-permute-start.32 = (bf16[512,640]{1,0:T(8,128)(2,1)}, bf16[512,640]{1,0:T(8,128)(2,1)}, u32[]{:S(2)}, u32[]{:S(2)}) collective-permute-start(bf16[512,640]{1,0:T(8,128)(2,1)} %get-tuple-element.237), channel_id=1, source_target_pairs={{2,0},{3,1},{6,4},{7,5},{10,8},{11,9},{14,12},{15,13},{18,16},{19,... | collective-permute-start | bytes 1966088 | tf_op jit(solution)/shard_map/ppermute | solution.py:78
  405.6 105.5 %collective-permute-start.33 = (bf16[512,640]{1,0:T(8,128)(2,1)}, bf16[512,640]{1,0:T(8,128)(2,1)}, u32[]{:S(2)}, u32[]{:S(2)}) collective-permute-start(bf16[512,640]{1,0:T(8,128)(2,1)} %get-tuple-element.237), channel_id=1, source_target_pairs={{0,2},{1,3},{4,6},{5,7},{8,10},{9,11},{12,14},{13,15},{16,18},{17,... | collective-permute-start | bytes 1966088 | tf_op jit(solution)/shard_map/ppermute | solution.py:77
  413.7 1290.0 %reduce-scatter.9.cloned.1.call-start = ((), (), s32[]{:S(2)}) async-start(), calls=%async_computation.14 | async-start | bytes 1179648 | tf_op jit(solution)/shard_map/reduce_scatter | solution.py:432
  413.8 100.7 %collective-permute-start.34 = (bf16[512,640]{1,0:T(8,128)(2,1)}, bf16[512,640]{1,0:T(8,128)(2,1)}, u32[]{:S(2)}, u32[]{:S(2)}) collective-permute-start(bf16[512,640]{1,0:T(8,128)(2,1)} %get-tuple-element.237), channel_id=1, source_target_pairs={{3,0},{7,4},{11,8},{15,12},{19,16},{23,20},{27,24},{31,28}} | collective-permute-start | bytes 1966088 | tf_op jit(solution)/shard_map/ppermute | solution.py:78
  420.0 99.8 %collective-permute-start.35 = (bf16[512,640]{1,0:T(8,128)(2,1)}, bf16[512,640]{1,0:T(8,128)(2,1)}, u32[]{:S(2)}, u32[]{:S(2)}) collective-permute-start(bf16[512,640]{1,0:T(8,128)(2,1)} %get-tuple-element.237), channel_id=1, source_target_pairs={{0,1},{1,2},{2,3},{4,5},{5,6},{6,7},{8,9},{9,10},{10,11},{12,13},{... | collective-permute-start | bytes 1966088 | tf_op jit(solution)/shard_map/ppermute | solution.py:77
  514.5 126.8 %collective-permute-start.25 = (bf16[512,1408]{1,0:T(8,128)(2,1)}, bf16[512,1408]{1,0:T(8,128)(2,1)S(1)}, u32[]{:S(2)}, u32[]{:S(2)}) collective-permute-start(bf16[512,1408]{1,0:T(8,128)(2,1)} %get-tuple-element.235), channel_id=1, source_target_pairs={{0,3},{4,7},{8,11},{12,15},{16,19},{20,23},{24,27},{28,31}} | collective-permute-start | bytes 4325384 | tf_op jit(solution)/shard_map/ppermute | solution.py:77
  519.8 147.4 %collective-permute-start.26 = (bf16[512,1408]{1,0:T(8,128)(2,1)}, bf16[512,1408]{1,0:T(8,128)(2,1)S(1)}, u32[]{:S(2)}, u32[]{:S(2)}) collective-permute-start(bf16[512,1408]{1,0:T(8,128)(2,1)} %get-tuple-element.235), channel_id=1, source_target_pairs={{2,0},{3,1},{6,4},{7,5},{10,8},{11,9},{14,12},{15,13},{18,16},{19,... | collective-permute-start | bytes 4325384 | tf_op jit(solution)/shard_map/ppermute | solution.py:78
  529.3 139.1 %collective-permute-start.27 = (bf16[512,1408]{1,0:T(8,128)(2,1)S(1)}, bf16[512,1408]{1,0:T(8,128)(2,1)S(1)}, u32[]{:S(2)}, u32[]{:S(2)}) collective-permute-start(bf16[512,1408]{1,0:T(8,128)(2,1)S(1)} %copy-done.86), channel_id=1, source_target_pairs={{0,2},{1,3},{4,6},{5,7},{8,10},{9,11},{12,14},{13,15},{16,18},{17,... | collective-permute-start | bytes 4325384 | tf_op jit(solution)/shard_map/ppermute | solution.py:77
  548.7 121.3 %collective-permute-start.28 = (bf16[512,1408]{1,0:T(8,128)(2,1)S(1)}, bf16[512,1408]{1,0:T(8,128)(2,1)S(1)}, u32[]{:S(2)}, u32[]{:S(2)}) collective-permute-start(bf16[512,1408]{1,0:T(8,128)(2,1)S(1)} %copy-done.86), channel_id=1, source_target_pairs={{3,0},{7,4},{11,8},{15,12},{19,16},{23,20},{27,24},{31,28}} | collective-permute-start | bytes 4325384 | tf_op jit(solution)/shard_map/ppermute | solution.py:78
  573.8 96.1 %collective-permute-start.29 = (bf16[512,1408]{1,0:T(8,128)(2,1)S(1)}, bf16[512,1408]{1,0:T(8,128)(2,1)S(1)}, u32[]{:S(2)}, u32[]{:S(2)}) collective-permute-start(bf16[512,1408]{1,0:T(8,128)(2,1)S(1)} %copy-done.86), channel_id=1, source_target_pairs={{0,1},{1,2},{2,3},{4,5},{5,6},{6,7},{8,9},{9,10},{10,11},{12,13},{... | collective-permute-start | bytes 4325384 | tf_op jit(solution)/shard_map/ppermute | solution.py:77
  1029.6 71.3 %collective-permute-start.41 = (bf16[512,2048]{1,0:T(8,128)(2,1)S(1)}, bf16[512,2048]{1,0:T(8,128)(2,1)S(1)}, u32[]{:S(2)}, u32[]{:S(2)}) collective-permute-start(bf16[512,2048]{1,0:T(8,128)(2,1)S(1)} %add_convert_fusion.4), channel_id=1, source_target_pairs={{1,0},{2,1},{3,2},{5,4},{6,5},{7,6},{9,8},{10,9},{11,10},{13,12},{... | collective-permute-start | bytes 6291464 | tf_op jit(solution)/shard_map/ppermute | solution.py:63
  1412.8 292.6 %reduce-scatter.11.cloned.1.call-start = ((), (), s32[]{:S(2)}) async-start(), calls=%async_computation.15 | async-start | bytes 1179648 | tf_op jit(solution)/shard_map/reduce_scatter | solution.py:438
  1413.5 293.5 %reduce-scatter.7.cloned.1.call-start = ((), (), s32[]{:S(2)}) async-start(), calls=%async_computation.13 | async-start | bytes 2359296 | tf_op jit(solution)/shard_map/reduce_scatter | solution.py:429
  1416.7 292.1 %reduce-scatter.13.cloned.1.call-start = ((), (), s32[]{:S(2)}) async-start(), calls=%async_computation.16 | async-start | bytes 2359296 | tf_op jit(solution)/shard_map/reduce_scatter | solution.py:386
  1417.5 341.9 %reduce-scatter.17.cloned.1.call-start = ((), (), s32[]{:S(2)}) async-start(), calls=%async_computation.18 | async-start | bytes 7077888 | tf_op jit(solution)/shard_map/reduce_scatter | solution.py:391
  1418.0 343.8 %reduce-scatter.15.cloned.1.call-start = ((), (), s32[]{:S(2)}) async-start(), calls=%async_computation.17 | async-start | bytes 14155776 | tf_op jit(solution)/shard_map/reduce_scatter | solution.py:382
  1546.0 73.7 %collective-permute-start.50 = (bf16[512,2048]{1,0:T(8,128)(2,1)S(1)}, bf16[512,2048]{1,0:T(8,128)(2,1)}, u32[]{:S(2)}, u32[]{:S(2)}) collective-permute-start(bf16[512,2048]{1,0:T(8,128)(2,1)S(1)} %copy-done.73), channel_id=1, source_target_pairs={{0,1},{1,2},{2,3},{4,5},{5,6},{6,7},{8,9},{9,10},{10,11},{12,13},{... | collective-permute-start | bytes 6291464 | tf_op jit(solution)/shard_map/ppermute | solution.py:62
  1556.7 88.6 %collective-permute-start.53 = (bf16[512,2048]{1,0:T(8,128)(2,1)S(1)}, bf16[512,2048]{1,0:T(8,128)(2,1)}, u32[]{:S(2)}, u32[]{:S(2)}) collective-permute-start(bf16[512,2048]{1,0:T(8,128)(2,1)S(1)} %add_convert_fusion), channel_id=1, source_target_pairs={{1,0},{2,1},{3,2},{5,4},{6,5},{7,6},{9,8},{10,9},{11,10},{13,12},{... | collective-permute-start | bytes 6291464 | tf_op jit(solution)/shard_map/ppermute | solution.py:63
  1558.0 183.6 %collective-permute-start.22 = (bf16[512,2048]{1,0:T(8,128)(2,1)}, bf16[512,2048]{1,0:T(8,128)(2,1)}, u32[]{:S(2)}, u32[]{:S(2)}) collective-permute-start(bf16[512,2048]{1,0:T(8,128)(2,1)} %get-tuple-element.212), channel_id=1, source_target_pairs={{0,3},{4,7},{8,11},{12,15},{16,19},{20,23},{24,27},{28,31}} | collective-permute-start | bytes 6291464 | tf_op jit(solution)/shard_map/ppermute | solution.py:99
  1610.3 133.5 %collective-permute-start.21 = (bf16[512,2048]{1,0:T(8,128)(2,1)}, bf16[512,2048]{1,0:T(8,128)(2,1)}, u32[]{:S(2)}, u32[]{:S(2)}) collective-permute-start(bf16[512,2048]{1,0:T(8,128)(2,1)} %get-tuple-element.213), channel_id=1, source_target_pairs={{2,0},{3,1},{6,4},{7,5},{10,8},{11,9},{14,12},{15,13},{18,16},{19,... | collective-permute-start | bytes 6291464 | tf_op jit(solution)/shard_map/ppermute | solution.py:104
  1611.6 132.2 %collective-permute-start.20 = (bf16[512,2048]{1,0:T(8,128)(2,1)}, bf16[512,2048]{1,0:T(8,128)(2,1)}, u32[]{:S(2)}, u32[]{:S(2)}) collective-permute-start(bf16[512,2048]{1,0:T(8,128)(2,1)} %get-tuple-element.214), channel_id=1, source_target_pairs={{0,2},{1,3},{4,6},{5,7},{8,10},{9,11},{12,14},{13,15},{16,18},{17,... | collective-permute-start | bytes 6291464 | tf_op jit(solution)/shard_map/ppermute | solution.py:99
  1619.7 124.1 %collective-permute-start.19 = (bf16[512,2048]{1,0:T(8,128)(2,1)}, bf16[512,2048]{1,0:T(8,128)(2,1)}, u32[]{:S(2)}, u32[]{:S(2)}) collective-permute-start(bf16[512,2048]{1,0:T(8,128)(2,1)} %get-tuple-element.215), channel_id=1, source_target_pairs={{1,0},{2,1},{3,2},{5,4},{6,5},{7,6},{9,8},{10,9},{11,10},{13,12},{... | collective-permute-start | bytes 6291464 | tf_op jit(solution)/shard_map/ppermute | solution.py:104
  1645.3 98.5 %collective-permute-start.18 = (bf16[512,2048]{1,0:T(8,128)(2,1)}, bf16[512,2048]{1,0:T(8,128)(2,1)}, u32[]{:S(2)}, u32[]{:S(2)}) collective-permute-start(bf16[512,2048]{1,0:T(8,128)(2,1)} %get-tuple-element.210), channel_id=1, source_target_pairs={{0,1},{1,2},{2,3},{4,5},{5,6},{6,7},{8,9},{9,10},{10,11},{12,13},{... | collective-permute-start | bytes 6291464 | tf_op jit(solution)/shard_map/ppermute | solution.py:99
  (190 other events, 4919.1 us)
Sparse Core Ops, SparseCore 0:
  10.5 30.5 all-gather.9
  42.9 23.3 all-gather.11
  68.2 23.3 all-gather.13
  93.9 28.0 all-gather.15
  123.8 45.4 all-gather.17
  171.0 45.3 all-gather.19
  413.9 44.0 all-gather.21
  1412.9 32.9 reduce-scatter.8
  1449.7 35.9 reduce-scatter.10
  1488.8 41.1 reduce-scatter.6
  1533.3 41.1 reduce-scatter.12
  1577.7 61.5 reduce-scatter.16
  1642.8 94.0 reduce-scatter.14

commit v6 on v5

--- a/solution.py
+++ b/solution.py
@@ -19,11 +19,23 @@
 CONTRACT_COLS = (((1,), (1,)), ((), ()))
 
 
+def place_blocks(rows, ups, downs, j, n):
+    blocks = []
+    for k in range(n):
+        block = rows
+        for s in range(1, n):
+            if k + s <= n - 1:
+                block = jnp.where(j == k + s, ups[s], block)
+            if k - s >= 0:
+                block = jnp.where(j == k - s, downs[s], block)
+        blocks.append(block)
+    return jnp.concatenate(blocks, axis=0)
+
+
 def tensor_gather(rows, n):
     if n == 1:
         return rows
     j = lax.axis_index("tensor")
-    count = rows.shape[0]
     up = rows
     down = rows
     ups = {}
@@ -33,13 +45,7 @@
         down = lax.ppermute(down, "tensor", [(i, i - 1) for i in range(1, n - s + 1)])
         ups[s] = up
         downs[s] = down
-    rel = [rows]
-    for m in range(1, n):
-        rel.append(jnp.where(j + m <= n - 1, downs[m], ups[n - m]))
-    rel = jnp.concatenate(rel, axis=0)
-    twice = jnp.concatenate([rel, rel], axis=0)
-    start = ((n - j) % n) * count
-    return lax.dynamic_slice_in_dim(twice, start, n * count, 0)
+    return place_blocks(rows, ups, downs, j, n)
 
 
 def tensor_scatter(partial, n):
@@ -70,19 +76,12 @@
     if n == 1:
         return rows
     j = lax.axis_index("tensor")
-    count = rows.shape[0]
     ups = {}
     downs = {}
     for d in range(1, n):
         ups[d] = lax.ppermute(rows, "tensor", [(i, i + d) for i in range(n - d)])
         downs[d] = lax.ppermute(rows, "tensor", [(i, i - d) for i in range(d, n)])
-    rel = [rows]
-    for m in range(1, n):
-        rel.append(jnp.where(j + m <= n - 1, downs[m], ups[n - m]))
-    rel = jnp.concatenate(rel, axis=0)
-    twice = jnp.concatenate([rel, rel], axis=0)
-    start = ((n - j) % n) * count
-    return lax.dynamic_slice_in_dim(twice, start, n * count, 0)
+    return place_blocks(rows, ups, downs, j, n)
 
 
 def tensor_scatter_direct(partial, n):

time: 1810 us -> 1860 us (1.028)
  waiting for transfers between devices: 604 us -> 789 us
  starting transfers between devices: 383 us -> 282 us
  other arithmetic: 270 us -> 235 us
  local copies, waits for them, and re-layouts: 127 us -> 103 us
  matrix products: 314 us -> 333 us
    ppermute x6, starting transfers between devices: 163 us -> 63.3 us  [tensor_gather_direct(): ups[d] = lax.ppermute(rows, 'tensor', [(i, i + d) for i in range(n - d)])]
    unnamed x31 -> x3, other arithmetic: 83.9 us -> 0.01 us
    ppermute x6, waiting for transfers between devices: 0.02 us -> 75.7 us  [tensor_gather_direct(): ups[d] = lax.ppermute(rows, 'tensor', [(i, i + d) for i in range(n - d)])]
    ppermute x6, waiting for transfers between devices: 42 us -> 112 us  [tensor_gather_direct(): downs[d] = lax.ppermute(rows, 'tensor', [(i, i - d) for i in range(d, n)])]
    ppermute x9, waiting for transfers between devices: 240 us -> 281 us  [tensor_scatter(): lax.ppermute(acc_up.astype(jnp.bfloat16), 'tensor', [(i, i + 1) for i in...]
    ppermute x9, waiting for transfers between devices: 167 us -> 135 us  [tensor_gather(): lax.ppermute(down, 'tensor', [(i, i - 1) for i in range(1, n - s + 1)])]
    concatenate x1, other arithmetic: 7.13 us -> 33.9 us  [on_device_body(): grad_whole = jnp.concatenate([grad_half_a, grad_half_b], axis=1)]
    ppermute x9, waiting for transfers between devices: 81.8 us -> 107 us  [tensor_scatter(): lax.ppermute(acc_down.astype(jnp.bfloat16), 'tensor', [(i, i - 1) for i i...]
  transfers between devices with their start and end apart: 67 -> 67, of which waited for: 25 -> 25; matrix products, arithmetic and copies ran while one was open for 24% -> 22% of each run, Pallas kernels for 0% -> 0%
where the time goes in v6:
time: 1860 us; the launch traced here: 1830 us
  waiting for transfers between devices  789 us (42%)
  matrix products  333 us (18%)
  starting transfers between devices  282 us (15%)
  other arithmetic  235 us (13%)
  local copies, waits for them, and re-layouts  103 us (6%)
  blocking collectives  64.1 us (3%)
  between operations  19.1 us (1%)
    ppermute x9, waiting for transfers between devices, tensor_scatter(): lax.ppermute(acc_up.astype(jnp.bfloat16), 'tensor', [(i, i + 1) for i in...  281 us
    ppermute x9, waiting for transfers between devices, tensor_gather(): lax.ppermute(down, 'tensor', [(i, i - 1) for i in range(1, n - s + 1)])  135 us
    ppermute x3, starting transfers between devices, tensor_scatter_direct(): lax.ppermute(block(jnp.minimum(j + d, n - 1)).astype(jnp.bfloat16), 'tens...  113 us
    ppermute x6, waiting for transfers between devices, tensor_gather_direct(): downs[d] = lax.ppermute(rows, 'tensor', [(i, i - d) for i in range(d, n)])  112 us
    ppermute x9, waiting for transfers between devices, tensor_scatter(): lax.ppermute(acc_down.astype(jnp.bfloat16), 'tensor', [(i, i - 1) for i i...  107 us
    ppermute x6, waiting for transfers between devices, tensor_gather_direct(): ups[d] = lax.ppermute(rows, 'tensor', [(i, i + d) for i in range(n - d)])  75.7 us
    ppermute x9, waiting for transfers between devices, tensor_gather(): up = lax.ppermute(up, 'tensor', [(i, i + 1) for i in range(s - 1, n - 1)])  74.9 us
    ppermute x6, starting transfers between devices, tensor_gather_direct(): ups[d] = lax.ppermute(rows, 'tensor', [(i, i + d) for i in range(n - d)])  63.3 us
  transfers between devices with their start and end apart: 67, of which 25 were waited for; matrix products, arithmetic and copies ran while one was open for 22% of the time, Pallas kernels for 0%

profile of v6, /device:TPU:0, one launch (start us, length us, event | category | flops | bytes accessed | tf_op | source)
XLA Modules:
  0.0 1825.3 jit_solution(11174454951912159771)
XLA Ops:
  36.4 41.6 %collective-permute-done = bf16[512,2048]{1,0:T(8,128)(2,1)} collective-permute-done((bf16[512,2048]{1,0:T(8,128)(2,1)}, bf16[512,2048]{1,0:T(8,128)(2,1)}, u32[]{:S(2)}, u32[]{:S(2)}) %collective-permute-start) | collective-permute-done | bytes 2097184 | tf_op jit(solution)/shard_map/ppermute | solution.py:44
  92.2 40.4 %collective-permute-done.4 = bf16[512,2048]{1,0:T(8,128)(2,1)} collective-permute-done((bf16[512,2048]{1,0:T(8,128)(2,1)}, bf16[512,2048]{1,0:T(8,128)(2,1)}, u32[]{:S(2)}, u32[]{:S(2)}) %collective-permute-start.4) | collective-permute-done | bytes 2097184 | tf_op jit(solution)/shard_map/ppermute | solution.py:45
  187.6 16.5 fusion.175
  292.8 39.8 %collective-permute-done.6 = bf16[512,2048]{1,0:T(8,128)(2,1)} collective-permute-done((bf16[512,2048]{1,0:T(8,128)(2,1)}, bf16[512,2048]{1,0:T(8,128)(2,1)}, u32[]{:S(2)}, u32[]{:S(2)}) %collective-permute-start.6) | collective-permute-done | bytes 2097184 | tf_op jit(solution)/shard_map/ppermute | solution.py:68
  344.2 40.1 %collective-permute-done.7 = bf16[512,2048]{1,0:T(8,128)(2,1)} collective-permute-done((bf16[512,2048]{1,0:T(8,128)(2,1)}, bf16[512,2048]{1,0:T(8,128)(2,1)}, u32[]{:S(2)}, u32[]{:S(2)}) %collective-permute-start.7) | collective-permute-done | bytes 2097184 | tf_op jit(solution)/shard_map/ppermute | solution.py:68
  407.9 46.8 %collective-permute-start.30 = (bf16[512,640]{1,0:T(8,128)(2,1)}, bf16[512,640]{1,0:T(8,128)(2,1)S(1)}, u32[]{:S(2)}, u32[]{:S(2)}) collective-permute-start(bf16[512,640]{1,0:T(8,128)(2,1)} %slice.380), channel_id=1, source_target_pairs={{0,3},{4,7},{8,11},{12,15},{16,19},{20,23},{24,27},{28,31}} | collective-permute-start | bytes 1966088 | tf_op jit(solution)/shard_map/ppermute | solution.py:82
  469.6 25.2 %collective-permute-done.11 = bf16[512,2048]{1,0:T(8,128)(2,1)} collective-permute-done((bf16[512,2048]{1,0:T(8,128)(2,1)}, bf16[512,2048]{1,0:T(8,128)(2,1)}, u32[]{:S(2)}, u32[]{:S(2)}) %collective-permute-start.11) | collective-permute-done | bytes 2097184 | tf_op jit(solution)/shard_map/ppermute | solution.py:69
  517.5 34.9 %collective-permute-done.34 = bf16[512,640]{1,0:T(8,128)(2,1)S(1)} collective-permute-done((bf16[512,640]{1,0:T(8,128)(2,1)}, bf16[512,640]{1,0:T(8,128)(2,1)S(1)}, u32[]{:S(2)}, u32[]{:S(2)}) %collective-permute-start.34) | collective-permute-done | bytes 655392 | tf_op jit(solution)/shard_map/ppermute | solution.py:83
  555.8 27.4 %collective-permute-done.24 = bf16[512,1408]{1,0:T(8,128)(2,1)S(1)} collective-permute-done((bf16[512,1408]{1,0:T(8,128)(2,1)S(1)}, bf16[512,1408]{1,0:T(8,128)(2,1)S(1)}, u32[]{:S(2)}, u32[]{:S(2)}) %collective-permute-start.24) | collective-permute-done | bytes 1441824 | tf_op jit(solution)/shard_map/ppermute | solution.py:82
  584.5 29.6 %collective-permute-done.25 = bf16[512,1408]{1,0:T(8,128)(2,1)S(1)} collective-permute-done((bf16[512,1408]{1,0:T(8,128)(2,1)S(1)}, bf16[512,1408]{1,0:T(8,128)(2,1)S(1)}, u32[]{:S(2)}, u32[]{:S(2)}) %collective-permute-start.25) | collective-permute-done | bytes 1441824 | tf_op jit(solution)/shard_map/ppermute | solution.py:82
  615.4 18.7 %collective-permute-done.26 = bf16[512,1408]{1,0:T(8,128)(2,1)S(1)} collective-permute-done((bf16[512,1408]{1,0:T(8,128)(2,1)S(1)}, bf16[512,1408]{1,0:T(8,128)(2,1)S(1)}, u32[]{:S(2)}, u32[]{:S(2)}) %collective-permute-start.26) | collective-permute-done | bytes 1441824 | tf_op jit(solution)/shard_map/ppermute | solution.py:82
  642.3 77.3 %collective-permute-done.28 = bf16[512,1408]{1,0:T(8,128)(2,1)} collective-permute-done((bf16[512,1408]{1,0:T(8,128)(2,1)S(1)}, bf16[512,1408]{1,0:T(8,128)(2,1)}, u32[]{:S(2)}, u32[]{:S(2)}) %collective-permute-start.28) | collective-permute-done | bytes 1441824 | tf_op jit(solution)/shard_map/ppermute | solution.py:83
  723.2 37.2 %collective-permute-done.16 = bf16[512,2048]{1,0:T(8,128)(2,1)} collective-permute-done((bf16[512,2048]{1,0:T(8,128)(2,1)}, bf16[512,2048]{1,0:T(8,128)(2,1)}, u32[]{:S(2)}, u32[]{:S(2)}) %collective-permute-start.16) | collective-permute-done | bytes 2097184 | tf_op jit(solution)/shard_map/ppermute | solution.py:45
  761.8 33.9 %maximum_maximum_fusion = bf16[2048,2048]{1,0:T(8,128)(2,1)} fusion(bf16[512,640]{1,0:T(8,128)(2,1)S(1)} %get-tuple-element.245, bf16[512,640]{1,0:T(8,128)(2,1)S(1)} %get-tuple-element.244, bf16[512,640]{1,0:T(8,128)(2,1)S(1)} %get-tuple-element.243, bf16[512,640]{1,0:T(8,128)(2,1)S(1)} %get-tuple-element.242, bf16[512,1408]{1,0:T(8,128)(2,1)S(1)} %get-tuple-element.233, ...), kind=kLoop, calls=%fused_computation.38 | loop fusion | flops 67108864 | bytes 16777216 | tf_op jit(solution)/shard_map/concatenate | solution.py:337
  819.3 33.2 %fusion.170 = f32[2048,3072]{1,0:T(8,128)} fusion(bf16[2048,3072]{1,0:T(8,128)(2,1)} %constant_dynamic-update-slice_fusion.3, bf16[512,2048]{1,0:T(8,128)(2,1)S(1)} %get-tuple-element.221, bf16[512,2048]{1,0:T(8,128)(2,1)S(1)} %get-tuple-element.220, bf16[512,2048]{1,0:T(8,128)(2,1)S(1)} %get-tuple-element.219, bf16[512,2048]{1,0:T(8,128)(2,1)S(1)} %get-tuple-element.218), kind=kOutput, calls=%fused_computation.322 | convolution fusion | flops 25803358208 | bytes 46137344 | tf_op jit(solution)/shard_map/dot_general | solution.py:324
  852.4 37.8 %fusion.9 = (bf16[2048,1536]{1,0:T(8,128)(2,1)}, bf16[2048,1536]{1,0:T(8,128)(2,1)}, bf16[2048,1536]{1,0:T(8,128)(2,1)}) fusion(f32[2048,3072]{1,0:T(8,128)} %fusion.170, bf16[1536,2048]{1,0:T(8,128)(2,1)} %all-gather.22.cloned.1.call-done, bf16[512,640]{1,0:T(8,128)(2,1)} %copy-done.70, bf16[512,640]{1,0:T(8,128)(2,1)} %copy-done.69, ...), kind=kOutput, calls=%fused_computation.16 | convolution fusion | flops 13002342400 | bytes 58720256 | tf_op jit(solution)/shard_map/dot_general | solution.py:338
  890.2 34.3 %fusion.169 = f32[2048,2048]{1,0:T(8,128)} fusion(bf16[2048,3072]{1,0:T(8,128)(2,1)} %constant_dynamic-update-slice_fusion.3, bf16[2048,1536]{1,0:T(8,128)(2,1)} %get-tuple-element.194, bf16[2048,1536]{1,0:T(8,128)(2,1)} %get-tuple-element.193), kind=kOutput, calls=%fused_computation.321 | convolution fusion | flops 25794969600 | bytes 41943040 | tf_op jit(solution)/shard_map/dot_general | solution.py:347
  944.2 43.8 %collective-permute-done.36 = bf16[512,2048]{1,0:T(8,128)(2,1)S(1)} collective-permute-done((bf16[512,2048]{1,0:T(8,128)(2,1)S(1)}, bf16[512,2048]{1,0:T(8,128)(2,1)S(1)}, u32[]{:S(2)}, u32[]{:S(2)}) %collective-permute-start.36) | collective-permute-done | bytes 2097184 | tf_op jit(solution)/shard_map/ppermute | solution.py:68
  994.6 42.6 %collective-permute-done.37 = bf16[512,2048]{1,0:T(8,128)(2,1)} collective-permute-done((bf16[512,2048]{1,0:T(8,128)(2,1)S(1)}, bf16[512,2048]{1,0:T(8,128)(2,1)}, u32[]{:S(2)}, u32[]{:S(2)}) %collective-permute-start.37) | collective-permute-done | bytes 2097184 | tf_op jit(solution)/shard_map/ppermute | solution.py:68
  1051.0 41.0 %collective-permute-done.38 = bf16[512,2048]{1,0:T(8,128)(2,1)S(1)} collective-permute-done((bf16[512,2048]{1,0:T(8,128)(2,1)}, bf16[512,2048]{1,0:T(8,128)(2,1)S(1)}, u32[]{:S(2)}, u32[]{:S(2)}) %collective-permute-start.38) | collective-permute-done | bytes 2097184 | tf_op jit(solution)/shard_map/ppermute | solution.py:68
  1092.0 46.6 %collective-permute-done.41 = bf16[512,2048]{1,0:T(8,128)(2,1)S(1)} collective-permute-done((bf16[512,2048]{1,0:T(8,128)(2,1)S(1)}, bf16[512,2048]{1,0:T(8,128)(2,1)S(1)}, u32[]{:S(2)}, u32[]{:S(2)}) %collective-permute-start.41) | collective-permute-done | bytes 2097184 | tf_op jit(solution)/shard_map/ppermute | solution.py:69
  1158.0 33.3 %collective-permute-done.42 = bf16[512,2048]{1,0:T(8,128)(2,1)} collective-permute-done((bf16[512,2048]{1,0:T(8,128)(2,1)S(1)}, bf16[512,2048]{1,0:T(8,128)(2,1)}, u32[]{:S(2)}, u32[]{:S(2)}) %collective-permute-start.42) | collective-permute-done | bytes 2097184 | tf_op jit(solution)/shard_map/ppermute | solution.py:44
  1198.2 33.0 %fusion.178 = bf16[2048,3072]{1,0:T(8,128)(2,1)} fusion(bf16[2048,2048]{1,0:T(8,128)(2,1)} %pad_maximum_fusion.2, bf16[2048,3072]{1,0:T(8,128)(2,1)} %pad_maximum_fusion), kind=kOutput, calls=%fused_computation.330 | convolution fusion | flops 25769803776 | bytes 33554432 | tf_op jit(solution)/shard_map/dot_general | solution.py:352
  1244.0 19.3 %fusion.179 = bf16[1536,2048]{1,0:T(8,128)(2,1)} fusion(bf16[2048,1536]{1,0:T(8,128)(2,1)} %get-tuple-element.195, bf16[2048,2048]{1,0:T(8,128)(2,1)} %maximum_maximum_fusion), kind=kOutput, calls=%fused_computation.331 | convolution fusion | flops 12884901888 | bytes 20971520 | tf_op jit(solution)/shard_map/dot_general | solution.py:351
  1263.3 23.5 %collective-permute-done.47 = bf16[512,2048]{1,0:T(8,128)(2,1)} collective-permute-done((bf16[512,2048]{1,0:T(8,128)(2,1)}, bf16[512,2048]{1,0:T(8,128)(2,1)}, u32[]{:S(2)}, u32[]{:S(2)}) %collective-permute-start.47) | collective-permute-done | bytes 2097184 | tf_op jit(solution)/shard_map/ppermute | solution.py:45
  1466.5 37.8 %collective-permute-done.48 = bf16[512,2048]{1,0:T(8,128)(2,1)S(1)} collective-permute-done((bf16[512,2048]{1,0:T(8,128)(2,1)S(1)}, bf16[512,2048]{1,0:T(8,128)(2,1)S(1)}, u32[]{:S(2)}, u32[]{:S(2)}) %collective-permute-start.48) | collective-permute-done | bytes 2097184 | tf_op jit(solution)/shard_map/ppermute | solution.py:68
  1511.0 36.3 %collective-permute-done.49 = bf16[512,2048]{1,0:T(8,128)(2,1)} collective-permute-done((bf16[512,2048]{1,0:T(8,128)(2,1)S(1)}, bf16[512,2048]{1,0:T(8,128)(2,1)}, u32[]{:S(2)}, u32[]{:S(2)}) %collective-permute-start.49) | collective-permute-done | bytes 2097184 | tf_op jit(solution)/shard_map/ppermute | solution.py:68
  1554.2 19.4 %fusion.177 = f32[2048,2048]{1,0:T(8,128)} fusion(bf16[2048,1536]{1,0:T(8,128)(2,1)} %get-tuple-element.195, bf16[1536,2048]{1,0:T(8,128)(2,1)} %all-gather.22.cloned.1.call-done), kind=kOutput, calls=%fused_computation.329 | convolution fusion | flops 12884901888 | bytes 29360128 | tf_op jit(solution)/shard_map/dot_general | solution.py:328
  1599.0 58.6 %collective-permute-start.22 = (bf16[512,2048]{1,0:T(8,128)(2,1)}, bf16[512,2048]{1,0:T(8,128)(2,1)}, u32[]{:S(2)}, u32[]{:S(2)}) collective-permute-start(bf16[512,2048]{1,0:T(8,128)(2,1)} %get-tuple-element.206), channel_id=1, source_target_pairs={{0,3},{4,7},{8,11},{12,15},{16,19},{20,23},{24,27},{28,31}} | collective-permute-start | bytes 6291464 | tf_op jit(solution)/shard_map/ppermute | solution.py:98
  1668.6 35.1 %collective-permute-done.53 = bf16[512,2048]{1,0:T(8,128)(2,1)} collective-permute-done((bf16[512,2048]{1,0:T(8,128)(2,1)S(1)}, bf16[512,2048]{1,0:T(8,128)(2,1)}, u32[]{:S(2)}, u32[]{:S(2)}) %collective-permute-start.53) | collective-permute-done | bytes 2097184 | tf_op jit(solution)/shard_map/ppermute | solution.py:69
  1703.7 45.8 %collective-permute-start.18 = (bf16[512,2048]{1,0:T(8,128)(2,1)}, bf16[512,2048]{1,0:T(8,128)(2,1)}, u32[]{:S(2)}, u32[]{:S(2)}) collective-permute-start(bf16[512,2048]{1,0:T(8,128)(2,1)} %get-tuple-element.204), channel_id=1, source_target_pairs={{0,1},{1,2},{2,3},{4,5},{5,6},{6,7},{8,9},{9,10},{10,11},{12,13},{... | collective-permute-start | bytes 6291464 | tf_op jit(solution)/shard_map/ppermute | solution.py:98
  1778.0 19.0 %all-reduce.12 = (f32[256]{0:T(256)}, f32[16]{0:T(128)}, f32[16]{0:T(128)}, f32[256]{0:T(256)}) all-reduce(f32[256]{0:T(256)S(1)} %dynamic-slice_convert_fusion.15, f32[16]{0:T(128)S(1)} %dynamic-slice_convert_fusion.14, f32[16]{0:T(128)S(1)} %dynamic-slice_convert_fusion.13, ...), channel_id=1, replica_groups=mesh['dp'=8,'tensor'=4] {'tensor'}, use_global_device_ids=true, to_apply=%region_24.25 | all-reduce | flops 544 | bytes 4352 | tf_op jit(solution)/shard_map/psum | solution.py:465
  (637 shorter events, 656.4 us)
Async XLA Ops:
  7.2 150.3 %all-gather.10.cloned.1.call-start = ((), (), s32[]{:S(2)}) async-start(), calls=%async_computation.6 | async-start | bytes 2359296 | tf_op jit(solution)/shard_map/all_gather | solution.py:259
  9.2 151.4 %all-gather.12.cloned.1.call-start = ((), (), s32[]{:S(2)}) async-start(), calls=%async_computation.7 | async-start | bytes 1179648 | tf_op jit(solution)/shard_map/all_gather | solution.py:260
  10.9 152.0 %all-gather.14.cloned.1.call-start = ((), (), s32[]{:S(2)}) async-start(), calls=%async_computation.8 | async-start | bytes 1179648 | tf_op jit(solution)/shard_map/all_gather | solution.py:261
  12.6 260.2 %all-gather.16.cloned.1.call-start = ((), (), s32[]{:S(2)}) async-start(), calls=%async_computation.9 | async-start | bytes 2359296 | tf_op jit(solution)/shard_map/all_gather | solution.py:262
  14.4 781.3 %all-gather.18.cloned.1.call-start = ((), (), s32[]{:S(2)}) async-start(), calls=%async_computation.10 | async-start | bytes 7077888 | tf_op jit(solution)/shard_map/all_gather | solution.py:311
  36.0 765.6 %all-gather.20.cloned.1.call-start = ((), (), s32[]{:S(2)}) async-start(), calls=%async_computation.11 | async-start | bytes 7077888 | tf_op jit(solution)/shard_map/all_gather | solution.py:312
  90.1 75.0 %collective-permute-start.2 = (bf16[512,2048]{1,0:T(8,128)(2,1)}, bf16[512,2048]{1,0:T(8,128)(2,1)}, u32[]{:S(2)}, u32[]{:S(2)}) collective-permute-start(bf16[512,2048]{1,0:T(8,128)(2,1)} %collective-permute-done.1), channel_id=1, source_target_pairs={{2,3},{6,7},{10,11},{14,15},{18,19},{22,23},{26,27},{30,31}} | collective-permute-start | bytes 6291464 | tf_op jit(solution)/shard_map/ppermute | solution.py:44
  344.1 508.3 %all-gather.22.cloned.1.call-start = ((), (), s32[]{:S(2)}) async-start(), calls=%async_computation.12 | async-start | bytes 7077888 | tf_op jit(solution)/shard_map/all_gather | solution.py:313
  404.6 90.2 %collective-permute-start.11 = (bf16[512,2048]{1,0:T(8,128)(2,1)}, bf16[512,2048]{1,0:T(8,128)(2,1)}, u32[]{:S(2)}, u32[]{:S(2)}) collective-permute-start(bf16[512,2048]{1,0:T(8,128)(2,1)} %add_convert_fusion.9), channel_id=1, source_target_pairs={{1,0},{2,1},{3,2},{5,4},{6,5},{7,6},{9,8},{10,9},{11,10},{13,12},{... | collective-permute-start | bytes 6291464 | tf_op jit(solution)/shard_map/ppermute | solution.py:69
  407.9 92.9 %collective-permute-start.30 = (bf16[512,640]{1,0:T(8,128)(2,1)}, bf16[512,640]{1,0:T(8,128)(2,1)S(1)}, u32[]{:S(2)}, u32[]{:S(2)}) collective-permute-start(bf16[512,640]{1,0:T(8,128)(2,1)} %slice.380), channel_id=1, source_target_pairs={{0,3},{4,7},{8,11},{12,15},{16,19},{20,23},{24,27},{28,31}} | collective-permute-start | bytes 1966088 | tf_op jit(solution)/shard_map/ppermute | solution.py:82
  502.8 132.6 %collective-permute-start.12 = (bf16[512,2048]{1,0:T(8,128)(2,1)S(1)}, bf16[512,2048]{1,0:T(8,128)(2,1)}, u32[]{:S(2)}, u32[]{:S(2)}) collective-permute-start(bf16[512,2048]{1,0:T(8,128)(2,1)S(1)} %multiply_convert_fusion.2), channel_id=1, source_target_pairs={{0,1},{1,2},{2,3},{4,5},{5,6},{6,7},{8,9},{9,10},{10,11},{12,13},{... | collective-permute-start | bytes 6291464 | tf_op jit(solution)/shard_map/ppermute | solution.py:44
  507.6 129.8 %collective-permute-start.15 = (bf16[512,2048]{1,0:T(8,128)(2,1)S(1)}, bf16[512,2048]{1,0:T(8,128)(2,1)}, u32[]{:S(2)}, u32[]{:S(2)}) collective-permute-start(bf16[512,2048]{1,0:T(8,128)(2,1)S(1)} %multiply_convert_fusion.2), channel_id=1, source_target_pairs={{1,0},{2,1},{3,2},{5,4},{6,5},{7,6},{9,8},{10,9},{11,10},{13,12},{... | collective-permute-start | bytes 6291464 | tf_op jit(solution)/shard_map/ppermute | solution.py:45
  554.5 79.7 %collective-permute-start.26 = (bf16[512,1408]{1,0:T(8,128)(2,1)S(1)}, bf16[512,1408]{1,0:T(8,128)(2,1)S(1)}, u32[]{:S(2)}, u32[]{:S(2)}) collective-permute-start(bf16[512,1408]{1,0:T(8,128)(2,1)S(1)} %slice.379), channel_id=1, source_target_pairs={{0,1},{1,2},{2,3},{4,5},{5,6},{6,7},{8,9},{9,10},{10,11},{12,13},{... | collective-permute-start | bytes 4325384 | tf_op jit(solution)/shard_map/ppermute | solution.py:82
  614.1 105.6 %collective-permute-start.28 = (bf16[512,1408]{1,0:T(8,128)(2,1)S(1)}, bf16[512,1408]{1,0:T(8,128)(2,1)}, u32[]{:S(2)}, u32[]{:S(2)}) collective-permute-start(bf16[512,1408]{1,0:T(8,128)(2,1)S(1)} %slice.379), channel_id=1, source_target_pairs={{2,0},{3,1},{6,4},{7,5},{10,8},{11,9},{14,12},{15,13},{18,16},{19,... | collective-permute-start | bytes 4325384 | tf_op jit(solution)/shard_map/ppermute | solution.py:83
  634.1 85.6 %collective-permute-start.29 = (bf16[512,1408]{1,0:T(8,128)(2,1)S(1)}, bf16[512,1408]{1,0:T(8,128)(2,1)}, u32[]{:S(2)}, u32[]{:S(2)}) collective-permute-start(bf16[512,1408]{1,0:T(8,128)(2,1)S(1)} %slice.379), channel_id=1, source_target_pairs={{3,0},{7,4},{11,8},{15,12},{19,16},{23,20},{27,24},{31,28}} | collective-permute-start | bytes 4325384 | tf_op jit(solution)/shard_map/ppermute | solution.py:83
  635.4 87.0 %collective-permute-start.13 = (bf16[512,2048]{1,0:T(8,128)(2,1)}, bf16[512,2048]{1,0:T(8,128)(2,1)}, u32[]{:S(2)}, u32[]{:S(2)}) collective-permute-start(bf16[512,2048]{1,0:T(8,128)(2,1)} %collective-permute-done.12), channel_id=1, source_target_pairs={{1,2},{2,3},{5,6},{6,7},{9,10},{10,11},{13,14},{14,15},{17,18},{18... | collective-permute-start | bytes 6291464 | tf_op jit(solution)/shard_map/ppermute | solution.py:44
  637.4 123.1 %collective-permute-start.16 = (bf16[512,2048]{1,0:T(8,128)(2,1)}, bf16[512,2048]{1,0:T(8,128)(2,1)}, u32[]{:S(2)}, u32[]{:S(2)}) collective-permute-start(bf16[512,2048]{1,0:T(8,128)(2,1)} %collective-permute-done.15), channel_id=1, source_target_pairs={{1,0},{2,1},{5,4},{6,5},{9,8},{10,9},{13,12},{14,13},{17,16},{18,1... | collective-permute-start | bytes 6291464 | tf_op jit(solution)/shard_map/ppermute | solution.py:45
  639.7 1111.1 %reduce-scatter.9.cloned.1.call-start = ((), (), s32[]{:S(2)}) async-start(), calls=%async_computation.14 | async-start | bytes 1179648 | tf_op jit(solution)/shard_map/reduce_scatter | solution.py:431
  722.4 85.2 %collective-permute-start.14 = (bf16[512,2048]{1,0:T(8,128)(2,1)}, bf16[512,2048]{1,0:T(8,128)(2,1)S(1)}, u32[]{:S(2)}, u32[]{:S(2)}) collective-permute-start(bf16[512,2048]{1,0:T(8,128)(2,1)} %collective-permute-done.13), channel_id=1, source_target_pairs={{2,3},{6,7},{10,11},{14,15},{18,19},{22,23},{26,27},{30,31}} | collective-permute-start | bytes 6291464 | tf_op jit(solution)/shard_map/ppermute | solution.py:44
  1049.5 89.0 %collective-permute-start.41 = (bf16[512,2048]{1,0:T(8,128)(2,1)S(1)}, bf16[512,2048]{1,0:T(8,128)(2,1)S(1)}, u32[]{:S(2)}, u32[]{:S(2)}) collective-permute-start(bf16[512,2048]{1,0:T(8,128)(2,1)S(1)} %add_convert_fusion.4), channel_id=1, source_target_pairs={{1,0},{2,1},{3,2},{5,4},{6,5},{7,6},{9,8},{10,9},{11,10},{13,12},{... | collective-permute-start | bytes 6291464 | tf_op jit(solution)/shard_map/ppermute | solution.py:69
  1443.2 309.2 %reduce-scatter.11.cloned.1.call-start = ((), (), s32[]{:S(2)}) async-start(), calls=%async_computation.15 | async-start | bytes 1179648 | tf_op jit(solution)/shard_map/reduce_scatter | solution.py:437
  1444.0 310.1 %reduce-scatter.7.cloned.1.call-start = ((), (), s32[]{:S(2)}) async-start(), calls=%async_computation.13 | async-start | bytes 2359296 | tf_op jit(solution)/shard_map/reduce_scatter | solution.py:428
  1447.1 308.8 %reduce-scatter.13.cloned.1.call-start = ((), (), s32[]{:S(2)}) async-start(), calls=%async_computation.16 | async-start | bytes 2359296 | tf_op jit(solution)/shard_map/reduce_scatter | solution.py:385
  1447.8 364.9 %reduce-scatter.17.cloned.1.call-start = ((), (), s32[]{:S(2)}) async-start(), calls=%async_computation.18 | async-start | bytes 7077888 | tf_op jit(solution)/shard_map/reduce_scatter | solution.py:390
  1448.4 366.7 %reduce-scatter.15.cloned.1.call-start = ((), (), s32[]{:S(2)}) async-start(), calls=%async_computation.17 | async-start | bytes 14155776 | tf_op jit(solution)/shard_map/reduce_scatter | solution.py:381
  1587.4 79.9 %collective-permute-start.50 = (bf16[512,2048]{1,0:T(8,128)(2,1)S(1)}, bf16[512,2048]{1,0:T(8,128)(2,1)}, u32[]{:S(2)}, u32[]{:S(2)}) collective-permute-start(bf16[512,2048]{1,0:T(8,128)(2,1)S(1)} %copy-done.73), channel_id=1, source_target_pairs={{0,1},{1,2},{2,3},{4,5},{5,6},{6,7},{8,9},{9,10},{10,11},{12,13},{... | collective-permute-start | bytes 6291464 | tf_op jit(solution)/shard_map/ppermute | solution.py:68
  1597.7 106.0 %collective-permute-start.53 = (bf16[512,2048]{1,0:T(8,128)(2,1)S(1)}, bf16[512,2048]{1,0:T(8,128)(2,1)}, u32[]{:S(2)}, u32[]{:S(2)}) collective-permute-start(bf16[512,2048]{1,0:T(8,128)(2,1)S(1)} %add_convert_fusion), channel_id=1, source_target_pairs={{1,0},{2,1},{3,2},{5,4},{6,5},{7,6},{9,8},{10,9},{11,10},{13,12},{... | collective-permute-start | bytes 6291464 | tf_op jit(solution)/shard_map/ppermute | solution.py:69
  1599.0 198.0 %collective-permute-start.22 = (bf16[512,2048]{1,0:T(8,128)(2,1)}, bf16[512,2048]{1,0:T(8,128)(2,1)}, u32[]{:S(2)}, u32[]{:S(2)}) collective-permute-start(bf16[512,2048]{1,0:T(8,128)(2,1)} %get-tuple-element.206), channel_id=1, source_target_pairs={{0,3},{4,7},{8,11},{12,15},{16,19},{20,23},{24,27},{28,31}} | collective-permute-start | bytes 6291464 | tf_op jit(solution)/shard_map/ppermute | solution.py:98
  1657.7 139.4 %collective-permute-start.21 = (bf16[512,2048]{1,0:T(8,128)(2,1)}, bf16[512,2048]{1,0:T(8,128)(2,1)}, u32[]{:S(2)}, u32[]{:S(2)}) collective-permute-start(bf16[512,2048]{1,0:T(8,128)(2,1)} %get-tuple-element.207), channel_id=1, source_target_pairs={{2,0},{3,1},{6,4},{7,5},{10,8},{11,9},{14,12},{15,13},{18,16},{19,... | collective-permute-start | bytes 6291464 | tf_op jit(solution)/shard_map/ppermute | solution.py:103
  1659.0 138.1 %collective-permute-start.20 = (bf16[512,2048]{1,0:T(8,128)(2,1)}, bf16[512,2048]{1,0:T(8,128)(2,1)}, u32[]{:S(2)}, u32[]{:S(2)}) collective-permute-start(bf16[512,2048]{1,0:T(8,128)(2,1)} %get-tuple-element.208), channel_id=1, source_target_pairs={{0,2},{1,3},{4,6},{5,7},{8,10},{9,11},{12,14},{13,15},{16,18},{17,... | collective-permute-start | bytes 6291464 | tf_op jit(solution)/shard_map/ppermute | solution.py:98
  1667.3 129.8 %collective-permute-start.19 = (bf16[512,2048]{1,0:T(8,128)(2,1)}, bf16[512,2048]{1,0:T(8,128)(2,1)}, u32[]{:S(2)}, u32[]{:S(2)}) collective-permute-start(bf16[512,2048]{1,0:T(8,128)(2,1)} %get-tuple-element.209), channel_id=1, source_target_pairs={{1,0},{2,1},{3,2},{5,4},{6,5},{7,6},{9,8},{10,9},{11,10},{13,12},{... | collective-permute-start | bytes 6291464 | tf_op jit(solution)/shard_map/ppermute | solution.py:103
  1703.7 93.4 %collective-permute-start.18 = (bf16[512,2048]{1,0:T(8,128)(2,1)}, bf16[512,2048]{1,0:T(8,128)(2,1)}, u32[]{:S(2)}, u32[]{:S(2)}) collective-permute-start(bf16[512,2048]{1,0:T(8,128)(2,1)} %get-tuple-element.204), channel_id=1, source_target_pairs={{0,1},{1,2},{2,3},{4,5},{5,6},{6,7},{8,9},{9,10},{10,11},{12,13},{... | collective-permute-start | bytes 6291464 | tf_op jit(solution)/shard_map/ppermute | solution.py:98
  (201 other events, 7153.8 us)
Sparse Core Ops, SparseCore 0:
  10.5 30.4 all-gather.9
  43.5 23.3 all-gather.11
  69.3 23.3 all-gather.13
  95.0 28.0 all-gather.15
  124.9 45.5 all-gather.17
  344.2 42.6 all-gather.19
  639.9 93.4 all-gather.21
  1443.4 33.2 reduce-scatter.8
  1480.4 35.9 reduce-scatter.10
  1519.6 41.0 reduce-scatter.6
  1564.0 41.1 reduce-scatter.12
  1608.4 61.6 reduce-scatter.16
  1673.5 92.6 reduce-scatter.14

commit v7 on v6

--- a/solution.py
+++ b/solution.py
@@ -255,15 +255,21 @@
     cosine_lookup, sine_lookup = rope_tables(SEQUENCE_TOKENS, HEAD_SIZE)
     seq_starts = doc_start.reshape(seq_count, SEQUENCE_TOKENS)
     seq_pieces = piece_ids.reshape(seq_count, SEQUENCE_TOKENS)
+    ga_local = attn_gain.shape[0]
+    gq_local = query_gain.shape[0]
+    gain_rows = lax.all_gather(
+        jnp.concatenate([attn_gain, query_gain, key_gain, mlp_gain]).astype(bf16), "dp", axis=0
+    )
     wq_b, wk_b, wv_b, wo_b, ga_b, gq_b, gk_b = (
         lax.all_gather(w_query.astype(bf16), "dp", axis=0, tiled=True),
         lax.all_gather(key_projection.astype(bf16), "dp", axis=0, tiled=True),
         lax.all_gather(value_projection.astype(bf16), "dp", axis=0, tiled=True),
         lax.all_gather(w_out.astype(bf16), "dp", axis=1, tiled=True),
-        lax.all_gather(attn_gain.astype(bf16), "dp", axis=0, tiled=True),
-        lax.all_gather(query_gain.astype(bf16), "dp", axis=0, tiled=True),
-        lax.all_gather(key_gain.astype(bf16), "dp", axis=0, tiled=True),
-    )
+        gain_rows[:, :ga_local].reshape(-1),
+        gain_rows[:, ga_local : ga_local + gq_local].reshape(-1),
+        gain_rows[:, ga_local + gq_local : ga_local + 2 * gq_local].reshape(-1),
+    )
+    gm_b = gain_rows[:, ga_local + 2 * gq_local :].reshape(-1)
     w_qkv = jnp.concatenate([wq_b, wk_b, wv_b], axis=1)
     q_width = wq_b.shape[1]
     kv_width = wk_b.shape[1]
@@ -273,8 +279,8 @@
     attn_g = ga_b.astype(f32)
     query_norm_gain = gq_b.astype(f32)
     gain_k = gk_b.astype(f32)
-    normalized_input = rms_scale(tok_rows, attn_g).astype(bf16)
-    gathered = tensor_gather(normalized_input, tensor_n)
+    gathered_tokens = tensor_gather(tokens, tensor_n)
+    gathered = rms_scale(gathered_tokens.astype(f32), attn_g).astype(bf16)
     half_width = (out_grad.shape[1] * 11 // 16) // 128 * 128
     grad_half_a = tensor_gather_direct(out_grad[:, :half_width], tensor_n)
     projected = jnp.dot(gathered, w_qkv, preferred_element_type=f32)
@@ -307,11 +313,10 @@
     attn_f = jnp.stack([r[0] for r in fwd_results])
     log_totals = jnp.stack([r[1] for r in fwd_results])
     attended = attn_f.reshape(total_rows, q_width).astype(bf16)
-    wg_b, wu_b, wd_b, gm_b = (
+    wg_b, wu_b, wd_b = (
         lax.all_gather(w_gate.astype(bf16), "dp", axis=0, tiled=True),
         lax.all_gather(w_up.astype(bf16), "dp", axis=0, tiled=True),
         lax.all_gather(w_down.astype(bf16), "dp", axis=1, tiled=True),
-        lax.all_gather(mlp_gain.astype(bf16), "dp", axis=0, tiled=True),
     )
     w_gu = jnp.concatenate([wg_b, wu_b], axis=1)
     hidden_width = wg_b.shape[1]

time: 1860 us -> 1840 us (0.989)
  blocking collectives: 64.1 us -> 38.6 us
    unnamed x340 -> x357, local copies, waits for them, and re-layouts: 42.8 us -> 42.4 us
where the time goes in v7:
time: 1840 us; the launch traced here: 1800 us
  waiting for transfers between devices  795 us (43%)
  matrix products  338 us (18%)
  starting transfers between devices  282 us (15%)
  other arithmetic  231 us (13%)
  local copies, waits for them, and re-layouts  101 us (5%)
  blocking collectives  38.6 us (2%)
    ppermute x9, waiting for transfers between devices, tensor_scatter(): lax.ppermute(acc_up.astype(jnp.bfloat16), 'tensor', [(i, i + 1) for i in...  278 us
    ppermute x9, waiting for transfers between devices, tensor_gather(): lax.ppermute(down, 'tensor', [(i, i - 1) for i in range(1, n - s + 1)])  137 us
    ppermute x9, waiting for transfers between devices, tensor_scatter(): lax.ppermute(acc_down.astype(jnp.bfloat16), 'tensor', [(i, i - 1) for i i...  116 us
    ppermute x6, waiting for transfers between devices, tensor_gather_direct(): downs[d] = lax.ppermute(rows, 'tensor', [(i, i - d) for i in range(d, n)])  113 us
    ppermute x3, starting transfers between devices, tensor_scatter_direct(): lax.ppermute(block(jnp.minimum(j + d, n - 1)).astype(jnp.bfloat16), 'tens...  112 us
    ppermute x6, waiting for transfers between devices, tensor_gather_direct(): ups[d] = lax.ppermute(rows, 'tensor', [(i, i + d) for i in range(n - d)])  75.1 us
    ppermute x9, waiting for transfers between devices, tensor_gather(): up = lax.ppermute(up, 'tensor', [(i, i + 1) for i in range(s - 1, n - 1)])  73.4 us
    ppermute x6, starting transfers between devices, tensor_gather_direct(): ups[d] = lax.ppermute(rows, 'tensor', [(i, i + d) for i in range(n - d)])  62.3 us
  transfers between devices with their start and end apart: 67, of which 25 were waited for; matrix products, arithmetic and copies ran while one was open for 22% of the time, Pallas kernels for 0%

profile of v7, /device:TPU:0, one launch (start us, length us, event | category | flops | bytes accessed | tf_op | source)
XLA Modules:
  0.0 1802.9 jit_solution(9804145830618572471)
XLA Ops:
  23.9 40.7 %collective-permute-done = bf16[512,2048]{1,0:T(8,128)(2,1)} collective-permute-done((bf16[512,2048]{1,0:T(8,128)(2,1)}, bf16[512,2048]{1,0:T(8,128)(2,1)}, u32[]{:S(2)}, u32[]{:S(2)}) %collective-permute-start) | collective-permute-done | bytes 2097184 | tf_op jit(solution)/shard_map/ppermute | solution.py:44
  87.6 31.1 %collective-permute-done.4 = bf16[512,2048]{1,0:T(8,128)(2,1)} collective-permute-done((bf16[512,2048]{1,0:T(8,128)(2,1)}, bf16[512,2048]{1,0:T(8,128)(2,1)}, u32[]{:S(2)}, u32[]{:S(2)}) %collective-permute-start.4) | collective-permute-done | bytes 2097184 | tf_op jit(solution)/shard_map/ppermute | solution.py:45
  136.1 30.1 %collective-permute-done.5 = bf16[512,2048]{1,0:T(8,128)(2,1)} collective-permute-done((bf16[512,2048]{1,0:T(8,128)(2,1)}, bf16[512,2048]{1,0:T(8,128)(2,1)}, u32[]{:S(2)}, u32[]{:S(2)}) %collective-permute-start.5) | collective-permute-done | bytes 2097184 | tf_op jit(solution)/shard_map/ppermute | solution.py:45
  174.2 17.7 fusion.176
  275.9 39.3 %collective-permute-done.6 = bf16[512,2048]{1,0:T(8,128)(2,1)} collective-permute-done((bf16[512,2048]{1,0:T(8,128)(2,1)}, bf16[512,2048]{1,0:T(8,128)(2,1)}, u32[]{:S(2)}, u32[]{:S(2)}) %collective-permute-start.6) | collective-permute-done | bytes 2097184 | tf_op jit(solution)/shard_map/ppermute | solution.py:68
  326.8 39.4 %collective-permute-done.7 = bf16[512,2048]{1,0:T(8,128)(2,1)} collective-permute-done((bf16[512,2048]{1,0:T(8,128)(2,1)}, bf16[512,2048]{1,0:T(8,128)(2,1)}, u32[]{:S(2)}, u32[]{:S(2)}) %collective-permute-start.7) | collective-permute-done | bytes 2097184 | tf_op jit(solution)/shard_map/ppermute | solution.py:68
  390.0 46.0 %collective-permute-start.30 = (bf16[512,640]{1,0:T(8,128)(2,1)}, bf16[512,640]{1,0:T(8,128)(2,1)S(1)}, u32[]{:S(2)}, u32[]{:S(2)}) collective-permute-start(bf16[512,640]{1,0:T(8,128)(2,1)} %slice.396), channel_id=1, source_target_pairs={{0,3},{4,7},{8,11},{12,15},{16,19},{20,23},{24,27},{28,31}} | collective-permute-start | bytes 1966088 | tf_op jit(solution)/shard_map/ppermute | solution.py:82
  441.9 34.1 %collective-permute-done.11 = bf16[512,2048]{1,0:T(8,128)(2,1)} collective-permute-done((bf16[512,2048]{1,0:T(8,128)(2,1)}, bf16[512,2048]{1,0:T(8,128)(2,1)}, u32[]{:S(2)}, u32[]{:S(2)}) %collective-permute-start.11) | collective-permute-done | bytes 2097184 | tf_op jit(solution)/shard_map/ppermute | solution.py:69
  499.5 34.0 %collective-permute-done.34 = bf16[512,640]{1,0:T(8,128)(2,1)S(1)} collective-permute-done((bf16[512,640]{1,0:T(8,128)(2,1)}, bf16[512,640]{1,0:T(8,128)(2,1)S(1)}, u32[]{:S(2)}, u32[]{:S(2)}) %collective-permute-start.34) | collective-permute-done | bytes 655392 | tf_op jit(solution)/shard_map/ppermute | solution.py:83
  536.8 28.4 %collective-permute-done.24 = bf16[512,1408]{1,0:T(8,128)(2,1)S(1)} collective-permute-done((bf16[512,1408]{1,0:T(8,128)(2,1)S(1)}, bf16[512,1408]{1,0:T(8,128)(2,1)S(1)}, u32[]{:S(2)}, u32[]{:S(2)}) %collective-permute-start.24) | collective-permute-done | bytes 1441824 | tf_op jit(solution)/shard_map/ppermute | solution.py:82
  566.6 29.6 %collective-permute-done.25 = bf16[512,1408]{1,0:T(8,128)(2,1)S(1)} collective-permute-done((bf16[512,1408]{1,0:T(8,128)(2,1)S(1)}, bf16[512,1408]{1,0:T(8,128)(2,1)S(1)}, u32[]{:S(2)}, u32[]{:S(2)}) %collective-permute-start.25) | collective-permute-done | bytes 1441824 | tf_op jit(solution)/shard_map/ppermute | solution.py:82
  597.5 17.1 collective-permute-done.26
  622.8 78.7 %collective-permute-done.28 = bf16[512,1408]{1,0:T(8,128)(2,1)} collective-permute-done((bf16[512,1408]{1,0:T(8,128)(2,1)S(1)}, bf16[512,1408]{1,0:T(8,128)(2,1)}, u32[]{:S(2)}, u32[]{:S(2)}) %collective-permute-start.28) | collective-permute-done | bytes 1441824 | tf_op jit(solution)/shard_map/ppermute | solution.py:83
  705.1 35.3 %collective-permute-done.16 = bf16[512,2048]{1,0:T(8,128)(2,1)} collective-permute-done((bf16[512,2048]{1,0:T(8,128)(2,1)}, bf16[512,2048]{1,0:T(8,128)(2,1)}, u32[]{:S(2)}, u32[]{:S(2)}) %collective-permute-start.16) | collective-permute-done | bytes 2097184 | tf_op jit(solution)/shard_map/ppermute | solution.py:45
  741.7 33.8 %maximum_maximum_fusion = bf16[2048,2048]{1,0:T(8,128)(2,1)} fusion(bf16[512,640]{1,0:T(8,128)(2,1)S(1)} %get-tuple-element.243, bf16[512,640]{1,0:T(8,128)(2,1)S(1)} %get-tuple-element.242, bf16[512,640]{1,0:T(8,128)(2,1)S(1)} %get-tuple-element.241, bf16[512,640]{1,0:T(8,128)(2,1)S(1)} %get-tuple-element.240, bf16[512,1408]{1,0:T(8,128)(2,1)S(1)} %get-tuple-element.231, ...), kind=kLoop, calls=%fused_computation.43 | loop fusion | flops 67108864 | bytes 16777216 | tf_op jit(solution)/shard_map/concatenate | solution.py:342
  798.5 33.6 %fusion.172 = f32[2048,3072]{1,0:T(8,128)} fusion(bf16[2048,3072]{1,0:T(8,128)(2,1)} %constant_dynamic-update-slice_fusion.3, bf16[512,2048]{1,0:T(8,128)(2,1)S(1)} %get-tuple-element.219, bf16[512,2048]{1,0:T(8,128)(2,1)S(1)} %get-tuple-element.218, bf16[512,2048]{1,0:T(8,128)(2,1)S(1)} %get-tuple-element.217, bf16[512,2048]{1,0:T(8,128)(2,1)S(1)} %get-tuple-element.216), kind=kOutput, calls=%fused_computation.333 | convolution fusion | flops 25803358208 | bytes 46137344 | tf_op jit(solution)/shard_map/dot_general | solution.py:329
  832.1 37.8 %fusion.12 = (bf16[2048,1536]{1,0:T(8,128)(2,1)}, bf16[2048,1536]{1,0:T(8,128)(2,1)}, bf16[2048,1536]{1,0:T(8,128)(2,1)}) fusion(f32[2048,3072]{1,0:T(8,128)} %fusion.172, bf16[1536,2048]{1,0:T(8,128)(2,1)} %all-gather.21.cloned.1.call-done, bf16[512,640]{1,0:T(8,128)(2,1)} %copy-done.77, bf16[512,640]{1,0:T(8,128)(2,1)} %copy-done.76, ...), kind=kOutput, calls=%fused_computation.21 | convolution fusion | flops 13002342400 | bytes 58720256 | tf_op jit(solution)/shard_map/dot_general | solution.py:343
  869.9 34.3 %fusion.171 = f32[2048,2048]{1,0:T(8,128)} fusion(bf16[2048,3072]{1,0:T(8,128)(2,1)} %constant_dynamic-update-slice_fusion.3, bf16[2048,1536]{1,0:T(8,128)(2,1)} %get-tuple-element.192, bf16[2048,1536]{1,0:T(8,128)(2,1)} %get-tuple-element.191), kind=kOutput, calls=%fused_computation.332 | convolution fusion | flops 25794969600 | bytes 41943040 | tf_op jit(solution)/shard_map/dot_general | solution.py:352
  924.5 43.2 %collective-permute-done.36 = bf16[512,2048]{1,0:T(8,128)(2,1)S(1)} collective-permute-done((bf16[512,2048]{1,0:T(8,128)(2,1)S(1)}, bf16[512,2048]{1,0:T(8,128)(2,1)S(1)}, u32[]{:S(2)}, u32[]{:S(2)}) %collective-permute-start.36) | collective-permute-done | bytes 2097184 | tf_op jit(solution)/shard_map/ppermute | solution.py:68
  974.3 41.9 %collective-permute-done.37 = bf16[512,2048]{1,0:T(8,128)(2,1)} collective-permute-done((bf16[512,2048]{1,0:T(8,128)(2,1)S(1)}, bf16[512,2048]{1,0:T(8,128)(2,1)}, u32[]{:S(2)}, u32[]{:S(2)}) %collective-permute-start.37) | collective-permute-done | bytes 2097184 | tf_op jit(solution)/shard_map/ppermute | solution.py:68
  1030.0 40.4 %collective-permute-done.38 = bf16[512,2048]{1,0:T(8,128)(2,1)S(1)} collective-permute-done((bf16[512,2048]{1,0:T(8,128)(2,1)}, bf16[512,2048]{1,0:T(8,128)(2,1)S(1)}, u32[]{:S(2)}, u32[]{:S(2)}) %collective-permute-start.38) | collective-permute-done | bytes 2097184 | tf_op jit(solution)/shard_map/ppermute | solution.py:68
  1070.4 46.0 %collective-permute-done.41 = bf16[512,2048]{1,0:T(8,128)(2,1)S(1)} collective-permute-done((bf16[512,2048]{1,0:T(8,128)(2,1)S(1)}, bf16[512,2048]{1,0:T(8,128)(2,1)S(1)}, u32[]{:S(2)}, u32[]{:S(2)}) %collective-permute-start.41) | collective-permute-done | bytes 2097184 | tf_op jit(solution)/shard_map/ppermute | solution.py:69
  1135.8 32.6 %collective-permute-done.42 = bf16[512,2048]{1,0:T(8,128)(2,1)} collective-permute-done((bf16[512,2048]{1,0:T(8,128)(2,1)S(1)}, bf16[512,2048]{1,0:T(8,128)(2,1)}, u32[]{:S(2)}, u32[]{:S(2)}) %collective-permute-start.42) | collective-permute-done | bytes 2097184 | tf_op jit(solution)/shard_map/ppermute | solution.py:44
  1176.0 32.9 %fusion.179 = bf16[2048,3072]{1,0:T(8,128)(2,1)} fusion(bf16[2048,2048]{1,0:T(8,128)(2,1)} %pad_maximum_fusion.2, bf16[2048,3072]{1,0:T(8,128)(2,1)} %pad_maximum_fusion), kind=kOutput, calls=%fused_computation.340 | convolution fusion | flops 25769803776 | bytes 33554432 | tf_op jit(solution)/shard_map/dot_general | solution.py:357
  1221.8 19.6 %fusion.180 = bf16[1536,2048]{1,0:T(8,128)(2,1)} fusion(bf16[2048,1536]{1,0:T(8,128)(2,1)} %get-tuple-element.193, bf16[2048,2048]{1,0:T(8,128)(2,1)} %maximum_maximum_fusion), kind=kOutput, calls=%fused_computation.341 | convolution fusion | flops 12884901888 | bytes 20971520 | tf_op jit(solution)/shard_map/dot_general | solution.py:356
  1241.4 22.6 %collective-permute-done.47 = bf16[512,2048]{1,0:T(8,128)(2,1)} collective-permute-done((bf16[512,2048]{1,0:T(8,128)(2,1)}, bf16[512,2048]{1,0:T(8,128)(2,1)}, u32[]{:S(2)}, u32[]{:S(2)}) %collective-permute-start.47) | collective-permute-done | bytes 2097184 | tf_op jit(solution)/shard_map/ppermute | solution.py:45
  1446.7 37.9 %collective-permute-done.48 = bf16[512,2048]{1,0:T(8,128)(2,1)S(1)} collective-permute-done((bf16[512,2048]{1,0:T(8,128)(2,1)S(1)}, bf16[512,2048]{1,0:T(8,128)(2,1)S(1)}, u32[]{:S(2)}, u32[]{:S(2)}) %collective-permute-start.48) | collective-permute-done | bytes 2097184 | tf_op jit(solution)/shard_map/ppermute | solution.py:68
  1491.1 35.8 %collective-permute-done.49 = bf16[512,2048]{1,0:T(8,128)(2,1)} collective-permute-done((bf16[512,2048]{1,0:T(8,128)(2,1)S(1)}, bf16[512,2048]{1,0:T(8,128)(2,1)}, u32[]{:S(2)}, u32[]{:S(2)}) %collective-permute-start.49) | collective-permute-done | bytes 2097184 | tf_op jit(solution)/shard_map/ppermute | solution.py:68
  1533.8 19.8 %fusion.178 = f32[2048,2048]{1,0:T(8,128)} fusion(bf16[2048,1536]{1,0:T(8,128)(2,1)} %get-tuple-element.193, bf16[1536,2048]{1,0:T(8,128)(2,1)} %all-gather.21.cloned.1.call-done), kind=kOutput, calls=%fused_computation.339 | convolution fusion | flops 12884901888 | bytes 29360128 | tf_op jit(solution)/shard_map/dot_general | solution.py:333
  1578.9 58.4 %collective-permute-start.22 = (bf16[512,2048]{1,0:T(8,128)(2,1)}, bf16[512,2048]{1,0:T(8,128)(2,1)}, u32[]{:S(2)}, u32[]{:S(2)}) collective-permute-start(bf16[512,2048]{1,0:T(8,128)(2,1)} %get-tuple-element.204), channel_id=1, source_target_pairs={{0,3},{4,7},{8,11},{12,15},{16,19},{20,23},{24,27},{28,31}} | collective-permute-start | bytes 6291464 | tf_op jit(solution)/shard_map/ppermute | solution.py:98
  1648.0 35.6 %collective-permute-done.53 = bf16[512,2048]{1,0:T(8,128)(2,1)} collective-permute-done((bf16[512,2048]{1,0:T(8,128)(2,1)S(1)}, bf16[512,2048]{1,0:T(8,128)(2,1)}, u32[]{:S(2)}, u32[]{:S(2)}) %collective-permute-start.53) | collective-permute-done | bytes 2097184 | tf_op jit(solution)/shard_map/ppermute | solution.py:69
  1683.7 45.4 %collective-permute-start.18 = (bf16[512,2048]{1,0:T(8,128)(2,1)}, bf16[512,2048]{1,0:T(8,128)(2,1)}, u32[]{:S(2)}, u32[]{:S(2)}) collective-permute-start(bf16[512,2048]{1,0:T(8,128)(2,1)} %get-tuple-element.202), channel_id=1, source_target_pairs={{0,1},{1,2},{2,3},{4,5},{5,6},{6,7},{8,9},{9,10},{10,11},{12,13},{... | collective-permute-start | bytes 6291464 | tf_op jit(solution)/shard_map/ppermute | solution.py:98
  (654 shorter events, 631.5 us)
Async XLA Ops:
  7.3 121.0 %all-gather.9.cloned.1.call-start = ((), (), s32[]{:S(2)}) async-start(), calls=%async_computation.6 | async-start | bytes 2359296 | tf_op jit(solution)/shard_map/all_gather | solution.py:264
  9.2 122.3 %all-gather.11.cloned.1.call-start = ((), (), s32[]{:S(2)}) async-start(), calls=%async_computation.7 | async-start | bytes 1179648 | tf_op jit(solution)/shard_map/all_gather | solution.py:265
  10.9 123.0 %all-gather.13.cloned.1.call-start = ((), (), s32[]{:S(2)}) async-start(), calls=%async_computation.8 | async-start | bytes 1179648 | tf_op jit(solution)/shard_map/all_gather | solution.py:266
  12.6 243.5 %all-gather.15.cloned.1.call-start = ((), (), s32[]{:S(2)}) async-start(), calls=%async_computation.9 | async-start | bytes 2359296 | tf_op jit(solution)/shard_map/all_gather | solution.py:267
  14.4 761.1 %all-gather.17.cloned.1.call-start = ((), (), s32[]{:S(2)}) async-start(), calls=%async_computation.10 | async-start | bytes 7077888 | tf_op jit(solution)/shard_map/all_gather | solution.py:317
  23.1 758.3 %all-gather.19.cloned.1.call-start = ((), (), s32[]{:S(2)}) async-start(), calls=%async_computation.11 | async-start | bytes 7077888 | tf_op jit(solution)/shard_map/all_gather | solution.py:318
  326.7 505.4 %all-gather.21.cloned.1.call-start = ((), (), s32[]{:S(2)}) async-start(), calls=%async_computation.12 | async-start | bytes 7077888 | tf_op jit(solution)/shard_map/all_gather | solution.py:319
  386.7 89.3 %collective-permute-start.11 = (bf16[512,2048]{1,0:T(8,128)(2,1)}, bf16[512,2048]{1,0:T(8,128)(2,1)}, u32[]{:S(2)}, u32[]{:S(2)}) collective-permute-start(bf16[512,2048]{1,0:T(8,128)(2,1)} %add_convert_fusion.9), channel_id=1, source_target_pairs={{1,0},{2,1},{3,2},{5,4},{6,5},{7,6},{9,8},{10,9},{11,10},{13,12},{... | collective-permute-start | bytes 6291464 | tf_op jit(solution)/shard_map/ppermute | solution.py:69
  390.0 92.9 %collective-permute-start.30 = (bf16[512,640]{1,0:T(8,128)(2,1)}, bf16[512,640]{1,0:T(8,128)(2,1)S(1)}, u32[]{:S(2)}, u32[]{:S(2)}) collective-permute-start(bf16[512,640]{1,0:T(8,128)(2,1)} %slice.396), channel_id=1, source_target_pairs={{0,3},{4,7},{8,11},{12,15},{16,19},{20,23},{24,27},{28,31}} | collective-permute-start | bytes 1966088 | tf_op jit(solution)/shard_map/ppermute | solution.py:82
  484.9 131.0 %collective-permute-start.12 = (bf16[512,2048]{1,0:T(8,128)(2,1)S(1)}, bf16[512,2048]{1,0:T(8,128)(2,1)}, u32[]{:S(2)}, u32[]{:S(2)}) collective-permute-start(bf16[512,2048]{1,0:T(8,128)(2,1)S(1)} %multiply_convert_fusion.2), channel_id=1, source_target_pairs={{0,1},{1,2},{2,3},{4,5},{5,6},{6,7},{8,9},{9,10},{10,11},{12,13},{... | collective-permute-start | bytes 6291464 | tf_op jit(solution)/shard_map/ppermute | solution.py:44
  489.6 128.2 %collective-permute-start.15 = (bf16[512,2048]{1,0:T(8,128)(2,1)S(1)}, bf16[512,2048]{1,0:T(8,128)(2,1)}, u32[]{:S(2)}, u32[]{:S(2)}) collective-permute-start(bf16[512,2048]{1,0:T(8,128)(2,1)S(1)} %multiply_convert_fusion.2), channel_id=1, source_target_pairs={{1,0},{2,1},{3,2},{5,4},{6,5},{7,6},{9,8},{10,9},{11,10},{13,12},{... | collective-permute-start | bytes 6291464 | tf_op jit(solution)/shard_map/ppermute | solution.py:45
  491.1 74.2 %collective-permute-start.24 = (bf16[512,1408]{1,0:T(8,128)(2,1)S(1)}, bf16[512,1408]{1,0:T(8,128)(2,1)S(1)}, u32[]{:S(2)}, u32[]{:S(2)}) collective-permute-start(bf16[512,1408]{1,0:T(8,128)(2,1)S(1)} %slice.395), channel_id=1, source_target_pairs={{0,3},{4,7},{8,11},{12,15},{16,19},{20,23},{24,27},{28,31}} | collective-permute-start | bytes 4325384 | tf_op jit(solution)/shard_map/ppermute | solution.py:82
  535.5 79.1 %collective-permute-start.26 = (bf16[512,1408]{1,0:T(8,128)(2,1)S(1)}, bf16[512,1408]{1,0:T(8,128)(2,1)S(1)}, u32[]{:S(2)}, u32[]{:S(2)}) collective-permute-start(bf16[512,1408]{1,0:T(8,128)(2,1)S(1)} %slice.395), channel_id=1, source_target_pairs={{0,1},{1,2},{2,3},{4,5},{5,6},{6,7},{8,9},{9,10},{10,11},{12,13},{... | collective-permute-start | bytes 4325384 | tf_op jit(solution)/shard_map/ppermute | solution.py:82
  596.2 105.3 %collective-permute-start.28 = (bf16[512,1408]{1,0:T(8,128)(2,1)S(1)}, bf16[512,1408]{1,0:T(8,128)(2,1)}, u32[]{:S(2)}, u32[]{:S(2)}) collective-permute-start(bf16[512,1408]{1,0:T(8,128)(2,1)S(1)} %slice.395), channel_id=1, source_target_pairs={{2,0},{3,1},{6,4},{7,5},{10,8},{11,9},{14,12},{15,13},{18,16},{19,... | collective-permute-start | bytes 4325384 | tf_op jit(solution)/shard_map/ppermute | solution.py:83
  614.6 86.9 %collective-permute-start.29 = (bf16[512,1408]{1,0:T(8,128)(2,1)S(1)}, bf16[512,1408]{1,0:T(8,128)(2,1)}, u32[]{:S(2)}, u32[]{:S(2)}) collective-permute-start(bf16[512,1408]{1,0:T(8,128)(2,1)S(1)} %slice.395), channel_id=1, source_target_pairs={{3,0},{7,4},{11,8},{15,12},{19,16},{23,20},{27,24},{31,28}} | collective-permute-start | bytes 4325384 | tf_op jit(solution)/shard_map/ppermute | solution.py:83
  615.9 88.4 %collective-permute-start.13 = (bf16[512,2048]{1,0:T(8,128)(2,1)}, bf16[512,2048]{1,0:T(8,128)(2,1)}, u32[]{:S(2)}, u32[]{:S(2)}) collective-permute-start(bf16[512,2048]{1,0:T(8,128)(2,1)} %collective-permute-done.12), channel_id=1, source_target_pairs={{1,2},{2,3},{5,6},{6,7},{9,10},{10,11},{13,14},{14,15},{17,18},{18... | collective-permute-start | bytes 6291464 | tf_op jit(solution)/shard_map/ppermute | solution.py:44
  617.9 122.5 %collective-permute-start.16 = (bf16[512,2048]{1,0:T(8,128)(2,1)}, bf16[512,2048]{1,0:T(8,128)(2,1)}, u32[]{:S(2)}, u32[]{:S(2)}) collective-permute-start(bf16[512,2048]{1,0:T(8,128)(2,1)} %collective-permute-done.15), channel_id=1, source_target_pairs={{1,0},{2,1},{5,4},{6,5},{9,8},{10,9},{13,12},{14,13},{17,16},{18,1... | collective-permute-start | bytes 6291464 | tf_op jit(solution)/shard_map/ppermute | solution.py:45
  620.2 1110.8 %reduce-scatter.9.cloned.1.call-start = ((), (), s32[]{:S(2)}) async-start(), calls=%async_computation.14 | async-start | bytes 1179648 | tf_op jit(solution)/shard_map/reduce_scatter | solution.py:436
  704.2 83.2 %collective-permute-start.14 = (bf16[512,2048]{1,0:T(8,128)(2,1)}, bf16[512,2048]{1,0:T(8,128)(2,1)S(1)}, u32[]{:S(2)}, u32[]{:S(2)}) collective-permute-start(bf16[512,2048]{1,0:T(8,128)(2,1)} %collective-permute-done.13), channel_id=1, source_target_pairs={{2,3},{6,7},{10,11},{14,15},{18,19},{22,23},{26,27},{30,31}} | collective-permute-start | bytes 6291464 | tf_op jit(solution)/shard_map/ppermute | solution.py:44
  1028.6 87.8 %collective-permute-start.41 = (bf16[512,2048]{1,0:T(8,128)(2,1)S(1)}, bf16[512,2048]{1,0:T(8,128)(2,1)S(1)}, u32[]{:S(2)}, u32[]{:S(2)}) collective-permute-start(bf16[512,2048]{1,0:T(8,128)(2,1)S(1)} %add_convert_fusion.4), channel_id=1, source_target_pairs={{1,0},{2,1},{3,2},{5,4},{6,5},{7,6},{9,8},{10,9},{11,10},{13,12},{... | collective-permute-start | bytes 6291464 | tf_op jit(solution)/shard_map/ppermute | solution.py:69
  1423.9 308.7 %reduce-scatter.11.cloned.1.call-start = ((), (), s32[]{:S(2)}) async-start(), calls=%async_computation.15 | async-start | bytes 1179648 | tf_op jit(solution)/shard_map/reduce_scatter | solution.py:442
  1424.6 309.6 %reduce-scatter.7.cloned.1.call-start = ((), (), s32[]{:S(2)}) async-start(), calls=%async_computation.13 | async-start | bytes 2359296 | tf_op jit(solution)/shard_map/reduce_scatter | solution.py:433
  1427.9 308.1 %reduce-scatter.13.cloned.1.call-start = ((), (), s32[]{:S(2)}) async-start(), calls=%async_computation.16 | async-start | bytes 2359296 | tf_op jit(solution)/shard_map/reduce_scatter | solution.py:390
  1428.7 361.7 %reduce-scatter.17.cloned.1.call-start = ((), (), s32[]{:S(2)}) async-start(), calls=%async_computation.18 | async-start | bytes 7077888 | tf_op jit(solution)/shard_map/reduce_scatter | solution.py:395
  1429.2 363.5 %reduce-scatter.15.cloned.1.call-start = ((), (), s32[]{:S(2)}) async-start(), calls=%async_computation.17 | async-start | bytes 14155776 | tf_op jit(solution)/shard_map/reduce_scatter | solution.py:386
  1567.4 79.4 %collective-permute-start.50 = (bf16[512,2048]{1,0:T(8,128)(2,1)S(1)}, bf16[512,2048]{1,0:T(8,128)(2,1)}, u32[]{:S(2)}, u32[]{:S(2)}) collective-permute-start(bf16[512,2048]{1,0:T(8,128)(2,1)S(1)} %copy-done.80), channel_id=1, source_target_pairs={{0,1},{1,2},{2,3},{4,5},{5,6},{6,7},{8,9},{9,10},{10,11},{12,13},{... | collective-permute-start | bytes 6291464 | tf_op jit(solution)/shard_map/ppermute | solution.py:68
  1577.6 106.0 %collective-permute-start.53 = (bf16[512,2048]{1,0:T(8,128)(2,1)S(1)}, bf16[512,2048]{1,0:T(8,128)(2,1)}, u32[]{:S(2)}, u32[]{:S(2)}) collective-permute-start(bf16[512,2048]{1,0:T(8,128)(2,1)S(1)} %add_convert_fusion), channel_id=1, source_target_pairs={{1,0},{2,1},{3,2},{5,4},{6,5},{7,6},{9,8},{10,9},{11,10},{13,12},{... | collective-permute-start | bytes 6291464 | tf_op jit(solution)/shard_map/ppermute | solution.py:69
  1578.9 195.7 %collective-permute-start.22 = (bf16[512,2048]{1,0:T(8,128)(2,1)}, bf16[512,2048]{1,0:T(8,128)(2,1)}, u32[]{:S(2)}, u32[]{:S(2)}) collective-permute-start(bf16[512,2048]{1,0:T(8,128)(2,1)} %get-tuple-element.204), channel_id=1, source_target_pairs={{0,3},{4,7},{8,11},{12,15},{16,19},{20,23},{24,27},{28,31}} | collective-permute-start | bytes 6291464 | tf_op jit(solution)/shard_map/ppermute | solution.py:98
  1637.3 137.4 %collective-permute-start.21 = (bf16[512,2048]{1,0:T(8,128)(2,1)}, bf16[512,2048]{1,0:T(8,128)(2,1)}, u32[]{:S(2)}, u32[]{:S(2)}) collective-permute-start(bf16[512,2048]{1,0:T(8,128)(2,1)} %get-tuple-element.205), channel_id=1, source_target_pairs={{2,0},{3,1},{6,4},{7,5},{10,8},{11,9},{14,12},{15,13},{18,16},{19,... | collective-permute-start | bytes 6291464 | tf_op jit(solution)/shard_map/ppermute | solution.py:103
  1638.6 136.1 %collective-permute-start.20 = (bf16[512,2048]{1,0:T(8,128)(2,1)}, bf16[512,2048]{1,0:T(8,128)(2,1)}, u32[]{:S(2)}, u32[]{:S(2)}) collective-permute-start(bf16[512,2048]{1,0:T(8,128)(2,1)} %get-tuple-element.206), channel_id=1, source_target_pairs={{0,2},{1,3},{4,6},{5,7},{8,10},{9,11},{12,14},{13,15},{16,18},{17,... | collective-permute-start | bytes 6291464 | tf_op jit(solution)/shard_map/ppermute | solution.py:98
  1646.7 128.0 %collective-permute-start.19 = (bf16[512,2048]{1,0:T(8,128)(2,1)}, bf16[512,2048]{1,0:T(8,128)(2,1)}, u32[]{:S(2)}, u32[]{:S(2)}) collective-permute-start(bf16[512,2048]{1,0:T(8,128)(2,1)} %get-tuple-element.207), channel_id=1, source_target_pairs={{1,0},{2,1},{3,2},{5,4},{6,5},{7,6},{9,8},{10,9},{11,10},{13,12},{... | collective-permute-start | bytes 6291464 | tf_op jit(solution)/shard_map/ppermute | solution.py:103
  1683.7 91.0 %collective-permute-start.18 = (bf16[512,2048]{1,0:T(8,128)(2,1)}, bf16[512,2048]{1,0:T(8,128)(2,1)}, u32[]{:S(2)}, u32[]{:S(2)}) collective-permute-start(bf16[512,2048]{1,0:T(8,128)(2,1)} %get-tuple-element.202), channel_id=1, source_target_pairs={{0,1},{1,2},{2,3},{4,5},{5,6},{6,7},{8,9},{9,10},{10,11},{12,13},{... | collective-permute-start | bytes 6291464 | tf_op jit(solution)/shard_map/ppermute | solution.py:98
  (211 other events, 6749.7 us)
Sparse Core Ops, SparseCore 0:
  10.5 30.4 all-gather.8
  43.5 23.3 all-gather.10
  69.4 23.3 all-gather.12
  95.1 28.0 all-gather.14
  125.0 45.3 all-gather.16
  326.8 43.6 all-gather.18
  620.3 94.6 all-gather.20
  1424.0 34.5 reduce-scatter.8
  1462.4 35.9 reduce-scatter.10
  1501.5 41.1 reduce-scatter.6
  1546.0 41.1 reduce-scatter.12
  1590.4 61.5 reduce-scatter.16
  1655.5 93.0 reduce-scatter.14

commit v8 on v7

--- a/solution.py
+++ b/solution.py
@@ -48,9 +48,11 @@
     return place_blocks(rows, ups, downs, j, n)
 
 
-def tensor_scatter(partial, n):
+def tensor_scatter(partial, n, extra=None):
     if n == 1:
-        return partial.astype(jnp.float32)
+        if extra is None:
+            return partial.astype(jnp.float32)
+        return partial.astype(jnp.float32), extra
     j = lax.axis_index("tensor")
     count = partial.shape[0] // n
 
@@ -69,7 +71,12 @@
         down = lax.ppermute(
             acc_down.astype(jnp.bfloat16), "tensor", [(i, i - 1) for i in range(n - s, n)]
         )
-    return block(j) + up.astype(jnp.float32) + down.astype(jnp.float32)
+        if s == 1 and extra is not None:
+            up, down, extra = lax.optimization_barrier((up, down, extra))
+    total = block(j) + up.astype(jnp.float32) + down.astype(jnp.float32)
+    if extra is None:
+        return total
+    return total, extra
 
 
 def tensor_gather_direct(rows, n):
@@ -279,8 +286,8 @@
     attn_g = ga_b.astype(f32)
     query_norm_gain = gq_b.astype(f32)
     gain_k = gk_b.astype(f32)
-    gathered_tokens = tensor_gather(tokens, tensor_n)
-    gathered = rms_scale(gathered_tokens.astype(f32), attn_g).astype(bf16)
+    normalized_input = rms_scale(tok_rows, attn_g).astype(bf16)
+    gathered = tensor_gather(normalized_input, tensor_n)
     half_width = (out_grad.shape[1] * 11 // 16) // 128 * 128
     grad_half_a = tensor_gather_direct(out_grad[:, :half_width], tensor_n)
     projected = jnp.dot(gathered, w_qkv, preferred_element_type=f32)
@@ -425,7 +432,11 @@
     ).astype(bf16)
     grad_qkv = lax.dot_general(gathered, d_qkv, CONTRACT_ROWS, preferred_element_type=bf16)
     rows_b = d_qkv
-    d_normed = tensor_scatter(lax.dot_general(rows_b, w_qkv_back, CONTRACT_COLS, preferred_element_type=f32), tensor_n)
+    d_normed, layer_out = tensor_scatter(
+        lax.dot_general(rows_b, w_qkv_back, CONTRACT_COLS, preferred_element_type=f32),
+        tensor_n,
+        extra=layer_out,
+    )
     _, norm_back = jax.vjp(rms_scale, tok_rows, attn_g)
     d_x_norm, d_attn_gain = norm_back(d_normed)
     grad_tokens = d_residual + d_x_norm

time: 1840 us -> 1970 us (1.071); the launches traced: 1800 us -> 1970 us
  waiting for transfers between devices: 795 us -> 895 us
  other arithmetic: 231 us -> 278 us
    reduce_scatter x1, waiting for transfers between devices: 0.01 us -> 93.4 us  [on_device_body(): lax.psum_scatter(grad_gate_up.astype(jnp.bfloat16), 'dp', scatter_dimensi...]
    ppermute x9, waiting for transfers between devices: 73.4 us -> 0.02 us  [tensor_gather(): up = lax.ppermute(up, 'tensor', [(i, i + 1) for i in range(s - 1, n - 1)])]
    ppermute x9, waiting for transfers between devices: 116 us -> 64.2 us  [tensor_scatter(): lax.ppermute(acc_down.astype(jnp.bfloat16), 'tensor', [(i, i - 1) for i i...]
    ppermute x9, waiting for transfers between devices: 137 us -> 187 us  [tensor_gather(): lax.ppermute(down, 'tensor', [(i, i - 1) for i in range(1, n - s + 1)])]
    ppermute x6, waiting for transfers between devices: 75.1 us -> 32.2 us  [tensor_gather_direct(): ups[d] = lax.ppermute(rows, 'tensor', [(i, i + d) for i in range(n - d)])]
    reduce_scatter x1, waiting for transfers between devices: 0.01 us -> 38.7 us  [on_device_body(): lax.psum_scatter(grad_qkv[:, :q_width].astype(jnp.bfloat16), 'dp', scatte...]
    another operation x10 -> x11, other arithmetic: 6.33 us -> 41.7 us
    ppermute x3, waiting for transfers between devices: 0.01 us -> 33.3 us  [tensor_scatter_direct(): lax.ppermute(block(jnp.maximum(j - d, 0)).astype(jnp.bfloat16), 'tensor',...]
  transfers between devices with their start and end apart: 67 -> 67, of which waited for: 25 -> 31; matrix products, arithmetic and copies ran while one was open for 22% -> 23% of each run, Pallas kernels for 0% -> 0%
where the time goes in v8:
time: 1970 us
  waiting for transfers between devices  895 us (45%)
  matrix products  349 us (18%)
  starting transfers between devices  290 us (15%)
  other arithmetic  278 us (14%)
  local copies, waits for them, and re-layouts  102 us (5%)
  blocking collectives  35.1 us (2%)
    ppermute x9, waiting for transfers between devices, tensor_scatter(): lax.ppermute(acc_up.astype(jnp.bfloat16), 'tensor', [(i, i + 1) for i in...  294 us
    ppermute x9, waiting for transfers between devices, tensor_gather(): lax.ppermute(down, 'tensor', [(i, i - 1) for i in range(1, n - s + 1)])  187 us
    ppermute x6, waiting for transfers between devices, tensor_gather_direct(): downs[d] = lax.ppermute(rows, 'tensor', [(i, i - d) for i in range(d, n)])  115 us
    reduce_scatter x1, waiting for transfers between devices, on_device_body(): lax.psum_scatter(grad_gate_up.astype(jnp.bfloat16), 'dp', scatter_dimensi...  93.4 us
    ppermute x3, starting transfers between devices, tensor_scatter_direct(): lax.ppermute(block(jnp.minimum(j + d, n - 1)).astype(jnp.bfloat16), 'tens...  83 us
    ppermute x9, waiting for transfers between devices, tensor_scatter(): lax.ppermute(acc_down.astype(jnp.bfloat16), 'tensor', [(i, i - 1) for i i...  64.2 us
    ppermute x9, starting transfers between devices, tensor_scatter(): lax.ppermute(acc_up.astype(jnp.bfloat16), 'tensor', [(i, i + 1) for i in...  61.8 us
    ppermute x6, starting transfers between devices, tensor_gather_direct(): ups[d] = lax.ppermute(rows, 'tensor', [(i, i + d) for i in range(n - d)])  56.2 us
  transfers between devices with their start and end apart: 67, of which 31 were waited for; matrix products, arithmetic and copies ran while one was open for 23% of the time, Pallas kernels for 0%

profile of v8, /device:TPU:0, one launch (start us, length us, event | category | flops | bytes accessed | tf_op | source)
XLA Modules:
  0.0 1967.1 jit_solution(17407168772579144584)
XLA Ops:
  39.2 41.4 %collective-permute-done.3 = bf16[512,2048]{1,0:T(8,128)(2,1)} collective-permute-done((bf16[512,2048]{1,0:T(8,128)(2,1)}, bf16[512,2048]{1,0:T(8,128)(2,1)}, u32[]{:S(2)}, u32[]{:S(2)}) %collective-permute-start.3) | collective-permute-done | bytes 2097184 | tf_op jit(solution)/shard_map/ppermute | solution.py:45
  89.2 40.6 %collective-permute-done.4 = bf16[512,2048]{1,0:T(8,128)(2,1)} collective-permute-done((bf16[512,2048]{1,0:T(8,128)(2,1)}, bf16[512,2048]{1,0:T(8,128)(2,1)}, u32[]{:S(2)}, u32[]{:S(2)}) %collective-permute-start.4) | collective-permute-done | bytes 2097184 | tf_op jit(solution)/shard_map/ppermute | solution.py:45
  150.7 27.5 %collective-permute-done.5 = bf16[512,2048]{1,0:T(8,128)(2,1)} collective-permute-done((bf16[512,2048]{1,0:T(8,128)(2,1)}, bf16[512,2048]{1,0:T(8,128)(2,1)}, u32[]{:S(2)}, u32[]{:S(2)}) %collective-permute-start.5) | collective-permute-done | bytes 2097184 | tf_op jit(solution)/shard_map/ppermute | solution.py:45
  288.8 38.9 %collective-permute-done.18 = bf16[512,2048]{1,0:T(8,128)(2,1)} collective-permute-done((bf16[512,2048]{1,0:T(8,128)(2,1)}, bf16[512,2048]{1,0:T(8,128)(2,1)}, u32[]{:S(2)}, u32[]{:S(2)}) %collective-permute-start.18) | collective-permute-done | bytes 2097184 | tf_op jit(solution)/shard_map/ppermute | solution.py:70
  338.3 41.2 %collective-permute-done.19 = bf16[512,2048]{1,0:T(8,128)(2,1)} collective-permute-done((bf16[512,2048]{1,0:T(8,128)(2,1)}, bf16[512,2048]{1,0:T(8,128)(2,1)}, u32[]{:S(2)}, u32[]{:S(2)}) %collective-permute-start.19) | collective-permute-done | bytes 2097184 | tf_op jit(solution)/shard_map/ppermute | solution.py:70
  407.3 28.0 %collective-permute-done.20 = bf16[512,2048]{1,0:T(8,128)(2,1)} collective-permute-done((bf16[512,2048]{1,0:T(8,128)(2,1)}, bf16[512,2048]{1,0:T(8,128)(2,1)}, u32[]{:S(2)}, u32[]{:S(2)}) %collective-permute-start.20) | collective-permute-done | bytes 2097184 | tf_op jit(solution)/shard_map/ppermute | solution.py:70
  454.4 48.3 %collective-permute-done.23 = bf16[512,2048]{1,0:T(8,128)(2,1)} collective-permute-done((bf16[512,2048]{1,0:T(8,128)(2,1)}, bf16[512,2048]{1,0:T(8,128)(2,1)}, u32[]{:S(2)}, u32[]{:S(2)}) %collective-permute-start.23) | collective-permute-done | bytes 2097184 | tf_op jit(solution)/shard_map/ppermute | solution.py:71
  516.0 60.2 %collective-permute-done.16 = bf16[512,640]{1,0:T(8,128)(2,1)} collective-permute-done((bf16[512,640]{1,0:T(8,128)(2,1)}, bf16[512,640]{1,0:T(8,128)(2,1)}, u32[]{:S(2)}, u32[]{:S(2)}) %collective-permute-start.16) | collective-permute-done | bytes 655392 | tf_op jit(solution)/shard_map/ppermute | solution.py:90
  592.4 22.4 %collective-permute-done.9 = bf16[512,1408]{1,0:T(8,128)(2,1)S(1)} collective-permute-done((bf16[512,1408]{1,0:T(8,128)(2,1)S(1)}, bf16[512,1408]{1,0:T(8,128)(2,1)S(1)}, u32[]{:S(2)}, u32[]{:S(2)}) %collective-permute-start.9) | collective-permute-done | bytes 1441824 | tf_op jit(solution)/shard_map/ppermute | solution.py:90
  614.7 26.9 %collective-permute-start.7 = (bf16[512,1408]{1,0:T(8,128)(2,1)S(1)}, bf16[512,1408]{1,0:T(8,128)(2,1)}, u32[]{:S(2)}, u32[]{:S(2)}) collective-permute-start(bf16[512,1408]{1,0:T(8,128)(2,1)S(1)} %slice.375), channel_id=1, source_target_pairs={{0,2},{1,3},{4,6},{5,7},{8,10},{9,11},{12,14},{13,15},{16,18},{17,... | collective-permute-start | bytes 4325384 | tf_op jit(solution)/shard_map/ppermute | solution.py:89
  641.6 30.3 %collective-permute-done.10 = bf16[512,1408]{1,0:T(8,128)(2,1)S(1)} collective-permute-done((bf16[512,1408]{1,0:T(8,128)(2,1)S(1)}, bf16[512,1408]{1,0:T(8,128)(2,1)S(1)}, u32[]{:S(2)}, u32[]{:S(2)}) %collective-permute-start.10) | collective-permute-done | bytes 1441824 | tf_op jit(solution)/shard_map/ppermute | solution.py:90
  695.3 21.2 %collective-permute-done.6 = bf16[512,1408]{1,0:T(8,128)(2,1)} collective-permute-done((bf16[512,1408]{1,0:T(8,128)(2,1)S(1)}, bf16[512,1408]{1,0:T(8,128)(2,1)}, u32[]{:S(2)}, u32[]{:S(2)}) %collective-permute-start.6) | collective-permute-done | bytes 1441824 | tf_op jit(solution)/shard_map/ppermute | solution.py:89
  719.2 33.9 %maximum_maximum_fusion.4 = bf16[2048,2048]{1,0:T(8,128)(2,1)} fusion(bf16[512,640]{1,0:T(8,128)(2,1)S(1)} %get-tuple-element.249, bf16[512,640]{1,0:T(8,128)(2,1)S(1)} %get-tuple-element.248, bf16[512,640]{1,0:T(8,128)(2,1)S(1)} %get-tuple-element.247, bf16[512,640]{1,0:T(8,128)(2,1)S(1)} %get-tuple-element.246, ...), kind=kLoop, calls=%fused_computation.37.clone.clone.1 | loop fusion | flops 67108864 | bytes 16777216 | tf_op jit(solution)/shard_map/convert.10
  756.9 33.9 %maximum_maximum_fusion = bf16[2048,2048]{1,0:T(8,128)(2,1)} fusion(bf16[512,640]{1,0:T(8,128)(2,1)S(1)} %get-tuple-element.249, bf16[512,640]{1,0:T(8,128)(2,1)S(1)} %get-tuple-element.248, bf16[512,640]{1,0:T(8,128)(2,1)S(1)} %get-tuple-element.247, bf16[512,640]{1,0:T(8,128)(2,1)S(1)} %get-tuple-element.246, bf16[512,1408]{1,0:T(8,128)(2,1)S(1)} %get-tuple-element.237, ...), kind=kLoop, calls=%fused_computation.37 | loop fusion | flops 67108864 | bytes 16777216 | tf_op jit(solution)/shard_map/concatenate | solution.py:349
  835.7 51.9 %fusion.170 = f32[2048,3072]{0,1:T(8,128)} fusion(bf16[2048,3072]{1,0:T(8,128)(2,1)} %constant_dynamic-update-slice_fusion.3, bf16[512,2048]{1,0:T(8,128)(2,1)} %copy-done.42, bf16[512,2048]{1,0:T(8,128)(2,1)} %copy-done.41, bf16[512,2048]{1,0:T(8,128)(2,1)} %copy-done.40, bf16[512,2048]{1,0:T(8,128)(2,1)S(1)} %get-tuple-element.222), kind=kOutput, calls=%fused_computation.330 | convolution fusion | flops 25803358208 | bytes 46137344 | tf_op jit(solution)/shard_map/dot_general | solution.py:336
  887.5 28.5 %fusion.9 = (bf16[2048,1536]{0,1:T(8,128)(2,1)}, bf16[2048,1536]{0,1:T(8,128)(2,1)}, bf16[2048,1536]{0,1:T(8,128)(2,1)}) fusion(f32[2048,3072]{0,1:T(8,128)} %fusion.170, bf16[1536,2048]{1,0:T(8,128)(2,1)} %all-gather.15.cloned.1.call-done, bf16[2048,2048]{1,0:T(8,128)(2,1)} %maximum_maximum_fusion.4), kind=kOutput, calls=%fused_computation.16 | convolution fusion | flops 12935233536 | bytes 58720256 | tf_op jit(solution)/shard_map/dot_general | solution.py:350
  916.0 34.6 %fusion.169 = f32[2048,2048]{1,0:T(8,128)} fusion(bf16[2048,3072]{1,0:T(8,128)(2,1)} %constant_dynamic-update-slice_fusion.3, bf16[2048,1536]{0,1:T(8,128)(2,1)} %get-tuple-element.198, bf16[2048,1536]{0,1:T(8,128)(2,1)} %get-tuple-element.197), kind=kOutput, calls=%fused_computation.329 | convolution fusion | flops 25794969600 | bytes 41943040 | tf_op jit(solution)/shard_map/dot_general | solution.py:359
  967.3 23.6 %collective-permute-start.30 = (bf16[512,2048]{1,0:T(8,128)(2,1)S(1)}, bf16[512,2048]{1,0:T(8,128)(2,1)S(1)}, u32[]{:S(2)}, u32[]{:S(2)}) collective-permute-start(bf16[512,2048]{1,0:T(8,128)(2,1)S(1)} %get-tuple-element.212), channel_id=1, source_target_pairs={{0,1},{4,5},{8,9},{12,13},{16,17},{20,21},{24,25},{28,29}} | collective-permute-start | bytes 6291464 | tf_op jit(solution)/shard_map/ppermute | solution.py:70
  991.8 39.7 %collective-permute-done.30 = bf16[512,2048]{1,0:T(8,128)(2,1)S(1)} collective-permute-done((bf16[512,2048]{1,0:T(8,128)(2,1)S(1)}, bf16[512,2048]{1,0:T(8,128)(2,1)S(1)}, u32[]{:S(2)}, u32[]{:S(2)}) %collective-permute-start.30) | collective-permute-done | bytes 2097184 | tf_op jit(solution)/shard_map/ppermute | solution.py:70
  1038.1 30.1 %collective-permute-done.31 = bf16[512,2048]{1,0:T(8,128)(2,1)} collective-permute-done((bf16[512,2048]{1,0:T(8,128)(2,1)S(1)}, bf16[512,2048]{1,0:T(8,128)(2,1)}, u32[]{:S(2)}, u32[]{:S(2)}) %collective-permute-start.31) | collective-permute-done | bytes 2097184 | tf_op jit(solution)/shard_map/ppermute | solution.py:70
  1075.5 20.5 %fusion.179 = f32[2048,2048]{1,0:T(8,128)} fusion(bf16[2048,1536]{0,1:T(8,128)(2,1)} %get-tuple-element.199, bf16[1536,2048]{1,0:T(8,128)(2,1)} %all-gather.15.cloned.1.call-done), kind=kOutput, calls=%fused_computation.339 | convolution fusion | flops 12884901888 | bytes 29360128 | tf_op jit(solution)/shard_map/dot_general | solution.py:340
  1129.4 28.3 %collective-permute-done.44 = bf16[512,2048]{1,0:T(8,128)(2,1)S(1)} collective-permute-done((bf16[512,2048]{1,0:T(8,128)(2,1)}, bf16[512,2048]{1,0:T(8,128)(2,1)S(1)}, u32[]{:S(2)}, u32[]{:S(2)}) %collective-permute-start.44) | collective-permute-done | bytes 2097184 | tf_op jit(solution)/shard_map/ppermute | solution.py:105
  1158.9 43.5 %collective-permute-done.32 = bf16[512,2048]{1,0:T(8,128)(2,1)S(1)} collective-permute-done((bf16[512,2048]{1,0:T(8,128)(2,1)S(1)}, bf16[512,2048]{1,0:T(8,128)(2,1)S(1)}, u32[]{:S(2)}, u32[]{:S(2)}) %collective-permute-start.32) | collective-permute-done | bytes 2097184 | tf_op jit(solution)/shard_map/ppermute | solution.py:70
  1202.5 72.5 %collective-permute-start.46 = (bf16[512,2048]{1,0:T(8,128)(2,1)S(1)}, bf16[512,2048]{1,0:T(8,128)(2,1)S(1)}, u32[]{:S(2)}, u32[]{:S(2)}) collective-permute-start(bf16[512,2048]{1,0:T(8,128)(2,1)S(1)} %get-tuple-element.206), channel_id=1, source_target_pairs={{0,2},{1,3},{4,6},{5,7},{8,10},{9,11},{12,14},{13,15},{16,18},{17,... | collective-permute-start | bytes 6291464 | tf_op jit(solution)/shard_map/ppermute | solution.py:105
  1281.8 22.9 %collective-permute-done.47 = bf16[512,2048]{1,0:T(8,128)(2,1)S(1)} collective-permute-done((bf16[512,2048]{1,0:T(8,128)(2,1)S(1)}, bf16[512,2048]{1,0:T(8,128)(2,1)S(1)}, u32[]{:S(2)}, u32[]{:S(2)}) %collective-permute-start.47) | collective-permute-done | bytes 2097184 | tf_op jit(solution)/shard_map/ppermute | solution.py:110
  1326.7 25.0 %collective-permute-start.36 = (bf16[512,2048]{1,0:T(8,128)(2,1)S(1)}, bf16[512,2048]{1,0:T(8,128)(2,1)}, u32[]{:S(2)}, u32[]{:S(2)}) collective-permute-start(bf16[512,2048]{1,0:T(8,128)(2,1)S(1)} %get-tuple-element.241), channel_id=1, source_target_pairs={{0,1},{1,2},{2,3},{4,5},{5,6},{6,7},{8,9},{9,10},{10,11},{12,13},{... | collective-permute-start | bytes 6291464 | tf_op jit(solution)/shard_map/ppermute | solution.py:44
  1357.1 33.1 %collective-permute-done.39 = bf16[512,2048]{1,0:T(8,128)(2,1)} collective-permute-done((bf16[512,2048]{1,0:T(8,128)(2,1)S(1)}, bf16[512,2048]{1,0:T(8,128)(2,1)}, u32[]{:S(2)}, u32[]{:S(2)}) %collective-permute-start.39) | collective-permute-done | bytes 2097184 | tf_op jit(solution)/shard_map/ppermute | solution.py:45
  1393.4 33.0 %fusion.176 = bf16[2048,3072]{1,0:T(8,128)(2,1)} fusion(bf16[2048,2048]{1,0:T(8,128)(2,1)} %pad_maximum_fusion.2, bf16[2048,3072]{0,1:T(8,128)(2,1)} %pad_maximum_fusion), kind=kOutput, calls=%fused_computation.336 | convolution fusion | flops 25769803776 | bytes 33554432 | tf_op jit(solution)/shard_map/dot_general | solution.py:364
  1651.7 40.5 %collective-permute-done.42 = bf16[512,2048]{1,0:T(8,128)(2,1)S(1)} collective-permute-done((bf16[512,2048]{1,0:T(8,128)(2,1)S(1)}, bf16[512,2048]{1,0:T(8,128)(2,1)S(1)}, u32[]{:S(2)}, u32[]{:S(2)}) %collective-permute-start.42) | collective-permute-done | bytes 2097184 | tf_op jit(solution)/shard_map/ppermute | solution.py:70
  1698.8 32.1 %collective-permute-done.50 = bf16[512,2048]{1,0:T(8,128)(2,1)} collective-permute-done((bf16[512,2048]{1,0:T(8,128)(2,1)S(1)}, bf16[512,2048]{1,0:T(8,128)(2,1)}, u32[]{:S(2)}, u32[]{:S(2)}) %collective-permute-start.50) | collective-permute-done | bytes 2097184 | tf_op jit(solution)/shard_map/ppermute | solution.py:70
  1757.0 38.7 %reduce-scatter.7.cloned.1.call-done = bf16[256,512]{1,0:T(8,128)(2,1)} async-done(((bf16[2048,512]{1,0:T(8,128)(2,1)}), bf16[256,512]{1,0:T(8,128)(2,1)}) %reduce-scatter.7.cloned.1.call-update) | async-done | bytes 262160 | tf_op jit(solution)/shard_map/reduce_scatter | solution.py:444
  1863.5 93.4 %reduce-scatter.15.cloned.1.call-done = bf16[256,3072]{1,0:T(8,128)(2,1)} async-done(((bf16[2048,3072]{1,0:T(8,128)(2,1)}), bf16[256,3072]{1,0:T(8,128)(2,1)}) %reduce-scatter.15.cloned.1.call-update) | async-done | bytes 1572880 | tf_op jit(solution)/shard_map/reduce_scatter | solution.py:393
  (629 shorter events, 762.6 us)
Async XLA Ops:
  7.2 135.9 %all-gather.9.cloned.1.call-start = ((), (), s32[]{:S(2)}) async-start(), calls=%async_computation.6 | async-start | bytes 2359296 | tf_op jit(solution)/shard_map/all_gather | solution.py:271
  9.2 136.9 %all-gather.11.cloned.1.call-start = ((), (), s32[]{:S(2)}) async-start(), calls=%async_computation.7 | async-start | bytes 1179648 | tf_op jit(solution)/shard_map/all_gather | solution.py:272
  10.9 137.5 %all-gather.13.cloned.1.call-start = ((), (), s32[]{:S(2)}) async-start(), calls=%async_computation.8 | async-start | bytes 1179648 | tf_op jit(solution)/shard_map/all_gather | solution.py:273
  12.6 255.1 %all-gather.17.cloned.1.call-start = ((), (), s32[]{:S(2)}) async-start(), calls=%async_computation.10 | async-start | bytes 2359296 | tf_op jit(solution)/shard_map/all_gather | solution.py:274
  14.4 776.4 %all-gather.19.cloned.1.call-start = ((), (), s32[]{:S(2)}) async-start(), calls=%async_computation.11 | async-start | bytes 7077888 | tf_op jit(solution)/shard_map/all_gather | solution.py:324
  38.6 758.0 %all-gather.21.cloned.1.call-start = ((), (), s32[]{:S(2)}) async-start(), calls=%async_computation.12 | async-start | bytes 7077888 | tf_op jit(solution)/shard_map/all_gather | solution.py:325
  286.7 600.8 %all-gather.15.cloned.1.call-start = ((), (), s32[]{:S(2)}) async-start(), calls=%async_computation.9 | async-start | bytes 7077888 | tf_op jit(solution)/shard_map/all_gather | solution.py:346
  400.0 102.8 %collective-permute-start.23 = (bf16[512,2048]{1,0:T(8,128)(2,1)}, bf16[512,2048]{1,0:T(8,128)(2,1)}, u32[]{:S(2)}, u32[]{:S(2)}) collective-permute-start(bf16[512,2048]{1,0:T(8,128)(2,1)} %add_convert_fusion.9), channel_id=1, source_target_pairs={{1,0},{2,1},{3,2},{5,4},{6,5},{7,6},{9,8},{10,9},{11,10},{13,12},{... | collective-permute-start | bytes 6291464 | tf_op jit(solution)/shard_map/ppermute | solution.py:71
  403.4 107.9 %collective-permute-start.17 = (bf16[512,640]{1,0:T(8,128)(2,1)}, bf16[512,640]{1,0:T(8,128)(2,1)}, u32[]{:S(2)}, u32[]{:S(2)}) collective-permute-start(bf16[512,640]{1,0:T(8,128)(2,1)} %slice.376), channel_id=1, source_target_pairs={{3,0},{7,4},{11,8},{15,12},{19,16},{23,20},{27,24},{31,28}} | collective-permute-start | bytes 1966088 | tf_op jit(solution)/shard_map/ppermute | solution.py:90
  404.7 110.0 %collective-permute-start.15 = (bf16[512,640]{1,0:T(8,128)(2,1)}, bf16[512,640]{1,0:T(8,128)(2,1)}, u32[]{:S(2)}, u32[]{:S(2)}) collective-permute-start(bf16[512,640]{1,0:T(8,128)(2,1)} %slice.376), channel_id=1, source_target_pairs={{1,0},{2,1},{3,2},{5,4},{6,5},{7,6},{9,8},{10,9},{11,10},{13,12},{... | collective-permute-start | bytes 1966088 | tf_op jit(solution)/shard_map/ppermute | solution.py:90
  406.0 170.3 %collective-permute-start.16 = (bf16[512,640]{1,0:T(8,128)(2,1)}, bf16[512,640]{1,0:T(8,128)(2,1)}, u32[]{:S(2)}, u32[]{:S(2)}) collective-permute-start(bf16[512,640]{1,0:T(8,128)(2,1)} %slice.376), channel_id=1, source_target_pairs={{2,0},{3,1},{6,4},{7,5},{10,8},{11,9},{14,12},{15,13},{18,16},{19,... | collective-permute-start | bytes 1966088 | tf_op jit(solution)/shard_map/ppermute | solution.py:90
  435.3 142.2 %collective-permute-start.14 = (bf16[512,640]{1,0:T(8,128)(2,1)}, bf16[512,640]{1,0:T(8,128)(2,1)}, u32[]{:S(2)}, u32[]{:S(2)}) collective-permute-start(bf16[512,640]{1,0:T(8,128)(2,1)} %slice.376), channel_id=1, source_target_pairs={{0,1},{1,2},{2,3},{4,5},{5,6},{6,7},{8,9},{9,10},{10,11},{12,13},{... | collective-permute-start | bytes 1966088 | tf_op jit(solution)/shard_map/ppermute | solution.py:89
  502.7 77.9 %collective-permute-start.13 = (bf16[512,640]{1,0:T(8,128)(2,1)}, bf16[512,640]{1,0:T(8,128)(2,1)S(1)}, u32[]{:S(2)}, u32[]{:S(2)}) collective-permute-start(bf16[512,640]{1,0:T(8,128)(2,1)} %slice.376), channel_id=1, source_target_pairs={{0,2},{1,3},{4,6},{5,7},{8,10},{9,11},{12,14},{13,15},{16,18},{17,... | collective-permute-start | bytes 1966088 | tf_op jit(solution)/shard_map/ppermute | solution.py:89
  514.7 73.9 %collective-permute-start.11 = (bf16[512,1408]{1,0:T(8,128)(2,1)S(1)}, bf16[512,1408]{1,0:T(8,128)(2,1)S(1)}, u32[]{:S(2)}, u32[]{:S(2)}) collective-permute-start(bf16[512,1408]{1,0:T(8,128)(2,1)S(1)} %slice.375), channel_id=1, source_target_pairs={{3,0},{7,4},{11,8},{15,12},{19,16},{23,20},{27,24},{31,28}} | collective-permute-start | bytes 4325384 | tf_op jit(solution)/shard_map/ppermute | solution.py:90
  577.5 94.4 %collective-permute-start.10 = (bf16[512,1408]{1,0:T(8,128)(2,1)S(1)}, bf16[512,1408]{1,0:T(8,128)(2,1)S(1)}, u32[]{:S(2)}, u32[]{:S(2)}) collective-permute-start(bf16[512,1408]{1,0:T(8,128)(2,1)S(1)} %slice.375), channel_id=1, source_target_pairs={{2,0},{3,1},{6,4},{7,5},{10,8},{11,9},{14,12},{15,13},{18,16},{19,... | collective-permute-start | bytes 4325384 | tf_op jit(solution)/shard_map/ppermute | solution.py:90
  580.6 100.4 %collective-permute-start.27 = (bf16[512,2048]{1,0:T(8,128)(2,1)}, bf16[512,2048]{1,0:T(8,128)(2,1)}, u32[]{:S(2)}, u32[]{:S(2)}) collective-permute-start(bf16[512,2048]{1,0:T(8,128)(2,1)} %multiply_convert_fusion.2), channel_id=1, source_target_pairs={{1,0},{2,1},{3,2},{5,4},{6,5},{7,6},{9,8},{10,9},{11,10},{13,12},{... | collective-permute-start | bytes 6291464 | tf_op jit(solution)/shard_map/ppermute | solution.py:45
  581.9 100.4 %collective-permute-start.24 = (bf16[512,2048]{1,0:T(8,128)(2,1)}, bf16[512,2048]{1,0:T(8,128)(2,1)}, u32[]{:S(2)}, u32[]{:S(2)}) collective-permute-start(bf16[512,2048]{1,0:T(8,128)(2,1)} %multiply_convert_fusion.2), channel_id=1, source_target_pairs={{0,1},{1,2},{2,3},{4,5},{5,6},{6,7},{8,9},{9,10},{10,11},{12,13},{... | collective-permute-start | bytes 6291464 | tf_op jit(solution)/shard_map/ppermute | solution.py:44
  588.6 95.7 %collective-permute-start.8 = (bf16[512,1408]{1,0:T(8,128)(2,1)S(1)}, bf16[512,1408]{1,0:T(8,128)(2,1)}, u32[]{:S(2)}, u32[]{:S(2)}) collective-permute-start(bf16[512,1408]{1,0:T(8,128)(2,1)S(1)} %slice.375), channel_id=1, source_target_pairs={{0,1},{1,2},{2,3},{4,5},{5,6},{6,7},{8,9},{9,10},{10,11},{12,13},{... | collective-permute-start | bytes 4325384 | tf_op jit(solution)/shard_map/ppermute | solution.py:89
  614.7 80.6 %collective-permute-start.7 = (bf16[512,1408]{1,0:T(8,128)(2,1)S(1)}, bf16[512,1408]{1,0:T(8,128)(2,1)}, u32[]{:S(2)}, u32[]{:S(2)}) collective-permute-start(bf16[512,1408]{1,0:T(8,128)(2,1)S(1)} %slice.375), channel_id=1, source_target_pairs={{0,2},{1,3},{4,6},{5,7},{8,10},{9,11},{12,14},{13,15},{16,18},{17,... | collective-permute-start | bytes 4325384 | tf_op jit(solution)/shard_map/ppermute | solution.py:89
  675.4 1076.5 %reduce-scatter.9.cloned.1.call-start = ((), (), s32[]{:S(2)}) async-start(), calls=%async_computation.14 | async-start | bytes 1179648 | tf_op jit(solution)/shard_map/reduce_scatter | solution.py:447
  681.0 72.4 %collective-permute-start.28 = (bf16[512,2048]{1,0:T(8,128)(2,1)}, bf16[512,2048]{1,0:T(8,128)(2,1)}, u32[]{:S(2)}, u32[]{:S(2)}) collective-permute-start(bf16[512,2048]{1,0:T(8,128)(2,1)} %collective-permute-done.27), channel_id=1, source_target_pairs={{1,0},{2,1},{5,4},{6,5},{9,8},{10,9},{13,12},{14,13},{17,16},{18,1... | collective-permute-start | bytes 6291464 | tf_op jit(solution)/shard_map/ppermute | solution.py:45
  1111.5 91.0 %collective-permute-start.32 = (bf16[512,2048]{1,0:T(8,128)(2,1)S(1)}, bf16[512,2048]{1,0:T(8,128)(2,1)S(1)}, u32[]{:S(2)}, u32[]{:S(2)}) collective-permute-start(bf16[512,2048]{1,0:T(8,128)(2,1)S(1)} %copy-done.71), channel_id=1, source_target_pairs={{0,1},{1,2},{2,3},{4,5},{5,6},{6,7},{8,9},{9,10},{10,11},{12,13},{... | collective-permute-start | bytes 6291464 | tf_op jit(solution)/shard_map/ppermute | solution.py:70
  1120.2 154.8 %collective-permute-start.35 = (bf16[512,2048]{1,0:T(8,128)(2,1)S(1)}, bf16[512,2048]{1,0:T(8,128)(2,1)S(1)}, u32[]{:S(2)}, u32[]{:S(2)}) collective-permute-start(bf16[512,2048]{1,0:T(8,128)(2,1)S(1)} %add_convert_fusion.5), channel_id=1, source_target_pairs={{1,0},{2,1},{3,2},{5,4},{6,5},{7,6},{9,8},{10,9},{11,10},{13,12},{... | collective-permute-start | bytes 6291464 | tf_op jit(solution)/shard_map/ppermute | solution.py:71
  1121.5 160.3 %collective-permute-start.49 = (bf16[512,2048]{1,0:T(8,128)(2,1)}, bf16[512,2048]{1,0:T(8,128)(2,1)S(1)}, u32[]{:S(2)}, u32[]{:S(2)}) collective-permute-start(bf16[512,2048]{1,0:T(8,128)(2,1)} %get-tuple-element.203), channel_id=1, source_target_pairs={{3,0},{7,4},{11,8},{15,12},{19,16},{23,20},{27,24},{31,28}} | collective-permute-start | bytes 6291464 | tf_op jit(solution)/shard_map/ppermute | solution.py:110
  1122.8 159.0 %collective-permute-start.48 = (bf16[512,2048]{1,0:T(8,128)(2,1)S(1)}, bf16[512,2048]{1,0:T(8,128)(2,1)S(1)}, u32[]{:S(2)}, u32[]{:S(2)}) collective-permute-start(bf16[512,2048]{1,0:T(8,128)(2,1)S(1)} %get-tuple-element.204), channel_id=1, source_target_pairs={{0,3},{4,7},{8,11},{12,15},{16,19},{20,23},{24,27},{28,31}} | collective-permute-start | bytes 6291464 | tf_op jit(solution)/shard_map/ppermute | solution.py:105
  1157.6 147.1 %collective-permute-start.47 = (bf16[512,2048]{1,0:T(8,128)(2,1)S(1)}, bf16[512,2048]{1,0:T(8,128)(2,1)S(1)}, u32[]{:S(2)}, u32[]{:S(2)}) collective-permute-start(bf16[512,2048]{1,0:T(8,128)(2,1)S(1)} %get-tuple-element.205), channel_id=1, source_target_pairs={{2,0},{3,1},{6,4},{7,5},{10,8},{11,9},{14,12},{15,13},{18,16},{19,... | collective-permute-start | bytes 6291464 | tf_op jit(solution)/shard_map/ppermute | solution.py:110
  1202.5 102.2 %collective-permute-start.46 = (bf16[512,2048]{1,0:T(8,128)(2,1)S(1)}, bf16[512,2048]{1,0:T(8,128)(2,1)S(1)}, u32[]{:S(2)}, u32[]{:S(2)}) collective-permute-start(bf16[512,2048]{1,0:T(8,128)(2,1)S(1)} %get-tuple-element.206), channel_id=1, source_target_pairs={{0,2},{1,3},{4,6},{5,7},{8,10},{9,11},{12,14},{13,15},{16,18},{17,... | collective-permute-start | bytes 6291464 | tf_op jit(solution)/shard_map/ppermute | solution.py:105
  1629.0 124.6 %reduce-scatter.11.cloned.1.call-start = ((), (), s32[]{:S(2)}) async-start(), calls=%async_computation.15 | async-start | bytes 1179648 | tf_op jit(solution)/shard_map/reduce_scatter | solution.py:453
  1629.7 125.5 %reduce-scatter.13.cloned.1.call-start = ((), (), s32[]{:S(2)}) async-start(), calls=%async_computation.16 | async-start | bytes 2359296 | tf_op jit(solution)/shard_map/reduce_scatter | solution.py:397
  1630.3 165.4 %reduce-scatter.7.cloned.1.call-start = ((), (), s32[]{:S(2)}) async-start(), calls=%async_computation.13 | async-start | bytes 2359296 | tf_op jit(solution)/shard_map/reduce_scatter | solution.py:444
  1633.4 227.7 %reduce-scatter.17.cloned.1.call-start = ((), (), s32[]{:S(2)}) async-start(), calls=%async_computation.18 | async-start | bytes 7077888 | tf_op jit(solution)/shard_map/reduce_scatter | solution.py:402
  1634.0 322.9 %reduce-scatter.15.cloned.1.call-start = ((), (), s32[]{:S(2)}) async-start(), calls=%async_computation.17 | async-start | bytes 14155776 | tf_op jit(solution)/shard_map/reduce_scatter | solution.py:393
  (198 other events, 6469.2 us)
Sparse Core Ops, SparseCore 0:
  10.5 30.5 all-gather.8
  43.5 23.3 all-gather.10
  69.3 23.3 all-gather.12
  95.1 28.0 all-gather.16
  124.9 45.3 all-gather.18
  286.9 47.8 all-gather.20
  675.6 43.8 all-gather.14
  1629.1 38.0 reduce-scatter.8
  1671.0 35.9 reduce-scatter.10
  1710.1 41.0 reduce-scatter.12
  1754.5 41.1 reduce-scatter.6
  1798.9 62.1 reduce-scatter.16
  1864.6 92.2 reduce-scatter.14

commit v9 on v7

--- a/solution.py
+++ b/solution.py
@@ -82,31 +82,6 @@
         ups[d] = lax.ppermute(rows, "tensor", [(i, i + d) for i in range(n - d)])
         downs[d] = lax.ppermute(rows, "tensor", [(i, i - d) for i in range(d, n)])
     return place_blocks(rows, ups, downs, j, n)
-
-
-def tensor_scatter_direct(partial, n):
-    if n == 1:
-        return partial.astype(jnp.float32)
-    j = lax.axis_index("tensor")
-    count = partial.shape[0] // n
-
-    def block(t):
-        return lax.dynamic_slice_in_dim(partial, t * count, count, 0).astype(jnp.float32)
-
-    total = block(j)
-    for d in range(1, n):
-        up = lax.ppermute(
-            block(jnp.minimum(j + d, n - 1)).astype(jnp.bfloat16),
-            "tensor",
-            [(i, i + d) for i in range(n - d)],
-        )
-        down = lax.ppermute(
-            block(jnp.maximum(j - d, 0)).astype(jnp.bfloat16),
-            "tensor",
-            [(i, i - d) for i in range(d, n)],
-        )
-        total = total + up.astype(jnp.float32) + down.astype(jnp.float32)
-    return total
 
 
 def rms_scale(row_data, gain_vec):
@@ -188,43 +163,43 @@
     d_value = jnp.zeros(key_rows.shape, jnp.float32)
     d_queries = []
     for index, row_start in enumerate(range(0, length, QB)):
-        key_end = row_start + QB
-        block_lse = log_totals[index]
-        q_rows = query_tensor[row_start:key_end]
-        g_rows = grad_rows[row_start:key_end]
-        if index > 0:
-            q_rows, g_rows, block_lse, d_key, d_value = lax.optimization_barrier(
-                (q_rows, g_rows, block_lse, d_key, d_value)
-            )
-        keys = key_rows[:key_end]
-        values = value_tensor[:key_end]
-        allowed = block_mask(seq_starts, seq_pieces, row_start, QB)[:, :key_end]
-        scores = (
-            jnp.einsum("qkgd,skd->kgqs", q_rows, keys, preferred_element_type=jnp.float32)
-            * scale
-        )
-        attn_probs = jnp.where(allowed[None, None], jnp.exp(scores - block_lse[..., None]), 0.0)
-        d_probs = jnp.einsum(
-            "qkgd,skd->kgqs", g_rows, values, preferred_element_type=jnp.float32
-        )
-        d_scores = attn_probs * (d_probs - jnp.sum(attn_probs * d_probs, axis=-1, keepdims=True))
-        d_scores_b = d_scores.astype(jnp.bfloat16)
-        d_queries.append(
-            jnp.einsum("kgqs,skd->qkgd", d_scores_b, keys, preferred_element_type=jnp.float32)
-            * scale
-        )
-        d_key = d_key.at[:key_end].add(
-            jnp.einsum("kgqs,qkgd->skd", d_scores_b, q_rows, preferred_element_type=jnp.float32)
-            * scale
-        )
-        d_value = d_value.at[:key_end].add(
-            jnp.einsum(
-                "kgqs,qkgd->skd",
-                attn_probs.astype(jnp.bfloat16),
-                g_rows,
-                preferred_element_type=jnp.float32,
-            )
-        )
+      key_end = row_start + QB
+      block_lse = log_totals[index]
+      q_rows = query_tensor[row_start:key_end]
+      g_rows = grad_rows[row_start:key_end]
+      if index > 0:
+          q_rows, g_rows, block_lse, d_key, d_value = lax.optimization_barrier(
+              (q_rows, g_rows, block_lse, d_key, d_value)
+          )
+      keys = key_rows[:key_end]
+      values = value_tensor[:key_end]
+      allowed = block_mask(seq_starts, seq_pieces, row_start, QB)[:, :key_end]
+      scores = (
+          jnp.einsum("qkgd,skd->kgqs", q_rows, keys, preferred_element_type=jnp.float32)
+          * scale
+      )
+      attn_probs = jnp.where(allowed[None, None], jnp.exp(scores - block_lse[..., None]), 0.0)
+      d_probs = jnp.einsum(
+          "qkgd,skd->kgqs", g_rows, values, preferred_element_type=jnp.float32
+      )
+      d_scores = attn_probs * (d_probs - jnp.sum(attn_probs * d_probs, axis=-1, keepdims=True))
+      d_scores_b = d_scores.astype(jnp.bfloat16)
+      d_queries.append(
+          jnp.einsum("kgqs,skd->qkgd", d_scores_b, keys, preferred_element_type=jnp.float32)
+          * scale
+      )
+      d_key = d_key.at[:key_end].add(
+          jnp.einsum("kgqs,qkgd->skd", d_scores_b, q_rows, preferred_element_type=jnp.float32)
+          * scale
+      )
+      d_value = d_value.at[:key_end].add(
+          jnp.einsum(
+              "kgqs,qkgd->skd",
+              attn_probs.astype(jnp.bfloat16),
+              g_rows,
+              preferred_element_type=jnp.float32,
+          )
+      )
     d_query = jnp.concatenate(d_queries, axis=0)
     return (d_query.reshape(query_tensor.shape), d_key, d_value)
 
@@ -279,8 +254,8 @@
     attn_g = ga_b.astype(f32)
     query_norm_gain = gq_b.astype(f32)
     gain_k = gk_b.astype(f32)
-    gathered_tokens = tensor_gather(tokens, tensor_n)
-    gathered = rms_scale(gathered_tokens.astype(f32), attn_g).astype(bf16)
+    normalized_input = rms_scale(tok_rows, attn_g).astype(bf16)
+    gathered = tensor_gather(normalized_input, tensor_n)
     half_width = (out_grad.shape[1] * 11 // 16) // 128 * 128
     grad_half_a = tensor_gather_direct(out_grad[:, :half_width], tensor_n)
     projected = jnp.dot(gathered, w_qkv, preferred_element_type=f32)
@@ -331,7 +306,7 @@
     up_pre = gate_up[:, hidden_width:]
     hidden_b = (jax.nn.silu(gate_pre) * up_pre).astype(bf16)
     down_partial = jnp.dot(hidden_b, wd_b, preferred_element_type=f32)
-    mlp_sum = tensor_scatter_direct(down_partial, tensor_n)
+    mlp_sum = tensor_scatter(down_partial, tensor_n)
     layer_out = (residual + mlp_sum).astype(bf16)
     wg_c, wu_c, wd_back = (
         lax.all_gather(w_gate.astype(bf16), "dp", axis=0, tiled=True),

time: 1840 us -> 1820 us (0.989); the launches traced: 1800 us -> 1800 us
  starting transfers between devices: 282 us -> 181 us
  waiting for transfers between devices: 795 us -> 849 us
  blocking collectives: 38.6 us -> 71.5 us
  other arithmetic: 231 us -> 252 us
    ppermute x6 -> x0, starting transfers between devices: 116 us -> none  [the longest x3 112 us: tensor_scatter_direct(): lax.ppermute(block(jnp.minimum(j + d, n - 1)).astype(jnp.bfloat16), 'tens...]
    ppermute x9 -> x12, waiting for transfers between devices: 278 us -> 346 us  [tensor_scatter(): lax.ppermute(acc_up.astype(jnp.bfloat16), 'tensor', [(i, i + 1) for i in...]
    psum x1, blocking collectives: 16.4 us -> 47 us  [on_device_body(): gains_sum = lax.psum((owned[7], owned[8], owned[9], owned[10]), 'tensor')]
    ppermute x9 -> x12, waiting for transfers between devices: 116 us -> 88 us  [tensor_scatter(): lax.ppermute(acc_down.astype(jnp.bfloat16), 'tensor', [(i, i - 1) for i i...]
    convert_element_type x6 -> x8, other arithmetic: 26.3 us -> 39.7 us  [tensor_scatter(): acc_up.astype(jnp.bfloat16)]
    ppermute x9 -> x12, starting transfers between devices: 43.9 us -> 56.5 us  [tensor_scatter(): lax.ppermute(acc_up.astype(jnp.bfloat16), 'tensor', [(i, i + 1) for i in...]
    unnamed x357 -> x335, local copies, waits for them, and re-layouts: 42.4 us -> 48 us
  transfers between devices with their start and end apart: 67 -> 67, of which waited for: 25 -> 28; matrix products, arithmetic and copies ran while one was open for 22% -> 23% of each run, Pallas kernels for 0% -> 0%
where the time goes in v9:
time: 1820 us; the launch traced here: 1800 us
  waiting for transfers between devices  849 us (47%)
  matrix products  331 us (18%)
  other arithmetic  252 us (14%)
  starting transfers between devices  181 us (10%)
  local copies, waits for them, and re-layouts  99.8 us (5%)
  blocking collectives  71.5 us (4%)
  between operations  18.4 us (1%)
    ppermute x12, waiting for transfers between devices, tensor_scatter(): lax.ppermute(acc_up.astype(jnp.bfloat16), 'tensor', [(i, i + 1) for i in...  346 us
    ppermute x9, waiting for transfers between devices, tensor_gather(): lax.ppermute(down, 'tensor', [(i, i - 1) for i in range(1, n - s + 1)])  148 us
    ppermute x6, waiting for transfers between devices, tensor_gather_direct(): downs[d] = lax.ppermute(rows, 'tensor', [(i, i - d) for i in range(d, n)])  112 us
    ppermute x12, waiting for transfers between devices, tensor_scatter(): lax.ppermute(acc_down.astype(jnp.bfloat16), 'tensor', [(i, i - 1) for i i...  88 us
    ppermute x6, waiting for transfers between devices, tensor_gather_direct(): ups[d] = lax.ppermute(rows, 'tensor', [(i, i + d) for i in range(n - d)])  75.9 us
    ppermute x9, waiting for transfers between devices, tensor_gather(): up = lax.ppermute(up, 'tensor', [(i, i + 1) for i in range(s - 1, n - 1)])  75.2 us
    ppermute x6, starting transfers between devices, tensor_gather_direct(): ups[d] = lax.ppermute(rows, 'tensor', [(i, i + d) for i in range(n - d)])  63 us
    ppermute x12, starting transfers between devices, tensor_scatter(): lax.ppermute(acc_up.astype(jnp.bfloat16), 'tensor', [(i, i + 1) for i in...  56.5 us
  transfers between devices with their start and end apart: 67, of which 28 were waited for; matrix products, arithmetic and copies ran while one was open for 23% of the time, Pallas kernels for 0%

profile of v9, /device:TPU:0, one launch (start us, length us, event | category | flops | bytes accessed | tf_op | source)
XLA Modules:
  0.0 1802.9 jit_solution(17367392256280936559)
XLA Ops:
  38.2 41.4 %collective-permute-done = bf16[512,2048]{1,0:T(8,128)(2,1)} collective-permute-done((bf16[512,2048]{1,0:T(8,128)(2,1)}, bf16[512,2048]{1,0:T(8,128)(2,1)}, u32[]{:S(2)}, u32[]{:S(2)}) %collective-permute-start) | collective-permute-done | bytes 2097184 | tf_op jit(solution)/shard_map/ppermute | solution.py:44
  93.8 40.4 %collective-permute-done.4 = bf16[512,2048]{1,0:T(8,128)(2,1)} collective-permute-done((bf16[512,2048]{1,0:T(8,128)(2,1)}, bf16[512,2048]{1,0:T(8,128)(2,1)}, u32[]{:S(2)}, u32[]{:S(2)}) %collective-permute-start.4) | collective-permute-done | bytes 2097184 | tf_op jit(solution)/shard_map/ppermute | solution.py:45
  152.9 29.5 %collective-permute-done.5 = bf16[512,2048]{1,0:T(8,128)(2,1)} collective-permute-done((bf16[512,2048]{1,0:T(8,128)(2,1)}, bf16[512,2048]{1,0:T(8,128)(2,1)}, u32[]{:S(2)}, u32[]{:S(2)}) %collective-permute-start.5) | collective-permute-done | bytes 2097184 | tf_op jit(solution)/shard_map/ppermute | solution.py:45
  294.3 39.7 %collective-permute-done.6 = bf16[512,2048]{1,0:T(8,128)(2,1)} collective-permute-done((bf16[512,2048]{1,0:T(8,128)(2,1)}, bf16[512,2048]{1,0:T(8,128)(2,1)}, u32[]{:S(2)}, u32[]{:S(2)}) %collective-permute-start.6) | collective-permute-done | bytes 2097184 | tf_op jit(solution)/shard_map/ppermute | solution.py:68
  345.6 40.0 %collective-permute-done.7 = bf16[512,2048]{1,0:T(8,128)(2,1)} collective-permute-done((bf16[512,2048]{1,0:T(8,128)(2,1)}, bf16[512,2048]{1,0:T(8,128)(2,1)}, u32[]{:S(2)}, u32[]{:S(2)}) %collective-permute-start.7) | collective-permute-done | bytes 2097184 | tf_op jit(solution)/shard_map/ppermute | solution.py:68
  409.2 46.8 %collective-permute-start.30 = (bf16[512,640]{1,0:T(8,128)(2,1)}, bf16[512,640]{1,0:T(8,128)(2,1)S(1)}, u32[]{:S(2)}, u32[]{:S(2)}) collective-permute-start(bf16[512,640]{1,0:T(8,128)(2,1)} %slice.396), channel_id=1, source_target_pairs={{0,3},{4,7},{8,11},{12,15},{16,19},{20,23},{24,27},{28,31}} | collective-permute-start | bytes 1966088 | tf_op jit(solution)/shard_map/ppermute | solution.py:82
  462.0 34.0 %collective-permute-done.11 = bf16[512,2048]{1,0:T(8,128)(2,1)} collective-permute-done((bf16[512,2048]{1,0:T(8,128)(2,1)}, bf16[512,2048]{1,0:T(8,128)(2,1)}, u32[]{:S(2)}, u32[]{:S(2)}) %collective-permute-start.11) | collective-permute-done | bytes 2097184 | tf_op jit(solution)/shard_map/ppermute | solution.py:69
  518.7 34.9 %collective-permute-done.34 = bf16[512,640]{1,0:T(8,128)(2,1)S(1)} collective-permute-done((bf16[512,640]{1,0:T(8,128)(2,1)}, bf16[512,640]{1,0:T(8,128)(2,1)S(1)}, u32[]{:S(2)}, u32[]{:S(2)}) %collective-permute-start.34) | collective-permute-done | bytes 655392 | tf_op jit(solution)/shard_map/ppermute | solution.py:83
  556.8 27.6 %collective-permute-done.24 = bf16[512,1408]{1,0:T(8,128)(2,1)S(1)} collective-permute-done((bf16[512,1408]{1,0:T(8,128)(2,1)S(1)}, bf16[512,1408]{1,0:T(8,128)(2,1)S(1)}, u32[]{:S(2)}, u32[]{:S(2)}) %collective-permute-start.24) | collective-permute-done | bytes 1441824 | tf_op jit(solution)/shard_map/ppermute | solution.py:82
  585.8 29.6 %collective-permute-done.25 = bf16[512,1408]{1,0:T(8,128)(2,1)S(1)} collective-permute-done((bf16[512,1408]{1,0:T(8,128)(2,1)S(1)}, bf16[512,1408]{1,0:T(8,128)(2,1)S(1)}, u32[]{:S(2)}, u32[]{:S(2)}) %collective-permute-start.25) | collective-permute-done | bytes 1441824 | tf_op jit(solution)/shard_map/ppermute | solution.py:82
  616.6 18.7 %collective-permute-done.26 = bf16[512,1408]{1,0:T(8,128)(2,1)S(1)} collective-permute-done((bf16[512,1408]{1,0:T(8,128)(2,1)S(1)}, bf16[512,1408]{1,0:T(8,128)(2,1)S(1)}, u32[]{:S(2)}, u32[]{:S(2)}) %collective-permute-start.26) | collective-permute-done | bytes 1441824 | tf_op jit(solution)/shard_map/ppermute | solution.py:82
  643.5 77.0 %collective-permute-done.28 = bf16[512,1408]{1,0:T(8,128)(2,1)} collective-permute-done((bf16[512,1408]{1,0:T(8,128)(2,1)S(1)}, bf16[512,1408]{1,0:T(8,128)(2,1)}, u32[]{:S(2)}, u32[]{:S(2)}) %collective-permute-start.28) | collective-permute-done | bytes 1441824 | tf_op jit(solution)/shard_map/ppermute | solution.py:83
  724.1 37.5 %collective-permute-done.16 = bf16[512,2048]{1,0:T(8,128)(2,1)} collective-permute-done((bf16[512,2048]{1,0:T(8,128)(2,1)}, bf16[512,2048]{1,0:T(8,128)(2,1)}, u32[]{:S(2)}, u32[]{:S(2)}) %collective-permute-start.16) | collective-permute-done | bytes 2097184 | tf_op jit(solution)/shard_map/ppermute | solution.py:45
  762.9 33.9 %maximum_maximum_fusion = bf16[2048,2048]{1,0:T(8,128)(2,1)} fusion(bf16[512,640]{1,0:T(8,128)(2,1)S(1)} %get-tuple-element.241, bf16[512,640]{1,0:T(8,128)(2,1)S(1)} %get-tuple-element.240, bf16[512,640]{1,0:T(8,128)(2,1)S(1)} %get-tuple-element.239, bf16[512,640]{1,0:T(8,128)(2,1)S(1)} %get-tuple-element.238, bf16[512,1408]{1,0:T(8,128)(2,1)S(1)} %get-tuple-element.229, ...), kind=kLoop, calls=%fused_computation.38 | loop fusion | flops 67108864 | bytes 16777216 | tf_op jit(solution)/shard_map/concatenate | solution.py:317
  820.4 33.2 %fusion.170 = f32[2048,3072]{1,0:T(8,128)} fusion(bf16[2048,3072]{1,0:T(8,128)(2,1)} %constant_dynamic-update-slice_fusion.3, bf16[512,2048]{1,0:T(8,128)(2,1)S(1)} %get-tuple-element.217, bf16[512,2048]{1,0:T(8,128)(2,1)S(1)} %get-tuple-element.216, bf16[512,2048]{1,0:T(8,128)(2,1)S(1)} %get-tuple-element.215, bf16[512,2048]{1,0:T(8,128)(2,1)S(1)} %get-tuple-element.214), kind=kOutput, calls=%fused_computation.330 | convolution fusion | flops 25803358208 | bytes 46137344 | tf_op jit(solution)/shard_map/dot_general | solution.py:304
  853.6 38.0 %fusion.9 = (bf16[2048,1536]{1,0:T(8,128)(2,1)}, bf16[2048,1536]{1,0:T(8,128)(2,1)}, bf16[2048,1536]{1,0:T(8,128)(2,1)}) fusion(f32[2048,3072]{1,0:T(8,128)} %fusion.170, bf16[1536,2048]{1,0:T(8,128)(2,1)} %all-gather.21.cloned.1.call-done, bf16[512,640]{1,0:T(8,128)(2,1)} %copy-done.72, bf16[512,640]{1,0:T(8,128)(2,1)} %copy-done.71, ...), kind=kOutput, calls=%fused_computation.16 | convolution fusion | flops 13002342400 | bytes 58720256 | tf_op jit(solution)/shard_map/dot_general | solution.py:318
  891.5 34.3 %fusion.169 = f32[2048,2048]{1,0:T(8,128)} fusion(bf16[2048,3072]{1,0:T(8,128)(2,1)} %constant_dynamic-update-slice_fusion.3, bf16[2048,1536]{1,0:T(8,128)(2,1)} %get-tuple-element.192, bf16[2048,1536]{1,0:T(8,128)(2,1)} %get-tuple-element.191), kind=kOutput, calls=%fused_computation.329 | convolution fusion | flops 25794969600 | bytes 41943040 | tf_op jit(solution)/shard_map/dot_general | solution.py:327
  945.7 43.8 %collective-permute-done.36 = bf16[512,2048]{1,0:T(8,128)(2,1)S(1)} collective-permute-done((bf16[512,2048]{1,0:T(8,128)(2,1)S(1)}, bf16[512,2048]{1,0:T(8,128)(2,1)S(1)}, u32[]{:S(2)}, u32[]{:S(2)}) %collective-permute-start.36) | collective-permute-done | bytes 2097184 | tf_op jit(solution)/shard_map/ppermute | solution.py:68
  996.0 42.5 %collective-permute-done.37 = bf16[512,2048]{1,0:T(8,128)(2,1)} collective-permute-done((bf16[512,2048]{1,0:T(8,128)(2,1)S(1)}, bf16[512,2048]{1,0:T(8,128)(2,1)}, u32[]{:S(2)}, u32[]{:S(2)}) %collective-permute-start.37) | collective-permute-done | bytes 2097184 | tf_op jit(solution)/shard_map/ppermute | solution.py:68
  1052.2 41.1 %collective-permute-done.38 = bf16[512,2048]{1,0:T(8,128)(2,1)S(1)} collective-permute-done((bf16[512,2048]{1,0:T(8,128)(2,1)}, bf16[512,2048]{1,0:T(8,128)(2,1)S(1)}, u32[]{:S(2)}, u32[]{:S(2)}) %collective-permute-start.38) | collective-permute-done | bytes 2097184 | tf_op jit(solution)/shard_map/ppermute | solution.py:68
  1093.3 46.5 %collective-permute-done.41 = bf16[512,2048]{1,0:T(8,128)(2,1)S(1)} collective-permute-done((bf16[512,2048]{1,0:T(8,128)(2,1)S(1)}, bf16[512,2048]{1,0:T(8,128)(2,1)S(1)}, u32[]{:S(2)}, u32[]{:S(2)}) %collective-permute-start.41) | collective-permute-done | bytes 2097184 | tf_op jit(solution)/shard_map/ppermute | solution.py:69
  1157.8 33.8 %collective-permute-done.42 = bf16[512,2048]{1,0:T(8,128)(2,1)S(1)} collective-permute-done((bf16[512,2048]{1,0:T(8,128)(2,1)}, bf16[512,2048]{1,0:T(8,128)(2,1)S(1)}, u32[]{:S(2)}, u32[]{:S(2)}) %collective-permute-start.42) | collective-permute-done | bytes 2097184 | tf_op jit(solution)/shard_map/ppermute | solution.py:44
  1197.2 32.9 %fusion.177 = bf16[2048,3072]{1,0:T(8,128)(2,1)} fusion(bf16[2048,2048]{1,0:T(8,128)(2,1)} %pad_maximum_fusion.2, bf16[2048,3072]{1,0:T(8,128)(2,1)} %pad_maximum_fusion), kind=kOutput, calls=%fused_computation.337 | convolution fusion | flops 25769803776 | bytes 33554432 | tf_op jit(solution)/shard_map/dot_general | solution.py:332
  1243.4 19.4 %fusion.178 = bf16[1536,2048]{1,0:T(8,128)(2,1)} fusion(bf16[2048,1536]{1,0:T(8,128)(2,1)} %get-tuple-element.193, bf16[2048,2048]{1,0:T(8,128)(2,1)} %maximum_maximum_fusion), kind=kOutput, calls=%fused_computation.338 | convolution fusion | flops 12884901888 | bytes 20971520 | tf_op jit(solution)/shard_map/dot_general | solution.py:331
  1262.8 24.1 %collective-permute-done.47 = bf16[512,2048]{1,0:T(8,128)(2,1)} collective-permute-done((bf16[512,2048]{1,0:T(8,128)(2,1)}, bf16[512,2048]{1,0:T(8,128)(2,1)}, u32[]{:S(2)}, u32[]{:S(2)}) %collective-permute-start.47) | collective-permute-done | bytes 2097184 | tf_op jit(solution)/shard_map/ppermute | solution.py:45
  1470.8 17.3 fusion.176
  1491.3 24.5 %collective-permute-done.48 = bf16[512,2048]{1,0:T(8,128)(2,1)} collective-permute-done((bf16[512,2048]{1,0:T(8,128)(2,1)}, bf16[512,2048]{1,0:T(8,128)(2,1)}, u32[]{:S(2)}, u32[]{:S(2)}) %collective-permute-start.48) | collective-permute-done | bytes 2097184 | tf_op jit(solution)/shard_map/ppermute | solution.py:68
  1527.1 33.5 %collective-permute-done.18 = bf16[512,2048]{1,0:T(8,128)(2,1)S(1)} collective-permute-done((bf16[512,2048]{1,0:T(8,128)(2,1)S(1)}, bf16[512,2048]{1,0:T(8,128)(2,1)S(1)}, u32[]{:S(2)}, u32[]{:S(2)}) %collective-permute-start.18) | collective-permute-done | bytes 2097184 | tf_op jit(solution)/shard_map/ppermute | solution.py:68
  1569.7 35.8 %collective-permute-done.49 = bf16[512,2048]{1,0:T(8,128)(2,1)} collective-permute-done((bf16[512,2048]{1,0:T(8,128)(2,1)S(1)}, bf16[512,2048]{1,0:T(8,128)(2,1)}, u32[]{:S(2)}, u32[]{:S(2)}) %collective-permute-start.49) | collective-permute-done | bytes 2097184 | tf_op jit(solution)/shard_map/ppermute | solution.py:68
  1616.1 27.8 %collective-permute-done.19 = bf16[512,2048]{1,0:T(8,128)(2,1)} collective-permute-done((bf16[512,2048]{1,0:T(8,128)(2,1)}, bf16[512,2048]{1,0:T(8,128)(2,1)}, u32[]{:S(2)}, u32[]{:S(2)}) %collective-permute-start.19) | collective-permute-done | bytes 2097184 | tf_op jit(solution)/shard_map/ppermute | solution.py:68
  1684.4 17.7 collective-permute-done.50
  1731.0 47.0 %all-reduce.10 = (f32[256]{0:T(256)}, f32[16]{0:T(128)}, f32[16]{0:T(128)}, f32[256]{0:T(256)}) all-reduce(f32[256]{0:T(256)S(1)} %dynamic-slice_convert_fusion.11, f32[16]{0:T(128)S(1)} %dynamic-slice_convert_fusion.10, f32[16]{0:T(128)S(1)} %dynamic-slice_convert_fusion.9, ...), channel_id=1, replica_groups=mesh['dp'=8,'tensor'=4] {'tensor'}, use_global_device_ids=true, to_apply=%region_24.25 | all-reduce | flops 544 | bytes 4352 | tf_op jit(solution)/shard_map/psum | solution.py:445
  (635 shorter events, 660.3 us)
Async XLA Ops:
  7.2 138.2 %all-gather.9.cloned.1.call-start = ((), (), s32[]{:S(2)}) async-start(), calls=%async_computation.6 | async-start | bytes 2359296 | tf_op jit(solution)/shard_map/all_gather | solution.py:239
  9.2 139.2 %all-gather.11.cloned.1.call-start = ((), (), s32[]{:S(2)}) async-start(), calls=%async_computation.7 | async-start | bytes 1179648 | tf_op jit(solution)/shard_map/all_gather | solution.py:240
  10.9 139.8 %all-gather.13.cloned.1.call-start = ((), (), s32[]{:S(2)}) async-start(), calls=%async_computation.8 | async-start | bytes 1179648 | tf_op jit(solution)/shard_map/all_gather | solution.py:241
  12.6 261.7 %all-gather.15.cloned.1.call-start = ((), (), s32[]{:S(2)}) async-start(), calls=%async_computation.9 | async-start | bytes 2359296 | tf_op jit(solution)/shard_map/all_gather | solution.py:242
  14.4 782.4 %all-gather.17.cloned.1.call-start = ((), (), s32[]{:S(2)}) async-start(), calls=%async_computation.10 | async-start | bytes 7077888 | tf_op jit(solution)/shard_map/all_gather | solution.py:292
  37.6 765.1 %all-gather.19.cloned.1.call-start = ((), (), s32[]{:S(2)}) async-start(), calls=%async_computation.11 | async-start | bytes 7077888 | tf_op jit(solution)/shard_map/all_gather | solution.py:293
  345.6 508.0 %all-gather.21.cloned.1.call-start = ((), (), s32[]{:S(2)}) async-start(), calls=%async_computation.12 | async-start | bytes 7077888 | tf_op jit(solution)/shard_map/all_gather | solution.py:294
  406.0 90.1 %collective-permute-start.11 = (bf16[512,2048]{1,0:T(8,128)(2,1)}, bf16[512,2048]{1,0:T(8,128)(2,1)}, u32[]{:S(2)}, u32[]{:S(2)}) collective-permute-start(bf16[512,2048]{1,0:T(8,128)(2,1)} %add_convert_fusion.13), channel_id=1, source_target_pairs={{1,0},{2,1},{3,2},{5,4},{6,5},{7,6},{9,8},{10,9},{11,10},{13,12},{... | collective-permute-start | bytes 6291464 | tf_op jit(solution)/shard_map/ppermute | solution.py:69
  409.2 92.8 %collective-permute-start.30 = (bf16[512,640]{1,0:T(8,128)(2,1)}, bf16[512,640]{1,0:T(8,128)(2,1)S(1)}, u32[]{:S(2)}, u32[]{:S(2)}) collective-permute-start(bf16[512,640]{1,0:T(8,128)(2,1)} %slice.396), channel_id=1, source_target_pairs={{0,3},{4,7},{8,11},{12,15},{16,19},{20,23},{24,27},{28,31}} | collective-permute-start | bytes 1966088 | tf_op jit(solution)/shard_map/ppermute | solution.py:82
  504.0 132.6 %collective-permute-start.12 = (bf16[512,2048]{1,0:T(8,128)(2,1)S(1)}, bf16[512,2048]{1,0:T(8,128)(2,1)}, u32[]{:S(2)}, u32[]{:S(2)}) collective-permute-start(bf16[512,2048]{1,0:T(8,128)(2,1)S(1)} %multiply_convert_fusion.2), channel_id=1, source_target_pairs={{0,1},{1,2},{2,3},{4,5},{5,6},{6,7},{8,9},{9,10},{10,11},{12,13},{... | collective-permute-start | bytes 6291464 | tf_op jit(solution)/shard_map/ppermute | solution.py:44
  508.8 129.8 %collective-permute-start.15 = (bf16[512,2048]{1,0:T(8,128)(2,1)S(1)}, bf16[512,2048]{1,0:T(8,128)(2,1)}, u32[]{:S(2)}, u32[]{:S(2)}) collective-permute-start(bf16[512,2048]{1,0:T(8,128)(2,1)S(1)} %multiply_convert_fusion.2), channel_id=1, source_target_pairs={{1,0},{2,1},{3,2},{5,4},{6,5},{7,6},{9,8},{10,9},{11,10},{13,12},{... | collective-permute-start | bytes 6291464 | tf_op jit(solution)/shard_map/ppermute | solution.py:45
  510.3 74.2 %collective-permute-start.24 = (bf16[512,1408]{1,0:T(8,128)(2,1)S(1)}, bf16[512,1408]{1,0:T(8,128)(2,1)S(1)}, u32[]{:S(2)}, u32[]{:S(2)}) collective-permute-start(bf16[512,1408]{1,0:T(8,128)(2,1)S(1)} %slice.395), channel_id=1, source_target_pairs={{0,3},{4,7},{8,11},{12,15},{16,19},{20,23},{24,27},{28,31}} | collective-permute-start | bytes 4325384 | tf_op jit(solution)/shard_map/ppermute | solution.py:82
  555.3 80.0 %collective-permute-start.26 = (bf16[512,1408]{1,0:T(8,128)(2,1)S(1)}, bf16[512,1408]{1,0:T(8,128)(2,1)S(1)}, u32[]{:S(2)}, u32[]{:S(2)}) collective-permute-start(bf16[512,1408]{1,0:T(8,128)(2,1)S(1)} %slice.395), channel_id=1, source_target_pairs={{0,1},{1,2},{2,3},{4,5},{5,6},{6,7},{8,9},{9,10},{10,11},{12,13},{... | collective-permute-start | bytes 4325384 | tf_op jit(solution)/shard_map/ppermute | solution.py:82
  615.4 105.1 %collective-permute-start.28 = (bf16[512,1408]{1,0:T(8,128)(2,1)S(1)}, bf16[512,1408]{1,0:T(8,128)(2,1)}, u32[]{:S(2)}, u32[]{:S(2)}) collective-permute-start(bf16[512,1408]{1,0:T(8,128)(2,1)S(1)} %slice.395), channel_id=1, source_target_pairs={{2,0},{3,1},{6,4},{7,5},{10,8},{11,9},{14,12},{15,13},{18,16},{19,... | collective-permute-start | bytes 4325384 | tf_op jit(solution)/shard_map/ppermute | solution.py:83
  635.3 85.2 %collective-permute-start.29 = (bf16[512,1408]{1,0:T(8,128)(2,1)S(1)}, bf16[512,1408]{1,0:T(8,128)(2,1)}, u32[]{:S(2)}, u32[]{:S(2)}) collective-permute-start(bf16[512,1408]{1,0:T(8,128)(2,1)S(1)} %slice.395), channel_id=1, source_target_pairs={{3,0},{7,4},{11,8},{15,12},{19,16},{23,20},{27,24},{31,28}} | collective-permute-start | bytes 4325384 | tf_op jit(solution)/shard_map/ppermute | solution.py:83
  636.6 86.7 %collective-permute-start.13 = (bf16[512,2048]{1,0:T(8,128)(2,1)}, bf16[512,2048]{1,0:T(8,128)(2,1)}, u32[]{:S(2)}, u32[]{:S(2)}) collective-permute-start(bf16[512,2048]{1,0:T(8,128)(2,1)} %collective-permute-done.12), channel_id=1, source_target_pairs={{1,2},{2,3},{5,6},{6,7},{9,10},{10,11},{13,14},{14,15},{17,18},{18... | collective-permute-start | bytes 6291464 | tf_op jit(solution)/shard_map/ppermute | solution.py:44
  638.6 123.0 %collective-permute-start.16 = (bf16[512,2048]{1,0:T(8,128)(2,1)}, bf16[512,2048]{1,0:T(8,128)(2,1)}, u32[]{:S(2)}, u32[]{:S(2)}) collective-permute-start(bf16[512,2048]{1,0:T(8,128)(2,1)} %collective-permute-done.15), channel_id=1, source_target_pairs={{1,0},{2,1},{5,4},{6,5},{9,8},{10,9},{13,12},{14,13},{17,16},{18,1... | collective-permute-start | bytes 6291464 | tf_op jit(solution)/shard_map/ppermute | solution.py:45
  640.9 1036.5 %reduce-scatter.9.cloned.1.call-start = ((), (), s32[]{:S(2)}) async-start(), calls=%async_computation.14 | async-start | bytes 1179648 | tf_op jit(solution)/shard_map/reduce_scatter | solution.py:411
  723.3 85.6 %collective-permute-start.14 = (bf16[512,2048]{1,0:T(8,128)(2,1)}, bf16[512,2048]{1,0:T(8,128)(2,1)S(1)}, u32[]{:S(2)}, u32[]{:S(2)}) collective-permute-start(bf16[512,2048]{1,0:T(8,128)(2,1)} %collective-permute-done.13), channel_id=1, source_target_pairs={{2,3},{6,7},{10,11},{14,15},{18,19},{22,23},{26,27},{30,31}} | collective-permute-start | bytes 6291464 | tf_op jit(solution)/shard_map/ppermute | solution.py:44
  1050.8 89.0 %collective-permute-start.41 = (bf16[512,2048]{1,0:T(8,128)(2,1)S(1)}, bf16[512,2048]{1,0:T(8,128)(2,1)S(1)}, u32[]{:S(2)}, u32[]{:S(2)}) collective-permute-start(bf16[512,2048]{1,0:T(8,128)(2,1)S(1)} %add_convert_fusion.4), channel_id=1, source_target_pairs={{1,0},{2,1},{3,2},{5,4},{6,5},{7,6},{9,8},{10,9},{11,10},{13,12},{... | collective-permute-start | bytes 6291464 | tf_op jit(solution)/shard_map/ppermute | solution.py:69
  1443.0 236.1 %reduce-scatter.11.cloned.1.call-start = ((), (), s32[]{:S(2)}) async-start(), calls=%async_computation.15 | async-start | bytes 1179648 | tf_op jit(solution)/shard_map/reduce_scatter | solution.py:417
  1443.7 237.0 %reduce-scatter.7.cloned.1.call-start = ((), (), s32[]{:S(2)}) async-start(), calls=%async_computation.13 | async-start | bytes 2359296 | tf_op jit(solution)/shard_map/reduce_scatter | solution.py:408
  1447.0 235.5 %reduce-scatter.13.cloned.1.call-start = ((), (), s32[]{:S(2)}) async-start(), calls=%async_computation.16 | async-start | bytes 2359296 | tf_op jit(solution)/shard_map/reduce_scatter | solution.py:365
  1447.8 342.4 %reduce-scatter.17.cloned.1.call-start = ((), (), s32[]{:S(2)}) async-start(), calls=%async_computation.18 | async-start | bytes 7077888 | tf_op jit(solution)/shard_map/reduce_scatter | solution.py:370
  1448.3 344.2 %reduce-scatter.15.cloned.1.call-start = ((), (), s32[]{:S(2)}) async-start(), calls=%async_computation.17 | async-start | bytes 14155776 | tf_op jit(solution)/shard_map/reduce_scatter | solution.py:361
  1488.8 71.8 %collective-permute-start.18 = (bf16[512,2048]{1,0:T(8,128)(2,1)S(1)}, bf16[512,2048]{1,0:T(8,128)(2,1)S(1)}, u32[]{:S(2)}, u32[]{:S(2)}) collective-permute-start(bf16[512,2048]{1,0:T(8,128)(2,1)S(1)} %get-tuple-element.204), channel_id=1, source_target_pairs={{0,1},{4,5},{8,9},{12,13},{16,17},{20,21},{24,25},{28,29}} | collective-permute-start | bytes 6291464 | tf_op jit(solution)/shard_map/ppermute | solution.py:68
  1490.3 78.1 %collective-permute-start.51 = (bf16[512,2048]{1,0:T(8,128)(2,1)S(1)}, bf16[512,2048]{1,0:T(8,128)(2,1)S(1)}, u32[]{:S(2)}, u32[]{:S(2)}) collective-permute-start(bf16[512,2048]{1,0:T(8,128)(2,1)S(1)} %get-tuple-element.197), channel_id=1, source_target_pairs={{3,2},{7,6},{11,10},{15,14},{19,18},{23,22},{27,26},{31,30}} | collective-permute-start | bytes 6291464 | tf_op jit(solution)/shard_map/ppermute | solution.py:69
  1519.3 86.3 %collective-permute-start.49 = (bf16[512,2048]{1,0:T(8,128)(2,1)S(1)}, bf16[512,2048]{1,0:T(8,128)(2,1)}, u32[]{:S(2)}, u32[]{:S(2)}) collective-permute-start(bf16[512,2048]{1,0:T(8,128)(2,1)S(1)} %add_convert_fusion.3), channel_id=1, source_target_pairs={{0,1},{1,2},{4,5},{5,6},{8,9},{9,10},{12,13},{13,14},{16,17},{17,1... | collective-permute-start | bytes 6291464 | tf_op jit(solution)/shard_map/ppermute | solution.py:68
  1525.1 91.0 %collective-permute-start.21 = (bf16[512,2048]{1,0:T(8,128)(2,1)S(1)}, bf16[512,2048]{1,0:T(8,128)(2,1)}, u32[]{:S(2)}, u32[]{:S(2)}) collective-permute-start(bf16[512,2048]{1,0:T(8,128)(2,1)S(1)} %get-tuple-element.205), channel_id=1, source_target_pairs={{3,2},{7,6},{11,10},{15,14},{19,18},{23,22},{27,26},{31,30}} | collective-permute-start | bytes 6291464 | tf_op jit(solution)/shard_map/ppermute | solution.py:69
  1562.7 81.2 %collective-permute-start.19 = (bf16[512,2048]{1,0:T(8,128)(2,1)}, bf16[512,2048]{1,0:T(8,128)(2,1)}, u32[]{:S(2)}, u32[]{:S(2)}) collective-permute-start(bf16[512,2048]{1,0:T(8,128)(2,1)} %add_convert_fusion.12), channel_id=1, source_target_pairs={{0,1},{1,2},{4,5},{5,6},{8,9},{9,10},{12,13},{13,14},{16,17},{17,1... | collective-permute-start | bytes 6291464 | tf_op jit(solution)/shard_map/ppermute | solution.py:68
  1663.7 114.3 %collective-permute-start.20 = (bf16[512,2048]{1,0:T(8,128)(2,1)}, bf16[512,2048]{1,0:T(8,128)(2,1)}, u32[]{:S(2)}, u32[]{:S(2)}) collective-permute-start(bf16[512,2048]{1,0:T(8,128)(2,1)} %get-tuple-element.202), channel_id=1, source_target_pairs={{0,1},{1,2},{2,3},{4,5},{5,6},{6,7},{8,9},{9,10},{10,11},{12,13},{... | collective-permute-start | bytes 6291464 | tf_op jit(solution)/shard_map/ppermute | solution.py:68
  1674.2 103.8 %collective-permute-start.23 = (bf16[512,2048]{1,0:T(8,128)(2,1)}, bf16[512,2048]{1,0:T(8,128)(2,1)}, u32[]{:S(2)}, u32[]{:S(2)}) collective-permute-start(bf16[512,2048]{1,0:T(8,128)(2,1)} %add_convert_fusion.9), channel_id=1, source_target_pairs={{1,0},{2,1},{3,2},{5,4},{6,5},{7,6},{9,8},{10,9},{11,10},{13,12},{... | collective-permute-start | bytes 6291464 | tf_op jit(solution)/shard_map/ppermute | solution.py:69
  (200 other events, 6735.4 us)
Sparse Core Ops, SparseCore 0:
  10.5 30.5 all-gather.8
  43.5 23.3 all-gather.10
  69.3 23.3 all-gather.12
  95.0 28.0 all-gather.14
  124.9 45.3 all-gather.16
  345.7 42.6 all-gather.18
  641.1 93.5 all-gather.20
  1443.1 33.4 reduce-scatter.8
  1480.3 35.9 reduce-scatter.10
  1519.5 41.0 reduce-scatter.6
  1563.9 41.1 reduce-scatter.12
  1608.3 61.5 reduce-scatter.16
  1673.4 93.1 reduce-scatter.14

commit v10 on v7

--- a/solution.py
+++ b/solution.py
@@ -192,10 +192,6 @@
         block_lse = log_totals[index]
         q_rows = query_tensor[row_start:key_end]
         g_rows = grad_rows[row_start:key_end]
-        if index > 0:
-            q_rows, g_rows, block_lse, d_key, d_value = lax.optimization_barrier(
-                (q_rows, g_rows, block_lse, d_key, d_value)
-            )
         keys = key_rows[:key_end]
         values = value_tensor[:key_end]
         allowed = block_mask(seq_starts, seq_pieces, row_start, QB)[:, :key_end]
@@ -279,8 +275,8 @@
     attn_g = ga_b.astype(f32)
     query_norm_gain = gq_b.astype(f32)
     gain_k = gk_b.astype(f32)
-    gathered_tokens = tensor_gather(tokens, tensor_n)
-    gathered = rms_scale(gathered_tokens.astype(f32), attn_g).astype(bf16)
+    normalized_input = rms_scale(tok_rows, attn_g).astype(bf16)
+    gathered = tensor_gather(normalized_input, tensor_n)
     half_width = (out_grad.shape[1] * 11 // 16) // 128 * 128
     grad_half_a = tensor_gather_direct(out_grad[:, :half_width], tensor_n)
     projected = jnp.dot(gathered, w_qkv, preferred_element_type=f32)

time: 1840 us -> 1880 us (1.022)
  waiting for transfers between devices: 795 us -> 814 us
    unnamed x357 -> x343, local copies, waits for them, and re-layouts: 42.4 us -> 39.6 us
where the time goes in v10:
time: 1880 us; the launch traced here: 1850 us
  waiting for transfers between devices  814 us (43%)
  matrix products  353 us (19%)
  starting transfers between devices  282 us (15%)
  other arithmetic  233 us (12%)
  local copies, waits for them, and re-layouts  103 us (5%)
  blocking collectives  41.9 us (2%)
    ppermute x9, waiting for transfers between devices, tensor_scatter(): lax.ppermute(acc_up.astype(jnp.bfloat16), 'tensor', [(i, i + 1) for i in...  281 us
    ppermute x9, waiting for transfers between devices, tensor_gather(): lax.ppermute(down, 'tensor', [(i, i - 1) for i in range(1, n - s + 1)])  146 us
    ppermute x9, waiting for transfers between devices, tensor_scatter(): lax.ppermute(acc_down.astype(jnp.bfloat16), 'tensor', [(i, i - 1) for i i...  116 us
    ppermute x6, waiting for transfers between devices, tensor_gather_direct(): downs[d] = lax.ppermute(rows, 'tensor', [(i, i - d) for i in range(d, n)])  113 us
    ppermute x3, starting transfers between devices, tensor_scatter_direct(): lax.ppermute(block(jnp.minimum(j + d, n - 1)).astype(jnp.bfloat16), 'tens...  112 us
    ppermute x9, waiting for transfers between devices, tensor_gather(): up = lax.ppermute(up, 'tensor', [(i, i + 1) for i in range(s - 1, n - 1)])  80 us
    ppermute x6, waiting for transfers between devices, tensor_gather_direct(): ups[d] = lax.ppermute(rows, 'tensor', [(i, i + d) for i in range(n - d)])  76.3 us
    ppermute x6, starting transfers between devices, tensor_gather_direct(): ups[d] = lax.ppermute(rows, 'tensor', [(i, i + d) for i in range(n - d)])  62 us
  transfers between devices with their start and end apart: 67, of which 25 were waited for; matrix products, arithmetic and copies ran while one was open for 22% of the time, Pallas kernels for 0%

profile of v10, /device:TPU:0, one launch (start us, length us, event | category | flops | bytes accessed | tf_op | source)
XLA Modules:
  0.0 1845.5 jit_solution(17741166481811663042)
XLA Ops:
  38.1 41.5 %collective-permute-done = bf16[512,2048]{1,0:T(8,128)(2,1)} collective-permute-done((bf16[512,2048]{1,0:T(8,128)(2,1)}, bf16[512,2048]{1,0:T(8,128)(2,1)}, u32[]{:S(2)}, u32[]{:S(2)}) %collective-permute-start) | collective-permute-done | bytes 2097184 | tf_op jit(solution)/shard_map/ppermute | solution.py:44
  94.4 39.8 %collective-permute-done.4 = bf16[512,2048]{1,0:T(8,128)(2,1)} collective-permute-done((bf16[512,2048]{1,0:T(8,128)(2,1)}, bf16[512,2048]{1,0:T(8,128)(2,1)}, u32[]{:S(2)}, u32[]{:S(2)}) %collective-permute-start.4) | collective-permute-done | bytes 2097184 | tf_op jit(solution)/shard_map/ppermute | solution.py:45
  153.7 28.8 %collective-permute-done.5 = bf16[512,2048]{1,0:T(8,128)(2,1)} collective-permute-done((bf16[512,2048]{1,0:T(8,128)(2,1)}, bf16[512,2048]{1,0:T(8,128)(2,1)}, u32[]{:S(2)}, u32[]{:S(2)}) %collective-permute-start.5) | collective-permute-done | bytes 2097184 | tf_op jit(solution)/shard_map/ppermute | solution.py:45
  301.4 39.9 %collective-permute-done.6 = bf16[512,2048]{1,0:T(8,128)(2,1)} collective-permute-done((bf16[512,2048]{1,0:T(8,128)(2,1)}, bf16[512,2048]{1,0:T(8,128)(2,1)}, u32[]{:S(2)}, u32[]{:S(2)}) %collective-permute-start.6) | collective-permute-done | bytes 2097184 | tf_op jit(solution)/shard_map/ppermute | solution.py:68
  353.0 40.1 %collective-permute-done.7 = bf16[512,2048]{1,0:T(8,128)(2,1)} collective-permute-done((bf16[512,2048]{1,0:T(8,128)(2,1)}, bf16[512,2048]{1,0:T(8,128)(2,1)}, u32[]{:S(2)}, u32[]{:S(2)}) %collective-permute-start.7) | collective-permute-done | bytes 2097184 | tf_op jit(solution)/shard_map/ppermute | solution.py:68
  416.8 46.7 %collective-permute-start.30 = (bf16[512,640]{1,0:T(8,128)(2,1)}, bf16[512,640]{1,0:T(8,128)(2,1)S(1)}, u32[]{:S(2)}, u32[]{:S(2)}) collective-permute-start(bf16[512,640]{1,0:T(8,128)(2,1)} %slice.396), channel_id=1, source_target_pairs={{0,3},{4,7},{8,11},{12,15},{16,19},{20,23},{24,27},{28,31}} | collective-permute-start | bytes 1966088 | tf_op jit(solution)/shard_map/ppermute | solution.py:82
  469.7 33.9 %collective-permute-done.11 = bf16[512,2048]{1,0:T(8,128)(2,1)} collective-permute-done((bf16[512,2048]{1,0:T(8,128)(2,1)}, bf16[512,2048]{1,0:T(8,128)(2,1)}, u32[]{:S(2)}, u32[]{:S(2)}) %collective-permute-start.11) | collective-permute-done | bytes 2097184 | tf_op jit(solution)/shard_map/ppermute | solution.py:69
  526.6 34.6 %collective-permute-done.34 = bf16[512,640]{1,0:T(8,128)(2,1)S(1)} collective-permute-done((bf16[512,640]{1,0:T(8,128)(2,1)}, bf16[512,640]{1,0:T(8,128)(2,1)S(1)}, u32[]{:S(2)}, u32[]{:S(2)}) %collective-permute-start.34) | collective-permute-done | bytes 655392 | tf_op jit(solution)/shard_map/ppermute | solution.py:83
  564.2 28.9 %collective-permute-done.24 = bf16[512,1408]{1,0:T(8,128)(2,1)S(1)} collective-permute-done((bf16[512,1408]{1,0:T(8,128)(2,1)S(1)}, bf16[512,1408]{1,0:T(8,128)(2,1)S(1)}, u32[]{:S(2)}, u32[]{:S(2)}) %collective-permute-start.24) | collective-permute-done | bytes 1441824 | tf_op jit(solution)/shard_map/ppermute | solution.py:82
  594.4 29.6 %collective-permute-done.25 = bf16[512,1408]{1,0:T(8,128)(2,1)S(1)} collective-permute-done((bf16[512,1408]{1,0:T(8,128)(2,1)S(1)}, bf16[512,1408]{1,0:T(8,128)(2,1)S(1)}, u32[]{:S(2)}, u32[]{:S(2)}) %collective-permute-start.25) | collective-permute-done | bytes 1441824 | tf_op jit(solution)/shard_map/ppermute | solution.py:82
  625.3 17.8 collective-permute-done.26
  651.4 78.0 %collective-permute-done.28 = bf16[512,1408]{1,0:T(8,128)(2,1)} collective-permute-done((bf16[512,1408]{1,0:T(8,128)(2,1)S(1)}, bf16[512,1408]{1,0:T(8,128)(2,1)}, u32[]{:S(2)}, u32[]{:S(2)}) %collective-permute-start.28) | collective-permute-done | bytes 1441824 | tf_op jit(solution)/shard_map/ppermute | solution.py:83
  733.1 36.1 %collective-permute-done.16 = bf16[512,2048]{1,0:T(8,128)(2,1)} collective-permute-done((bf16[512,2048]{1,0:T(8,128)(2,1)}, bf16[512,2048]{1,0:T(8,128)(2,1)}, u32[]{:S(2)}, u32[]{:S(2)}) %collective-permute-start.16) | collective-permute-done | bytes 2097184 | tf_op jit(solution)/shard_map/ppermute | solution.py:45
  770.5 33.9 %maximum_maximum_fusion = bf16[2048,2048]{1,0:T(8,128)(2,1)} fusion(bf16[512,640]{1,0:T(8,128)(2,1)S(1)} %get-tuple-element.213, bf16[512,640]{1,0:T(8,128)(2,1)S(1)} %get-tuple-element.212, bf16[512,640]{1,0:T(8,128)(2,1)S(1)} %get-tuple-element.211, bf16[512,640]{1,0:T(8,128)(2,1)S(1)} %get-tuple-element.210, bf16[512,1408]{1,0:T(8,128)(2,1)S(1)} %get-tuple-element.201, ...), kind=kLoop, calls=%fused_computation.38 | loop fusion | flops 67108864 | bytes 16777216 | tf_op jit(solution)/shard_map/concatenate | solution.py:338
  827.7 33.6 %fusion.179 = f32[2048,3072]{1,0:T(8,128)} fusion(bf16[2048,3072]{1,0:T(8,128)(2,1)} %constant_dynamic-update-slice_fusion.3, bf16[512,2048]{1,0:T(8,128)(2,1)S(1)} %get-tuple-element.189, bf16[512,2048]{1,0:T(8,128)(2,1)S(1)} %get-tuple-element.188, bf16[512,2048]{1,0:T(8,128)(2,1)S(1)} %get-tuple-element.187, bf16[512,2048]{1,0:T(8,128)(2,1)S(1)} %get-tuple-element.186), kind=kOutput, calls=%fused_computation.337 | convolution fusion | flops 25803358208 | bytes 46137344 | tf_op jit(solution)/shard_map/dot_general | solution.py:325
  861.3 37.8 %fusion.9 = (bf16[2048,1536]{1,0:T(8,128)(2,1)}, bf16[2048,1536]{1,0:T(8,128)(2,1)}, bf16[2048,1536]{1,0:T(8,128)(2,1)}) fusion(f32[2048,3072]{1,0:T(8,128)} %fusion.179, bf16[1536,2048]{1,0:T(8,128)(2,1)} %all-gather.21.cloned.1.call-done, bf16[512,640]{1,0:T(8,128)(2,1)} %copy-done.67, bf16[512,640]{1,0:T(8,128)(2,1)} %copy-done.66, ...), kind=kOutput, calls=%fused_computation.16 | convolution fusion | flops 13002342400 | bytes 58720256 | tf_op jit(solution)/shard_map/dot_general | solution.py:339
  899.1 34.3 %fusion.178 = f32[2048,2048]{1,0:T(8,128)} fusion(bf16[2048,3072]{1,0:T(8,128)(2,1)} %constant_dynamic-update-slice_fusion.3, bf16[2048,1536]{1,0:T(8,128)(2,1)} %get-tuple-element.162, bf16[2048,1536]{1,0:T(8,128)(2,1)} %get-tuple-element.161), kind=kOutput, calls=%fused_computation.336 | convolution fusion | flops 25794969600 | bytes 41943040 | tf_op jit(solution)/shard_map/dot_general | solution.py:348
  953.4 43.7 %collective-permute-done.36 = bf16[512,2048]{1,0:T(8,128)(2,1)S(1)} collective-permute-done((bf16[512,2048]{1,0:T(8,128)(2,1)S(1)}, bf16[512,2048]{1,0:T(8,128)(2,1)S(1)}, u32[]{:S(2)}, u32[]{:S(2)}) %collective-permute-start.36) | collective-permute-done | bytes 2097184 | tf_op jit(solution)/shard_map/ppermute | solution.py:68
  1003.6 42.5 %collective-permute-done.37 = bf16[512,2048]{1,0:T(8,128)(2,1)} collective-permute-done((bf16[512,2048]{1,0:T(8,128)(2,1)S(1)}, bf16[512,2048]{1,0:T(8,128)(2,1)}, u32[]{:S(2)}, u32[]{:S(2)}) %collective-permute-start.37) | collective-permute-done | bytes 2097184 | tf_op jit(solution)/shard_map/ppermute | solution.py:68
  1059.9 40.9 %collective-permute-done.38 = bf16[512,2048]{1,0:T(8,128)(2,1)S(1)} collective-permute-done((bf16[512,2048]{1,0:T(8,128)(2,1)}, bf16[512,2048]{1,0:T(8,128)(2,1)S(1)}, u32[]{:S(2)}, u32[]{:S(2)}) %collective-permute-start.38) | collective-permute-done | bytes 2097184 | tf_op jit(solution)/shard_map/ppermute | solution.py:68
  1100.8 46.5 %collective-permute-done.41 = bf16[512,2048]{1,0:T(8,128)(2,1)S(1)} collective-permute-done((bf16[512,2048]{1,0:T(8,128)(2,1)S(1)}, bf16[512,2048]{1,0:T(8,128)(2,1)S(1)}, u32[]{:S(2)}, u32[]{:S(2)}) %collective-permute-start.41) | collective-permute-done | bytes 2097184 | tf_op jit(solution)/shard_map/ppermute | solution.py:69
  1161.4 38.4 %collective-permute-done.42 = bf16[512,2048]{1,0:T(8,128)(2,1)} collective-permute-done((bf16[512,2048]{1,0:T(8,128)(2,1)S(1)}, bf16[512,2048]{1,0:T(8,128)(2,1)}, u32[]{:S(2)}, u32[]{:S(2)}) %collective-permute-start.42) | collective-permute-done | bytes 2097184 | tf_op jit(solution)/shard_map/ppermute | solution.py:44
  1206.8 32.9 %fusion.186 = bf16[2048,3072]{1,0:T(8,128)(2,1)} fusion(bf16[2048,2048]{1,0:T(8,128)(2,1)} %pad_maximum_fusion.2, bf16[2048,3072]{1,0:T(8,128)(2,1)} %pad_maximum_fusion), kind=kOutput, calls=%fused_computation.344 | convolution fusion | flops 25769803776 | bytes 33554432 | tf_op jit(solution)/shard_map/dot_general | solution.py:353
  1252.6 19.5 %fusion.187 = bf16[1536,2048]{1,0:T(8,128)(2,1)} fusion(bf16[2048,1536]{1,0:T(8,128)(2,1)} %get-tuple-element.163, bf16[2048,2048]{1,0:T(8,128)(2,1)} %maximum_maximum_fusion), kind=kOutput, calls=%fused_computation.345 | convolution fusion | flops 12884901888 | bytes 20971520 | tf_op jit(solution)/shard_map/dot_general | solution.py:352
  1272.1 23.1 %collective-permute-done.47 = bf16[512,2048]{1,0:T(8,128)(2,1)} collective-permute-done((bf16[512,2048]{1,0:T(8,128)(2,1)}, bf16[512,2048]{1,0:T(8,128)(2,1)}, u32[]{:S(2)}, u32[]{:S(2)}) %collective-permute-start.47) | collective-permute-done | bytes 2097184 | tf_op jit(solution)/shard_map/ppermute | solution.py:45
  1487.1 37.9 %collective-permute-done.48 = bf16[512,2048]{1,0:T(8,128)(2,1)S(1)} collective-permute-done((bf16[512,2048]{1,0:T(8,128)(2,1)S(1)}, bf16[512,2048]{1,0:T(8,128)(2,1)S(1)}, u32[]{:S(2)}, u32[]{:S(2)}) %collective-permute-start.48) | collective-permute-done | bytes 2097184 | tf_op jit(solution)/shard_map/ppermute | solution.py:68
  1531.5 36.3 %collective-permute-done.49 = bf16[512,2048]{1,0:T(8,128)(2,1)} collective-permute-done((bf16[512,2048]{1,0:T(8,128)(2,1)S(1)}, bf16[512,2048]{1,0:T(8,128)(2,1)}, u32[]{:S(2)}, u32[]{:S(2)}) %collective-permute-start.49) | collective-permute-done | bytes 2097184 | tf_op jit(solution)/shard_map/ppermute | solution.py:68
  1574.7 19.4 %fusion.185 = f32[2048,2048]{1,0:T(8,128)} fusion(bf16[2048,1536]{1,0:T(8,128)(2,1)} %get-tuple-element.163, bf16[1536,2048]{1,0:T(8,128)(2,1)} %all-gather.21.cloned.1.call-done), kind=kOutput, calls=%fused_computation.343 | convolution fusion | flops 12884901888 | bytes 29360128 | tf_op jit(solution)/shard_map/dot_general | solution.py:329
  1619.5 58.6 %collective-permute-start.22 = (bf16[512,2048]{1,0:T(8,128)(2,1)}, bf16[512,2048]{1,0:T(8,128)(2,1)}, u32[]{:S(2)}, u32[]{:S(2)}) collective-permute-start(bf16[512,2048]{1,0:T(8,128)(2,1)} %get-tuple-element.174), channel_id=1, source_target_pairs={{0,3},{4,7},{8,11},{12,15},{16,19},{20,23},{24,27},{28,31}} | collective-permute-start | bytes 6291464 | tf_op jit(solution)/shard_map/ppermute | solution.py:98
  1688.9 35.3 %collective-permute-done.53 = bf16[512,2048]{1,0:T(8,128)(2,1)} collective-permute-done((bf16[512,2048]{1,0:T(8,128)(2,1)S(1)}, bf16[512,2048]{1,0:T(8,128)(2,1)}, u32[]{:S(2)}, u32[]{:S(2)}) %collective-permute-start.53) | collective-permute-done | bytes 2097184 | tf_op jit(solution)/shard_map/ppermute | solution.py:69
  1724.2 45.6 %collective-permute-start.18 = (bf16[512,2048]{1,0:T(8,128)(2,1)}, bf16[512,2048]{1,0:T(8,128)(2,1)}, u32[]{:S(2)}, u32[]{:S(2)}) collective-permute-start(bf16[512,2048]{1,0:T(8,128)(2,1)} %get-tuple-element.172), channel_id=1, source_target_pairs={{0,1},{1,2},{2,3},{4,5},{5,6},{6,7},{8,9},{9,10},{10,11},{12,13},{... | collective-permute-start | bytes 6291464 | tf_op jit(solution)/shard_map/ppermute | solution.py:98
  1798.9 18.3 all-reduce.10
  (635 shorter events, 653.0 us)
Async XLA Ops:
  7.2 138.7 %all-gather.9.cloned.1.call-start = ((), (), s32[]{:S(2)}) async-start(), calls=%async_computation.6 | async-start | bytes 2359296 | tf_op jit(solution)/shard_map/all_gather | solution.py:260
  9.2 139.7 %all-gather.11.cloned.1.call-start = ((), (), s32[]{:S(2)}) async-start(), calls=%async_computation.7 | async-start | bytes 1179648 | tf_op jit(solution)/shard_map/all_gather | solution.py:261
  10.9 140.6 %all-gather.13.cloned.1.call-start = ((), (), s32[]{:S(2)}) async-start(), calls=%async_computation.8 | async-start | bytes 1179648 | tf_op jit(solution)/shard_map/all_gather | solution.py:262
  12.6 268.9 %all-gather.15.cloned.1.call-start = ((), (), s32[]{:S(2)}) async-start(), calls=%async_computation.9 | async-start | bytes 2359296 | tf_op jit(solution)/shard_map/all_gather | solution.py:263
  14.4 790.0 %all-gather.17.cloned.1.call-start = ((), (), s32[]{:S(2)}) async-start(), calls=%async_computation.10 | async-start | bytes 7077888 | tf_op jit(solution)/shard_map/all_gather | solution.py:313
  37.6 772.8 %all-gather.19.cloned.1.call-start = ((), (), s32[]{:S(2)}) async-start(), calls=%async_computation.11 | async-start | bytes 7077888 | tf_op jit(solution)/shard_map/all_gather | solution.py:314
  353.0 508.4 %all-gather.21.cloned.1.call-start = ((), (), s32[]{:S(2)}) async-start(), calls=%async_computation.12 | async-start | bytes 7077888 | tf_op jit(solution)/shard_map/all_gather | solution.py:315
  413.6 90.1 %collective-permute-start.11 = (bf16[512,2048]{1,0:T(8,128)(2,1)}, bf16[512,2048]{1,0:T(8,128)(2,1)}, u32[]{:S(2)}, u32[]{:S(2)}) collective-permute-start(bf16[512,2048]{1,0:T(8,128)(2,1)} %add_convert_fusion.9), channel_id=1, source_target_pairs={{1,0},{2,1},{3,2},{5,4},{6,5},{7,6},{9,8},{10,9},{11,10},{13,12},{... | collective-permute-start | bytes 6291464 | tf_op jit(solution)/shard_map/ppermute | solution.py:69
  416.8 92.8 %collective-permute-start.30 = (bf16[512,640]{1,0:T(8,128)(2,1)}, bf16[512,640]{1,0:T(8,128)(2,1)S(1)}, u32[]{:S(2)}, u32[]{:S(2)}) collective-permute-start(bf16[512,640]{1,0:T(8,128)(2,1)} %slice.396), channel_id=1, source_target_pairs={{0,3},{4,7},{8,11},{12,15},{16,19},{20,23},{24,27},{28,31}} | collective-permute-start | bytes 1966088 | tf_op jit(solution)/shard_map/ppermute | solution.py:82
  512.1 132.3 %collective-permute-start.12 = (bf16[512,2048]{1,0:T(8,128)(2,1)S(1)}, bf16[512,2048]{1,0:T(8,128)(2,1)}, u32[]{:S(2)}, u32[]{:S(2)}) collective-permute-start(bf16[512,2048]{1,0:T(8,128)(2,1)S(1)} %multiply_convert_fusion.2), channel_id=1, source_target_pairs={{0,1},{1,2},{2,3},{4,5},{5,6},{6,7},{8,9},{9,10},{10,11},{12,13},{... | collective-permute-start | bytes 6291464 | tf_op jit(solution)/shard_map/ppermute | solution.py:44
  517.5 129.0 %collective-permute-start.15 = (bf16[512,2048]{1,0:T(8,128)(2,1)S(1)}, bf16[512,2048]{1,0:T(8,128)(2,1)}, u32[]{:S(2)}, u32[]{:S(2)}) collective-permute-start(bf16[512,2048]{1,0:T(8,128)(2,1)S(1)} %multiply_convert_fusion.2), channel_id=1, source_target_pairs={{1,0},{2,1},{3,2},{5,4},{6,5},{7,6},{9,8},{10,9},{11,10},{13,12},{... | collective-permute-start | bytes 6291464 | tf_op jit(solution)/shard_map/ppermute | solution.py:45
  519.0 74.2 %collective-permute-start.24 = (bf16[512,1408]{1,0:T(8,128)(2,1)S(1)}, bf16[512,1408]{1,0:T(8,128)(2,1)S(1)}, u32[]{:S(2)}, u32[]{:S(2)}) collective-permute-start(bf16[512,1408]{1,0:T(8,128)(2,1)S(1)} %slice.395), channel_id=1, source_target_pairs={{0,3},{4,7},{8,11},{12,15},{16,19},{20,23},{24,27},{28,31}} | collective-permute-start | bytes 4325384 | tf_op jit(solution)/shard_map/ppermute | solution.py:82
  562.9 80.3 %collective-permute-start.26 = (bf16[512,1408]{1,0:T(8,128)(2,1)S(1)}, bf16[512,1408]{1,0:T(8,128)(2,1)S(1)}, u32[]{:S(2)}, u32[]{:S(2)}) collective-permute-start(bf16[512,1408]{1,0:T(8,128)(2,1)S(1)} %slice.395), channel_id=1, source_target_pairs={{0,1},{1,2},{2,3},{4,5},{5,6},{6,7},{8,9},{9,10},{10,11},{12,13},{... | collective-permute-start | bytes 4325384 | tf_op jit(solution)/shard_map/ppermute | solution.py:82
  624.0 105.5 %collective-permute-start.28 = (bf16[512,1408]{1,0:T(8,128)(2,1)S(1)}, bf16[512,1408]{1,0:T(8,128)(2,1)}, u32[]{:S(2)}, u32[]{:S(2)}) collective-permute-start(bf16[512,1408]{1,0:T(8,128)(2,1)S(1)} %slice.395), channel_id=1, source_target_pairs={{2,0},{3,1},{6,4},{7,5},{10,8},{11,9},{14,12},{15,13},{18,16},{19,... | collective-permute-start | bytes 4325384 | tf_op jit(solution)/shard_map/ppermute | solution.py:83
  643.1 86.4 %collective-permute-start.29 = (bf16[512,1408]{1,0:T(8,128)(2,1)S(1)}, bf16[512,1408]{1,0:T(8,128)(2,1)}, u32[]{:S(2)}, u32[]{:S(2)}) collective-permute-start(bf16[512,1408]{1,0:T(8,128)(2,1)S(1)} %slice.395), channel_id=1, source_target_pairs={{3,0},{7,4},{11,8},{15,12},{19,16},{23,20},{27,24},{31,28}} | collective-permute-start | bytes 4325384 | tf_op jit(solution)/shard_map/ppermute | solution.py:83
  644.4 87.8 %collective-permute-start.13 = (bf16[512,2048]{1,0:T(8,128)(2,1)}, bf16[512,2048]{1,0:T(8,128)(2,1)}, u32[]{:S(2)}, u32[]{:S(2)}) collective-permute-start(bf16[512,2048]{1,0:T(8,128)(2,1)} %collective-permute-done.12), channel_id=1, source_target_pairs={{1,2},{2,3},{5,6},{6,7},{9,10},{10,11},{13,14},{14,15},{17,18},{18... | collective-permute-start | bytes 6291464 | tf_op jit(solution)/shard_map/ppermute | solution.py:44
  646.5 122.7 %collective-permute-start.16 = (bf16[512,2048]{1,0:T(8,128)(2,1)}, bf16[512,2048]{1,0:T(8,128)(2,1)}, u32[]{:S(2)}, u32[]{:S(2)}) collective-permute-start(bf16[512,2048]{1,0:T(8,128)(2,1)} %collective-permute-done.15), channel_id=1, source_target_pairs={{1,0},{2,1},{5,4},{6,5},{9,8},{10,9},{13,12},{14,13},{17,16},{18,1... | collective-permute-start | bytes 6291464 | tf_op jit(solution)/shard_map/ppermute | solution.py:45
  648.8 1122.8 %reduce-scatter.9.cloned.1.call-start = ((), (), s32[]{:S(2)}) async-start(), calls=%async_computation.14 | async-start | bytes 1179648 | tf_op jit(solution)/shard_map/reduce_scatter | solution.py:432
  732.3 84.2 %collective-permute-start.14 = (bf16[512,2048]{1,0:T(8,128)(2,1)}, bf16[512,2048]{1,0:T(8,128)(2,1)S(1)}, u32[]{:S(2)}, u32[]{:S(2)}) collective-permute-start(bf16[512,2048]{1,0:T(8,128)(2,1)} %collective-permute-done.13), channel_id=1, source_target_pairs={{2,3},{6,7},{10,11},{14,15},{18,19},{22,23},{26,27},{30,31}} | collective-permute-start | bytes 6291464 | tf_op jit(solution)/shard_map/ppermute | solution.py:44
  1058.5 88.8 %collective-permute-start.41 = (bf16[512,2048]{1,0:T(8,128)(2,1)S(1)}, bf16[512,2048]{1,0:T(8,128)(2,1)S(1)}, u32[]{:S(2)}, u32[]{:S(2)}) collective-permute-start(bf16[512,2048]{1,0:T(8,128)(2,1)S(1)} %add_convert_fusion.4), channel_id=1, source_target_pairs={{1,0},{2,1},{3,2},{5,4},{6,5},{7,6},{9,8},{10,9},{11,10},{13,12},{... | collective-permute-start | bytes 6291464 | tf_op jit(solution)/shard_map/ppermute | solution.py:69
  1463.8 309.6 %reduce-scatter.11.cloned.1.call-start = ((), (), s32[]{:S(2)}) async-start(), calls=%async_computation.15 | async-start | bytes 1179648 | tf_op jit(solution)/shard_map/reduce_scatter | solution.py:438
  1464.5 310.5 %reduce-scatter.7.cloned.1.call-start = ((), (), s32[]{:S(2)}) async-start(), calls=%async_computation.13 | async-start | bytes 2359296 | tf_op jit(solution)/shard_map/reduce_scatter | solution.py:429
  1467.6 309.1 %reduce-scatter.13.cloned.1.call-start = ((), (), s32[]{:S(2)}) async-start(), calls=%async_computation.16 | async-start | bytes 2359296 | tf_op jit(solution)/shard_map/reduce_scatter | solution.py:386
  1468.4 364.5 %reduce-scatter.17.cloned.1.call-start = ((), (), s32[]{:S(2)}) async-start(), calls=%async_computation.18 | async-start | bytes 7077888 | tf_op jit(solution)/shard_map/reduce_scatter | solution.py:391
  1469.0 366.3 %reduce-scatter.15.cloned.1.call-start = ((), (), s32[]{:S(2)}) async-start(), calls=%async_computation.17 | async-start | bytes 14155776 | tf_op jit(solution)/shard_map/reduce_scatter | solution.py:382
  1608.0 79.6 %collective-permute-start.50 = (bf16[512,2048]{1,0:T(8,128)(2,1)S(1)}, bf16[512,2048]{1,0:T(8,128)(2,1)}, u32[]{:S(2)}, u32[]{:S(2)}) collective-permute-start(bf16[512,2048]{1,0:T(8,128)(2,1)S(1)} %copy-done.70), channel_id=1, source_target_pairs={{0,1},{1,2},{2,3},{4,5},{5,6},{6,7},{8,9},{9,10},{10,11},{12,13},{... | collective-permute-start | bytes 6291464 | tf_op jit(solution)/shard_map/ppermute | solution.py:68
  1618.2 105.9 %collective-permute-start.53 = (bf16[512,2048]{1,0:T(8,128)(2,1)S(1)}, bf16[512,2048]{1,0:T(8,128)(2,1)}, u32[]{:S(2)}, u32[]{:S(2)}) collective-permute-start(bf16[512,2048]{1,0:T(8,128)(2,1)S(1)} %add_convert_fusion), channel_id=1, source_target_pairs={{1,0},{2,1},{3,2},{5,4},{6,5},{7,6},{9,8},{10,9},{11,10},{13,12},{... | collective-permute-start | bytes 6291464 | tf_op jit(solution)/shard_map/ppermute | solution.py:69
  1619.5 197.6 %collective-permute-start.22 = (bf16[512,2048]{1,0:T(8,128)(2,1)}, bf16[512,2048]{1,0:T(8,128)(2,1)}, u32[]{:S(2)}, u32[]{:S(2)}) collective-permute-start(bf16[512,2048]{1,0:T(8,128)(2,1)} %get-tuple-element.174), channel_id=1, source_target_pairs={{0,3},{4,7},{8,11},{12,15},{16,19},{20,23},{24,27},{28,31}} | collective-permute-start | bytes 6291464 | tf_op jit(solution)/shard_map/ppermute | solution.py:98
  1678.1 139.0 %collective-permute-start.21 = (bf16[512,2048]{1,0:T(8,128)(2,1)}, bf16[512,2048]{1,0:T(8,128)(2,1)}, u32[]{:S(2)}, u32[]{:S(2)}) collective-permute-start(bf16[512,2048]{1,0:T(8,128)(2,1)} %get-tuple-element.175), channel_id=1, source_target_pairs={{2,0},{3,1},{6,4},{7,5},{10,8},{11,9},{14,12},{15,13},{18,16},{19,... | collective-permute-start | bytes 6291464 | tf_op jit(solution)/shard_map/ppermute | solution.py:103
  1679.4 137.7 %collective-permute-start.20 = (bf16[512,2048]{1,0:T(8,128)(2,1)}, bf16[512,2048]{1,0:T(8,128)(2,1)}, u32[]{:S(2)}, u32[]{:S(2)}) collective-permute-start(bf16[512,2048]{1,0:T(8,128)(2,1)} %get-tuple-element.176), channel_id=1, source_target_pairs={{0,2},{1,3},{4,6},{5,7},{8,10},{9,11},{12,14},{13,15},{16,18},{17,... | collective-permute-start | bytes 6291464 | tf_op jit(solution)/shard_map/ppermute | solution.py:98
  1687.6 129.6 %collective-permute-start.19 = (bf16[512,2048]{1,0:T(8,128)(2,1)}, bf16[512,2048]{1,0:T(8,128)(2,1)}, u32[]{:S(2)}, u32[]{:S(2)}) collective-permute-start(bf16[512,2048]{1,0:T(8,128)(2,1)} %get-tuple-element.177), channel_id=1, source_target_pairs={{1,0},{2,1},{3,2},{5,4},{6,5},{7,6},{9,8},{10,9},{11,10},{13,12},{... | collective-permute-start | bytes 6291464 | tf_op jit(solution)/shard_map/ppermute | solution.py:103
  1724.2 93.1 %collective-permute-start.18 = (bf16[512,2048]{1,0:T(8,128)(2,1)}, bf16[512,2048]{1,0:T(8,128)(2,1)}, u32[]{:S(2)}, u32[]{:S(2)}) collective-permute-start(bf16[512,2048]{1,0:T(8,128)(2,1)} %get-tuple-element.172), channel_id=1, source_target_pairs={{0,1},{1,2},{2,3},{4,5},{5,6},{6,7},{8,9},{9,10},{10,11},{12,13},{... | collective-permute-start | bytes 6291464 | tf_op jit(solution)/shard_map/ppermute | solution.py:98
  (204 other events, 6913.8 us)
Sparse Core Ops, SparseCore 0:
  10.5 30.5 all-gather.8
  43.5 23.3 all-gather.10
  69.3 23.3 all-gather.12
  94.5 28.0 all-gather.14
  124.4 45.3 all-gather.16
  353.1 42.6 all-gather.18
  649.0 93.1 all-gather.20
  1463.9 33.1 reduce-scatter.8
  1500.8 35.9 reduce-scatter.10
  1540.0 41.0 reduce-scatter.6
  1584.4 41.1 reduce-scatter.12
  1628.8 61.5 reduce-scatter.16
  1693.9 92.5 reduce-scatter.14

commit v11 on v10

--- a/solution.py
+++ b/solution.py
@@ -192,6 +192,10 @@
         block_lse = log_totals[index]
         q_rows = query_tensor[row_start:key_end]
         g_rows = grad_rows[row_start:key_end]
+        if index > 0:
+            q_rows, g_rows, block_lse, d_key, d_value = lax.optimization_barrier(
+                (q_rows, g_rows, block_lse, d_key, d_value)
+            )
         keys = key_rows[:key_end]
         values = value_tensor[:key_end]
         allowed = block_mask(seq_starts, seq_pieces, row_start, QB)[:, :key_end]
@@ -277,7 +281,7 @@
     gain_k = gk_b.astype(f32)
     normalized_input = rms_scale(tok_rows, attn_g).astype(bf16)
     gathered = tensor_gather(normalized_input, tensor_n)
-    half_width = (out_grad.shape[1] * 11 // 16) // 128 * 128
+    half_width = (out_grad.shape[1] * 3 // 4) // 128 * 128
     grad_half_a = tensor_gather_direct(out_grad[:, :half_width], tensor_n)
     projected = jnp.dot(gathered, w_qkv, preferred_element_type=f32)
     query_unrotated = projected[:, :q_width].reshape(

time: 1880 us -> 1870 us (level)
  waiting for transfers between devices: 814 us -> 792 us
    ppermute x6, waiting for transfers between devices: 113 us -> 74 us  [tensor_gather_direct(): downs[d] = lax.ppermute(rows, 'tensor', [(i, i - d) for i in range(d, n)])]
    ppermute x9, waiting for transfers between devices: 80 us -> 106 us  [tensor_gather(): up = lax.ppermute(up, 'tensor', [(i, i + 1) for i in range(s - 1, n - 1)])]
    ppermute x6, starting transfers between devices: 62 us -> 82.2 us  [tensor_gather_direct(): ups[d] = lax.ppermute(rows, 'tensor', [(i, i + d) for i in range(n - d)])]
    unnamed x343 -> x329, local copies, waits for them, and re-layouts: 39.6 us -> 42.2 us
  transfers between devices with their start and end apart: 67 -> 67, of which waited for: 25 -> 26; matrix products, arithmetic and copies ran while one was open for 22% -> 22% of each run, Pallas kernels for 0% -> 0%
where the time goes in v11:
time: 1870 us; the launch traced here: 1840 us
  waiting for transfers between devices  792 us (42%)
  matrix products  347 us (19%)
  starting transfers between devices  299 us (16%)
  other arithmetic  237 us (13%)
  local copies, waits for them, and re-layouts  104 us (6%)
  blocking collectives  41.6 us (2%)
    ppermute x9, waiting for transfers between devices, tensor_scatter(): lax.ppermute(acc_up.astype(jnp.bfloat16), 'tensor', [(i, i + 1) for i in...  281 us
    ppermute x9, waiting for transfers between devices, tensor_gather(): lax.ppermute(down, 'tensor', [(i, i - 1) for i in range(1, n - s + 1)])  145 us
    ppermute x9, waiting for transfers between devices, tensor_scatter(): lax.ppermute(acc_down.astype(jnp.bfloat16), 'tensor', [(i, i - 1) for i i...  113 us
    ppermute x3, starting transfers between devices, tensor_scatter_direct(): lax.ppermute(block(jnp.minimum(j + d, n - 1)).astype(jnp.bfloat16), 'tens...  113 us
    ppermute x9, waiting for transfers between devices, tensor_gather(): up = lax.ppermute(up, 'tensor', [(i, i + 1) for i in range(s - 1, n - 1)])  106 us
    ppermute x6, starting transfers between devices, tensor_gather_direct(): ups[d] = lax.ppermute(rows, 'tensor', [(i, i + d) for i in range(n - d)])  82.2 us
    ppermute x6, waiting for transfers between devices, tensor_gather_direct(): downs[d] = lax.ppermute(rows, 'tensor', [(i, i - d) for i in range(d, n)])  74 us
    ppermute x6, waiting for transfers between devices, tensor_gather_direct(): ups[d] = lax.ppermute(rows, 'tensor', [(i, i + d) for i in range(n - d)])  69.8 us
  transfers between devices with their start and end apart: 67, of which 26 were waited for; matrix products, arithmetic and copies ran while one was open for 22% of the time, Pallas kernels for 0%

profile of v11, /device:TPU:0, one launch (start us, length us, event | category | flops | bytes accessed | tf_op | source)
XLA Modules:
  0.0 1838.6 jit_solution(14909653276830358551)
XLA Ops:
  38.2 41.5 %collective-permute-done = bf16[512,2048]{1,0:T(8,128)(2,1)} collective-permute-done((bf16[512,2048]{1,0:T(8,128)(2,1)}, bf16[512,2048]{1,0:T(8,128)(2,1)}, u32[]{:S(2)}, u32[]{:S(2)}) %collective-permute-start) | collective-permute-done | bytes 2097184 | tf_op jit(solution)/shard_map/ppermute | solution.py:44
  93.8 40.5 %collective-permute-done.4 = bf16[512,2048]{1,0:T(8,128)(2,1)} collective-permute-done((bf16[512,2048]{1,0:T(8,128)(2,1)}, bf16[512,2048]{1,0:T(8,128)(2,1)}, u32[]{:S(2)}, u32[]{:S(2)}) %collective-permute-start.4) | collective-permute-done | bytes 2097184 | tf_op jit(solution)/shard_map/ppermute | solution.py:45
  153.0 29.5 %collective-permute-done.5 = bf16[512,2048]{1,0:T(8,128)(2,1)} collective-permute-done((bf16[512,2048]{1,0:T(8,128)(2,1)}, bf16[512,2048]{1,0:T(8,128)(2,1)}, u32[]{:S(2)}, u32[]{:S(2)}) %collective-permute-start.5) | collective-permute-done | bytes 2097184 | tf_op jit(solution)/shard_map/ppermute | solution.py:45
  294.2 39.8 %collective-permute-done.6 = bf16[512,2048]{1,0:T(8,128)(2,1)} collective-permute-done((bf16[512,2048]{1,0:T(8,128)(2,1)}, bf16[512,2048]{1,0:T(8,128)(2,1)}, u32[]{:S(2)}, u32[]{:S(2)}) %collective-permute-start.6) | collective-permute-done | bytes 2097184 | tf_op jit(solution)/shard_map/ppermute | solution.py:68
  345.6 40.1 %collective-permute-done.7 = bf16[512,2048]{1,0:T(8,128)(2,1)} collective-permute-done((bf16[512,2048]{1,0:T(8,128)(2,1)}, bf16[512,2048]{1,0:T(8,128)(2,1)}, u32[]{:S(2)}, u32[]{:S(2)}) %collective-permute-start.7) | collective-permute-done | bytes 2097184 | tf_op jit(solution)/shard_map/ppermute | solution.py:68
  408.4 46.8 %collective-permute-start.30 = (bf16[512,512]{1,0:T(8,128)(2,1)S(1)}, bf16[512,512]{1,0:T(8,128)(2,1)S(1)}, u32[]{:S(2)}, u32[]{:S(2)}) collective-permute-start(bf16[512,512]{1,0:T(8,128)(2,1)S(1)} %slice.396), channel_id=1, source_target_pairs={{0,3},{4,7},{8,11},{12,15},{16,19},{20,23},{24,27},{28,31}} | collective-permute-start | bytes 1572872 | tf_op jit(solution)/shard_map/ppermute | solution.py:82
  464.6 31.7 %collective-permute-done.11 = bf16[512,2048]{1,0:T(8,128)(2,1)} collective-permute-done((bf16[512,2048]{1,0:T(8,128)(2,1)}, bf16[512,2048]{1,0:T(8,128)(2,1)}, u32[]{:S(2)}, u32[]{:S(2)}) %collective-permute-start.11) | collective-permute-done | bytes 2097184 | tf_op jit(solution)/shard_map/ppermute | solution.py:69
  512.4 21.4 %collective-permute-start.26 = (bf16[512,1536]{1,0:T(8,128)(2,1)}, bf16[512,1536]{1,0:T(8,128)(2,1)S(1)}, u32[]{:S(2)}, u32[]{:S(2)}) collective-permute-start(bf16[512,1536]{1,0:T(8,128)(2,1)} %slice.395), channel_id=1, source_target_pairs={{0,1},{1,2},{2,3},{4,5},{5,6},{6,7},{8,9},{9,10},{10,11},{12,13},{... | collective-permute-start | bytes 4718600 | tf_op jit(solution)/shard_map/ppermute | solution.py:82
  547.3 32.4 %collective-permute-done.25 = bf16[512,1536]{1,0:T(8,128)(2,1)S(1)} collective-permute-done((bf16[512,1536]{1,0:T(8,128)(2,1)}, bf16[512,1536]{1,0:T(8,128)(2,1)S(1)}, u32[]{:S(2)}, u32[]{:S(2)}) %collective-permute-start.25) | collective-permute-done | bytes 1572896 | tf_op jit(solution)/shard_map/ppermute | solution.py:82
  581.1 32.2 %collective-permute-done.26 = bf16[512,1536]{1,0:T(8,128)(2,1)S(1)} collective-permute-done((bf16[512,1536]{1,0:T(8,128)(2,1)}, bf16[512,1536]{1,0:T(8,128)(2,1)S(1)}, u32[]{:S(2)}, u32[]{:S(2)}) %collective-permute-start.26) | collective-permute-done | bytes 1572896 | tf_op jit(solution)/shard_map/ppermute | solution.py:82
  614.7 31.4 %collective-permute-done.12 = bf16[512,2048]{1,0:T(8,128)(2,1)} collective-permute-done((bf16[512,2048]{1,0:T(8,128)(2,1)S(1)}, bf16[512,2048]{1,0:T(8,128)(2,1)}, u32[]{:S(2)}, u32[]{:S(2)}) %collective-permute-start.12) | collective-permute-done | bytes 2097184 | tf_op jit(solution)/shard_map/ppermute | solution.py:44
  652.5 71.3 %collective-permute-done.28 = bf16[512,1536]{1,0:T(8,128)(2,1)} collective-permute-done((bf16[512,1536]{1,0:T(8,128)(2,1)}, bf16[512,1536]{1,0:T(8,128)(2,1)}, u32[]{:S(2)}, u32[]{:S(2)}) %collective-permute-start.28) | collective-permute-done | bytes 1572896 | tf_op jit(solution)/shard_map/ppermute | solution.py:83
  727.4 34.5 %collective-permute-done.16 = bf16[512,2048]{1,0:T(8,128)(2,1)} collective-permute-done((bf16[512,2048]{1,0:T(8,128)(2,1)}, bf16[512,2048]{1,0:T(8,128)(2,1)}, u32[]{:S(2)}, u32[]{:S(2)}) %collective-permute-start.16) | collective-permute-done | bytes 2097184 | tf_op jit(solution)/shard_map/ppermute | solution.py:45
  763.2 33.9 %maximum_maximum_fusion = bf16[2048,2048]{1,0:T(8,128)(2,1)} fusion(bf16[512,512]{1,0:T(8,128)(2,1)S(1)} %get-tuple-element.243, bf16[512,512]{1,0:T(8,128)(2,1)S(1)} %get-tuple-element.242, bf16[512,512]{1,0:T(8,128)(2,1)S(1)} %get-tuple-element.241, bf16[512,512]{1,0:T(8,128)(2,1)S(1)} %get-tuple-element.240, bf16[512,1536]{1,0:T(8,128)(2,1)S(1)} %get-tuple-element.229, ...), kind=kLoop, calls=%fused_computation.38 | loop fusion | flops 67108864 | bytes 16777216 | tf_op jit(solution)/shard_map/concatenate | solution.py:342
  820.6 33.2 %fusion.170 = f32[2048,3072]{1,0:T(8,128)} fusion(bf16[2048,3072]{1,0:T(8,128)(2,1)} %constant_dynamic-update-slice_fusion.3, bf16[512,2048]{1,0:T(8,128)(2,1)S(1)} %get-tuple-element.219, bf16[512,2048]{1,0:T(8,128)(2,1)S(1)} %get-tuple-element.218, bf16[512,2048]{1,0:T(8,128)(2,1)S(1)} %get-tuple-element.217, bf16[512,2048]{1,0:T(8,128)(2,1)S(1)} %get-tuple-element.216), kind=kOutput, calls=%fused_computation.330 | convolution fusion | flops 25803358208 | bytes 46137344 | tf_op jit(solution)/shard_map/dot_general | solution.py:329
  853.8 50.7 %fusion.9 = (bf16[2048,1536]{1,0:T(8,128)(2,1)}, bf16[2048,1536]{1,0:T(8,128)(2,1)}, bf16[2048,1536]{1,0:T(8,128)(2,1)}) fusion(f32[2048,3072]{1,0:T(8,128)} %fusion.170, bf16[1536,2048]{1,0:T(8,128)(2,1)} %all-gather.21.cloned.1.call-done, bf16[512,512]{1,0:T(8,128)(2,1)} %copy-done.81, bf16[512,512]{1,0:T(8,128)(2,1)} %copy-done.80, ...), kind=kOutput, calls=%fused_computation.16 | convolution fusion | flops 13002342400 | bytes 58720256 | tf_op jit(solution)/shard_map/dot_general | solution.py:343
  904.5 34.4 %fusion.169 = f32[2048,2048]{1,0:T(8,128)} fusion(bf16[2048,3072]{1,0:T(8,128)(2,1)} %constant_dynamic-update-slice_fusion.3, bf16[2048,1536]{1,0:T(8,128)(2,1)} %get-tuple-element.192, bf16[2048,1536]{1,0:T(8,128)(2,1)} %get-tuple-element.191), kind=kOutput, calls=%fused_computation.329 | convolution fusion | flops 25794969600 | bytes 41943040 | tf_op jit(solution)/shard_map/dot_general | solution.py:352
  958.8 43.7 %collective-permute-done.36 = bf16[512,2048]{1,0:T(8,128)(2,1)S(1)} collective-permute-done((bf16[512,2048]{1,0:T(8,128)(2,1)S(1)}, bf16[512,2048]{1,0:T(8,128)(2,1)S(1)}, u32[]{:S(2)}, u32[]{:S(2)}) %collective-permute-start.36) | collective-permute-done | bytes 2097184 | tf_op jit(solution)/shard_map/ppermute | solution.py:68
  1009.0 42.4 %collective-permute-done.37 = bf16[512,2048]{1,0:T(8,128)(2,1)} collective-permute-done((bf16[512,2048]{1,0:T(8,128)(2,1)S(1)}, bf16[512,2048]{1,0:T(8,128)(2,1)}, u32[]{:S(2)}, u32[]{:S(2)}) %collective-permute-start.37) | collective-permute-done | bytes 2097184 | tf_op jit(solution)/shard_map/ppermute | solution.py:68
  1065.2 40.8 %collective-permute-done.38 = bf16[512,2048]{1,0:T(8,128)(2,1)S(1)} collective-permute-done((bf16[512,2048]{1,0:T(8,128)(2,1)}, bf16[512,2048]{1,0:T(8,128)(2,1)S(1)}, u32[]{:S(2)}, u32[]{:S(2)}) %collective-permute-start.38) | collective-permute-done | bytes 2097184 | tf_op jit(solution)/shard_map/ppermute | solution.py:68
  1106.1 46.4 %collective-permute-done.41 = bf16[512,2048]{1,0:T(8,128)(2,1)S(1)} collective-permute-done((bf16[512,2048]{1,0:T(8,128)(2,1)S(1)}, bf16[512,2048]{1,0:T(8,128)(2,1)S(1)}, u32[]{:S(2)}, u32[]{:S(2)}) %collective-permute-start.41) | collective-permute-done | bytes 2097184 | tf_op jit(solution)/shard_map/ppermute | solution.py:69
  1172.1 33.2 %collective-permute-done.42 = bf16[512,2048]{1,0:T(8,128)(2,1)} collective-permute-done((bf16[512,2048]{1,0:T(8,128)(2,1)S(1)}, bf16[512,2048]{1,0:T(8,128)(2,1)}, u32[]{:S(2)}, u32[]{:S(2)}) %collective-permute-start.42) | collective-permute-done | bytes 2097184 | tf_op jit(solution)/shard_map/ppermute | solution.py:44
  1212.4 33.0 %fusion.177 = bf16[2048,3072]{1,0:T(8,128)(2,1)} fusion(bf16[2048,2048]{1,0:T(8,128)(2,1)} %pad_maximum_fusion.2, bf16[2048,3072]{1,0:T(8,128)(2,1)} %pad_maximum_fusion), kind=kOutput, calls=%fused_computation.337 | convolution fusion | flops 25769803776 | bytes 33554432 | tf_op jit(solution)/shard_map/dot_general | solution.py:357
  1258.2 19.5 %fusion.178 = bf16[1536,2048]{1,0:T(8,128)(2,1)} fusion(bf16[2048,1536]{1,0:T(8,128)(2,1)} %get-tuple-element.193, bf16[2048,2048]{1,0:T(8,128)(2,1)} %maximum_maximum_fusion), kind=kOutput, calls=%fused_computation.338 | convolution fusion | flops 12884901888 | bytes 20971520 | tf_op jit(solution)/shard_map/dot_general | solution.py:356
  1277.7 23.1 %collective-permute-done.47 = bf16[512,2048]{1,0:T(8,128)(2,1)} collective-permute-done((bf16[512,2048]{1,0:T(8,128)(2,1)}, bf16[512,2048]{1,0:T(8,128)(2,1)}, u32[]{:S(2)}, u32[]{:S(2)}) %collective-permute-start.47) | collective-permute-done | bytes 2097184 | tf_op jit(solution)/shard_map/ppermute | solution.py:45
  1480.6 37.8 %collective-permute-done.48 = bf16[512,2048]{1,0:T(8,128)(2,1)S(1)} collective-permute-done((bf16[512,2048]{1,0:T(8,128)(2,1)S(1)}, bf16[512,2048]{1,0:T(8,128)(2,1)S(1)}, u32[]{:S(2)}, u32[]{:S(2)}) %collective-permute-start.48) | collective-permute-done | bytes 2097184 | tf_op jit(solution)/shard_map/ppermute | solution.py:68
  1525.0 36.2 %collective-permute-done.49 = bf16[512,2048]{1,0:T(8,128)(2,1)} collective-permute-done((bf16[512,2048]{1,0:T(8,128)(2,1)S(1)}, bf16[512,2048]{1,0:T(8,128)(2,1)}, u32[]{:S(2)}, u32[]{:S(2)}) %collective-permute-start.49) | collective-permute-done | bytes 2097184 | tf_op jit(solution)/shard_map/ppermute | solution.py:68
  1568.1 19.6 %fusion.176 = f32[2048,2048]{1,0:T(8,128)} fusion(bf16[2048,1536]{1,0:T(8,128)(2,1)} %get-tuple-element.193, bf16[1536,2048]{1,0:T(8,128)(2,1)} %all-gather.21.cloned.1.call-done), kind=kOutput, calls=%fused_computation.336 | convolution fusion | flops 12884901888 | bytes 29360128 | tf_op jit(solution)/shard_map/dot_general | solution.py:333
  1612.9 58.7 %collective-permute-start.22 = (bf16[512,2048]{1,0:T(8,128)(2,1)}, bf16[512,2048]{1,0:T(8,128)(2,1)}, u32[]{:S(2)}, u32[]{:S(2)}) collective-permute-start(bf16[512,2048]{1,0:T(8,128)(2,1)} %get-tuple-element.204), channel_id=1, source_target_pairs={{0,3},{4,7},{8,11},{12,15},{16,19},{20,23},{24,27},{28,31}} | collective-permute-start | bytes 6291464 | tf_op jit(solution)/shard_map/ppermute | solution.py:98
  1682.5 35.0 %collective-permute-done.53 = bf16[512,2048]{1,0:T(8,128)(2,1)} collective-permute-done((bf16[512,2048]{1,0:T(8,128)(2,1)S(1)}, bf16[512,2048]{1,0:T(8,128)(2,1)}, u32[]{:S(2)}, u32[]{:S(2)}) %collective-permute-start.53) | collective-permute-done | bytes 2097184 | tf_op jit(solution)/shard_map/ppermute | solution.py:69
  1717.5 45.9 %collective-permute-start.18 = (bf16[512,2048]{1,0:T(8,128)(2,1)}, bf16[512,2048]{1,0:T(8,128)(2,1)}, u32[]{:S(2)}, u32[]{:S(2)}) collective-permute-start(bf16[512,2048]{1,0:T(8,128)(2,1)} %get-tuple-element.202), channel_id=1, source_target_pairs={{0,1},{1,2},{2,3},{4,5},{5,6},{6,7},{8,9},{9,10},{10,11},{12,13},{... | collective-permute-start | bytes 6291464 | tf_op jit(solution)/shard_map/ppermute | solution.py:98
  1792.4 18.0 all-reduce.10
  (626 shorter events, 641.9 us)
Async XLA Ops:
  7.2 138.2 %all-gather.9.cloned.1.call-start = ((), (), s32[]{:S(2)}) async-start(), calls=%async_computation.6 | async-start | bytes 2359296 | tf_op jit(solution)/shard_map/all_gather | solution.py:264
  9.2 139.3 %all-gather.11.cloned.1.call-start = ((), (), s32[]{:S(2)}) async-start(), calls=%async_computation.7 | async-start | bytes 1179648 | tf_op jit(solution)/shard_map/all_gather | solution.py:265
  10.9 139.9 %all-gather.13.cloned.1.call-start = ((), (), s32[]{:S(2)}) async-start(), calls=%async_computation.8 | async-start | bytes 1179648 | tf_op jit(solution)/shard_map/all_gather | solution.py:266
  12.6 261.6 %all-gather.15.cloned.1.call-start = ((), (), s32[]{:S(2)}) async-start(), calls=%async_computation.9 | async-start | bytes 2359296 | tf_op jit(solution)/shard_map/all_gather | solution.py:267
  14.4 782.7 %all-gather.17.cloned.1.call-start = ((), (), s32[]{:S(2)}) async-start(), calls=%async_computation.10 | async-start | bytes 7077888 | tf_op jit(solution)/shard_map/all_gather | solution.py:317
  37.6 765.4 %all-gather.19.cloned.1.call-start = ((), (), s32[]{:S(2)}) async-start(), calls=%async_computation.11 | async-start | bytes 7077888 | tf_op jit(solution)/shard_map/all_gather | solution.py:318
  345.5 508.2 %all-gather.21.cloned.1.call-start = ((), (), s32[]{:S(2)}) async-start(), calls=%async_computation.12 | async-start | bytes 7077888 | tf_op jit(solution)/shard_map/all_gather | solution.py:319
  405.9 90.3 %collective-permute-start.11 = (bf16[512,2048]{1,0:T(8,128)(2,1)}, bf16[512,2048]{1,0:T(8,128)(2,1)}, u32[]{:S(2)}, u32[]{:S(2)}) collective-permute-start(bf16[512,2048]{1,0:T(8,128)(2,1)} %add_convert_fusion.9), channel_id=1, source_target_pairs={{1,0},{2,1},{3,2},{5,4},{6,5},{7,6},{9,8},{10,9},{11,10},{13,12},{... | collective-permute-start | bytes 6291464 | tf_op jit(solution)/shard_map/ppermute | solution.py:69
  408.4 93.8 %collective-permute-start.30 = (bf16[512,512]{1,0:T(8,128)(2,1)S(1)}, bf16[512,512]{1,0:T(8,128)(2,1)S(1)}, u32[]{:S(2)}, u32[]{:S(2)}) collective-permute-start(bf16[512,512]{1,0:T(8,128)(2,1)S(1)} %slice.396), channel_id=1, source_target_pairs={{0,3},{4,7},{8,11},{12,15},{16,19},{20,23},{24,27},{28,31}} | collective-permute-start | bytes 1572872 | tf_op jit(solution)/shard_map/ppermute | solution.py:82
  512.4 101.0 %collective-permute-start.26 = (bf16[512,1536]{1,0:T(8,128)(2,1)}, bf16[512,1536]{1,0:T(8,128)(2,1)S(1)}, u32[]{:S(2)}, u32[]{:S(2)}) collective-permute-start(bf16[512,1536]{1,0:T(8,128)(2,1)} %slice.395), channel_id=1, source_target_pairs={{0,1},{1,2},{2,3},{4,5},{5,6},{6,7},{8,9},{9,10},{10,11},{12,13},{... | collective-permute-start | bytes 4718600 | tf_op jit(solution)/shard_map/ppermute | solution.py:82
  537.0 109.1 %collective-permute-start.12 = (bf16[512,2048]{1,0:T(8,128)(2,1)S(1)}, bf16[512,2048]{1,0:T(8,128)(2,1)}, u32[]{:S(2)}, u32[]{:S(2)}) collective-permute-start(bf16[512,2048]{1,0:T(8,128)(2,1)S(1)} %multiply_convert_fusion.2), channel_id=1, source_target_pairs={{0,1},{1,2},{2,3},{4,5},{5,6},{6,7},{8,9},{9,10},{10,11},{12,13},{... | collective-permute-start | bytes 6291464 | tf_op jit(solution)/shard_map/ppermute | solution.py:44
  539.6 108.4 %collective-permute-start.15 = (bf16[512,2048]{1,0:T(8,128)(2,1)S(1)}, bf16[512,2048]{1,0:T(8,128)(2,1)}, u32[]{:S(2)}, u32[]{:S(2)}) collective-permute-start(bf16[512,2048]{1,0:T(8,128)(2,1)S(1)} %multiply_convert_fusion.2), channel_id=1, source_target_pairs={{1,0},{2,1},{3,2},{5,4},{6,5},{7,6},{9,8},{10,9},{11,10},{13,12},{... | collective-permute-start | bytes 6291464 | tf_op jit(solution)/shard_map/ppermute | solution.py:45
  546.0 106.6 %collective-permute-start.27 = (bf16[512,1536]{1,0:T(8,128)(2,1)}, bf16[512,1536]{1,0:T(8,128)(2,1)}, u32[]{:S(2)}, u32[]{:S(2)}) collective-permute-start(bf16[512,1536]{1,0:T(8,128)(2,1)} %slice.395), channel_id=1, source_target_pairs={{1,0},{2,1},{3,2},{5,4},{6,5},{7,6},{9,8},{10,9},{11,10},{13,12},{... | collective-permute-start | bytes 4718600 | tf_op jit(solution)/shard_map/ppermute | solution.py:83
  579.7 144.1 %collective-permute-start.28 = (bf16[512,1536]{1,0:T(8,128)(2,1)}, bf16[512,1536]{1,0:T(8,128)(2,1)}, u32[]{:S(2)}, u32[]{:S(2)}) collective-permute-start(bf16[512,1536]{1,0:T(8,128)(2,1)} %slice.395), channel_id=1, source_target_pairs={{2,0},{3,1},{6,4},{7,5},{10,8},{11,9},{14,12},{15,13},{18,16},{19,... | collective-permute-start | bytes 4718600 | tf_op jit(solution)/shard_map/ppermute | solution.py:83
  613.4 110.4 %collective-permute-start.29 = (bf16[512,1536]{1,0:T(8,128)(2,1)}, bf16[512,1536]{1,0:T(8,128)(2,1)}, u32[]{:S(2)}, u32[]{:S(2)}) collective-permute-start(bf16[512,1536]{1,0:T(8,128)(2,1)} %slice.395), channel_id=1, source_target_pairs={{3,0},{7,4},{11,8},{15,12},{19,16},{23,20},{27,24},{31,28}} | collective-permute-start | bytes 4718600 | tf_op jit(solution)/shard_map/ppermute | solution.py:83
  646.0 80.6 %collective-permute-start.13 = (bf16[512,2048]{1,0:T(8,128)(2,1)}, bf16[512,2048]{1,0:T(8,128)(2,1)}, u32[]{:S(2)}, u32[]{:S(2)}) collective-permute-start(bf16[512,2048]{1,0:T(8,128)(2,1)} %collective-permute-done.12), channel_id=1, source_target_pairs={{1,2},{2,3},{5,6},{6,7},{9,10},{10,11},{13,14},{14,15},{17,18},{18... | collective-permute-start | bytes 6291464 | tf_op jit(solution)/shard_map/ppermute | solution.py:44
  648.0 113.9 %collective-permute-start.16 = (bf16[512,2048]{1,0:T(8,128)(2,1)}, bf16[512,2048]{1,0:T(8,128)(2,1)}, u32[]{:S(2)}, u32[]{:S(2)}) collective-permute-start(bf16[512,2048]{1,0:T(8,128)(2,1)} %collective-permute-done.15), channel_id=1, source_target_pairs={{1,0},{2,1},{5,4},{6,5},{9,8},{10,9},{13,12},{14,13},{17,16},{18,1... | collective-permute-start | bytes 6291464 | tf_op jit(solution)/shard_map/ppermute | solution.py:45
  650.4 1114.9 %reduce-scatter.9.cloned.1.call-start = ((), (), s32[]{:S(2)}) async-start(), calls=%async_computation.14 | async-start | bytes 1179648 | tf_op jit(solution)/shard_map/reduce_scatter | solution.py:436
  726.6 82.5 %collective-permute-start.14 = (bf16[512,2048]{1,0:T(8,128)(2,1)}, bf16[512,2048]{1,0:T(8,128)(2,1)S(1)}, u32[]{:S(2)}, u32[]{:S(2)}) collective-permute-start(bf16[512,2048]{1,0:T(8,128)(2,1)} %collective-permute-done.13), channel_id=1, source_target_pairs={{2,3},{6,7},{10,11},{14,15},{18,19},{22,23},{26,27},{30,31}} | collective-permute-start | bytes 6291464 | tf_op jit(solution)/shard_map/ppermute | solution.py:44
  1063.8 88.7 %collective-permute-start.41 = (bf16[512,2048]{1,0:T(8,128)(2,1)S(1)}, bf16[512,2048]{1,0:T(8,128)(2,1)S(1)}, u32[]{:S(2)}, u32[]{:S(2)}) collective-permute-start(bf16[512,2048]{1,0:T(8,128)(2,1)S(1)} %add_convert_fusion.4), channel_id=1, source_target_pairs={{1,0},{2,1},{3,2},{5,4},{6,5},{7,6},{9,8},{10,9},{11,10},{13,12},{... | collective-permute-start | bytes 6291464 | tf_op jit(solution)/shard_map/ppermute | solution.py:69
  1457.0 309.9 %reduce-scatter.11.cloned.1.call-start = ((), (), s32[]{:S(2)}) async-start(), calls=%async_computation.15 | async-start | bytes 1179648 | tf_op jit(solution)/shard_map/reduce_scatter | solution.py:442
  1457.8 310.8 %reduce-scatter.7.cloned.1.call-start = ((), (), s32[]{:S(2)}) async-start(), calls=%async_computation.13 | async-start | bytes 2359296 | tf_op jit(solution)/shard_map/reduce_scatter | solution.py:433
  1460.9 309.5 %reduce-scatter.13.cloned.1.call-start = ((), (), s32[]{:S(2)}) async-start(), calls=%async_computation.16 | async-start | bytes 2359296 | tf_op jit(solution)/shard_map/reduce_scatter | solution.py:390
  1461.6 364.5 %reduce-scatter.17.cloned.1.call-start = ((), (), s32[]{:S(2)}) async-start(), calls=%async_computation.18 | async-start | bytes 7077888 | tf_op jit(solution)/shard_map/reduce_scatter | solution.py:395
  1462.2 366.3 %reduce-scatter.15.cloned.1.call-start = ((), (), s32[]{:S(2)}) async-start(), calls=%async_computation.17 | async-start | bytes 14155776 | tf_op jit(solution)/shard_map/reduce_scatter | solution.py:386
  1601.4 79.8 %collective-permute-start.50 = (bf16[512,2048]{1,0:T(8,128)(2,1)S(1)}, bf16[512,2048]{1,0:T(8,128)(2,1)}, u32[]{:S(2)}, u32[]{:S(2)}) collective-permute-start(bf16[512,2048]{1,0:T(8,128)(2,1)S(1)} %copy-done.70), channel_id=1, source_target_pairs={{0,1},{1,2},{2,3},{4,5},{5,6},{6,7},{8,9},{9,10},{10,11},{12,13},{... | collective-permute-start | bytes 6291464 | tf_op jit(solution)/shard_map/ppermute | solution.py:68
  1611.6 105.9 %collective-permute-start.53 = (bf16[512,2048]{1,0:T(8,128)(2,1)S(1)}, bf16[512,2048]{1,0:T(8,128)(2,1)}, u32[]{:S(2)}, u32[]{:S(2)}) collective-permute-start(bf16[512,2048]{1,0:T(8,128)(2,1)S(1)} %add_convert_fusion), channel_id=1, source_target_pairs={{1,0},{2,1},{3,2},{5,4},{6,5},{7,6},{9,8},{10,9},{11,10},{13,12},{... | collective-permute-start | bytes 6291464 | tf_op jit(solution)/shard_map/ppermute | solution.py:69
  1612.9 197.5 %collective-permute-start.22 = (bf16[512,2048]{1,0:T(8,128)(2,1)}, bf16[512,2048]{1,0:T(8,128)(2,1)}, u32[]{:S(2)}, u32[]{:S(2)}) collective-permute-start(bf16[512,2048]{1,0:T(8,128)(2,1)} %get-tuple-element.204), channel_id=1, source_target_pairs={{0,3},{4,7},{8,11},{12,15},{16,19},{20,23},{24,27},{28,31}} | collective-permute-start | bytes 6291464 | tf_op jit(solution)/shard_map/ppermute | solution.py:98
  1671.6 138.8 %collective-permute-start.21 = (bf16[512,2048]{1,0:T(8,128)(2,1)}, bf16[512,2048]{1,0:T(8,128)(2,1)}, u32[]{:S(2)}, u32[]{:S(2)}) collective-permute-start(bf16[512,2048]{1,0:T(8,128)(2,1)} %get-tuple-element.205), channel_id=1, source_target_pairs={{2,0},{3,1},{6,4},{7,5},{10,8},{11,9},{14,12},{15,13},{18,16},{19,... | collective-permute-start | bytes 6291464 | tf_op jit(solution)/shard_map/ppermute | solution.py:103
  1672.9 137.5 %collective-permute-start.20 = (bf16[512,2048]{1,0:T(8,128)(2,1)}, bf16[512,2048]{1,0:T(8,128)(2,1)}, u32[]{:S(2)}, u32[]{:S(2)}) collective-permute-start(bf16[512,2048]{1,0:T(8,128)(2,1)} %get-tuple-element.206), channel_id=1, source_target_pairs={{0,2},{1,3},{4,6},{5,7},{8,10},{9,11},{12,14},{13,15},{16,18},{17,... | collective-permute-start | bytes 6291464 | tf_op jit(solution)/shard_map/ppermute | solution.py:98
  1681.2 129.2 %collective-permute-start.19 = (bf16[512,2048]{1,0:T(8,128)(2,1)}, bf16[512,2048]{1,0:T(8,128)(2,1)}, u32[]{:S(2)}, u32[]{:S(2)}) collective-permute-start(bf16[512,2048]{1,0:T(8,128)(2,1)} %get-tuple-element.207), channel_id=1, source_target_pairs={{1,0},{2,1},{3,2},{5,4},{6,5},{7,6},{9,8},{10,9},{11,10},{13,12},{... | collective-permute-start | bytes 6291464 | tf_op jit(solution)/shard_map/ppermute | solution.py:103
  1717.5 92.9 %collective-permute-start.18 = (bf16[512,2048]{1,0:T(8,128)(2,1)}, bf16[512,2048]{1,0:T(8,128)(2,1)}, u32[]{:S(2)}, u32[]{:S(2)}) collective-permute-start(bf16[512,2048]{1,0:T(8,128)(2,1)} %get-tuple-element.202), channel_id=1, source_target_pairs={{0,1},{1,2},{2,3},{4,5},{5,6},{6,7},{8,9},{9,10},{10,11},{12,13},{... | collective-permute-start | bytes 6291464 | tf_op jit(solution)/shard_map/ppermute | solution.py:98
  (197 other events, 7314.9 us)
Sparse Core Ops, SparseCore 0:
  10.5 30.5 all-gather.8
  43.5 23.3 all-gather.10
  69.3 23.3 all-gather.12
  95.0 28.0 all-gather.14
  124.9 45.3 all-gather.16
  345.7 42.6 all-gather.18
  650.5 85.8 all-gather.20
  1457.2 33.8 reduce-scatter.8
  1494.8 35.9 reduce-scatter.10
  1533.9 41.1 reduce-scatter.6
  1578.4 41.1 reduce-scatter.12
  1622.7 61.5 reduce-scatter.16
  1687.9 92.5 reduce-scatter.14
